TPU v7x, 128 devices: a whole 4x4x4 slice. The times are simulated.
128 devices in a mesh: row: 4 (over y), col: 32 (over x, z, core).
Axes of the slice: x: 4, y: 4, z: 4, core: 2. Of those that a mesh axis runs over, the one named last changes fastest.
Arguments:
- depth: float32 [1024, 16384], P('row', 'col'), may hold values from 0.5 to 3
- bed: float32 [1024, 16384], P('row', 'col'), may hold values from -1 to 1
- mass: float32 [1024, 16384], P('row', 'col'), may hold values from 0.2 to 2
- conduct: float32 [1024, 16384], P('row', 'col'), may hold values from 0.02 to 0.2
- settle: float32 [1024, 16384], P('row', 'col'), may hold values from 0.02 to 0.5
- wet: int32 [1024, 16384], P('row', 'col'), may hold values 0 or 1
- link_block: int32 [65536], P(('row', 'col')), may hold values from 0 to 1023
- link_owner: int32 [65536, 1], P(('row', 'col')), may hold values from 0 to 127; in each aligned block of 512 rows (0 to 511, 512 to 1023, ...) at most 8 rows name the same one
- link_reach: int32 [65536], P(('row', 'col')), may hold values from 0 to 15
- link_coef: float32 [65536], P(('row', 'col')), may hold values from 0.05 to 0.5
- chan_phase: float32 [2048, 128], P(('row', 'col')), may hold values from -0.5 to 2
- chan_conc: float32 [2048, 128], P(('row', 'col')), may hold values from 0.1 to 1
- chan_area: float32 [2048, 128], P(('row', 'col')), may hold values from 2 to 20
Outputs:
- depth_out: float32 [1024, 16384], P('row', 'col')
- mass_out: float32 [1024, 16384], P('row', 'col')
- phase_out: float32 [2048, 128], P(('row', 'col'))
- conc_out: float32 [2048, 128], P(('row', 'col'))
Inputs may be any that keep to these rules, and one draw needn't show every extreme that they name: `link_block`: block index within a tile. `link_owner`: among the 512 links of one tile, at most 8 name the same owner.
All inputs are finite; a program needn't handle non-finite values. No bound on the sum of `wet` on one device may be relied on, other than what follows from the above.
Results may differ from a plain program's by a relative error of at most 0.00005.
Values sent between devices are 32-bit elements; how exact they have to be, the bound alone decides.
No kernel may reach another device: no remote copies, remote signals or barrier semaphores. Data moves between devices by JAX's collectives and lax.ppermute only.
A program may use at most 64 MiB of HBM per device.

v0:
```python
import jax
import jax.numpy as jnp
from jax import lax
from jax.sharding import PartitionSpec as P


def padded_2(block, sides, width):
    for axis, dim in sides:
        count = lax.axis_size(axis)
        forward = [(i, i + 1) for i in range(count - 1)]
        backward = [(target, source) for source, target in forward]
        low = lax.ppermute(
            lax.slice_in_dim(block, block.shape[dim] - width, None, axis=dim), axis, forward
        )
        high = lax.ppermute(lax.slice_in_dim(block, 0, width, axis=dim), axis, backward)
        block = jnp.concatenate([low, block, high], axis=dim)
    return block


def smooth_reach(values):
    left = jnp.concatenate([values[:, :1], values[:, :-1]], axis=1)
    right = jnp.concatenate([values[:, 1:], values[:, -1:]], axis=1)
    return values + 0.25 * (left - 2.0 * values + right)


def body(
    depth,
    bed,
    mass,
    conduct,
    settle,
    wet,
    link_block,
    link_owner,
    link_reach,
    link_coef,
    chan_phase,
    chan_conc,
    chan_area,
):
    tile_y, tile_x = depth.shape
    opened = wet.astype(jnp.float32)
    surface = depth + bed
    stacked = jnp.stack([surface, mass, conduct, opened])
    padded = padded_2(stacked, (("row", 1), ("col", 2)), 1)
    water_gain = jnp.zeros_like(depth)
    mass_gain = jnp.zeros_like(depth)
    for step_y, step_x in ((1, 0), (-1, 0), (0, 1), (0, -1)):
        beside = padded[:, 1 + step_y : 1 + step_y + tile_y, 1 + step_x : 1 + step_x + tile_x]
        coeff = 0.5 * (conduct + beside[2]) * opened * beside[3]
        water_gain = water_gain + coeff * (beside[0] - surface)
        mass_gain = mass_gain + coeff * (beside[1] - mass)
    depth1 = depth + water_gain
    mass1 = (mass + mass_gain) * jnp.exp(-settle)
    surface1 = depth1 + bed
    blocks = tile_y * tile_x // 128
    surf_blocks = surface1.reshape(blocks, 128)
    mass_blocks = mass1.reshape(blocks, 128)
    open_blocks = opened.reshape(blocks, 128)
    surf_rows = surf_blocks[link_block]
    mass_rows = mass_blocks[link_block]
    weight = link_coef[:, None] * open_blocks[link_block]
    lat_rows = jnp.stack([weight * surf_rows, weight * mass_rows, weight], axis=1)
    n_row = lax.axis_size("row")
    n_col = lax.axis_size("col")
    devices = n_row * n_col
    links_here = link_owner.shape[0]
    slot_cap = max(2, 2 * links_here // devices)
    target = link_owner[:, 0]
    owner_hot = (target[:, None] == jnp.arange(devices, dtype=jnp.int32)[None, :]).astype(jnp.int32)
    ranking = jnp.sum((jnp.cumsum(owner_hot, axis=0) - 1) * owner_hot, axis=1)
    slot_of = target * slot_cap + ranking
    outgoing = jnp.zeros((devices * slot_cap, 3, 128), jnp.float32).at[slot_of].set(lat_rows)
    reach_tags = (
        jnp.full((devices * slot_cap,), -1.0, jnp.float32)
        .at[slot_of]
        .set(link_reach.astype(jnp.float32))
    )
    arrived, arrived_tags = (
        lax.all_to_all(
            outgoing.reshape(devices, slot_cap, 3, 128),
            ("row", "col"),
            split_axis=0,
            concat_axis=0,
            tiled=True,
        ),
        lax.all_to_all(
            reach_tags.reshape(devices, slot_cap),
            ("row", "col"),
            split_axis=0,
            concat_axis=0,
            tiled=True,
        ),
    )
    arrived = arrived.reshape(devices * slot_cap, 384)
    arrived_tags = arrived_tags.reshape(devices * slot_cap)
    reach_dev = chan_phase.shape[0]
    reach_hot = (arrived_tags[None, :] == jnp.arange(reach_dev, dtype=jnp.float32)[:, None]).astype(
        jnp.float32
    )
    totals = jnp.dot(reach_hot, arrived, precision=lax.Precision.HIGHEST)
    inflow = totals[:, :128]
    sediment = totals[:, 128:256]
    wet_sum = totals[:, 256:]
    phase_new = (chan_area * chan_phase + inflow) / (chan_area + wet_sum)
    conc_new = (chan_area * chan_conc + sediment) / (chan_area + wet_sum)
    phase_out = smooth_reach(phase_new)
    conc_out = smooth_reach(conc_new)
    reply = jnp.dot(
        reach_hot.T, jnp.concatenate([phase_out, conc_out], axis=1), precision=lax.Precision.HIGHEST
    )
    answered = lax.all_to_all(
        reply.reshape(devices, slot_cap, 256),
        ("row", "col"),
        split_axis=0,
        concat_axis=0,
        tiled=True,
    )
    own_rows = answered.reshape(devices * slot_cap, 256)[slot_of]
    applied = jnp.concatenate(
        [
            0.5 * weight * (own_rows[:, :128] - surf_rows),
            0.5 * weight * (own_rows[:, 128:] - mass_rows),
        ],
        axis=1,
    )
    block_hot = (jnp.arange(blocks, dtype=jnp.int32)[:, None] == link_block[None, :]).astype(
        jnp.float32
    )
    gained = jnp.dot(block_hot, applied, precision=lax.Precision.HIGHEST)
    depth_out = (depth1.reshape(blocks, 128) + gained[:, :128]).reshape(tile_y, tile_x)
    mass_out = (mass_blocks + gained[:, 128:]).reshape(tile_y, tile_x)
    return (depth_out, mass_out, phase_out, conc_out)


def solution(mesh):
    return jax.shard_map(
        body,
        mesh=mesh,
        in_specs=(
            P("row", "col"),
            P("row", "col"),
            P("row", "col"),
            P("row", "col"),
            P("row", "col"),
            P("row", "col"),
            P(("row", "col")),
            P(("row", "col"), None),
            P(("row", "col")),
            P(("row", "col")),
            P(("row", "col"), None),
            P(("row", "col"), None),
            P(("row", "col"), None),
        ),
        out_specs=(
            P("row", "col"),
            P("row", "col"),
            P(("row", "col"), None),
            P(("row", "col"), None),
        ),
        check_vma=False,
    )
```

profile of v0, /device:TPU:1, one launch (start us, length us, event | category | flops | bytes accessed | tf_op | source)
XLA Modules:
  0.0 201.5 jit_solution(12747054025347321039)
XLA Ops:
  0.7 1.2 fusion.75
  1.9 0.5 copy.57
  2.5 0.1 add.88
  2.6 0.8 copy-done.10
  3.4 0.5 copy.56
  3.9 0.4 stack.22
  4.3 0.4 stack.23
  4.7 2.0 pad_maximum_fusion.1
  6.7 1.3 copy-done.5
  8.1 1.3 collective-permute-start
  9.3 4.7 %collective-permute-start.1 = (f32[4,1,512]{2,0,1:T(4,128)S(1)}, f32[4,1,512]{2,0,1:T(4,128)S(1)}, u32[]{:S(2)}, u32[]{:S(2)}) collective-permute-start(f32[4,1,512]{2,0,1:T(4,128)S(1)} %get-tuple-element.16), channel_id=1, source_target_pairs={{0,32},{32,64},{64,96},{1,33},{33,65},{65,97},{2,34},{34,66},{66,9... | collective-permute-start | bytes 24584 | tf_op jit(solution)/shard_map/ppermute | solution.py:12
  14.0 0.1 copy.70
  14.1 0.2 fusion.51
  14.5 0.2 fusion.50
  14.8 2.4 %scatter_custom_fusion = f32[1024]{0:T(1024)S(1)} fusion(s32[512]{0:T(512)S(1)} %bitcast.205, f32[512]{0:T(512)S(1)} %convert_element_type.15, f32[]{:T(128)} %constant.4.clone.1), kind=kCustom, calls=%fused_computation.127 | custom fusion | bytes 4100 | tf_op jit(solution)/shard_map/scatter | solution.py:77
  17.2 0.7 all_to_all.12
  17.9 11.4 %all-to-all-start = ((f32[128,1,8]{2,1,0:T(1,128)}), f32[128,1,8]{2,1,0:T(1,128)S(1)}, u32[]{:S(2)}, u32[]{:S(2)}) async-start(f32[128,1,8]{2,1,0:T(1,128)} %bitcast.21), calls=%async_computation | async-start | bytes 131072 | tf_op jit(solution)/shard_map/all_to_all | solution.py:87
  29.3 4.3 %constant_dynamic-update-slice_fusion = (f32[4,257,512]{2,1,0:T(8,128)}, f32[4,256,512]{2,1,0:T(8,128)}) fusion(f32[4,256,512]{2,0,1:T(4,128)} %copy-done.5), kind=kLoop, calls=%fused_computation.126 | loop fusion | bytes 6291456
  33.6 2.0 %pad_maximum_fusion = f32[4,258,512]{2,0,1:T(4,128)S(1)} fusion(f32[4,1,512]{2,0,1:T(4,128)S(1)} %collective-permute-done, f32[1,256,512]{2,0,1:T(1,128)S(1)} %copy.57, f32[1,256,512]{2,0,1:T(1,128)S(1)} %stack.23, f32[1,256,512]{2,0,1:T(1,128)S(1)} %stack.22, f32[1,256,512]{2,0,1:T(1,128)S(1)} %copy.56, f32[4,1,512]{2,0,1:T(4,128)S(1)} %collective-permute-done.1), kind=kLoop, calls=%fused_computation.6 | loop fusion | flops 2641920 | bytes 4227072 | tf_op jit(solution)/shard_map/concatenate | solution.py:16
  35.7 1.3 copy-done
  37.0 1.1 fusion.73
  38.2 0.9 copy.65
  39.0 3.7 %collective-permute-start.3 = (f32[4,258,1]{1,0,2:T(4,128)}, f32[4,258,1]{1,0,2:T(4,128)}, u32[]{:S(2)}, u32[]{:S(2)}) collective-permute-start(f32[4,258,1]{1,0,2:T(4,128)} %copy.65), channel_id=1, source_target_pairs={{0,1},{1,2},{2,3},{3,4},{4,5},{5,6},{6,7},{7,8},{8,9},{9,10},{10,1... | collective-permute-start | bytes 12392 | tf_op jit(solution)/shard_map/ppermute | solution.py:12
  42.8 0.5 copy-done.19
  43.3 1.0 gather_fusion
  44.3 2.3 %copy.63 = f32[4,258,512]{2,1,0:T(8,128)S(1)} copy(f32[4,258,512]{2,0,1:T(4,128)} %copy-done) | data formatting | bytes 4227072 | tf_op jit(solution)/shard_map/concatenate | solution.py:16
  46.6 1.9 copy.62
  48.5 2.1 %collective-permute-start.2 = (f32[4,258,1]{1,0,2:T(4,128)}, f32[4,258,1]{1,0,2:T(4,128)}, u32[]{:S(2)}, u32[]{:S(2)}) collective-permute-start(f32[4,258,1]{1,0,2:T(4,128)} %copy.62), channel_id=1, source_target_pairs={{1,0},{2,1},{3,2},{4,3},{5,4},{6,5},{7,6},{8,7},{9,8},{10,9},{11,1... | collective-permute-start | bytes 12392 | tf_op jit(solution)/shard_map/ppermute | solution.py:15
  50.6 0.6 copy.59
  51.2 1.5 dynamic-update-slice.1
  52.7 0.6 copy.60
  53.3 1.8 copy.66
  55.1 15.4 %pad_maximum_fusion.13 = (f32[1,256,512]{2,0,1:T(1,128)}, f32[1,256,512]{2,0,1:T(1,128)}) fusion(f32[4,258,1]{2,0,1:T(4,128)} %copy.66, f32[4,1,512]{2,0,1:T(4,128)S(1)} %collective-permute-done, f32[4,1,512]{2,0,1:T(4,128)S(1)} %collective-permute-done.1, f32[1,256,512]{2,0,1:T(1,128)S(1)} %copy.57, f32[1,256,512]{2,0,1:T(1,128)} %copy-done.3, ...), kind=kLoop, calls=%fused_computation.41 | loop fusion | flops 1572864 | bytes 3166240 | tf_op jit(solution)/shard_map/slice | solution.py:50
  70.6 14.2 %pad_maximum_fusion.3 = (f32[1,256,512]{2,0,1:T(1,128)}, f32[1,256,512]{2,0,1:T(1,128)}) fusion(f32[4,258,1]{2,0,1:T(4,128)S(1)} %copy-done.7, f32[4,1,512]{2,0,1:T(4,128)S(1)} %collective-permute-done, f32[4,1,512]{2,0,1:T(4,128)S(1)} %collective-permute-done.1, f32[1,256,512]{2,0,1:T(1,128)S(1)} %copy.57, f32[1,256,512]{2,0,1:T(1,128)S(1)} %copy-done.4, ...), kind=kLoop, calls=%fused_computation.17 | loop fusion | flops 1572864 | bytes 3166240 | tf_op jit(solution)/shard_map/concatenate | solution.py:16
  84.8 0.9 copy.64
  85.8 5.3 %fusion.71 = (f32[256,512]{1,0:T(8,128)}, f32[256,512]{1,0:T(8,128)}) fusion(f32[256,512]{1,0:T(8,128)} %param.14, f32[256,512]{1,0:T(8,128)} %param.13, f32[256,512]{1,0:T(8,128)} %copy-done.10, f32[1,256,512]{2,0,1:T(1,128)} %get-tuple-element.9, f32[1,256,512]{2,0,1:T(1,128)} %get-tuple-element.11, f32[256,512]{1,0:T(8,128)} %param.16, ...), kind=kLoop, calls=%fused_computation.132 | loop fusion | flops 4718592 | bytes 11038752 | tf_op jit(solution)/shard_map/add | solution.py:55
  91.1 1.1 reshape.145
  92.2 1.7 gather_fusion.1
  93.9 4.8 %fusion.10 = f32[256,512]{1,0:T(8,128)} fusion(f32[256,512]{1,0:T(8,128)} %param.15, f32[4,258,1]{2,1,0:T(8,128)} %copy-done.6, f32[4,258,512]{2,1,0:T(8,128)S(1)} %copy.63, f32[4,256,512]{2,1,0:T(8,128)} %get-tuple-element.15, f32[4,1,512]{2,1,0:T(1,128)S(1)} %copy-done.16, f32[4,257,512]{2,1,0:T(8,128)} %dynamic-update-slice.1, f32[256,512]{1,0:T(8,128)} %param.16, ...), kind=kLoop, calls=%fused_computation.30 | loop fusion | flops 4849664 | bytes 9990176 | tf_op jit(solution)/shard_map/mul | solution.py:54
  98.7 1.1 reshape.146
  99.9 1.0 gather_fusion.2
  100.9 0.1 bitcast_multiply_fusion.1
  101.1 0.1 pad_maximum_fusion.2
  101.2 1.5 copy.73
  102.7 0.3 broadcast_in_dim.8
  103.0 31.4 %scatter_fusion = f32[1024,3,128]{2,1,0:T(4,128)S(1)} fusion(f32[1024,3,128]{2,1,0:T(4,128)S(1)} %broadcast_in_dim.8, s32[512]{0:T(512)S(1)} %bitcast.206, f32[512,3,128]{2,1,0:T(4,128)} %copy.73), kind=kCustom, calls=%fused_computation.5 | custom fusion | bytes 2361344 | tf_op jit(solution)/shard_map/scatter | solution.py:73
  134.4 1.3 copy.74
  135.7 9.7 %all-to-all-start.1 = ((f32[128,8,3,128]{3,1,2,0:T(8,128)}), f32[128,8,3,128]{3,1,2,0:T(8,128)S(1)}, u32[]{:S(2)}, u32[]{:S(2)}) async-start(f32[128,8,3,128]{3,1,2,0:T(8,128)} %copy.74), calls=%async_computation.1 | async-start | bytes 3145728 | tf_op jit(solution)/shard_map/all_to_all | solution.py:80
  145.4 0.5 broadcast.133
  146.0 0.8 reduce.3
  146.8 0.1 eq.64
  146.9 23.3 %all-to-all-done.1 = f32[128,8,3,128]{3,1,2,0:T(8,128)S(1)} async-done(((f32[128,8,3,128]{3,1,2,0:T(8,128)}), f32[128,8,3,128]{3,1,2,0:T(8,128)S(1)}, u32[]{:S(2)}, u32[]{:S(2)}) %all-to-all-start.1) | async-done | bytes 1572896 | tf_op jit(solution)/shard_map/all_to_all | solution.py:80
  170.1 0.6 fusion.1
  170.8 0.1 fusion.76
  171.1 0.1 fusion.63
  171.2 1.6 convolution_bitcast_fusion
  172.8 4.7 %all-to-all-start.2 = ((f32[128,8,256]{2,1,0:T(8,128)}), f32[128,8,256]{2,1,0:T(8,128)S(1)}, u32[]{:S(2)}, u32[]{:S(2)}) async-start(f32[128,8,256]{2,1,0:T(8,128)} %convolution_bitcast_fusion), calls=%async_computation.2 | async-start | bytes 2097152 | tf_op jit(solution)/shard_map/all_to_all | solution.py:112
  177.6 19.2 %all-to-all-done.2 = f32[128,8,256]{2,1,0:T(8,128)S(1)} async-done(((f32[128,8,256]{2,1,0:T(8,128)}), f32[128,8,256]{2,1,0:T(8,128)S(1)}, u32[]{:S(2)}, u32[]{:S(2)}) %all-to-all-start.2) | async-done | bytes 1048608 | tf_op jit(solution)/shard_map/all_to_all | solution.py:112
  196.8 1.6 gather_fusion.3
  198.4 0.1 fusion.49
  198.6 1.1 fusion
  199.7 0.1 slice_add_fusion
  199.8 0.9 reshape.151
  200.6 0.9 reshape.152
  (81 shorter events, 0.6 us)
Async XLA Ops:
  0.6 1.8 copy-start.12
  0.6 1.8 copy-start.13
  1.9 2.0 %copy-start.14 = (f32[256,512]{1,0:T(8,128)S(1)}, f32[256,512]{1,0:T(8,128)}, u32[]{:S(2)}) copy-start(f32[256,512]{1,0:T(8,128)} %param.15) | copy-start | bytes 1572868
  2.5 1.8 copy-start.9
  2.6 0.8 copy-start.10
  4.3 29.3 %copy-start.1 = (f32[1,256,512]{2,0,1:T(1,128)}, f32[1,256,512]{2,0,1:T(1,128)S(1)}, u32[]{:S(2)}) copy-start(f32[1,256,512]{2,0,1:T(1,128)S(1)} %stack.22) | copy-start | bytes 1572868
  4.7 28.9 %copy-start.3 = (f32[1,256,512]{2,0,1:T(1,128)}, f32[1,256,512]{2,0,1:T(1,128)S(1)}, u32[]{:S(2)}) copy-start(f32[1,256,512]{2,0,1:T(1,128)S(1)} %stack.23) | copy-start | bytes 1572868
  4.7 9.3 %copy-start.21 = (s32[512,1]{0,1:T(1,128)S(1)}, s32[512,1]{0,1:T(1,128)}, u32[]{:S(2)}) copy-start(s32[512,1]{0,1:T(1,128)} %param.20) | copy-start | bytes 6148
  4.7 10.0 %copy-start.28 = (s32[512]{0:T(512)S(1)}, s32[512]{0:T(512)}, u32[]{:S(2)}) copy-start(s32[512]{0:T(512)} %param.21) | copy-start | bytes 6148
  6.7 1.3 copy-start.5
  8.1 25.5 %collective-permute-start = (f32[4,1,512]{2,0,1:T(4,128)S(1)}, f32[4,1,512]{2,0,1:T(4,128)S(1)}, u32[]{:S(2)}, u32[]{:S(2)}) collective-permute-start(f32[4,1,512]{2,0,1:T(4,128)S(1)} %get-tuple-element.17), channel_id=1, source_target_pairs={{32,0},{64,32},{96,64},{33,1},{65,33},{97,65},{34,2},{66,34},{98,6... | collective-permute-start | bytes 24584 | tf_op jit(solution)/shard_map/ppermute | solution.py:15
  9.3 24.3 %collective-permute-start.1 = (f32[4,1,512]{2,0,1:T(4,128)S(1)}, f32[4,1,512]{2,0,1:T(4,128)S(1)}, u32[]{:S(2)}, u32[]{:S(2)}) collective-permute-start(f32[4,1,512]{2,0,1:T(4,128)S(1)} %get-tuple-element.16), channel_id=1, source_target_pairs={{0,32},{32,64},{64,96},{1,33},{33,65},{65,97},{2,34},{34,66},{66,9... | collective-permute-start | bytes 24584 | tf_op jit(solution)/shard_map/ppermute | solution.py:12
  14.7 18.8 %copy-start.22 = (s32[512,1]{0,1:T(1,128)}, s32[512,1]{0,1:T(1,128)S(1)}, u32[]{:S(2)}) copy-start(s32[512,1]{0,1:T(1,128)S(1)} %compare_select_fusion) | copy-start | bytes 6148
  17.9 117.8 %all-to-all-start = ((f32[128,1,8]{2,1,0:T(1,128)}), f32[128,1,8]{2,1,0:T(1,128)S(1)}, u32[]{:S(2)}, u32[]{:S(2)}) async-start(f32[128,1,8]{2,1,0:T(1,128)} %bitcast.21), calls=%async_computation | async-start | bytes 131072 | tf_op jit(solution)/shard_map/all_to_all | solution.py:87
  29.3 4.3 %copy-start.29 = (s32[512]{0:T(512)S(1)}, s32[512]{0:T(512)}, u32[]{:S(2)}) copy-start(s32[512]{0:T(512)} %param.19) | copy-start | bytes 6148
  35.7 1.3 copy-start
  39.0 14.3 %collective-permute-start.3 = (f32[4,258,1]{1,0,2:T(4,128)}, f32[4,258,1]{1,0,2:T(4,128)}, u32[]{:S(2)}, u32[]{:S(2)}) collective-permute-start(f32[4,258,1]{1,0,2:T(4,128)} %copy.65), channel_id=1, source_target_pairs={{0,1},{1,2},{2,3},{3,4},{4,5},{5,6},{6,7},{7,8},{8,9},{9,10},{10,1... | collective-permute-start | bytes 12392 | tf_op jit(solution)/shard_map/ppermute | solution.py:12
  42.7 0.6 copy-start.19
  48.5 36.3 %collective-permute-start.2 = (f32[4,258,1]{1,0,2:T(4,128)}, f32[4,258,1]{1,0,2:T(4,128)}, u32[]{:S(2)}, u32[]{:S(2)}) collective-permute-start(f32[4,258,1]{1,0,2:T(4,128)} %copy.62), channel_id=1, source_target_pairs={{1,0},{2,1},{3,2},{4,3},{5,4},{6,5},{7,6},{8,7},{9,8},{10,9},{11,1... | collective-permute-start | bytes 12392 | tf_op jit(solution)/shard_map/ppermute | solution.py:15
  55.1 15.4 %copy-start.2 = (f32[1,256,512]{2,0,1:T(1,128)S(1)}, f32[1,256,512]{2,0,1:T(1,128)}, u32[]{:S(2)}) copy-start(f32[1,256,512]{2,0,1:T(1,128)} %copy-done.1) | copy-start | bytes 1572868
  55.1 15.4 %copy-start.4 = (f32[1,256,512]{2,0,1:T(1,128)S(1)}, f32[1,256,512]{2,0,1:T(1,128)}, u32[]{:S(2)}) copy-start(f32[1,256,512]{2,0,1:T(1,128)} %copy-done.3) | copy-start | bytes 1572868
  55.1 15.4 %copy-start.7 = (f32[4,258,1]{2,0,1:T(4,128)S(1)}, f32[4,258,1]{2,0,1:T(4,128)}, u32[]{:S(2)}) copy-start(f32[4,258,1]{2,0,1:T(4,128)} %copy.66) | copy-start | bytes 12388
  85.7 5.3 %copy-start.6 = (f32[4,258,1]{2,1,0:T(8,128)}, f32[4,258,1]{2,1,0:T(8,128)S(1)}, u32[]{:S(2)}) copy-start(f32[4,258,1]{2,1,0:T(8,128)S(1)} %copy.64) | copy-start | bytes 12388
  85.7 6.5 %copy-start.20 = (s32[1024]{0:T(1024)S(1)}, s32[1024]{0:T(1024)}, u32[]{:S(2)}) copy-start(s32[1024]{0:T(1024)} %copy-done.19) | copy-start | bytes 12292
  91.1 2.8 %copy-start.16 = (f32[4,1,512]{2,1,0:T(1,128)S(1)}, f32[4,1,512]{2,1,0:T(1,128)}, u32[]{:S(2)}) copy-start(f32[4,1,512]{2,1,0:T(1,128)} %copy.60) | copy-start | bytes 24580
  91.1 2.8 %copy-start.8 = (s32[256,512]{1,0:T(8,128)S(1)}, s32[256,512]{1,0:T(8,128)}, u32[]{:S(2)}) copy-start(s32[256,512]{1,0:T(8,128)} %param.18) | copy-start | bytes 1572868
  98.7 2.2 %copy-start.11 = (f32[512,128]{1,0:T(8,128)S(1)}, f32[512,128]{1,0:T(8,128)}, u32[]{:S(2)}) copy-start(f32[512,128]{1,0:T(8,128)} %gather_fusion.1) | copy-start | bytes 786436
  98.7 2.2 %copy-start.27 = (f32[512]{0:T(512)S(1)}, f32[512]{0:T(512)}, u32[]{:S(2)}) copy-start(f32[512]{0:T(512)} %param.22) | copy-start | bytes 6148
  101.2 1.8 copy-start.23
  135.7 35.1 %copy-start.24 = (f32[16,128]{1,0:T(8,128)S(1)}, f32[16,128]{1,0:T(8,128)}, u32[]{:S(2)}) copy-start(f32[16,128]{1,0:T(8,128)} %param.25) | copy-start | bytes 24580
  135.7 35.1 %copy-start.25 = (f32[16,128]{1,0:T(8,128)S(1)}, f32[16,128]{1,0:T(8,128)}, u32[]{:S(2)}) copy-start(f32[16,128]{1,0:T(8,128)} %param.23) | copy-start | bytes 24580
  135.7 35.1 %copy-start.26 = (f32[16,128]{1,0:T(8,128)S(1)}, f32[16,128]{1,0:T(8,128)}, u32[]{:S(2)}) copy-start(f32[16,128]{1,0:T(8,128)} %param.24) | copy-start | bytes 24580
  135.7 34.4 %all-to-all-start.1 = ((f32[128,8,3,128]{3,1,2,0:T(8,128)}), f32[128,8,3,128]{3,1,2,0:T(8,128)S(1)}, u32[]{:S(2)}, u32[]{:S(2)}) async-start(f32[128,8,3,128]{3,1,2,0:T(8,128)} %copy.74), calls=%async_computation.1 | async-start | bytes 3145728 | tf_op jit(solution)/shard_map/all_to_all | solution.py:80
  170.8 6.7 %copy-start.15 = (f32[256,512]{1,0:T(8,128)S(1)}, f32[256,512]{1,0:T(8,128)}, u32[]{:S(2)}) copy-start(f32[256,512]{1,0:T(8,128)} %get-tuple-element.7) | copy-start | bytes 1572868
  171.2 6.4 %copy-start.17 = (f32[16,128]{1,0:T(8,128)}, f32[16,128]{1,0:T(8,128)S(1)}, u32[]{:S(2)}) copy-start(f32[16,128]{1,0:T(8,128)S(1)} %get-tuple-element.34) | copy-start | bytes 24580
  171.2 6.4 %copy-start.18 = (f32[16,128]{1,0:T(8,128)}, f32[16,128]{1,0:T(8,128)S(1)}, u32[]{:S(2)}) copy-start(f32[16,128]{1,0:T(8,128)S(1)} %get-tuple-element.35) | copy-start | bytes 24580
  172.8 24.0 %all-to-all-start.2 = ((f32[128,8,256]{2,1,0:T(8,128)}), f32[128,8,256]{2,1,0:T(8,128)S(1)}, u32[]{:S(2)}, u32[]{:S(2)}) async-start(f32[128,8,256]{2,1,0:T(8,128)} %convolution_bitcast_fusion), calls=%async_computation.2 | async-start | bytes 2097152 | tf_op jit(solution)/shard_map/all_to_all | solution.py:112
  196.8 1.7 copy-start.30
where the time goes:
time: 204 us; the launch traced here: 202 us
  local copies, waits for them, and re-layouts  69.8 us (34%)
  other arithmetic  47.1 us (23%)
  waiting for transfers between devices  42.5 us (21%)
  starting transfers between devices  37.5 us (18%)
  matrix products  3.34 us (2%)
    scatter x1, local copies, waits for them, and re-layouts, body(): jnp.zeros((devices * slot_cap, 3, 128), jnp.float32).at[slot_of]  31.4 us
    all_to_all x1, waiting for transfers between devices, body(): lax.all_to_all(outgoing.reshape(devices, slot_cap, 3, 128), ('row', 'col'...  23.3 us
    all_to_all x1, waiting for transfers between devices, body(): lax.all_to_all(reply.reshape(devices, slot_cap, 256), ('row', 'col'), spl...  19.2 us
    concatenate x2, other arithmetic, padded_2(): block = jnp.concatenate([low, block, high], axis=dim)  16.3 us
    slice x1, other arithmetic, body(): coeff = 0.5 * (conduct + beside[2]) * opened * beside[3]  15.4 us
    all_to_all x1, starting transfers between devices, body(): lax.all_to_all(reach_tags.reshape(devices, slot_cap), ('row', 'col'), spl...  11.4 us
    all_to_all x1, starting transfers between devices, body(): lax.all_to_all(outgoing.reshape(devices, slot_cap, 3, 128), ('row', 'col'...  9.75 us
    unnamed x63, local copies, waits for them, and re-layouts  8.37 us
  transfers between devices with their start and end apart: 7, of which 2 were waited for; matrix products, arithmetic and copies ran while one was open for 51% of the time, Pallas kernels for 0%

commit v1 on v0

v1 whole, which is shorter than its diff:
```python
import jax
import jax.numpy as jnp
from jax import lax
from jax.experimental import pallas as pl
from jax.experimental.pallas import tpu as pltpu
from jax.sharding import PartitionSpec as P


def halo(fields, axis, dim):
    count = lax.axis_size(axis)
    forward = [(i, i + 1) for i in range(count - 1)]
    backward = [(target, source) for source, target in forward]
    size = fields.shape[dim]
    low = lax.ppermute(lax.index_in_dim(fields, size - 1, axis=dim, keepdims=False), axis, forward)
    high = lax.ppermute(lax.index_in_dim(fields, 0, axis=dim, keepdims=False), axis, backward)
    return low, high


def stencil_kernel(depth_ref, bed_ref, mass_ref, cond_ref, settle_ref, wet_ref, rows_ref, cols_ref,
                   depth1_ref, mass1_ref, surf1_ref):
    depth = depth_ref[...]
    bed = bed_ref[...]
    mass = mass_ref[...]
    cond = cond_ref[...]
    opened = wet_ref[...].astype(jnp.float32)
    surface = depth + bed
    tile_y, tile_x = depth.shape
    own = (surface, mass, cond, opened)
    row_id = lax.broadcasted_iota(jnp.int32, (tile_y, tile_x), 0)
    col_id = lax.broadcasted_iota(jnp.int32, (tile_y, tile_x), 1)
    rows = rows_ref[...]
    cols = cols_ref[...]

    def neighbour(field, step_y, step_x):
        value = own[field]
        if step_y == 1:
            edge = rows[4 + field : 5 + field, :]
            return jnp.where(row_id == tile_y - 1, edge, pltpu.roll(value, tile_y - 1, 0))
        if step_y == -1:
            edge = rows[field : field + 1, :]
            return jnp.where(row_id == 0, edge, pltpu.roll(value, 1, 0))
        if step_x == 1:
            edge = cols[:, 4 + field : 5 + field]
            return jnp.where(col_id == tile_x - 1, edge, pltpu.roll(value, tile_x - 1, 1))
        edge = cols[:, field : field + 1]
        return jnp.where(col_id == 0, edge, pltpu.roll(value, 1, 1))

    water_gain = jnp.zeros_like(depth)
    mass_gain = jnp.zeros_like(depth)
    for step_y, step_x in ((1, 0), (-1, 0), (0, 1), (0, -1)):
        coeff = 0.5 * (cond + neighbour(2, step_y, step_x)) * opened * neighbour(3, step_y, step_x)
        water_gain = water_gain + coeff * (neighbour(0, step_y, step_x) - surface)
        mass_gain = mass_gain + coeff * (neighbour(1, step_y, step_x) - mass)
    depth1 = depth + water_gain
    depth1_ref[...] = depth1
    mass1_ref[...] = (mass + mass_gain) * jnp.exp(-settle_ref[...])
    surf1_ref[...] = depth1 + bed


def smooth_reach(values):
    left = jnp.concatenate([values[:, :1], values[:, :-1]], axis=1)
    right = jnp.concatenate([values[:, 1:], values[:, -1:]], axis=1)
    return values + 0.25 * (left - 2.0 * values + right)


def body(
    depth,
    bed,
    mass,
    conduct,
    settle,
    wet,
    link_block,
    link_owner,
    link_reach,
    link_coef,
    chan_phase,
    chan_conc,
    chan_area,
):
    tile_y, tile_x = depth.shape
    opened = wet.astype(jnp.float32)
    surface = depth + bed
    stacked = jnp.stack([surface, mass, conduct, opened])
    top, bottom = halo(stacked, "row", 1)
    left, right = halo(stacked, "col", 2)
    rows = jnp.concatenate([top, bottom], axis=0)
    cols = jnp.concatenate([left, right], axis=0).T
    tile = jax.ShapeDtypeStruct((tile_y, tile_x), jnp.float32)
    vmem = pl.BlockSpec(memory_space=pltpu.VMEM)
    depth1, mass1, surface1 = pl.pallas_call(
        stencil_kernel,
        out_shape=[tile, tile, tile],
        in_specs=[vmem] * 8,
        out_specs=[vmem] * 3,
        cost_estimate=pl.CostEstimate(
            flops=60 * tile_y * tile_x, transcendentals=tile_y * tile_x, bytes_accessed=36 * tile_y * tile_x
        ),
    )(depth, bed, mass, conduct, settle, wet, rows, cols)

    blocks = tile_y * tile_x // 128
    surf_rows = surface1.reshape(blocks, 128)[link_block]
    mass_rows = mass1.reshape(blocks, 128)[link_block]
    weight = link_coef[:, None] * opened.reshape(blocks, 128)[link_block]
    ws = weight * surf_rows
    wm = weight * mass_rows

    n_row = lax.axis_size("row")
    n_col = lax.axis_size("col")
    devices = n_row * n_col
    links_here = link_owner.shape[0]
    slot_cap = max(2, 2 * links_here // devices)
    target = link_owner[:, 0]
    owner_hot = (target[:, None] == jnp.arange(devices, dtype=jnp.int32)[None, :]).astype(jnp.int32)
    ranking = jnp.sum((jnp.cumsum(owner_hot, axis=0) - 1) * owner_hot, axis=1)
    slot_of = target * slot_cap + ranking
    slot_ids = jnp.arange(devices * slot_cap, dtype=jnp.int32)
    slot_hit = slot_of[None, :] == slot_ids[:, None]
    link_ids = jnp.arange(links_here, dtype=jnp.int32)
    filler = jnp.max(jnp.where(slot_hit, link_ids[None, :], -1), axis=1)
    used = filler >= 0
    source = jnp.maximum(filler, 0)
    payload = jnp.where(used[:, None, None], jnp.stack([ws, wm], axis=1)[source], 0.0)
    tags = jnp.where(used, link_reach[source].astype(jnp.float32), -1.0)
    coefs = jnp.where(used, link_coef[source], 0.0)
    meta = jnp.concatenate(
        [tags.reshape(devices, slot_cap), coefs.reshape(devices, slot_cap),
         jnp.zeros((devices, 128 - 2 * slot_cap), jnp.float32)],
        axis=1,
    )
    outgoing = jnp.concatenate(
        [payload.reshape(devices, 2 * slot_cap, 128), meta[:, None, :]], axis=1
    )
    arrived = lax.all_to_all(outgoing, ("row", "col"), split_axis=0, concat_axis=0, tiled=True)
    got = arrived[:, : 2 * slot_cap, :].reshape(devices * slot_cap, 2, 128)
    arrived_tags = arrived[:, 2 * slot_cap, :slot_cap].reshape(devices * slot_cap)
    arrived_coef = arrived[:, 2 * slot_cap, slot_cap : 2 * slot_cap].reshape(devices * slot_cap)
    got_ws = got[:, 0, :]
    got_wm = got[:, 1, :]
    got_w = jnp.where(got_wm > 0.0, arrived_coef[:, None], 0.0)
    reach_dev = chan_phase.shape[0]
    reach_hot = (arrived_tags[None, :] == jnp.arange(reach_dev, dtype=jnp.float32)[:, None]).astype(
        jnp.float32
    )
    totals = jnp.dot(
        reach_hot, jnp.concatenate([got_ws, got_wm, got_w], axis=1), precision=lax.Precision.HIGHEST
    )
    inflow = totals[:, :128]
    sediment = totals[:, 128:256]
    wet_sum = totals[:, 256:]
    phase_new = (chan_area * chan_phase + inflow) / (chan_area + wet_sum)
    conc_new = (chan_area * chan_conc + sediment) / (chan_area + wet_sum)
    phase_out = smooth_reach(phase_new)
    conc_out = smooth_reach(conc_new)
    reply = jnp.dot(
        reach_hot.T, jnp.concatenate([phase_out, conc_out], axis=1), precision=lax.Precision.HIGHEST
    )
    answered = lax.all_to_all(
        reply.reshape(devices, slot_cap * 2, 128),
        ("row", "col"),
        split_axis=0,
        concat_axis=0,
        tiled=True,
    )
    own_rows = answered.reshape(devices * slot_cap, 256)[slot_of]
    applied = jnp.concatenate(
        [
            0.5 * weight * (own_rows[:, :128] - surf_rows),
            0.5 * weight * (own_rows[:, 128:] - mass_rows),
        ],
        axis=1,
    )
    block_hot = (jnp.arange(blocks, dtype=jnp.int32)[:, None] == link_block[None, :]).astype(
        jnp.float32
    )
    gained = jnp.dot(block_hot, applied, precision=lax.Precision.HIGHEST)
    depth_out = (depth1.reshape(blocks, 128) + gained[:, :128]).reshape(tile_y, tile_x)
    mass_out = (mass1.reshape(blocks, 128) + gained[:, 128:]).reshape(tile_y, tile_x)
    return (depth_out, mass_out, phase_out, conc_out)


def solution(mesh):
    return jax.shard_map(
        body,
        mesh=mesh,
        in_specs=(
            P("row", "col"),
            P("row", "col"),
            P("row", "col"),
            P("row", "col"),
            P("row", "col"),
            P("row", "col"),
            P(("row", "col")),
            P(("row", "col"), None),
            P(("row", "col")),
            P(("row", "col")),
            P(("row", "col"), None),
            P(("row", "col"), None),
            P(("row", "col"), None),
        ),
        out_specs=(
            P("row", "col"),
            P("row", "col"),
            P(("row", "col"), None),
            P(("row", "col"), None),
        ),
        check_vma=False,
    )
```

time: 204 us -> 117 us (0.57); the launches traced: 202 us -> 117 us
  other arithmetic: 47.1 us -> 4.69 us
  local copies, waits for them, and re-layouts: 69.8 us -> 31.4 us
  blocking collectives: 0 us -> 35.7 us
  waiting for transfers between devices: 42.5 us -> 19.2 us
  starting transfers between devices: 37.5 us -> 17.5 us
  Pallas kernels: 0 us -> 4.84 us
    all_to_all x0 -> x1, blocking collectives: none -> 35.7 us  [body(): lax.all_to_all(outgoing, ('row', 'col'), split_axis=0, concat_axis=0, til...]
    scatter x2 -> x0, local copies, waits for them, and re-layouts: 33.8 us -> none  [the longest x1 31.4 us: body(): jnp.zeros((devices * slot_cap, 3, 128), jnp.float32).at[slot_of]]
    all_to_all x3 -> x1, waiting for transfers between devices: 42.5 us -> 19.2 us  [body(): lax.all_to_all(reply.reshape(devices, slot_cap * 2, 128), ('row', 'col'),...]
    all_to_all x3 -> x1, starting transfers between devices: 25.8 us -> 4.8 us  [body(): lax.all_to_all(reply.reshape(devices, slot_cap * 2, 128), ('row', 'col'),...]
    gather x3 -> x7, local copies, waits for them, and re-layouts: 3.73 us -> 20.5 us  [the longest x2 6.95 us: body(): coefs = jnp.where(used, link_coef[source], 0.0)]
    concatenate x2 -> x4, other arithmetic: 16.3 us -> 0.81 us  [the longest x1 0.61 us: body(): rows = jnp.concatenate([top, bottom], axis=0)]
    slice x1 -> x2, other arithmetic: 15.4 us -> 0.53 us  [halo(): lax.index_in_dim(fields, size - 1, axis=dim, keepdims=False)]
    unnamed x63 -> x38, local copies, waits for them, and re-layouts: 8.37 us -> 0.49 us
  transfers between devices with their start and end apart: 7 -> 5, of which waited for: 2 -> 1; matrix products, arithmetic and copies ran while one was open for 51% -> 15% of each run, Pallas kernels for 0% -> 0%
where the time goes in v1:
time: 117 us
  blocking collectives  35.7 us (31%)
  local copies, waits for them, and re-layouts  31.4 us (27%)
  waiting for transfers between devices  19.2 us (16%)
  starting transfers between devices  17.5 us (15%)
  Pallas kernels  4.84 us (4%)
  other arithmetic  4.69 us (4%)
  matrix products  2.36 us (2%)
  between operations  1.29 us (1%)
    all_to_all x1, blocking collectives, body(): lax.all_to_all(outgoing, ('row', 'col'), split_axis=0, concat_axis=0, til...  35.7 us
    all_to_all x1, waiting for transfers between devices, body(): lax.all_to_all(reply.reshape(devices, slot_cap * 2, 128), ('row', 'col'),...  19.2 us
    ppermute x2, starting transfers between devices, halo(): lax.ppermute(lax.index_in_dim(fields, size - 1, axis=dim, keepdims=False)...  8.18 us
    gather x2, local copies, waits for them, and re-layouts, body(): coefs = jnp.where(used, link_coef[source], 0.0)  6.95 us
    gather x1, local copies, waits for them, and re-layouts, body(): tags = jnp.where(used, link_reach[source].astype(jnp.float32), -1.0)  6.87 us
    pallas_call x1, Pallas kernels, body(): pl.pallas_call(stencil_kernel, out_shape=[tile, tile, tile], in_specs=[vm...  4.84 us
    all_to_all x1, starting transfers between devices, body(): lax.all_to_all(reply.reshape(devices, slot_cap * 2, 128), ('row', 'col'),...  4.8 us
    ppermute x2, starting transfers between devices, halo(): lax.ppermute(lax.index_in_dim(fields, 0, axis=dim, keepdims=False), axis,...  4.5 us
  transfers between devices with their start and end apart: 5, of which 1 were waited for; matrix products, arithmetic and copies ran while one was open for 15% of the time, Pallas kernels for 0%

profile of v1, /device:TPU:1, one launch (start us, length us, event | category | flops | bytes accessed | tf_op | source)
XLA Modules:
  0.0 117.0 jit_solution(8621324035442145317)
XLA Ops:
  0.6 0.0 copy-start
  0.7 1.3 %fusion.36 = (f32[256,512]{1,0:T(8,128)S(1)}, f32[1,256,512]{2,1,0:T(8,128)S(1)}) fusion(s32[256,512]{1,0:T(8,128)} %wet_ref.1), kind=kLoop, calls=%fused_computation.93 | loop fusion | flops 131072 | bytes 1572864 | tf_op jit(solution)/shard_map/convert_element_type | solution.py:82
  2.0 0.0 copy-done.9
  2.0 0.1 add_bitcast_fusion
  2.1 0.1 copy-done.3
  2.2 0.2 copy-done.2
  2.4 1.3 %collective-permute-start.1 = (f32[4,512]{1,0:T(4,128)S(1)}, f32[4,512]{1,0:T(4,128)S(1)}, u32[]{:S(2)}, u32[]{:S(2)}) collective-permute-start(f32[4,512]{1,0:T(4,128)S(1)} %bitcast.62), channel_id=1, source_target_pairs={{32,0},{64,32},{96,64},{33,1},{65,33},{97,65},{34,2},{66,34},{98,6... | collective-permute-start | bytes 24584 | tf_op jit(solution)/shard_map/ppermute | solution.py:15
  3.7 4.7 %collective-permute-start = (f32[4,512]{1,0:T(4,128)S(1)}, f32[4,512]{1,0:T(4,128)S(1)}, u32[]{:S(2)}, u32[]{:S(2)}) collective-permute-start(f32[4,512]{1,0:T(4,128)S(1)} %bitcast.63), channel_id=1, source_target_pairs={{0,32},{32,64},{64,96},{1,33},{33,65},{65,97},{2,34},{34,66},{66,9... | collective-permute-start | bytes 24584 | tf_op jit(solution)/shard_map/ppermute | solution.py:14
  8.4 0.5 maximum_reduce_fusion
  8.9 3.2 %collective-permute-start.3 = (f32[4,256]{1,0:T(4,128)S(1)}, f32[4,256]{1,0:T(4,128)S(1)}, u32[]{:S(2)}, u32[]{:S(2)}) collective-permute-start(f32[4,256]{1,0:T(4,128)S(1)} %get-tuple-element.11), channel_id=1, source_target_pairs={{1,0},{2,1},{3,2},{4,3},{5,4},{6,5},{7,6},{8,7},{9,8},{10,9},{11,1... | collective-permute-start | bytes 12296 | tf_op jit(solution)/shard_map/ppermute | solution.py:15
  12.1 3.5 %collective-permute-start.2 = (f32[4,256]{1,0:T(4,128)S(1)}, f32[4,256]{1,0:T(4,128)S(1)}, u32[]{:S(2)}, u32[]{:S(2)}) collective-permute-start(f32[4,256]{1,0:T(4,128)S(1)} %get-tuple-element.10), channel_id=1, source_target_pairs={{0,1},{1,2},{2,3},{3,4},{4,5},{5,6},{6,7},{7,8},{8,9},{9,10},{10,1... | collective-permute-start | bytes 12296 | tf_op jit(solution)/shard_map/ppermute | solution.py:14
  15.6 0.1 copy.53
  15.8 0.2 fusion.15
  16.0 0.1 add_add_fusion
  16.1 0.2 fusion.14
  16.4 0.4 select_reduce_fusion
  16.8 0.1 ge.13
  16.9 6.9 %gather_fusion.4 = s32[1024]{0:T(1024)S(1)} fusion(s32[512]{0:T(512)S(1)} %copy-done, s32[1024]{0:T(1024)S(1)} %maximum_clamp_fusion), kind=kCustom, calls=%fused_computation.4 | custom fusion | bytes 12288 | tf_op jit(solution)/shard_map/gather | solution.py:124
  23.8 0.1 convert_element_type.20
  23.9 6.9 %gather_fusion.5 = f32[1024]{0:T(1024)S(1)} fusion(f32[512]{0:T(512)S(1)} %copy-done.1, s32[1024]{0:T(1024)S(1)} %maximum_clamp_fusion), kind=kCustom, calls=%fused_computation.5 | custom fusion | bytes 12288 | tf_op jit(solution)/shard_map/gather | solution.py:125
  30.7 0.1 gather.41
  30.8 0.1 pad.19.clone
  30.9 0.1 maximum_maximum_fusion
  31.0 0.1 copy.55
  31.1 0.1 copy.56
  31.3 1.0 gather_fusion
  32.4 0.8 copy.52
  33.2 0.6 pad_maximum_fusion.5.rows_ref
  33.8 4.8 %shard_map.156 = (f32[256,512]{1,0:T(8,128)}, f32[256,512]{1,0:T(8,128)}, f32[256,512]{1,0:T(8,128)}) custom-call(f32[256,512]{1,0:T(8,128)} %depth_ref.1, f32[256,512]{1,0:T(8,128)} %bed_ref.1, f32[256,512]{1,0:T(8,128)} %mass_ref.1, f32[256,512]{1,0:T(8,128)} %cond_ref.1, f32[256,512]{1,0:T(8,128)} %settle_ref.1, s32[256,512]{1,0:T(8,128)} %wet_ref.1, ...), custom_call_target="tpu_custom_call" | custom-call | flops 7864320 | bytes 4718592 | tf_op jit(solution)/shard_map/pallas_call | solution.py:91
  38.7 1.1 reshape.156
  39.7 1.1 reshape.155
  40.8 1.0 gather_fusion.1
  41.9 1.0 gather_fusion.2
  42.9 0.1 bitcast_multiply_fusion.1
  43.1 0.4 copy.57
  43.5 0.1 copy-done.6
  43.6 3.6 %gather_fusion.3 = f32[1024,2,128]{2,1,0:T(2,128)S(1)} fusion(f32[512,2,128]{2,1,0:T(2,128)S(1)} %copy.57, s32[1024]{0:T(1024)S(1)} %maximum_clamp_fusion), kind=kCustom, calls=%fused_computation.3 | custom fusion | bytes 2101248 | tf_op jit(solution)/shard_map/gather | solution.py:123
  47.2 0.3 bitcast_select_fusion
  47.6 0.1 pad_maximum_fusion
  47.7 35.7 %all_to_all.10 = f32[128,17,128]{2,1,0:T(8,128)S(1)} all-to-all(f32[128,17,128]{2,1,0:T(8,128)S(1)} %pad_maximum_fusion), channel_id=1, replica_groups=mesh['row'=4,'col'=32] {'row','col'}, dimensions={0} | all-to-all | bytes 2228224 | tf_op jit(solution)/shard_map/all_to_all | solution.py:134
  83.4 0.4 slice_reduce_fusion
  83.8 0.1 eq.77
  83.8 0.1 slice.120
  83.9 0.8 fusion.35
  84.8 0.1 broadcast_in_dim.82
  84.9 0.2 compare_select_fusion
  85.1 0.6 fusion.1
  85.8 0.1 fusion.37
  85.8 0.1 fusion.38
  85.9 0.1 fusion.40
  86.0 0.1 fusion.39
  86.1 0.1 fusion.28
  86.2 0.0 copy-start.12
  86.2 0.6 fusion.18
  86.8 1.0 reshape.158
  87.9 4.8 %all-to-all-start.1 = ((f32[128,16,128]{2,1,0:T(8,128)}), f32[128,16,128]{2,1,0:T(8,128)S(1)}, u32[]{:S(2)}, u32[]{:S(2)}) async-start(f32[128,16,128]{2,1,0:T(8,128)} %reshape.158), calls=%async_computation.1 | async-start | bytes 2097152 | tf_op jit(solution)/shard_map/all_to_all | solution.py:158
  92.7 19.2 %all-to-all-done.1 = f32[128,16,128]{2,1,0:T(8,128)S(1)} async-done(((f32[128,16,128]{2,1,0:T(8,128)}), f32[128,16,128]{2,1,0:T(8,128)S(1)}, u32[]{:S(2)}, u32[]{:S(2)}) %all-to-all-start.1) | async-done | bytes 1048608 | tf_op jit(solution)/shard_map/all_to_all | solution.py:158
  112.0 0.3 reshape.159
  112.3 1.6 %gather_fusion.6 = f32[512,256]{1,0:T(8,128)S(1)} fusion(f32[1024,256]{1,0:T(8,128)S(1)} %reshape.159, s32[1024]{0:T(1024)S(1)} %pad_clamp_fusion), kind=kCustom, calls=%fused_computation.6 | custom fusion | bytes 1050624 | tf_op jit(solution)/shard_map/gather | solution.py:165
  113.9 0.2 fusion.13
  114.0 1.1 fusion
  115.1 0.1 slice_add_fusion
  115.3 0.9 reshape.160
  116.1 0.9 reshape.161
  (58 shorter events, 0.4 us)
Async XLA Ops:
  0.6 16.2 %copy-start = (s32[512]{0:T(512)S(1)}, s32[512]{0:T(512)}, u32[]{:S(2)}) copy-start(s32[512]{0:T(512)} %param.21) | copy-start | bytes 6148
  0.6 1.3 %copy-start.8 = (f32[256,512]{1,0:T(8,128)S(1)}, f32[256,512]{1,0:T(8,128)}, u32[]{:S(2)}) copy-start(f32[256,512]{1,0:T(8,128)} %depth_ref.1) | copy-start | bytes 1572868
  0.7 1.4 %copy-start.9 = (f32[256,512]{1,0:T(8,128)S(1)}, f32[256,512]{1,0:T(8,128)}, u32[]{:S(2)}) copy-start(f32[256,512]{1,0:T(8,128)} %bed_ref.1) | copy-start | bytes 1572868
  0.7 1.5 %copy-start.3 = (f32[256,512]{1,0:T(8,128)S(1)}, f32[256,512]{1,0:T(8,128)}, u32[]{:S(2)}) copy-start(f32[256,512]{1,0:T(8,128)} %cond_ref.1) | copy-start | bytes 1572868
  0.7 1.6 %copy-start.2 = (f32[256,512]{1,0:T(8,128)S(1)}, f32[256,512]{1,0:T(8,128)}, u32[]{:S(2)}) copy-start(f32[256,512]{1,0:T(8,128)} %mass_ref.1) | copy-start | bytes 1572868
  2.3 13.3 %copy-start.13 = (s32[512,1]{0,1:T(1,128)S(1)}, s32[512,1]{0,1:T(1,128)}, u32[]{:S(2)}) copy-start(s32[512,1]{0,1:T(1,128)} %param.20) | copy-start | bytes 6148
  2.4 30.8 %collective-permute-start.1 = (f32[4,512]{1,0:T(4,128)S(1)}, f32[4,512]{1,0:T(4,128)S(1)}, u32[]{:S(2)}, u32[]{:S(2)}) collective-permute-start(f32[4,512]{1,0:T(4,128)S(1)} %bitcast.62), channel_id=1, source_target_pairs={{32,0},{64,32},{96,64},{33,1},{65,33},{97,65},{34,2},{66,34},{98,6... | collective-permute-start | bytes 24584 | tf_op jit(solution)/shard_map/ppermute | solution.py:15
  3.7 13.1 %copy-start.17 = (s32[512]{0:T(512)S(1)}, s32[512]{0:T(512)}, u32[]{:S(2)}) copy-start(s32[512]{0:T(512)} %param.19) | copy-start | bytes 6148
  3.7 29.5 %collective-permute-start = (f32[4,512]{1,0:T(4,128)S(1)}, f32[4,512]{1,0:T(4,128)S(1)}, u32[]{:S(2)}, u32[]{:S(2)}) collective-permute-start(f32[4,512]{1,0:T(4,128)S(1)} %bitcast.63), channel_id=1, source_target_pairs={{0,32},{32,64},{64,96},{1,33},{33,65},{65,97},{2,34},{34,66},{66,9... | collective-permute-start | bytes 24584 | tf_op jit(solution)/shard_map/ppermute | solution.py:14
  8.9 23.5 %collective-permute-start.3 = (f32[4,256]{1,0:T(4,128)S(1)}, f32[4,256]{1,0:T(4,128)S(1)}, u32[]{:S(2)}, u32[]{:S(2)}) collective-permute-start(f32[4,256]{1,0:T(4,128)S(1)} %get-tuple-element.11), channel_id=1, source_target_pairs={{1,0},{2,1},{3,2},{4,3},{5,4},{6,5},{7,6},{8,7},{9,8},{10,9},{11,1... | collective-permute-start | bytes 12296 | tf_op jit(solution)/shard_map/ppermute | solution.py:15
  12.1 20.3 %collective-permute-start.2 = (f32[4,256]{1,0:T(4,128)S(1)}, f32[4,256]{1,0:T(4,128)S(1)}, u32[]{:S(2)}, u32[]{:S(2)}) collective-permute-start(f32[4,256]{1,0:T(4,128)S(1)} %get-tuple-element.10), channel_id=1, source_target_pairs={{0,1},{1,2},{2,3},{3,4},{4,5},{5,6},{6,7},{7,8},{8,9},{9,10},{10,1... | collective-permute-start | bytes 12296 | tf_op jit(solution)/shard_map/ppermute | solution.py:14
  16.9 7.0 %copy-start.1 = (f32[512]{0:T(512)S(1)}, f32[512]{0:T(512)}, u32[]{:S(2)}) copy-start(f32[512]{0:T(512)} %param.22) | copy-start | bytes 6148
  41.9 1.2 %copy-start.4 = (f32[512,128]{1,0:T(8,128)}, f32[512,128]{1,0:T(8,128)S(1)}, u32[]{:S(2)}) copy-start(f32[512,128]{1,0:T(8,128)S(1)} %gather_fusion.1) | copy-start | bytes 786436
  42.9 0.7 copy-start.6
  84.8 1.0 copy-start.14
  84.8 1.0 copy-start.15
  84.8 1.0 copy-start.16
  86.1 1.7 %copy-start.11 = (f32[16,128]{1,0:T(8,128)}, f32[16,128]{1,0:T(8,128)S(1)}, u32[]{:S(2)}) copy-start(f32[16,128]{1,0:T(8,128)S(1)} %get-tuple-element.38) | copy-start | bytes 24580
  86.2 1.7 %copy-start.12 = (f32[16,128]{1,0:T(8,128)}, f32[16,128]{1,0:T(8,128)S(1)}, u32[]{:S(2)}) copy-start(f32[16,128]{1,0:T(8,128)S(1)} %get-tuple-element.39) | copy-start | bytes 24580
  87.9 4.8 %copy-start.10 = (f32[256,512]{1,0:T(8,128)S(1)}, f32[256,512]{1,0:T(8,128)}, u32[]{:S(2)}) copy-start(f32[256,512]{1,0:T(8,128)} %get-tuple-element.7) | copy-start | bytes 1572868
  87.9 24.1 %all-to-all-start.1 = ((f32[128,16,128]{2,1,0:T(8,128)}), f32[128,16,128]{2,1,0:T(8,128)S(1)}, u32[]{:S(2)}, u32[]{:S(2)}) async-start(f32[128,16,128]{2,1,0:T(8,128)} %reshape.158), calls=%async_computation.1 | async-start | bytes 2097152 | tf_op jit(solution)/shard_map/all_to_all | solution.py:158
  112.3 1.6 %copy-start.5 = (f32[512,128]{1,0:T(8,128)S(1)}, f32[512,128]{1,0:T(8,128)}, u32[]{:S(2)}) copy-start(f32[512,128]{1,0:T(8,128)} %copy-done.4) | copy-start | bytes 786436
  112.3 1.6 %copy-start.7 = (f32[512,128]{1,0:T(8,128)S(1)}, f32[512,128]{1,0:T(8,128)}, u32[]{:S(2)}) copy-start(f32[512,128]{1,0:T(8,128)} %copy-done.6) | copy-start | bytes 786436

commit v2 on v1

--- a/solution.py
+++ b/solution.py
@@ -121,20 +121,20 @@
     used = filler >= 0
     source = jnp.maximum(filler, 0)
     payload = jnp.where(used[:, None, None], jnp.stack([ws, wm], axis=1)[source], 0.0)
-    tags = jnp.where(used, link_reach[source].astype(jnp.float32), -1.0)
-    coefs = jnp.where(used, link_coef[source], 0.0)
+    tags = jnp.max(jnp.where(slot_hit, link_reach[None, :].astype(jnp.float32), -1.0), axis=1)
+    coefs = jnp.maximum(jnp.max(jnp.where(slot_hit, link_coef[None, :], -1.0), axis=1), 0.0)
     meta = jnp.concatenate(
         [tags.reshape(devices, slot_cap), coefs.reshape(devices, slot_cap),
          jnp.zeros((devices, 128 - 2 * slot_cap), jnp.float32)],
         axis=1,
     )
-    outgoing = jnp.concatenate(
-        [payload.reshape(devices, 2 * slot_cap, 128), meta[:, None, :]], axis=1
-    )
+    outgoing = jnp.concatenate([payload.reshape(devices, 2 * slot_cap * 128), meta], axis=1)
     arrived = lax.all_to_all(outgoing, ("row", "col"), split_axis=0, concat_axis=0, tiled=True)
-    got = arrived[:, : 2 * slot_cap, :].reshape(devices * slot_cap, 2, 128)
-    arrived_tags = arrived[:, 2 * slot_cap, :slot_cap].reshape(devices * slot_cap)
-    arrived_coef = arrived[:, 2 * slot_cap, slot_cap : 2 * slot_cap].reshape(devices * slot_cap)
+    got = arrived[:, : 2 * slot_cap * 128].reshape(devices * slot_cap, 2, 128)
+    arrived_tags = arrived[:, 2 * slot_cap * 128 : 2 * slot_cap * 128 + slot_cap].reshape(devices * slot_cap)
+    arrived_coef = arrived[:, 2 * slot_cap * 128 + slot_cap : 2 * slot_cap * 128 + 2 * slot_cap].reshape(
+        devices * slot_cap
+    )
     got_ws = got[:, 0, :]
     got_wm = got[:, 1, :]
     got_w = jnp.where(got_wm > 0.0, arrived_coef[:, None], 0.0)
@@ -156,7 +156,7 @@
         reach_hot.T, jnp.concatenate([phase_out, conc_out], axis=1), precision=lax.Precision.HIGHEST
     )
     answered = lax.all_to_all(
-        reply.reshape(devices, slot_cap * 2, 128),
+        reply.reshape(devices, slot_cap * 256),
         ("row", "col"),
         split_axis=0,
         concat_axis=0,

time: 117 us -> 114 us (0.974)
  other arithmetic: 4.69 us -> 11.7 us
  local copies, waits for them, and re-layouts: 31.4 us -> 26.4 us
  blocking collectives: 35.7 us -> 30.9 us
    gather x3 -> x0, local copies, waits for them, and re-layouts: 13.8 us -> none  [the longest x2 6.95 us: body(): coefs = jnp.where(used, link_coef[source], 0.0)]
    all_to_all x1, blocking collectives: 35.7 us -> 30.9 us  [body(): lax.all_to_all(outgoing, ('row', 'col'), split_axis=0, concat_axis=0, til...]
    select_n x1, other arithmetic: 0.34 us -> 4.49 us  [body(): jnp.where(used[:, None, None], jnp.stack([ws, wm], axis=1)[source], 0.0)]
    all_to_all x0 -> x2, local copies, waits for them, and re-layouts: none -> 3.18 us  [the longest x1 2.04 us: body(): lax.all_to_all(reply.reshape(devices, slot_cap * 256), ('row', 'col'), sp...]
    all_to_all x0 -> x1, other arithmetic: none -> 2.49 us  [body(): lax.all_to_all(reply.reshape(devices, slot_cap * 256), ('row', 'col'), sp...]
    select_n x0 -> x1, local copies, waits for them, and re-layouts: none -> 2.06 us  [body(): jnp.where(used[:, None, None], jnp.stack([ws, wm], axis=1)[source], 0.0)]
    unnamed x38 -> x37, local copies, waits for them, and re-layouts: 0.49 us -> 2.12 us
  transfers between devices with their start and end apart: 5 -> 5, of which waited for: 1 -> 1; matrix products, arithmetic and copies ran while one was open for 15% -> 5% of each run, Pallas kernels for 0% -> 0%
where the time goes in v2:
time: 114 us; the launch traced here: 113 us
  blocking collectives  30.9 us (27%)
  local copies, waits for them, and re-layouts  26.4 us (23%)
  waiting for transfers between devices  18.4 us (16%)
  starting transfers between devices  17.6 us (15%)
  other arithmetic  11.7 us (10%)
  Pallas kernels  4.85 us (4%)
  matrix products  2.35 us (2%)
  between operations  1.19 us (1%)
    all_to_all x1, blocking collectives, body(): lax.all_to_all(outgoing, ('row', 'col'), split_axis=0, concat_axis=0, til...  30.9 us
    all_to_all x1, waiting for transfers between devices, body(): lax.all_to_all(reply.reshape(devices, slot_cap * 256), ('row', 'col'), sp...  18.4 us
    ppermute x2, starting transfers between devices, halo(): lax.ppermute(lax.index_in_dim(fields, size - 1, axis=dim, keepdims=False)...  8.18 us
    pallas_call x1, Pallas kernels, body(): pl.pallas_call(stencil_kernel, out_shape=[tile, tile, tile], in_specs=[vm...  4.85 us
    all_to_all x1, starting transfers between devices, body(): lax.all_to_all(reply.reshape(devices, slot_cap * 256), ('row', 'col'), sp...  4.74 us
    ppermute x2, starting transfers between devices, halo(): lax.ppermute(lax.index_in_dim(fields, 0, axis=dim, keepdims=False), axis,...  4.64 us
    select_n x1, other arithmetic, body(): jnp.where(used[:, None, None], jnp.stack([ws, wm], axis=1)[source], 0.0)  4.49 us
    gather x1, local copies, waits for them, and re-layouts, body(): jnp.stack([ws, wm], axis=1)[source]  3.54 us
  transfers between devices with their start and end apart: 5, of which 1 were waited for; matrix products, arithmetic and copies ran while one was open for 5% of the time, Pallas kernels for 0%

profile of v2, /device:TPU:1, one launch (start us, length us, event | category | flops | bytes accessed | tf_op | source)
XLA Modules:
  0.0 113.4 jit_solution(6494072154805737198)
XLA Ops:
  0.7 1.2 %fusion.37 = (f32[256,512]{1,0:T(8,128)S(1)}, f32[1,256,512]{2,1,0:T(8,128)S(1)}) fusion(s32[256,512]{1,0:T(8,128)} %wet_ref.1), kind=kLoop, calls=%fused_computation.90 | loop fusion | flops 131072 | bytes 1572864 | tf_op jit(solution)/shard_map/convert_element_type | solution.py:82
  1.9 0.1 copy-done.3
  2.0 0.1 add_bitcast_fusion
  2.1 1.0 copy-done
  3.0 0.2 copy-done.1
  3.2 1.3 %collective-permute-start.1 = (f32[4,512]{1,0:T(4,128)S(1)}, f32[4,512]{1,0:T(4,128)S(1)}, u32[]{:S(2)}, u32[]{:S(2)}) collective-permute-start(f32[4,512]{1,0:T(4,128)S(1)} %bitcast.59), channel_id=1, source_target_pairs={{32,0},{64,32},{96,64},{33,1},{65,33},{97,65},{34,2},{66,34},{98,6... | collective-permute-start | bytes 24584 | tf_op jit(solution)/shard_map/ppermute | solution.py:15
  4.5 4.7 %collective-permute-start = (f32[4,512]{1,0:T(4,128)S(1)}, f32[4,512]{1,0:T(4,128)S(1)}, u32[]{:S(2)}, u32[]{:S(2)}) collective-permute-start(f32[4,512]{1,0:T(4,128)S(1)} %bitcast.60), channel_id=1, source_target_pairs={{0,32},{32,64},{64,96},{1,33},{33,65},{65,97},{2,34},{34,66},{66,9... | collective-permute-start | bytes 24584 | tf_op jit(solution)/shard_map/ppermute | solution.py:14
  9.2 0.5 maximum_reduce_fusion
  9.8 3.3 %collective-permute-start.3 = (f32[4,256]{1,0:T(4,128)S(1)}, f32[4,256]{1,0:T(4,128)S(1)}, u32[]{:S(2)}, u32[]{:S(2)}) collective-permute-start(f32[4,256]{1,0:T(4,128)S(1)} %get-tuple-element.11), channel_id=1, source_target_pairs={{1,0},{2,1},{3,2},{4,3},{5,4},{6,5},{7,6},{8,7},{9,8},{10,9},{11,1... | collective-permute-start | bytes 12296 | tf_op jit(solution)/shard_map/ppermute | solution.py:15
  13.1 3.5 %collective-permute-start.2 = (f32[4,256]{1,0:T(4,128)S(1)}, f32[4,256]{1,0:T(4,128)S(1)}, u32[]{:S(2)}, u32[]{:S(2)}) collective-permute-start(f32[4,256]{1,0:T(4,128)S(1)} %get-tuple-element.10), channel_id=1, source_target_pairs={{0,1},{1,2},{2,3},{3,4},{4,5},{5,6},{6,7},{7,8},{8,9},{9,10},{10,1... | collective-permute-start | bytes 12296 | tf_op jit(solution)/shard_map/ppermute | solution.py:14
  16.7 0.1 copy.51
  16.8 0.2 fusion.15
  17.0 0.1 add_add_fusion
  17.1 0.2 fusion.14
  17.4 0.4 select_reduce_fusion.2
  17.8 0.6 select_reduce_fusion
  18.5 0.1 reshape.160
  18.6 0.7 max.27
  19.3 1.0 gather_fusion
  20.4 0.8 copy.50
  21.2 0.6 pad_maximum_fusion.4.rows_ref
  21.8 4.9 %shard_map.156 = (f32[256,512]{1,0:T(8,128)}, f32[256,512]{1,0:T(8,128)}, f32[256,512]{1,0:T(8,128)}) custom-call(f32[256,512]{1,0:T(8,128)} %depth_ref.1, f32[256,512]{1,0:T(8,128)} %bed_ref.1, f32[256,512]{1,0:T(8,128)} %mass_ref.1, f32[256,512]{1,0:T(8,128)} %cond_ref.1, f32[256,512]{1,0:T(8,128)} %settle_ref.1, s32[256,512]{1,0:T(8,128)} %wet_ref.1, ...), custom_call_target="tpu_custom_call" | custom-call | flops 7864320 | bytes 4718592 | tf_op jit(solution)/shard_map/pallas_call | solution.py:91
  26.6 1.1 reshape.159
  27.8 0.1 copy-done.6
  27.9 1.0 gather_fusion.1
  28.9 1.0 gather_fusion.2
  30.0 0.1 bitcast_multiply_fusion.1
  30.2 0.4 copy.53
  30.6 3.5 %gather_fusion.3 = f32[1024,2,128]{2,1,0:T(2,128)S(1)} fusion(f32[512,2,128]{2,1,0:T(2,128)S(1)} %copy.53, s32[1024]{0:T(1024)S(1)} %maximum_clamp_fusion), kind=kCustom, calls=%fused_computation.3 | custom fusion | bytes 2101248 | tf_op jit(solution)/shard_map/gather | solution.py:123
  34.1 4.5 %broadcast_select_fusion = f32[1024,2,128]{2,1,0:T(2,128)} fusion(f32[1024,2,128]{2,1,0:T(2,128)S(1)} %gather_fusion.3, pred[1024]{0:T(1024)(128)(4,1)S(1)} %broadcast_compare_fusion), kind=kLoop, calls=%fused_computation.19 | loop fusion | flops 262144 | bytes 2098176 | tf_op jit(solution)/shard_map/jit(_where)/select_n | solution.py:123
  38.6 2.1 %select_n.36 = f32[128,2048]{1,0:T(8,128)S(1)} reshape(f32[1024,2,128]{2,1,0:T(2,128)} %broadcast_select_fusion) | data formatting | bytes 2097152 | tf_op jit(solution)/shard_map/jit(_where)/select_n | solution.py:123
  40.7 0.6 broadcast_in_dim.83
  41.3 1.0 concatenate.32
  42.3 1.1 %copy.54 = f32[128,1,2176]{2,1,0:T(1,128)S(1)} copy(f32[128,1,2176]{2,0,1:T(8,128)S(1)} %bitcast.49) | data formatting | bytes 2228224 | tf_op jit(solution)/shard_map/all_to_all | solution.py:132
  43.5 30.9 %all_to_all.22 = f32[128,1,2176]{2,1,0:T(1,128)S(1)} all-to-all(f32[128,1,2176]{2,1,0:T(1,128)S(1)} %copy.54), channel_id=1, replica_groups=mesh['row'=4,'col'=32] {'row','col'}, dimensions={0} | all-to-all | bytes 2228224 | tf_op jit(solution)/shard_map/all_to_all | solution.py:132
  74.3 0.1 copy.64
  74.4 0.1 fusion.35
  74.5 0.1 slice.116
  74.6 0.1 eq.77
  74.7 0.9 reshape.161
  75.6 1.6 %fusion.36 = (f32[1024,1,128]{2,1,0:T(1,128)}, f32[1024,1,128]{2,1,0:T(1,128)S(1)}) fusion(f32[1024,2,128]{2,1,0:T(2,128)S(1)} %reshape.161), kind=kLoop, calls=%fused_computation.89 | loop fusion | bytes 2097152 | tf_op jit(solution)/shard_map/slice | solution.py:138
  77.2 0.1 broadcast_in_dim.84
  77.3 0.2 compare_select_fusion
  77.5 0.7 copy-done.7
  78.2 0.6 fusion.1
  78.9 0.1 fusion.38
  79.0 0.1 fusion.39
  79.1 0.1 fusion.41
  79.1 0.1 fusion.40
  79.2 0.1 fusion.28
  79.3 0.0 copy-start.9
  79.3 0.6 fusion.18
  80.0 2.0 %all_to_all.19 = f32[128,1,2048]{2,1,0:T(1,128)} reshape(f32[1024,256]{1,0:T(8,128)S(1)} %fusion.18) | data formatting | bytes 2097152 | tf_op jit(solution)/shard_map/all_to_all | solution.py:158
  82.0 4.7 %all-to-all-start.1 = ((f32[128,1,2048]{2,1,0:T(1,128)}), f32[128,1,2048]{2,1,0:T(1,128)S(1)}, u32[]{:S(2)}, u32[]{:S(2)}) async-start(f32[128,1,2048]{2,1,0:T(1,128)} %all_to_all.19), calls=%async_computation.1 | async-start | bytes 2097152 | tf_op jit(solution)/shard_map/all_to_all | solution.py:158
  86.8 0.8 reshape.155
  87.6 18.4 %all-to-all-done.1 = f32[128,1,2048]{2,1,0:T(1,128)S(1)} async-done(((f32[128,1,2048]{2,1,0:T(1,128)}), f32[128,1,2048]{2,1,0:T(1,128)S(1)}, u32[]{:S(2)}, u32[]{:S(2)}) %all-to-all-start.1) | async-done | bytes 1048608 | tf_op jit(solution)/shard_map/all_to_all | solution.py:158
  106.1 2.5 %reduce.2 = f32[128,2048]{1,0:T(8,128)S(1)} reduce(f32[128,1,2048]{2,1,0:T(1,128)S(1)} %all-to-all-done.1, f32[]{:T(128)} %constant.38), dimensions={1}, to_apply=%all_to_all.18.reduce_sub_computation | reduce | bytes 2097156 | tf_op jit(solution)/shard_map/all_to_all | solution.py:158
  108.5 0.2 reshape.162
  108.7 1.6 %gather_fusion.4 = f32[512,256]{1,0:T(8,128)S(1)} fusion(f32[1024,256]{1,0:T(8,128)S(1)} %reshape.162, s32[1024]{0:T(1024)S(1)} %pad_clamp_fusion), kind=kCustom, calls=%fused_computation.4 | custom fusion | bytes 1050624 | tf_op jit(solution)/shard_map/gather | solution.py:165
  110.3 0.1 fusion.13
  110.5 1.1 fusion
  111.6 0.1 slice_add_fusion
  111.7 0.9 reshape.163
  112.6 0.9 reshape.164
  (53 shorter events, 0.3 us)
Async XLA Ops:
  0.6 1.3 %copy-start.2 = (f32[256,512]{1,0:T(8,128)S(1)}, f32[256,512]{1,0:T(8,128)}, u32[]{:S(2)}) copy-start(f32[256,512]{1,0:T(8,128)} %depth_ref.1) | copy-start | bytes 1572868
  0.6 1.4 %copy-start.3 = (f32[256,512]{1,0:T(8,128)S(1)}, f32[256,512]{1,0:T(8,128)}, u32[]{:S(2)}) copy-start(f32[256,512]{1,0:T(8,128)} %bed_ref.1) | copy-start | bytes 1572868
  2.0 1.0 copy-start
  2.0 1.2 %copy-start.1 = (f32[256,512]{1,0:T(8,128)S(1)}, f32[256,512]{1,0:T(8,128)}, u32[]{:S(2)}) copy-start(f32[256,512]{1,0:T(8,128)} %cond_ref.1) | copy-start | bytes 1572868
  3.2 13.4 %copy-start.10 = (s32[512,1]{0,1:T(1,128)S(1)}, s32[512,1]{0,1:T(1,128)}, u32[]{:S(2)}) copy-start(s32[512,1]{0,1:T(1,128)} %param.20) | copy-start | bytes 6148
  3.2 18.0 %collective-permute-start.1 = (f32[4,512]{1,0:T(4,128)S(1)}, f32[4,512]{1,0:T(4,128)S(1)}, u32[]{:S(2)}, u32[]{:S(2)}) collective-permute-start(f32[4,512]{1,0:T(4,128)S(1)} %bitcast.59), channel_id=1, source_target_pairs={{32,0},{64,32},{96,64},{33,1},{65,33},{97,65},{34,2},{66,34},{98,6... | collective-permute-start | bytes 24584 | tf_op jit(solution)/shard_map/ppermute | solution.py:15
  4.5 16.6 %collective-permute-start = (f32[4,512]{1,0:T(4,128)S(1)}, f32[4,512]{1,0:T(4,128)S(1)}, u32[]{:S(2)}, u32[]{:S(2)}) collective-permute-start(f32[4,512]{1,0:T(4,128)S(1)} %bitcast.60), channel_id=1, source_target_pairs={{0,32},{32,64},{64,96},{1,33},{33,65},{65,97},{2,34},{34,66},{66,9... | collective-permute-start | bytes 24584 | tf_op jit(solution)/shard_map/ppermute | solution.py:14
  9.7 8.0 %copy-start.16 = (s32[512]{0:T(512)S(1)}, s32[512]{0:T(512)}, u32[]{:S(2)}) copy-start(s32[512]{0:T(512)} %param.19) | copy-start | bytes 6148
  9.7 8.0 %copy-start.15 = (s32[512]{0:T(512)S(1)}, s32[512]{0:T(512)}, u32[]{:S(2)}) copy-start(s32[512]{0:T(512)} %param.21) | copy-start | bytes 6148
  9.8 8.0 %copy-start.11 = (f32[512]{0:T(512)S(1)}, f32[512]{0:T(512)}, u32[]{:S(2)}) copy-start(f32[512]{0:T(512)} %param.22) | copy-start | bytes 6148
  9.8 10.6 %collective-permute-start.3 = (f32[4,256]{1,0:T(4,128)S(1)}, f32[4,256]{1,0:T(4,128)S(1)}, u32[]{:S(2)}, u32[]{:S(2)}) collective-permute-start(f32[4,256]{1,0:T(4,128)S(1)} %get-tuple-element.11), channel_id=1, source_target_pairs={{1,0},{2,1},{3,2},{4,3},{5,4},{6,5},{7,6},{8,7},{9,8},{10,9},{11,1... | collective-permute-start | bytes 12296 | tf_op jit(solution)/shard_map/ppermute | solution.py:15
  13.1 7.3 %collective-permute-start.2 = (f32[4,256]{1,0:T(4,128)S(1)}, f32[4,256]{1,0:T(4,128)S(1)}, u32[]{:S(2)}, u32[]{:S(2)}) collective-permute-start(f32[4,256]{1,0:T(4,128)S(1)} %get-tuple-element.10), channel_id=1, source_target_pairs={{0,1},{1,2},{2,3},{3,4},{4,5},{5,6},{6,7},{7,8},{8,9},{9,10},{10,1... | collective-permute-start | bytes 12296 | tf_op jit(solution)/shard_map/ppermute | solution.py:14
  26.6 1.2 %copy-start.6 = (f32[256,512]{1,0:T(8,128)S(1)}, f32[256,512]{1,0:T(8,128)}, u32[]{:S(2)}) copy-start(f32[256,512]{1,0:T(8,128)} %get-tuple-element.8) | copy-start | bytes 1572868
  77.2 1.0 copy-start.7
  77.5 1.4 %copy-start.12 = (f32[16,128]{1,0:T(8,128)S(1)}, f32[16,128]{1,0:T(8,128)}, u32[]{:S(2)}) copy-start(f32[16,128]{1,0:T(8,128)} %param.25) | copy-start | bytes 24580
  77.5 1.4 %copy-start.13 = (f32[16,128]{1,0:T(8,128)S(1)}, f32[16,128]{1,0:T(8,128)}, u32[]{:S(2)}) copy-start(f32[16,128]{1,0:T(8,128)} %param.23) | copy-start | bytes 24580
  77.5 1.4 %copy-start.14 = (f32[16,128]{1,0:T(8,128)S(1)}, f32[16,128]{1,0:T(8,128)}, u32[]{:S(2)}) copy-start(f32[16,128]{1,0:T(8,128)} %param.24) | copy-start | bytes 24580
  79.3 2.7 %copy-start.8 = (f32[16,128]{1,0:T(8,128)}, f32[16,128]{1,0:T(8,128)S(1)}, u32[]{:S(2)}) copy-start(f32[16,128]{1,0:T(8,128)S(1)} %get-tuple-element.38) | copy-start | bytes 24580
  79.3 2.7 %copy-start.9 = (f32[16,128]{1,0:T(8,128)}, f32[16,128]{1,0:T(8,128)S(1)}, u32[]{:S(2)}) copy-start(f32[16,128]{1,0:T(8,128)S(1)} %get-tuple-element.39) | copy-start | bytes 24580
  82.0 4.8 %copy-start.5 = (f32[256,512]{1,0:T(8,128)S(1)}, f32[256,512]{1,0:T(8,128)}, u32[]{:S(2)}) copy-start(f32[256,512]{1,0:T(8,128)} %get-tuple-element.7) | copy-start | bytes 1572868
  82.0 24.1 %all-to-all-start.1 = ((f32[128,1,2048]{2,1,0:T(1,128)}), f32[128,1,2048]{2,1,0:T(1,128)S(1)}, u32[]{:S(2)}, u32[]{:S(2)}) async-start(f32[128,1,2048]{2,1,0:T(1,128)} %all_to_all.19), calls=%async_computation.1 | async-start | bytes 2097152 | tf_op jit(solution)/shard_map/all_to_all | solution.py:158
  110.4 1.1 copy-start.4

commit v3 on v2

--- a/solution.py
+++ b/solution.py
@@ -116,11 +116,8 @@
     slot_of = target * slot_cap + ranking
     slot_ids = jnp.arange(devices * slot_cap, dtype=jnp.int32)
     slot_hit = slot_of[None, :] == slot_ids[:, None]
-    link_ids = jnp.arange(links_here, dtype=jnp.int32)
-    filler = jnp.max(jnp.where(slot_hit, link_ids[None, :], -1), axis=1)
-    used = filler >= 0
-    source = jnp.maximum(filler, 0)
-    payload = jnp.where(used[:, None, None], jnp.stack([ws, wm], axis=1)[source], 0.0)
+    hit = slot_hit.astype(jnp.float32)
+    payload = jnp.dot(hit, jnp.concatenate([ws, wm], axis=1), precision=lax.Precision.HIGHEST)
     tags = jnp.max(jnp.where(slot_hit, link_reach[None, :].astype(jnp.float32), -1.0), axis=1)
     coefs = jnp.maximum(jnp.max(jnp.where(slot_hit, link_coef[None, :], -1.0), axis=1), 0.0)
     meta = jnp.concatenate(
@@ -130,13 +127,13 @@
     )
     outgoing = jnp.concatenate([payload.reshape(devices, 2 * slot_cap * 128), meta], axis=1)
     arrived = lax.all_to_all(outgoing, ("row", "col"), split_axis=0, concat_axis=0, tiled=True)
-    got = arrived[:, : 2 * slot_cap * 128].reshape(devices * slot_cap, 2, 128)
+    got = arrived[:, : 2 * slot_cap * 128].reshape(devices * slot_cap, 256)
     arrived_tags = arrived[:, 2 * slot_cap * 128 : 2 * slot_cap * 128 + slot_cap].reshape(devices * slot_cap)
     arrived_coef = arrived[:, 2 * slot_cap * 128 + slot_cap : 2 * slot_cap * 128 + 2 * slot_cap].reshape(
         devices * slot_cap
     )
-    got_ws = got[:, 0, :]
-    got_wm = got[:, 1, :]
+    got_ws = got[:, :128]
+    got_wm = got[:, 128:]
     got_w = jnp.where(got_wm > 0.0, arrived_coef[:, None], 0.0)
     reach_dev = chan_phase.shape[0]
     reach_hot = (arrived_tags[None, :] == jnp.arange(reach_dev, dtype=jnp.float32)[:, None]).astype(

time: 114 us -> 101 us (0.89)
  local copies, waits for them, and re-layouts: 26.4 us -> 17.1 us
  other arithmetic: 11.7 us -> 6.84 us
    select_n x1 -> x0, other arithmetic: 4.49 us -> none  [body(): jnp.where(used[:, None, None], jnp.stack([ws, wm], axis=1)[source], 0.0)]
    gather x1 -> x0, local copies, waits for them, and re-layouts: 3.54 us -> none  [body(): jnp.stack([ws, wm], axis=1)[source]]
    select_n x1 -> x0, local copies, waits for them, and re-layouts: 2.06 us -> none  [body(): jnp.where(used[:, None, None], jnp.stack([ws, wm], axis=1)[source], 0.0)]
    slice x2 -> x1, local copies, waits for them, and re-layouts: 1.7 us -> 0.1 us  [body(): got = arrived[:, :2 * slot_cap * 128].reshape(devices * slot_cap, 256)]
where the time goes in v3:
time: 101 us; the launch traced here: 100 us
  blocking collectives  30.9 us (31%)
  waiting for transfers between devices  18.4 us (18%)
  starting transfers between devices  17.6 us (17%)
  local copies, waits for them, and re-layouts  17.1 us (17%)
  other arithmetic  6.84 us (7%)
  Pallas kernels  4.84 us (5%)
  matrix products  3.45 us (3%)
  between operations  1.15 us (1%)
    all_to_all x1, blocking collectives, body(): lax.all_to_all(outgoing, ('row', 'col'), split_axis=0, concat_axis=0, til...  30.9 us
    all_to_all x1, waiting for transfers between devices, body(): lax.all_to_all(reply.reshape(devices, slot_cap * 256), ('row', 'col'), sp...  18.4 us
    ppermute x2, starting transfers between devices, halo(): lax.ppermute(lax.index_in_dim(fields, size - 1, axis=dim, keepdims=False)...  8.18 us
    pallas_call x1, Pallas kernels, body(): pl.pallas_call(stencil_kernel, out_shape=[tile, tile, tile], in_specs=[vm...  4.84 us
    all_to_all x1, starting transfers between devices, body(): lax.all_to_all(reply.reshape(devices, slot_cap * 256), ('row', 'col'), sp...  4.75 us
    ppermute x2, starting transfers between devices, halo(): lax.ppermute(lax.index_in_dim(fields, 0, axis=dim, keepdims=False), axis,...  4.64 us
    all_to_all x1, other arithmetic, body(): lax.all_to_all(reply.reshape(devices, slot_cap * 256), ('row', 'col'), sp...  2.49 us
    all_to_all x1, local copies, waits for them, and re-layouts, body(): lax.all_to_all(reply.reshape(devices, slot_cap * 256), ('row', 'col'), sp...  2.03 us
  transfers between devices with their start and end apart: 5, of which 1 were waited for; matrix products, arithmetic and copies ran while one was open for 5% of the time, Pallas kernels for 0%

profile of v3, /device:TPU:1, one launch (start us, length us, event | category | flops | bytes accessed | tf_op | source)
XLA Modules:
  0.0 100.3 jit_solution(5962700022319223720)
XLA Ops:
  0.6 0.0 copy-start.2
  0.6 0.0 copy-start.3
  0.7 1.2 %fusion.41 = (f32[256,512]{1,0:T(8,128)S(1)}, f32[1,256,512]{2,1,0:T(8,128)S(1)}) fusion(s32[256,512]{1,0:T(8,128)} %wet_ref.1), kind=kLoop, calls=%fused_computation.86 | loop fusion | flops 131072 | bytes 1572864 | tf_op jit(solution)/shard_map/convert_element_type | solution.py:82
  1.9 0.1 copy-done.3
  2.0 0.1 add_bitcast_fusion
  2.1 1.0 copy-done
  3.0 0.2 copy-done.1
  3.2 0.0 copy-start.15
  3.2 0.0 copy-start.9
  3.2 1.3 %collective-permute-start.1 = (f32[4,512]{1,0:T(4,128)S(1)}, f32[4,512]{1,0:T(4,128)S(1)}, u32[]{:S(2)}, u32[]{:S(2)}) collective-permute-start(f32[4,512]{1,0:T(4,128)S(1)} %bitcast.40), channel_id=1, source_target_pairs={{32,0},{64,32},{96,64},{33,1},{65,33},{97,65},{34,2},{66,34},{98,6... | collective-permute-start | bytes 24584 | tf_op jit(solution)/shard_map/ppermute | solution.py:15
  4.6 4.7 %collective-permute-start = (f32[4,512]{1,0:T(4,128)S(1)}, f32[4,512]{1,0:T(4,128)S(1)}, u32[]{:S(2)}, u32[]{:S(2)}) collective-permute-start(f32[4,512]{1,0:T(4,128)S(1)} %bitcast.41), channel_id=1, source_target_pairs={{0,32},{32,64},{64,96},{1,33},{33,65},{65,97},{2,34},{34,66},{66,9... | collective-permute-start | bytes 24584 | tf_op jit(solution)/shard_map/ppermute | solution.py:14
  9.2 0.5 maximum_reduce_fusion
  9.8 3.3 %collective-permute-start.3 = (f32[4,256]{1,0:T(4,128)S(1)}, f32[4,256]{1,0:T(4,128)S(1)}, u32[]{:S(2)}, u32[]{:S(2)}) collective-permute-start(f32[4,256]{1,0:T(4,128)S(1)} %get-tuple-element.11), channel_id=1, source_target_pairs={{1,0},{2,1},{3,2},{4,3},{5,4},{6,5},{7,6},{8,7},{9,8},{10,9},{11,1... | collective-permute-start | bytes 12296 | tf_op jit(solution)/shard_map/ppermute | solution.py:15
  13.1 3.5 %collective-permute-start.2 = (f32[4,256]{1,0:T(4,128)S(1)}, f32[4,256]{1,0:T(4,128)S(1)}, u32[]{:S(2)}, u32[]{:S(2)}) collective-permute-start(f32[4,256]{1,0:T(4,128)S(1)} %get-tuple-element.10), channel_id=1, source_target_pairs={{0,1},{1,2},{2,3},{3,4},{4,5},{5,6},{6,7},{7,8},{8,9},{9,10},{10,1... | collective-permute-start | bytes 12296 | tf_op jit(solution)/shard_map/ppermute | solution.py:14
  16.7 0.1 copy.42
  16.8 0.2 fusion.19
  17.1 0.1 add_add_fusion
  17.1 0.2 fusion.18
  17.4 0.6 select_reduce_fusion
  18.1 0.1 reshape.90
  18.2 0.7 max.12
  18.9 1.0 %gather_fusion = f32[512,128]{1,0:T(8,128)S(1)} fusion(f32[1024,128]{1,0:T(8,128)S(1)} %reshape.85, s32[1024]{0:T(1024)S(1)} %pad_clamp_fusion.1), kind=kCustom, calls=%fused_computation | custom fusion | bytes 526336 | tf_op jit(solution)/shard_map/gather | solution.py:104
  20.0 0.8 copy.41
  20.8 0.6 pad_maximum_fusion.3.rows_ref
  21.4 4.8 %shard_map.156 = (f32[256,512]{1,0:T(8,128)}, f32[256,512]{1,0:T(8,128)}, f32[256,512]{1,0:T(8,128)}) custom-call(f32[256,512]{1,0:T(8,128)} %depth_ref.1, f32[256,512]{1,0:T(8,128)} %bed_ref.1, f32[256,512]{1,0:T(8,128)} %mass_ref.1, f32[256,512]{1,0:T(8,128)} %cond_ref.1, f32[256,512]{1,0:T(8,128)} %settle_ref.1, s32[256,512]{1,0:T(8,128)} %wet_ref.1, ...), custom_call_target="tpu_custom_call" | custom-call | flops 7864320 | bytes 4718592 | tf_op jit(solution)/shard_map/pallas_call | solution.py:91
  26.2 1.1 %reshape.88 = f32[1024,128]{1,0:T(8,128)S(1)} reshape(f32[256,512]{1,0:T(8,128)} %get-tuple-element.9) | data formatting | bytes 1048576 | tf_op jit(solution)/shard_map/reshape | solution.py:103
  27.4 0.1 copy-done.6
  27.5 1.0 %gather_fusion.1 = f32[512,128]{1,0:T(8,128)S(1)} fusion(f32[1024,128]{1,0:T(8,128)S(1)} %reshape.87, s32[1024]{0:T(1024)S(1)} %pad_clamp_fusion.1), kind=kCustom, calls=%fused_computation.1 | custom fusion | bytes 526336 | tf_op jit(solution)/shard_map/gather | solution.py:102
  28.5 1.0 %gather_fusion.2 = f32[512,128]{1,0:T(8,128)S(1)} fusion(f32[1024,128]{1,0:T(8,128)S(1)} %reshape.88, s32[1024]{0:T(1024)S(1)} %pad_clamp_fusion.1), kind=kCustom, calls=%fused_computation.2 | custom fusion | bytes 526336 | tf_op jit(solution)/shard_map/gather | solution.py:103
  29.6 0.1 multiply_multiply_fusion.1
  29.7 1.1 %fusion = f32[1024,256]{1,0:T(8,128)S(1)} fusion(s32[512]{0:T(512)S(1)} %multiply_add_fusion, f32[512,128]{1,0:T(8,128)S(1)} %get-tuple-element.25, f32[512,128]{1,0:T(8,128)S(1)} %get-tuple-element.24), kind=kOutput, calls=%fused_computation.7 | convolution fusion | flops 1611268096 | bytes 1574912 | tf_op jit(solution)/shard_map/dot_general | solution.py:120
  30.8 0.2 reshape.89
  31.0 0.6 broadcast_in_dim.52
  31.6 1.0 %concatenate.37 = f32[128,2176]{1,0:T(8,128)S(1)} concatenate(f32[128,2048]{1,0:T(8,128)S(1)} %reshape.89, f32[128,8]{1,0:T(8,128)S(1)} %reshape.90, f32[128,8]{1,0:T(8,128)} %max.12, f32[128,112]{1,0:T(8,128)} %broadcast_in_dim.52), dimensions={1} | concatenate | bytes 2228224 | tf_op jit(solution)/shard_map/concatenate | solution.py:128
  32.6 0.8 all_to_all.14
  33.4 30.9 %all_to_all.22 = f32[128,1,2176]{2,1,0:T(1,128)S(1)} all-to-all(f32[128,1,2176]{2,1,0:T(1,128)S(1)} %all_to_all.14), channel_id=1, replica_groups=mesh['row'=4,'col'=32] {'row','col'}, dimensions={0} | all-to-all | bytes 2228224 | tf_op jit(solution)/shard_map/all_to_all | solution.py:129
  64.3 0.1 copy.51
  64.3 0.1 fusion.40
  64.4 0.1 slice.112
  64.5 0.1 eq.77
  64.6 0.2 reshape.91
  64.8 0.1 broadcast_in_dim.53
  64.9 0.0 copy-start.11
  64.9 0.2 fusion.15
  65.1 0.6 fusion.2
  65.8 0.1 fusion.42
  65.9 0.1 fusion.43
  65.9 0.1 fusion.45
  66.0 0.1 fusion.44
  66.1 0.1 fusion.32
  66.2 0.0 copy-start.8
  66.2 0.6 fusion.22
  66.8 2.0 %all_to_all.19 = f32[128,1,2048]{2,1,0:T(1,128)} reshape(f32[1024,256]{1,0:T(8,128)S(1)} %fusion.22) | data formatting | bytes 2097152 | tf_op jit(solution)/shard_map/all_to_all | solution.py:155
  68.9 4.8 %all-to-all-start.1 = ((f32[128,1,2048]{2,1,0:T(1,128)}), f32[128,1,2048]{2,1,0:T(1,128)S(1)}, u32[]{:S(2)}, u32[]{:S(2)}) async-start(f32[128,1,2048]{2,1,0:T(1,128)} %all_to_all.19), calls=%async_computation.1 | async-start | bytes 2097152 | tf_op jit(solution)/shard_map/all_to_all | solution.py:155
  73.7 0.8 reshape.84
  74.5 18.4 %all-to-all-done.1 = f32[128,1,2048]{2,1,0:T(1,128)S(1)} async-done(((f32[128,1,2048]{2,1,0:T(1,128)}), f32[128,1,2048]{2,1,0:T(1,128)S(1)}, u32[]{:S(2)}, u32[]{:S(2)}) %all-to-all-start.1) | async-done | bytes 1048608 | tf_op jit(solution)/shard_map/all_to_all | solution.py:155
  92.9 2.5 %reduce.2 = f32[128,2048]{1,0:T(8,128)S(1)} reduce(f32[128,1,2048]{2,1,0:T(1,128)S(1)} %all-to-all-done.1, f32[]{:T(128)} %constant.32), dimensions={1}, to_apply=%all_to_all.18.reduce_sub_computation | reduce | bytes 2097156 | tf_op jit(solution)/shard_map/all_to_all | solution.py:155
  95.4 0.2 reshape.92
  95.6 1.6 %gather_fusion.3 = f32[512,256]{1,0:T(8,128)S(1)} fusion(f32[1024,256]{1,0:T(8,128)S(1)} %reshape.92, s32[1024]{0:T(1024)S(1)} %pad_clamp_fusion), kind=kCustom, calls=%fused_computation.3 | custom fusion | bytes 1050624 | tf_op jit(solution)/shard_map/gather | solution.py:162
  97.2 0.1 fusion.17
  97.3 1.1 %fusion.1 = f32[1024,256]{1,0:T(8,128)S(1)} fusion(s32[512]{0:T(512)S(1)} %copy-done.15, f32[512,128]{1,0:T(8,128)S(1)} %get-tuple-element.21, f32[512,128]{1,0:T(8,128)S(1)} %get-tuple-element.20), kind=kOutput, calls=%fused_computation.9 | convolution fusion | flops 1611268096 | bytes 1574912 | tf_op jit(solution)/shard_map/dot_general | solution.py:173
  98.4 0.1 slice_add_fusion
  98.6 0.9 reshape.93
  99.4 0.9 reshape.94
  (44 shorter events, 0.3 us)
Async XLA Ops:
  0.6 1.3 %copy-start.2 = (f32[256,512]{1,0:T(8,128)S(1)}, f32[256,512]{1,0:T(8,128)}, u32[]{:S(2)}) copy-start(f32[256,512]{1,0:T(8,128)} %depth_ref.1) | copy-start | bytes 1572868
  0.6 1.4 %copy-start.3 = (f32[256,512]{1,0:T(8,128)S(1)}, f32[256,512]{1,0:T(8,128)}, u32[]{:S(2)}) copy-start(f32[256,512]{1,0:T(8,128)} %bed_ref.1) | copy-start | bytes 1572868
  2.0 1.0 %copy-start = (f32[256,512]{1,0:T(8,128)S(1)}, f32[256,512]{1,0:T(8,128)}, u32[]{:S(2)}) copy-start(f32[256,512]{1,0:T(8,128)} %mass_ref.1) | copy-start | bytes 1572868
  2.0 1.2 %copy-start.1 = (f32[256,512]{1,0:T(8,128)S(1)}, f32[256,512]{1,0:T(8,128)}, u32[]{:S(2)}) copy-start(f32[256,512]{1,0:T(8,128)} %cond_ref.1) | copy-start | bytes 1572868
  3.2 13.4 %copy-start.15 = (s32[512]{0:T(512)S(1)}, s32[512]{0:T(512)}, u32[]{:S(2)}) copy-start(s32[512]{0:T(512)} %param.19) | copy-start | bytes 6148
  3.2 13.5 %copy-start.9 = (s32[512,1]{0,1:T(1,128)S(1)}, s32[512,1]{0,1:T(1,128)}, u32[]{:S(2)}) copy-start(s32[512,1]{0,1:T(1,128)} %param.20) | copy-start | bytes 6148
  3.2 17.5 %collective-permute-start.1 = (f32[4,512]{1,0:T(4,128)S(1)}, f32[4,512]{1,0:T(4,128)S(1)}, u32[]{:S(2)}, u32[]{:S(2)}) collective-permute-start(f32[4,512]{1,0:T(4,128)S(1)} %bitcast.40), channel_id=1, source_target_pairs={{32,0},{64,32},{96,64},{33,1},{65,33},{97,65},{34,2},{66,34},{98,6... | collective-permute-start | bytes 24584 | tf_op jit(solution)/shard_map/ppermute | solution.py:15
  4.6 16.2 %collective-permute-start = (f32[4,512]{1,0:T(4,128)S(1)}, f32[4,512]{1,0:T(4,128)S(1)}, u32[]{:S(2)}, u32[]{:S(2)}) collective-permute-start(f32[4,512]{1,0:T(4,128)S(1)} %bitcast.41), channel_id=1, source_target_pairs={{0,32},{32,64},{64,96},{1,33},{33,65},{65,97},{2,34},{34,66},{66,9... | collective-permute-start | bytes 24584 | tf_op jit(solution)/shard_map/ppermute | solution.py:14
  9.7 7.6 %copy-start.14 = (s32[512]{0:T(512)S(1)}, s32[512]{0:T(512)}, u32[]{:S(2)}) copy-start(s32[512]{0:T(512)} %param.21) | copy-start | bytes 6148
  9.8 7.7 %copy-start.10 = (f32[512]{0:T(512)S(1)}, f32[512]{0:T(512)}, u32[]{:S(2)}) copy-start(f32[512]{0:T(512)} %param.22) | copy-start | bytes 6148
  9.8 10.2 %collective-permute-start.3 = (f32[4,256]{1,0:T(4,128)S(1)}, f32[4,256]{1,0:T(4,128)S(1)}, u32[]{:S(2)}, u32[]{:S(2)}) collective-permute-start(f32[4,256]{1,0:T(4,128)S(1)} %get-tuple-element.11), channel_id=1, source_target_pairs={{1,0},{2,1},{3,2},{4,3},{5,4},{6,5},{7,6},{8,7},{9,8},{10,9},{11,1... | collective-permute-start | bytes 12296 | tf_op jit(solution)/shard_map/ppermute | solution.py:15
  13.1 6.9 %collective-permute-start.2 = (f32[4,256]{1,0:T(4,128)S(1)}, f32[4,256]{1,0:T(4,128)S(1)}, u32[]{:S(2)}, u32[]{:S(2)}) collective-permute-start(f32[4,256]{1,0:T(4,128)S(1)} %get-tuple-element.10), channel_id=1, source_target_pairs={{0,1},{1,2},{2,3},{3,4},{4,5},{5,6},{6,7},{7,8},{8,9},{9,10},{10,1... | collective-permute-start | bytes 12296 | tf_op jit(solution)/shard_map/ppermute | solution.py:14
  26.2 1.2 %copy-start.6 = (f32[256,512]{1,0:T(8,128)S(1)}, f32[256,512]{1,0:T(8,128)}, u32[]{:S(2)}) copy-start(f32[256,512]{1,0:T(8,128)} %get-tuple-element.8) | copy-start | bytes 1572868
  64.9 0.9 copy-start.11
  64.9 0.9 copy-start.12
  64.9 0.9 copy-start.13
  66.2 2.7 %copy-start.7 = (f32[16,128]{1,0:T(8,128)}, f32[16,128]{1,0:T(8,128)S(1)}, u32[]{:S(2)}) copy-start(f32[16,128]{1,0:T(8,128)S(1)} %get-tuple-element.36) | copy-start | bytes 24580
  66.2 2.7 %copy-start.8 = (f32[16,128]{1,0:T(8,128)}, f32[16,128]{1,0:T(8,128)S(1)}, u32[]{:S(2)}) copy-start(f32[16,128]{1,0:T(8,128)S(1)} %get-tuple-element.37) | copy-start | bytes 24580
  68.9 4.8 %copy-start.5 = (f32[256,512]{1,0:T(8,128)S(1)}, f32[256,512]{1,0:T(8,128)}, u32[]{:S(2)}) copy-start(f32[256,512]{1,0:T(8,128)} %get-tuple-element.7) | copy-start | bytes 1572868
  68.9 24.1 %all-to-all-start.1 = ((f32[128,1,2048]{2,1,0:T(1,128)}), f32[128,1,2048]{2,1,0:T(1,128)S(1)}, u32[]{:S(2)}, u32[]{:S(2)}) async-start(f32[128,1,2048]{2,1,0:T(1,128)} %all_to_all.19), calls=%async_computation.1 | async-start | bytes 2097152 | tf_op jit(solution)/shard_map/all_to_all | solution.py:155
  97.3 1.1 %copy-start.4 = (f32[1024,128]{1,0:T(8,128)S(1)}, f32[1024,128]{1,0:T(8,128)}, u32[]{:S(2)}) copy-start(f32[1024,128]{1,0:T(8,128)} %reshape.84) | copy-start | bytes 1572868

commit v4 on v3

--- a/solution.py
+++ b/solution.py
@@ -6,14 +6,11 @@
 from jax.sharding import PartitionSpec as P
 
 
-def halo(fields, axis, dim):
+def halo_pair(last, first, axis):
     count = lax.axis_size(axis)
     forward = [(i, i + 1) for i in range(count - 1)]
     backward = [(target, source) for source, target in forward]
-    size = fields.shape[dim]
-    low = lax.ppermute(lax.index_in_dim(fields, size - 1, axis=dim, keepdims=False), axis, forward)
-    high = lax.ppermute(lax.index_in_dim(fields, 0, axis=dim, keepdims=False), axis, backward)
-    return low, high
+    return lax.ppermute(last, axis, forward), lax.ppermute(first, axis, backward)
 
 
 def stencil_kernel(depth_ref, bed_ref, mass_ref, cond_ref, settle_ref, wet_ref, rows_ref, cols_ref,
@@ -80,10 +77,14 @@
 ):
     tile_y, tile_x = depth.shape
     opened = wet.astype(jnp.float32)
-    surface = depth + bed
-    stacked = jnp.stack([surface, mass, conduct, opened])
-    top, bottom = halo(stacked, "row", 1)
-    left, right = halo(stacked, "col", 2)
+
+    def edges(index, dim):
+        def cut(a):
+            return lax.index_in_dim(a, index, axis=dim, keepdims=False)
+        return jnp.stack([cut(depth) + cut(bed), cut(mass), cut(conduct), cut(wet).astype(jnp.float32)])
+
+    top, bottom = halo_pair(edges(tile_y - 1, 0), edges(0, 0), "row")
+    left, right = halo_pair(edges(tile_x - 1, 1), edges(0, 1), "col")
     rows = jnp.concatenate([top, bottom], axis=0)
     cols = jnp.concatenate([left, right], axis=0).T
     tile = jax.ShapeDtypeStruct((tile_y, tile_x), jnp.float32)
@@ -153,7 +154,7 @@
         reach_hot.T, jnp.concatenate([phase_out, conc_out], axis=1), precision=lax.Precision.HIGHEST
     )
     answered = lax.all_to_all(
-        reply.reshape(devices, slot_cap * 256),
+        reply.reshape(devices, slot_cap, 256),
         ("row", "col"),
         split_axis=0,
         concat_axis=0,

time: 101 us -> 102 us (level)
    slice x0 -> x3, local copies, waits for them, and re-layouts: none -> 3.14 us  [cut(): return lax.index_in_dim(a, index, axis=dim, keepdims=False)]
    all_to_all x1 -> x0, other arithmetic: 2.49 us -> none  [body(): lax.all_to_all(reply.reshape(devices, slot_cap * 256), ('row', 'col'), sp...]
    add x0 -> x2, other arithmetic: none -> 2.22 us  [edges(): cut(depth) + cut(bed)]
    all_to_all x1 -> x0, local copies, waits for them, and re-layouts: 2.03 us -> none  [body(): lax.all_to_all(reply.reshape(devices, slot_cap * 256), ('row', 'col'), sp...]
    convert_element_type x0 -> x2, other arithmetic: none -> 1.95 us  [edges(): cut(wet).astype(jnp.float32)]
    unnamed x35 -> x25, local copies, waits for them, and re-layouts: 1.41 us -> 0.19 us
    convert_element_type x1, other arithmetic: 1.24 us -> 0.04 us  [body(): opened = wet.astype(jnp.float32)]
  transfers between devices with their start and end apart: 5 -> 5, of which waited for: 1 -> 1; matrix products, arithmetic and copies ran while one was open for 5% -> 9% of each run, Pallas kernels for 0% -> 0%
where the time goes in v4:
time: 102 us; the launch traced here: 101 us
  blocking collectives  30.9 us (30%)
  waiting for transfers between devices  19.2 us (19%)
  starting transfers between devices  17.4 us (17%)
  local copies, waits for them, and re-layouts  16.1 us (16%)
  other arithmetic  6.84 us (7%)
  Pallas kernels  4.83 us (5%)
  matrix products  4.44 us (4%)
  between operations  1.13 us (1%)
    all_to_all x1, blocking collectives, body(): lax.all_to_all(outgoing, ('row', 'col'), split_axis=0, concat_axis=0, til...  30.9 us
    all_to_all x1, waiting for transfers between devices, body(): lax.all_to_all(reply.reshape(devices, slot_cap, 256), ('row', 'col'), spl...  19.2 us
    ppermute x2, starting transfers between devices, halo_pair(): lax.ppermute(last, axis, forward)  8.18 us
    pallas_call x1, Pallas kernels, body(): pl.pallas_call(stencil_kernel, out_shape=[tile, tile, tile], in_specs=[vm...  4.83 us
    all_to_all x1, starting transfers between devices, body(): lax.all_to_all(reply.reshape(devices, slot_cap, 256), ('row', 'col'), spl...  4.74 us
    ppermute x2, starting transfers between devices, halo_pair(): lax.ppermute(first, axis, backward)  4.51 us
    slice x3, local copies, waits for them, and re-layouts, cut(): return lax.index_in_dim(a, index, axis=dim, keepdims=False)  3.14 us
    add x2, other arithmetic, edges(): cut(depth) + cut(bed)  2.22 us
  transfers between devices with their start and end apart: 5, of which 1 were waited for; matrix products, arithmetic and copies ran while one was open for 9% of the time, Pallas kernels for 0%

profile of v4, /device:TPU:1, one launch (start us, length us, event | category | flops | bytes accessed | tf_op | source)
XLA Modules:
  0.0 100.9 jit_solution(18073132959896446288)
XLA Ops:
  0.7 0.8 slice_convert_fusion.1
  1.4 0.7 fusion.40
  2.1 0.8 slice_add_fusion.6
  3.0 1.3 %collective-permute-start.1 = (f32[4,512]{1,0:T(4,128)S(1)}, f32[4,512]{1,0:T(4,128)S(1)}, u32[]{:S(2)}, u32[]{:S(2)}) collective-permute-start(f32[4,512]{1,0:T(4,128)S(1)} %pad_maximum_fusion.2), channel_id=1, source_target_pairs={{32,0},{64,32},{96,64},{33,1},{65,33},{97,65},{34,2},{66,34},{98,6... | collective-permute-start | bytes 24584 | tf_op jit(solution)/shard_map/ppermute | solution.py:13
  4.3 4.7 %collective-permute-start = (f32[4,512]{1,0:T(4,128)S(1)}, f32[4,512]{1,0:T(4,128)S(1)}, u32[]{:S(2)}, u32[]{:S(2)}) collective-permute-start(f32[4,512]{1,0:T(4,128)S(1)} %pad_maximum_fusion.1), channel_id=1, source_target_pairs={{0,32},{32,64},{64,96},{1,33},{33,65},{65,97},{2,34},{34,66},{66,9... | collective-permute-start | bytes 24584 | tf_op jit(solution)/shard_map/ppermute | solution.py:13
  9.0 1.2 %convert_reduce_fusion.1 = (f32[256]{0:T(256)S(1)}, f32[256]{0:T(256)S(1)}) fusion(s32[256,512]{1,0:T(8,128)} %wet_ref.1), kind=kLoop, calls=%fused_computation.46 | loop fusion | flops 512 | bytes 4096 | tf_op jit(solution)/shard_map/convert_element_type | solution.py:84
  10.2 1.2 %slice_reduce_fusion.2 = (f32[256]{0:T(256)S(1)}, f32[256]{0:T(256)S(1)}) fusion(f32[256,512]{1,0:T(8,128)} %cond_ref.1), kind=kLoop, calls=%fused_computation.47 | loop fusion | bytes 4096 | tf_op jit(solution)/shard_map/slice | solution.py:83
  11.4 1.2 %slice_reduce_fusion.3 = (f32[256]{0:T(256)S(1)}, f32[256]{0:T(256)S(1)}) fusion(f32[256,512]{1,0:T(8,128)} %mass_ref.1), kind=kLoop, calls=%fused_computation.48 | loop fusion | bytes 4096 | tf_op jit(solution)/shard_map/slice | solution.py:83
  12.6 0.0 copy-start.10
  12.6 0.0 copy-start.6
  12.6 0.0 copy-start
  12.6 1.4 %add_reduce_fusion.1 = (f32[256]{0:T(256)S(1)}, f32[256]{0:T(256)S(1)}) fusion(f32[256,512]{1,0:T(8,128)} %bed_ref.1, f32[256,512]{1,0:T(8,128)} %depth_ref.1), kind=kLoop, calls=%fused_computation.49 | loop fusion | flops 512 | bytes 6144 | tf_op jit(solution)/shard_map/add | solution.py:84
  14.0 3.2 %collective-permute-start.3 = (f32[4,256]{1,0:T(4,128)S(1)}, f32[4,256]{1,0:T(4,128)S(1)}, u32[]{:S(2)}, u32[]{:S(2)}) collective-permute-start(f32[4,256]{1,0:T(4,128)S(1)} %pad_maximum_fusion.5), channel_id=1, source_target_pairs={{1,0},{2,1},{3,2},{4,3},{5,4},{6,5},{7,6},{8,7},{9,8},{10,9},{11,1... | collective-permute-start | bytes 12296 | tf_op jit(solution)/shard_map/ppermute | solution.py:13
  17.3 3.5 %collective-permute-start.2 = (f32[4,256]{1,0:T(4,128)S(1)}, f32[4,256]{1,0:T(4,128)S(1)}, u32[]{:S(2)}, u32[]{:S(2)}) collective-permute-start(f32[4,256]{1,0:T(4,128)S(1)} %pad_maximum_fusion.4), channel_id=1, source_target_pairs={{0,1},{1,2},{2,3},{3,4},{4,5},{5,6},{6,7},{7,8},{8,9},{9,10},{10,1... | collective-permute-start | bytes 12296 | tf_op jit(solution)/shard_map/ppermute | solution.py:13
  20.9 0.1 copy.27
  21.0 0.2 fusion.18
  21.2 0.1 add_add_fusion
  21.3 0.2 fusion.17
  21.6 0.6 select_reduce_fusion
  22.4 0.1 reshape.146
  22.4 0.7 max.12
  23.2 1.0 %gather_fusion = f32[512,128]{1,0:T(8,128)S(1)} fusion(f32[1024,128]{1,0:T(8,128)S(1)} %reshape.141, s32[1024]{0:T(1024)S(1)} %pad_clamp_fusion.1), kind=kCustom, calls=%fused_computation | custom fusion | bytes 526336 | tf_op jit(solution)/shard_map/gather | solution.py:105
  24.2 0.0 collective-permute-done.3
  24.2 0.8 copy.26
  25.0 0.6 pad_maximum_fusion.rows_ref
  25.6 4.8 %shard_map.156 = (f32[256,512]{1,0:T(8,128)}, f32[256,512]{1,0:T(8,128)}, f32[256,512]{1,0:T(8,128)}) custom-call(f32[256,512]{1,0:T(8,128)} %depth_ref.1, f32[256,512]{1,0:T(8,128)} %bed_ref.1, f32[256,512]{1,0:T(8,128)} %mass_ref.1, f32[256,512]{1,0:T(8,128)} %cond_ref.1, f32[256,512]{1,0:T(8,128)} %settle_ref.1, s32[256,512]{1,0:T(8,128)} %wet_ref.1, ...), custom_call_target="tpu_custom_call" | custom-call | flops 7864320 | bytes 4718592 | tf_op jit(solution)/shard_map/pallas_call | solution.py:92
  30.5 1.1 %reshape.144 = f32[1024,128]{1,0:T(8,128)S(1)} reshape(f32[256,512]{1,0:T(8,128)} %get-tuple-element.9) | data formatting | bytes 1048576 | tf_op jit(solution)/shard_map/reshape | solution.py:104
  31.6 0.1 copy-done.2
  31.7 1.0 %gather_fusion.1 = f32[512,128]{1,0:T(8,128)S(1)} fusion(f32[1024,128]{1,0:T(8,128)S(1)} %reshape.143, s32[1024]{0:T(1024)S(1)} %pad_clamp_fusion.1), kind=kCustom, calls=%fused_computation.1 | custom fusion | bytes 526336 | tf_op jit(solution)/shard_map/gather | solution.py:103
  32.7 1.0 %gather_fusion.2 = f32[512,128]{1,0:T(8,128)S(1)} fusion(f32[1024,128]{1,0:T(8,128)S(1)} %reshape.144, s32[1024]{0:T(1024)S(1)} %pad_clamp_fusion.1), kind=kCustom, calls=%fused_computation.2 | custom fusion | bytes 526336 | tf_op jit(solution)/shard_map/gather | solution.py:104
  33.8 0.1 multiply_multiply_fusion.1
  33.9 1.1 %fusion = f32[1024,256]{1,0:T(8,128)S(1)} fusion(s32[512]{0:T(512)S(1)} %multiply_add_fusion, f32[512,128]{1,0:T(8,128)S(1)} %get-tuple-element.35, f32[512,128]{1,0:T(8,128)S(1)} %get-tuple-element.34), kind=kOutput, calls=%fused_computation.7 | convolution fusion | flops 1611268096 | bytes 1574912 | tf_op jit(solution)/shard_map/dot_general | solution.py:121
  35.0 0.2 reshape.145
  35.2 0.6 broadcast_in_dim.52
  35.8 1.0 %concatenate.37 = f32[128,2176]{1,0:T(8,128)S(1)} concatenate(f32[128,2048]{1,0:T(8,128)S(1)} %reshape.145, f32[128,8]{1,0:T(8,128)S(1)} %reshape.146, f32[128,8]{1,0:T(8,128)} %max.12, f32[128,112]{1,0:T(8,128)} %broadcast_in_dim.52), dimensions={1} | concatenate | bytes 2228224 | tf_op jit(solution)/shard_map/concatenate | solution.py:129
  36.9 0.8 all_to_all.11
  37.6 30.9 %all_to_all.17 = f32[128,1,2176]{2,1,0:T(1,128)S(1)} all-to-all(f32[128,1,2176]{2,1,0:T(1,128)S(1)} %all_to_all.11), channel_id=1, replica_groups=mesh['row'=4,'col'=32] {'row','col'}, dimensions={0} | all-to-all | bytes 2228224 | tf_op jit(solution)/shard_map/all_to_all | solution.py:130
  68.5 0.1 copy.31
  68.6 0.1 fusion.38
  68.6 0.1 slice.176
  68.8 0.1 eq.77
  68.8 0.2 reshape.147
  69.0 0.1 broadcast_in_dim.53
  69.1 0.0 copy-start.7
  69.1 0.0 copy-start.8
  69.1 0.0 copy-start.9
  69.1 0.2 fusion.14
  69.3 0.6 fusion.2
  70.0 0.0 copy-done.7
  70.0 0.1 fusion.43
  70.1 0.1 fusion.44
  70.2 0.1 fusion.41
  70.2 0.1 fusion.42
  70.3 0.1 fusion.33
  70.4 0.1 fusion.30
  70.5 1.6 %convolution_bitcast_fusion = f32[128,8,256]{2,1,0:T(8,128)} fusion(f32[1024]{0:T(1024)S(1)} %eq.77, f32[16,128]{1,0:T(8,128)S(1)} %fusion.33, f32[16,128]{1,0:T(8,128)S(1)} %fusion.30), kind=kOutput, calls=%fused_computation.14 | convolution fusion | flops 50352128 | bytes 1069056 | tf_op jit(solution)/shard_map/dot_general | solution.py:153
  72.1 4.7 %all-to-all-start.1 = ((f32[128,8,256]{2,1,0:T(8,128)}), f32[128,8,256]{2,1,0:T(8,128)S(1)}, u32[]{:S(2)}, u32[]{:S(2)}) async-start(f32[128,8,256]{2,1,0:T(8,128)} %convolution_bitcast_fusion), calls=%async_computation.1 | async-start | bytes 2097152 | tf_op jit(solution)/shard_map/all_to_all | solution.py:156
  77.0 19.2 %all-to-all-done.1 = f32[128,8,256]{2,1,0:T(8,128)S(1)} async-done(((f32[128,8,256]{2,1,0:T(8,128)}), f32[128,8,256]{2,1,0:T(8,128)S(1)}, u32[]{:S(2)}, u32[]{:S(2)}) %all-to-all-start.1) | async-done | bytes 1048608 | tf_op jit(solution)/shard_map/all_to_all | solution.py:156
  96.2 1.6 %gather_fusion.3 = f32[512,256]{1,0:T(8,128)S(1)} fusion(f32[1024,256]{1,0:T(8,128)S(1)} %bitcast.27, s32[1024]{0:T(1024)S(1)} %pad_clamp_fusion), kind=kCustom, calls=%fused_computation.3 | custom fusion | bytes 1050624 | tf_op jit(solution)/shard_map/gather | solution.py:163
  97.7 0.1 fusion.16
  97.9 1.1 %fusion.1 = f32[1024,256]{1,0:T(8,128)S(1)} fusion(s32[512]{0:T(512)S(1)} %copy-done.11, f32[512,128]{1,0:T(8,128)S(1)} %get-tuple-element.27, f32[512,128]{1,0:T(8,128)S(1)} %get-tuple-element.26), kind=kOutput, calls=%fused_computation.9 | convolution fusion | flops 1611268096 | bytes 1574912 | tf_op jit(solution)/shard_map/dot_general | solution.py:174
  99.0 0.1 slice_add_fusion
  99.1 0.9 reshape.150
  100.0 0.9 reshape.151
  (40 shorter events, 0.4 us)
Async XLA Ops:
  0.6 20.2 %copy-start.11 = (s32[512]{0:T(512)S(1)}, s32[512]{0:T(512)}, u32[]{:S(2)}) copy-start(s32[512]{0:T(512)} %param.19) | copy-start | bytes 6148
  0.6 20.2 %copy-start.5 = (s32[512,1]{0,1:T(1,128)S(1)}, s32[512,1]{0,1:T(1,128)}, u32[]{:S(2)}) copy-start(s32[512,1]{0,1:T(1,128)} %param.20) | copy-start | bytes 6148
  3.0 22.0 %collective-permute-start.1 = (f32[4,512]{1,0:T(4,128)S(1)}, f32[4,512]{1,0:T(4,128)S(1)}, u32[]{:S(2)}, u32[]{:S(2)}) collective-permute-start(f32[4,512]{1,0:T(4,128)S(1)} %pad_maximum_fusion.2), channel_id=1, source_target_pairs={{32,0},{64,32},{96,64},{33,1},{65,33},{97,65},{34,2},{66,34},{98,6... | collective-permute-start | bytes 24584 | tf_op jit(solution)/shard_map/ppermute | solution.py:13
  4.3 20.7 %collective-permute-start = (f32[4,512]{1,0:T(4,128)S(1)}, f32[4,512]{1,0:T(4,128)S(1)}, u32[]{:S(2)}, u32[]{:S(2)}) collective-permute-start(f32[4,512]{1,0:T(4,128)S(1)} %pad_maximum_fusion.1), channel_id=1, source_target_pairs={{0,32},{32,64},{64,96},{1,33},{33,65},{65,97},{2,34},{34,66},{66,9... | collective-permute-start | bytes 24584 | tf_op jit(solution)/shard_map/ppermute | solution.py:13
  12.6 9.0 %copy-start.10 = (s32[512]{0:T(512)S(1)}, s32[512]{0:T(512)}, u32[]{:S(2)}) copy-start(s32[512]{0:T(512)} %param.21) | copy-start | bytes 6148
  12.6 9.0 %copy-start.6 = (f32[512]{0:T(512)S(1)}, f32[512]{0:T(512)}, u32[]{:S(2)}) copy-start(f32[512]{0:T(512)} %param.22) | copy-start | bytes 6148
  12.6 9.7 %copy-start = (s32[256,512]{1,0:T(8,128)S(1)}, s32[256,512]{1,0:T(8,128)}, u32[]{:S(2)}) copy-start(s32[256,512]{1,0:T(8,128)} %wet_ref.1) | copy-start | bytes 1572868
  14.0 10.2 %collective-permute-start.3 = (f32[4,256]{1,0:T(4,128)S(1)}, f32[4,256]{1,0:T(4,128)S(1)}, u32[]{:S(2)}, u32[]{:S(2)}) collective-permute-start(f32[4,256]{1,0:T(4,128)S(1)} %pad_maximum_fusion.5), channel_id=1, source_target_pairs={{1,0},{2,1},{3,2},{4,3},{5,4},{6,5},{7,6},{8,7},{9,8},{10,9},{11,1... | collective-permute-start | bytes 12296 | tf_op jit(solution)/shard_map/ppermute | solution.py:13
  17.3 6.9 %collective-permute-start.2 = (f32[4,256]{1,0:T(4,128)S(1)}, f32[4,256]{1,0:T(4,128)S(1)}, u32[]{:S(2)}, u32[]{:S(2)}) collective-permute-start(f32[4,256]{1,0:T(4,128)S(1)} %pad_maximum_fusion.4), channel_id=1, source_target_pairs={{0,1},{1,2},{2,3},{3,4},{4,5},{5,6},{6,7},{7,8},{8,9},{9,10},{10,1... | collective-permute-start | bytes 12296 | tf_op jit(solution)/shard_map/ppermute | solution.py:13
  30.5 1.2 %copy-start.2 = (f32[256,512]{1,0:T(8,128)S(1)}, f32[256,512]{1,0:T(8,128)}, u32[]{:S(2)}) copy-start(f32[256,512]{1,0:T(8,128)} %get-tuple-element.8) | copy-start | bytes 1572868
  69.1 0.9 copy-start.7
  69.1 0.9 copy-start.8
  69.1 0.9 copy-start.9
  70.4 1.7 %copy-start.3 = (f32[16,128]{1,0:T(8,128)}, f32[16,128]{1,0:T(8,128)S(1)}, u32[]{:S(2)}) copy-start(f32[16,128]{1,0:T(8,128)S(1)} %fusion.33) | copy-start | bytes 24580
  70.5 1.6 %copy-start.4 = (f32[16,128]{1,0:T(8,128)}, f32[16,128]{1,0:T(8,128)S(1)}, u32[]{:S(2)}) copy-start(f32[16,128]{1,0:T(8,128)S(1)} %fusion.30) | copy-start | bytes 24580
  72.1 4.8 %copy-start.1 = (f32[256,512]{1,0:T(8,128)S(1)}, f32[256,512]{1,0:T(8,128)}, u32[]{:S(2)}) copy-start(f32[256,512]{1,0:T(8,128)} %get-tuple-element.7) | copy-start | bytes 1572868
  72.1 24.1 %all-to-all-start.1 = ((f32[128,8,256]{2,1,0:T(8,128)}), f32[128,8,256]{2,1,0:T(8,128)S(1)}, u32[]{:S(2)}, u32[]{:S(2)}) async-start(f32[128,8,256]{2,1,0:T(8,128)} %convolution_bitcast_fusion), calls=%async_computation.1 | async-start | bytes 2097152 | tf_op jit(solution)/shard_map/all_to_all | solution.py:156

commit v5 on v4

--- a/solution.py
+++ b/solution.py
@@ -78,13 +78,9 @@
     tile_y, tile_x = depth.shape
     opened = wet.astype(jnp.float32)
 
-    def edges(index, dim):
-        def cut(a):
-            return lax.index_in_dim(a, index, axis=dim, keepdims=False)
-        return jnp.stack([cut(depth) + cut(bed), cut(mass), cut(conduct), cut(wet).astype(jnp.float32)])
-
-    top, bottom = halo_pair(edges(tile_y - 1, 0), edges(0, 0), "row")
-    left, right = halo_pair(edges(tile_x - 1, 1), edges(0, 1), "col")
+    stacked = jnp.stack([depth + bed, mass, conduct, opened])
+    top, bottom = halo_pair(stacked[:, tile_y - 1, :], stacked[:, 0, :], "row")
+    left, right = halo_pair(stacked[:, :, tile_x - 1], stacked[:, :, 0], "col")
     rows = jnp.concatenate([top, bottom], axis=0)
     cols = jnp.concatenate([left, right], axis=0).T
     tile = jax.ShapeDtypeStruct((tile_y, tile_x), jnp.float32)

time: 102 us -> 97 us (0.951)
  other arithmetic: 6.84 us -> 4.36 us
  local copies, waits for them, and re-layouts: 16.1 us -> 14.1 us
    slice x3 -> x0, local copies, waits for them, and re-layouts: 3.14 us -> none  [cut(): return lax.index_in_dim(a, index, axis=dim, keepdims=False)]
    add x2 -> x0, other arithmetic: 2.22 us -> none  [edges(): cut(depth) + cut(bed)]
    convert_element_type x2 -> x0, other arithmetic: 1.95 us -> none  [edges(): cut(wet).astype(jnp.float32)]
    unnamed x25 -> x33, local copies, waits for them, and re-layouts: 0.19 us -> 1.4 us
    convert_element_type x1, other arithmetic: 0.04 us -> 1.24 us  [body(): opened = wet.astype(jnp.float32)]
  transfers between devices with their start and end apart: 5 -> 5, of which waited for: 1 -> 1; matrix products, arithmetic and copies ran while one was open for 9% -> 5% of each run, Pallas kernels for 0% -> 0%
where the time goes in v5:
time: 97 us; the launch traced here: 96.6 us
  blocking collectives  30.9 us (32%)
  waiting for transfers between devices  19.2 us (20%)
  starting transfers between devices  17.6 us (18%)
  local copies, waits for them, and re-layouts  14.1 us (15%)
  Pallas kernels  4.83 us (5%)
  matrix products  4.43 us (5%)
  other arithmetic  4.36 us (4%)
  between operations  1.13 us (1%)
    all_to_all x1, blocking collectives, body(): lax.all_to_all(outgoing, ('row', 'col'), split_axis=0, concat_axis=0, til...  30.9 us
    all_to_all x1, waiting for transfers between devices, body(): lax.all_to_all(reply.reshape(devices, slot_cap, 256), ('row', 'col'), spl...  19.2 us
    ppermute x2, starting transfers between devices, halo_pair(): lax.ppermute(last, axis, forward)  8.18 us
    pallas_call x1, Pallas kernels, body(): pl.pallas_call(stencil_kernel, out_shape=[tile, tile, tile], in_specs=[vm...  4.83 us
    all_to_all x1, starting transfers between devices, body(): lax.all_to_all(reply.reshape(devices, slot_cap, 256), ('row', 'col'), spl...  4.74 us
    ppermute x2, starting transfers between devices, halo_pair(): lax.ppermute(first, axis, backward)  4.64 us
  transfers between devices with their start and end apart: 5, of which 1 were waited for; matrix products, arithmetic and copies ran while one was open for 5% of the time, Pallas kernels for 0%

profile of v5, /device:TPU:1, one launch (start us, length us, event | category | flops | bytes accessed | tf_op | source)
XLA Modules:
  0.0 96.6 jit_solution(11825948006156033085)
XLA Ops:
  0.6 0.0 copy-start.2
  0.6 0.0 copy-start.3
  0.7 1.2 %fusion.40 = (f32[256,512]{1,0:T(8,128)S(1)}, f32[1,256,512]{2,1,0:T(8,128)S(1)}) fusion(s32[256,512]{1,0:T(8,128)} %wet_ref.1), kind=kLoop, calls=%fused_computation.86 | loop fusion | flops 131072 | bytes 1572864 | tf_op jit(solution)/shard_map/convert_element_type | solution.py:79
  1.9 0.1 copy-done.3
  2.0 0.1 add_bitcast_fusion
  2.1 1.0 copy-done
  3.0 0.2 copy-done.1
  3.2 0.0 copy-start.14
  3.2 0.0 copy-start.8
  3.2 1.3 %collective-permute-start.1 = (f32[4,512]{1,0:T(4,128)S(1)}, f32[4,512]{1,0:T(4,128)S(1)}, u32[]{:S(2)}, u32[]{:S(2)}) collective-permute-start(f32[4,512]{1,0:T(4,128)S(1)} %bitcast.44), channel_id=1, source_target_pairs={{32,0},{64,32},{96,64},{33,1},{65,33},{97,65},{34,2},{66,34},{98,6... | collective-permute-start | bytes 24584 | tf_op jit(solution)/shard_map/ppermute | solution.py:13
  4.6 4.7 %collective-permute-start = (f32[4,512]{1,0:T(4,128)S(1)}, f32[4,512]{1,0:T(4,128)S(1)}, u32[]{:S(2)}, u32[]{:S(2)}) collective-permute-start(f32[4,512]{1,0:T(4,128)S(1)} %bitcast.45), channel_id=1, source_target_pairs={{0,32},{32,64},{64,96},{1,33},{33,65},{65,97},{2,34},{34,66},{66,9... | collective-permute-start | bytes 24584 | tf_op jit(solution)/shard_map/ppermute | solution.py:13
  9.2 0.5 maximum_reduce_fusion
  9.8 0.0 copy-start.9
  9.8 3.3 %collective-permute-start.3 = (f32[4,256]{1,0:T(4,128)S(1)}, f32[4,256]{1,0:T(4,128)S(1)}, u32[]{:S(2)}, u32[]{:S(2)}) collective-permute-start(f32[4,256]{1,0:T(4,128)S(1)} %get-tuple-element.11), channel_id=1, source_target_pairs={{1,0},{2,1},{3,2},{4,3},{5,4},{6,5},{7,6},{8,7},{9,8},{10,9},{11,1... | collective-permute-start | bytes 12296 | tf_op jit(solution)/shard_map/ppermute | solution.py:13
  13.1 3.5 %collective-permute-start.2 = (f32[4,256]{1,0:T(4,128)S(1)}, f32[4,256]{1,0:T(4,128)S(1)}, u32[]{:S(2)}, u32[]{:S(2)}) collective-permute-start(f32[4,256]{1,0:T(4,128)S(1)} %get-tuple-element.10), channel_id=1, source_target_pairs={{0,1},{1,2},{2,3},{3,4},{4,5},{5,6},{6,7},{7,8},{8,9},{9,10},{10,1... | collective-permute-start | bytes 12296 | tf_op jit(solution)/shard_map/ppermute | solution.py:13
  16.7 0.1 copy.40
  16.8 0.2 fusion.19
  17.1 0.1 add_add_fusion
  17.1 0.2 fusion.18
  17.4 0.6 select_reduce_fusion
  18.1 0.1 reshape.88
  18.2 0.7 max.12
  18.9 1.0 %gather_fusion = f32[512,128]{1,0:T(8,128)S(1)} fusion(f32[1024,128]{1,0:T(8,128)S(1)} %reshape.83, s32[1024]{0:T(1024)S(1)} %pad_clamp_fusion.1), kind=kCustom, calls=%fused_computation | custom fusion | bytes 526336 | tf_op jit(solution)/shard_map/gather | solution.py:101
  20.0 0.8 copy.39
  20.8 0.6 pad_maximum_fusion.3.rows_ref
  21.4 4.8 %shard_map.156 = (f32[256,512]{1,0:T(8,128)}, f32[256,512]{1,0:T(8,128)}, f32[256,512]{1,0:T(8,128)}) custom-call(f32[256,512]{1,0:T(8,128)} %depth_ref.1, f32[256,512]{1,0:T(8,128)} %bed_ref.1, f32[256,512]{1,0:T(8,128)} %mass_ref.1, f32[256,512]{1,0:T(8,128)} %cond_ref.1, f32[256,512]{1,0:T(8,128)} %settle_ref.1, s32[256,512]{1,0:T(8,128)} %wet_ref.1, ...), custom_call_target="tpu_custom_call" | custom-call | flops 7864320 | bytes 4718592 | tf_op jit(solution)/shard_map/pallas_call | solution.py:88
  26.2 1.1 %reshape.86 = f32[1024,128]{1,0:T(8,128)S(1)} reshape(f32[256,512]{1,0:T(8,128)} %get-tuple-element.9) | data formatting | bytes 1048576 | tf_op jit(solution)/shard_map/reshape | solution.py:100
  27.4 0.1 copy-done.5
  27.5 1.0 %gather_fusion.1 = f32[512,128]{1,0:T(8,128)S(1)} fusion(f32[1024,128]{1,0:T(8,128)S(1)} %reshape.85, s32[1024]{0:T(1024)S(1)} %pad_clamp_fusion.1), kind=kCustom, calls=%fused_computation.1 | custom fusion | bytes 526336 | tf_op jit(solution)/shard_map/gather | solution.py:99
  28.5 1.0 %gather_fusion.2 = f32[512,128]{1,0:T(8,128)S(1)} fusion(f32[1024,128]{1,0:T(8,128)S(1)} %reshape.86, s32[1024]{0:T(1024)S(1)} %pad_clamp_fusion.1), kind=kCustom, calls=%fused_computation.2 | custom fusion | bytes 526336 | tf_op jit(solution)/shard_map/gather | solution.py:100
  29.6 0.1 multiply_multiply_fusion.1
  29.7 1.1 %fusion = f32[1024,256]{1,0:T(8,128)S(1)} fusion(s32[512]{0:T(512)S(1)} %multiply_add_fusion, f32[512,128]{1,0:T(8,128)S(1)} %get-tuple-element.25, f32[512,128]{1,0:T(8,128)S(1)} %get-tuple-element.24), kind=kOutput, calls=%fused_computation.7 | convolution fusion | flops 1611268096 | bytes 1574912 | tf_op jit(solution)/shard_map/dot_general | solution.py:117
  30.8 0.2 reshape.87
  31.0 0.6 broadcast_in_dim.52
  31.6 1.0 %concatenate.37 = f32[128,2176]{1,0:T(8,128)S(1)} concatenate(f32[128,2048]{1,0:T(8,128)S(1)} %reshape.87, f32[128,8]{1,0:T(8,128)S(1)} %reshape.88, f32[128,8]{1,0:T(8,128)} %max.12, f32[128,112]{1,0:T(8,128)} %broadcast_in_dim.52), dimensions={1} | concatenate | bytes 2228224 | tf_op jit(solution)/shard_map/concatenate | solution.py:125
  32.6 0.8 all_to_all.11
  33.4 30.9 %all_to_all.17 = f32[128,1,2176]{2,1,0:T(1,128)S(1)} all-to-all(f32[128,1,2176]{2,1,0:T(1,128)S(1)} %all_to_all.11), channel_id=1, replica_groups=mesh['row'=4,'col'=32] {'row','col'}, dimensions={0} | all-to-all | bytes 2228224 | tf_op jit(solution)/shard_map/all_to_all | solution.py:126
  64.3 0.1 copy.48
  64.3 0.1 fusion.39
  64.4 0.1 slice.112
  64.5 0.1 eq.77
  64.6 0.2 reshape.89
  64.8 0.1 broadcast_in_dim.53
  64.9 0.0 copy-start.10
  64.9 0.0 copy-start.11
  64.9 0.0 copy-start.12
  64.9 0.2 fusion.15
  65.1 0.6 fusion.2
  65.8 0.0 copy-done.10
  65.8 0.1 fusion.41
  65.9 0.1 fusion.42
  65.9 0.1 fusion.44
  66.0 0.1 fusion.43
  66.1 0.1 fusion.31
  66.2 0.0 copy-start.7
  66.2 1.6 %convolution_bitcast_fusion = f32[128,8,256]{2,1,0:T(8,128)} fusion(f32[1024]{0:T(1024)S(1)} %eq.77, f32[16,128]{1,0:T(8,128)S(1)} %get-tuple-element.37, f32[16,128]{1,0:T(8,128)S(1)} %get-tuple-element.36), kind=kOutput, calls=%fused_computation.14 | convolution fusion | flops 50352128 | bytes 1069056 | tf_op jit(solution)/shard_map/dot_general | solution.py:149
  67.8 4.7 %all-to-all-start.1 = ((f32[128,8,256]{2,1,0:T(8,128)}), f32[128,8,256]{2,1,0:T(8,128)S(1)}, u32[]{:S(2)}, u32[]{:S(2)}) async-start(f32[128,8,256]{2,1,0:T(8,128)} %convolution_bitcast_fusion), calls=%async_computation.1 | async-start | bytes 2097152 | tf_op jit(solution)/shard_map/all_to_all | solution.py:152
  72.7 19.2 %all-to-all-done.1 = f32[128,8,256]{2,1,0:T(8,128)S(1)} async-done(((f32[128,8,256]{2,1,0:T(8,128)}), f32[128,8,256]{2,1,0:T(8,128)S(1)}, u32[]{:S(2)}, u32[]{:S(2)}) %all-to-all-start.1) | async-done | bytes 1048608 | tf_op jit(solution)/shard_map/all_to_all | solution.py:152
  91.9 1.6 %gather_fusion.3 = f32[512,256]{1,0:T(8,128)S(1)} fusion(f32[1024,256]{1,0:T(8,128)S(1)} %bitcast.31, s32[1024]{0:T(1024)S(1)} %pad_clamp_fusion), kind=kCustom, calls=%fused_computation.3 | custom fusion | bytes 1050624 | tf_op jit(solution)/shard_map/gather | solution.py:159
  93.5 0.1 fusion.17
  93.6 1.1 %fusion.1 = f32[1024,256]{1,0:T(8,128)S(1)} fusion(s32[512]{0:T(512)S(1)} %copy-done.14, f32[512,128]{1,0:T(8,128)S(1)} %get-tuple-element.21, f32[512,128]{1,0:T(8,128)S(1)} %get-tuple-element.20), kind=kOutput, calls=%fused_computation.9 | convolution fusion | flops 1611268096 | bytes 1574912 | tf_op jit(solution)/shard_map/dot_general | solution.py:170
  94.7 0.1 slice_add_fusion
  94.8 0.9 reshape.92
  95.7 0.9 reshape.93
  (39 shorter events, 0.3 us)
Async XLA Ops:
  0.6 1.3 %copy-start.2 = (f32[256,512]{1,0:T(8,128)S(1)}, f32[256,512]{1,0:T(8,128)}, u32[]{:S(2)}) copy-start(f32[256,512]{1,0:T(8,128)} %depth_ref.1) | copy-start | bytes 1572868
  0.6 1.4 %copy-start.3 = (f32[256,512]{1,0:T(8,128)S(1)}, f32[256,512]{1,0:T(8,128)}, u32[]{:S(2)}) copy-start(f32[256,512]{1,0:T(8,128)} %bed_ref.1) | copy-start | bytes 1572868
  2.0 1.0 %copy-start = (f32[256,512]{1,0:T(8,128)S(1)}, f32[256,512]{1,0:T(8,128)}, u32[]{:S(2)}) copy-start(f32[256,512]{1,0:T(8,128)} %mass_ref.1) | copy-start | bytes 1572868
  2.0 1.2 %copy-start.1 = (f32[256,512]{1,0:T(8,128)S(1)}, f32[256,512]{1,0:T(8,128)}, u32[]{:S(2)}) copy-start(f32[256,512]{1,0:T(8,128)} %cond_ref.1) | copy-start | bytes 1572868
  3.2 13.4 %copy-start.14 = (s32[512]{0:T(512)S(1)}, s32[512]{0:T(512)}, u32[]{:S(2)}) copy-start(s32[512]{0:T(512)} %param.19) | copy-start | bytes 6148
  3.2 13.5 %copy-start.8 = (s32[512,1]{0,1:T(1,128)S(1)}, s32[512,1]{0,1:T(1,128)}, u32[]{:S(2)}) copy-start(s32[512,1]{0,1:T(1,128)} %param.20) | copy-start | bytes 6148
  3.2 17.5 %collective-permute-start.1 = (f32[4,512]{1,0:T(4,128)S(1)}, f32[4,512]{1,0:T(4,128)S(1)}, u32[]{:S(2)}, u32[]{:S(2)}) collective-permute-start(f32[4,512]{1,0:T(4,128)S(1)} %bitcast.44), channel_id=1, source_target_pairs={{32,0},{64,32},{96,64},{33,1},{65,33},{97,65},{34,2},{66,34},{98,6... | collective-permute-start | bytes 24584 | tf_op jit(solution)/shard_map/ppermute | solution.py:13
  4.6 16.2 %collective-permute-start = (f32[4,512]{1,0:T(4,128)S(1)}, f32[4,512]{1,0:T(4,128)S(1)}, u32[]{:S(2)}, u32[]{:S(2)}) collective-permute-start(f32[4,512]{1,0:T(4,128)S(1)} %bitcast.45), channel_id=1, source_target_pairs={{0,32},{32,64},{64,96},{1,33},{33,65},{65,97},{2,34},{34,66},{66,9... | collective-permute-start | bytes 24584 | tf_op jit(solution)/shard_map/ppermute | solution.py:13
  9.7 7.7 %copy-start.13 = (s32[512]{0:T(512)S(1)}, s32[512]{0:T(512)}, u32[]{:S(2)}) copy-start(s32[512]{0:T(512)} %param.21) | copy-start | bytes 6148
  9.8 7.7 %copy-start.9 = (f32[512]{0:T(512)S(1)}, f32[512]{0:T(512)}, u32[]{:S(2)}) copy-start(f32[512]{0:T(512)} %param.22) | copy-start | bytes 6148
  9.8 10.2 %collective-permute-start.3 = (f32[4,256]{1,0:T(4,128)S(1)}, f32[4,256]{1,0:T(4,128)S(1)}, u32[]{:S(2)}, u32[]{:S(2)}) collective-permute-start(f32[4,256]{1,0:T(4,128)S(1)} %get-tuple-element.11), channel_id=1, source_target_pairs={{1,0},{2,1},{3,2},{4,3},{5,4},{6,5},{7,6},{8,7},{9,8},{10,9},{11,1... | collective-permute-start | bytes 12296 | tf_op jit(solution)/shard_map/ppermute | solution.py:13
  13.1 6.9 %collective-permute-start.2 = (f32[4,256]{1,0:T(4,128)S(1)}, f32[4,256]{1,0:T(4,128)S(1)}, u32[]{:S(2)}, u32[]{:S(2)}) collective-permute-start(f32[4,256]{1,0:T(4,128)S(1)} %get-tuple-element.10), channel_id=1, source_target_pairs={{0,1},{1,2},{2,3},{3,4},{4,5},{5,6},{6,7},{7,8},{8,9},{9,10},{10,1... | collective-permute-start | bytes 12296 | tf_op jit(solution)/shard_map/ppermute | solution.py:13
  26.2 1.2 %copy-start.5 = (f32[256,512]{1,0:T(8,128)S(1)}, f32[256,512]{1,0:T(8,128)}, u32[]{:S(2)}) copy-start(f32[256,512]{1,0:T(8,128)} %get-tuple-element.8) | copy-start | bytes 1572868
  64.9 0.9 copy-start.10
  64.9 0.9 copy-start.11
  64.9 0.9 copy-start.12
  66.2 1.6 %copy-start.6 = (f32[16,128]{1,0:T(8,128)}, f32[16,128]{1,0:T(8,128)S(1)}, u32[]{:S(2)}) copy-start(f32[16,128]{1,0:T(8,128)S(1)} %get-tuple-element.36) | copy-start | bytes 24580
  66.2 1.6 %copy-start.7 = (f32[16,128]{1,0:T(8,128)}, f32[16,128]{1,0:T(8,128)S(1)}, u32[]{:S(2)}) copy-start(f32[16,128]{1,0:T(8,128)S(1)} %get-tuple-element.37) | copy-start | bytes 24580
  67.8 4.8 %copy-start.4 = (f32[256,512]{1,0:T(8,128)S(1)}, f32[256,512]{1,0:T(8,128)}, u32[]{:S(2)}) copy-start(f32[256,512]{1,0:T(8,128)} %get-tuple-element.7) | copy-start | bytes 1572868
  67.8 24.1 %all-to-all-start.1 = ((f32[128,8,256]{2,1,0:T(8,128)}), f32[128,8,256]{2,1,0:T(8,128)S(1)}, u32[]{:S(2)}, u32[]{:S(2)}) async-start(f32[128,8,256]{2,1,0:T(8,128)} %convolution_bitcast_fusion), calls=%async_computation.1 | async-start | bytes 2097152 | tf_op jit(solution)/shard_map/all_to_all | solution.py:152

commit v6 on v5

--- a/solution.py
+++ b/solution.py
@@ -14,7 +14,7 @@
 
 
 def stencil_kernel(depth_ref, bed_ref, mass_ref, cond_ref, settle_ref, wet_ref, rows_ref, cols_ref,
-                   depth1_ref, mass1_ref, surf1_ref):
+                   depth1_ref, mass1_ref, surf_blocks_ref, mass_blocks_ref, open_blocks_ref):
     depth = depth_ref[...]
     bed = bed_ref[...]
     mass = mass_ref[...]
@@ -49,9 +49,16 @@
         water_gain = water_gain + coeff * (neighbour(0, step_y, step_x) - surface)
         mass_gain = mass_gain + coeff * (neighbour(1, step_y, step_x) - mass)
     depth1 = depth + water_gain
+    mass1 = (mass + mass_gain) * jnp.exp(-settle_ref[...])
     depth1_ref[...] = depth1
-    mass1_ref[...] = (mass + mass_gain) * jnp.exp(-settle_ref[...])
-    surf1_ref[...] = depth1 + bed
+    mass1_ref[...] = mass1
+    per_row = tile_x // 128
+    for j in range(per_row):
+        lanes = slice(j * 128, (j + 1) * 128)
+        rows_j = pl.ds(j, tile_y, stride=per_row)
+        surf_blocks_ref[rows_j, :] = (depth1 + bed)[:, lanes]
+        mass_blocks_ref[rows_j, :] = mass1[:, lanes]
+        open_blocks_ref[rows_j, :] = opened[:, lanes]
 
 
 def smooth_reach(values):
@@ -85,20 +92,21 @@
     cols = jnp.concatenate([left, right], axis=0).T
     tile = jax.ShapeDtypeStruct((tile_y, tile_x), jnp.float32)
     vmem = pl.BlockSpec(memory_space=pltpu.VMEM)
-    depth1, mass1, surface1 = pl.pallas_call(
+    blocks = tile_y * tile_x // 128
+    block_rows = jax.ShapeDtypeStruct((blocks, 128), jnp.float32)
+    depth1, mass1, surf_blocks, mass_blocks, open_blocks = pl.pallas_call(
         stencil_kernel,
-        out_shape=[tile, tile, tile],
+        out_shape=[tile, tile, block_rows, block_rows, block_rows],
         in_specs=[vmem] * 8,
-        out_specs=[vmem] * 3,
+        out_specs=[vmem] * 5,
         cost_estimate=pl.CostEstimate(
-            flops=60 * tile_y * tile_x, transcendentals=tile_y * tile_x, bytes_accessed=36 * tile_y * tile_x
+            flops=60 * tile_y * tile_x, transcendentals=tile_y * tile_x, bytes_accessed=44 * tile_y * tile_x
         ),
     )(depth, bed, mass, conduct, settle, wet, rows, cols)
 
-    blocks = tile_y * tile_x // 128
-    surf_rows = surface1.reshape(blocks, 128)[link_block]
-    mass_rows = mass1.reshape(blocks, 128)[link_block]
-    weight = link_coef[:, None] * opened.reshape(blocks, 128)[link_block]
+    surf_rows = surf_blocks[link_block]
+    mass_rows = mass_blocks[link_block]
+    weight = link_coef[:, None] * open_blocks[link_block]
     ws = weight * surf_rows
     wm = weight * mass_rows
 
@@ -164,12 +172,18 @@
         ],
         axis=1,
     )
-    block_hot = (jnp.arange(blocks, dtype=jnp.int32)[:, None] == link_block[None, :]).astype(
-        jnp.float32
-    )
-    gained = jnp.dot(block_hot, applied, precision=lax.Precision.HIGHEST)
-    depth_out = (depth1.reshape(blocks, 128) + gained[:, :128]).reshape(tile_y, tile_x)
-    mass_out = (mass1.reshape(blocks, 128) + gained[:, 128:]).reshape(tile_y, tile_x)
+    per_row = tile_x // 128
+    row_ids = jnp.arange(tile_y, dtype=jnp.int32)[:, None]
+    gained = [
+        jnp.dot(
+            (row_ids * per_row + j == link_block[None, :]).astype(jnp.float32),
+            applied,
+            precision=lax.Precision.HIGHEST,
+        )
+        for j in range(per_row)
+    ]
+    depth_out = depth1 + jnp.concatenate([g[:, :128] for g in gained], axis=1)
+    mass_out = mass1 + jnp.concatenate([g[:, 128:] for g in gained], axis=1)
     return (depth_out, mass_out, phase_out, conc_out)
 
 

time: 97 us -> 95.3 us (0.982)
  local copies, waits for them, and re-layouts: 14.1 us -> 10.1 us
  other arithmetic: 4.36 us -> 5.43 us
    reshape x6 -> x0, local copies, waits for them, and re-layouts: 2.98 us -> none  [the longest x1 1.13 us: body(): mass_rows = mass1.reshape(blocks, 128)[link_block]]
    convert_element_type x1 -> x0, other arithmetic: 1.24 us -> none  [body(): opened = wet.astype(jnp.float32)]
    another operation x1 -> x2, other arithmetic: 0.08 us -> 1.3 us  [body(): stacked = jnp.stack([depth + bed, mass, conduct, opened])]
    gather x3, local copies, waits for them, and re-layouts: 3.11 us -> 4.2 us  [the longest x1 2.13 us: body(): surf_rows = surf_blocks[link_block]]
    add x1 -> x4, other arithmetic: 0.11 us -> 1.12 us  [the longest x1 1.11 us: body(): depth_out = depth1 + jnp.concatenate([g[:, :128] for g in gained], axis=1)]
  transfers between devices with their start and end apart: 5 -> 5, of which waited for: 1 -> 1; matrix products, arithmetic and copies ran while one was open for 5% -> 3% of each run, Pallas kernels for 0% -> 0%
where the time goes in v6:
time: 95.3 us; the launch traced here: 94.9 us
  blocking collectives  31 us (33%)
  waiting for transfers between devices  19.2 us (20%)
  starting transfers between devices  17.4 us (18%)
  local copies, waits for them, and re-layouts  10.1 us (11%)
  other arithmetic  5.43 us (6%)
  Pallas kernels  5.24 us (5%)
  matrix products  5.17 us (5%)
  between operations  1.22 us (1%)
    all_to_all x1, blocking collectives, body(): lax.all_to_all(outgoing, ('row', 'col'), split_axis=0, concat_axis=0, til...  31 us
    all_to_all x1, waiting for transfers between devices, body(): lax.all_to_all(reply.reshape(devices, slot_cap, 256), ('row', 'col'), spl...  19.2 us
    ppermute x2, starting transfers between devices, halo_pair(): lax.ppermute(last, axis, forward)  8.18 us
    pallas_call x1, Pallas kernels, body(): pl.pallas_call(stencil_kernel, out_shape=[tile, tile, block_rows, block_r...  5.24 us
    ppermute x2, starting transfers between devices, halo_pair(): lax.ppermute(first, axis, backward)  4.64 us
    all_to_all x1, starting transfers between devices, body(): lax.all_to_all(reply.reshape(devices, slot_cap, 256), ('row', 'col'), spl...  4.62 us
    gather x1, local copies, waits for them, and re-layouts, body(): surf_rows = surf_blocks[link_block]  2.13 us
  transfers between devices with their start and end apart: 5, of which 1 were waited for; matrix products, arithmetic and copies ran while one was open for 3% of the time, Pallas kernels for 0%

profile of v6, /device:TPU:1, one launch (start us, length us, event | category | flops | bytes accessed | tf_op | source)
XLA Modules:
  0.0 94.9 jit_solution(13596182271165742603)
XLA Ops:
  0.6 0.0 copy-start.4
  0.6 0.0 copy-start.5
  0.7 0.0 copy-start.3
  0.7 0.0 copy-start.2
  0.7 1.2 %convert_bitcast_fusion = f32[1,256,512]{2,1,0:T(8,128)S(1)} fusion(s32[256,512]{1,0:T(8,128)} %wet_ref.1), kind=kLoop, calls=%fused_computation.27 | loop fusion | flops 131072 | bytes 1048576 | tf_op jit(solution)/shard_map/stack | solution.py:88
  1.9 0.1 copy-done.5
  2.0 0.1 add_bitcast_fusion
  2.1 0.1 copy-done.3
  2.2 0.2 copy-done.2
  2.3 0.0 copy-start.8
  2.3 0.0 copy-start.11
  2.4 1.3 %collective-permute-start.1 = (f32[4,512]{1,0:T(4,128)S(1)}, f32[4,512]{1,0:T(4,128)S(1)}, u32[]{:S(2)}, u32[]{:S(2)}) collective-permute-start(f32[4,512]{1,0:T(4,128)S(1)} %bitcast.44), channel_id=1, source_target_pairs={{32,0},{64,32},{96,64},{33,1},{65,33},{97,65},{34,2},{66,34},{98,6... | collective-permute-start | bytes 24584 | tf_op jit(solution)/shard_map/ppermute | solution.py:13
  3.7 4.7 %collective-permute-start = (f32[4,512]{1,0:T(4,128)S(1)}, f32[4,512]{1,0:T(4,128)S(1)}, u32[]{:S(2)}, u32[]{:S(2)}) collective-permute-start(f32[4,512]{1,0:T(4,128)S(1)} %bitcast.45), channel_id=1, source_target_pairs={{0,32},{32,64},{64,96},{1,33},{33,65},{65,97},{2,34},{34,66},{66,9... | collective-permute-start | bytes 24584 | tf_op jit(solution)/shard_map/ppermute | solution.py:13
  8.3 0.5 maximum_reduce_fusion
  8.9 0.0 copy-start.12
  8.9 3.3 %collective-permute-start.3 = (f32[4,256]{1,0:T(4,128)S(1)}, f32[4,256]{1,0:T(4,128)S(1)}, u32[]{:S(2)}, u32[]{:S(2)}) collective-permute-start(f32[4,256]{1,0:T(4,128)S(1)} %get-tuple-element.15), channel_id=1, source_target_pairs={{1,0},{2,1},{3,2},{4,3},{5,4},{6,5},{7,6},{8,7},{9,8},{10,9},{11,1... | collective-permute-start | bytes 12296 | tf_op jit(solution)/shard_map/ppermute | solution.py:13
  12.2 3.5 %collective-permute-start.2 = (f32[4,256]{1,0:T(4,128)S(1)}, f32[4,256]{1,0:T(4,128)S(1)}, u32[]{:S(2)}, u32[]{:S(2)}) collective-permute-start(f32[4,256]{1,0:T(4,128)S(1)} %get-tuple-element.14), channel_id=1, source_target_pairs={{0,1},{1,2},{2,3},{3,4},{4,5},{5,6},{6,7},{7,8},{8,9},{9,10},{10,1... | collective-permute-start | bytes 12296 | tf_op jit(solution)/shard_map/ppermute | solution.py:13
  15.8 0.1 copy.72
  15.9 0.2 fusion.22
  16.2 0.1 add_add_fusion
  16.3 0.2 fusion.21
  16.5 0.6 select_reduce_fusion
  17.2 0.1 reshape.79
  17.3 0.1 max.12
  17.4 0.8 copy.71
  18.2 0.6 pad_maximum_fusion.8.rows_ref
  18.8 5.2 %shard_map.156 = (f32[256,512]{1,0:T(8,128)}, f32[256,512]{1,0:T(8,128)}, f32[1024,128]{1,0:T(8,128)}, f32[1024,128]{1,0:T(8,128)}, f32[1024,128]{1,0:T(8,128)}) custom-call(f32[256,512]{1,0:T(8,128)} %depth_ref.1, f32[256,512]{1,0:T(8,128)} %bed_ref.1, f32[256,512]{1,0:T(8,128)} %mass_ref.1, f32[256,512]{1,0:T(8,128)} %cond_ref.1, f32[256,512]{1,0:T(8,128)} %settle_ref.1, ...), custom_call_target="tpu_custom_call" | custom-call | flops 7864320 | bytes 5767168 | tf_op jit(solution)/shard_map/pallas_call | solution.py:97
  24.1 2.1 %gather_fusion.1 = f32[512,128]{1,0:T(8,128)S(1)} fusion(f32[1024,128]{1,0:T(8,128)} %get-tuple-element.11, s32[1024]{0:T(1024)S(1)} %pad_clamp_fusion.1), kind=kCustom, calls=%fused_computation.1 | custom fusion | bytes 526336 | tf_op jit(solution)/shard_map/gather | solution.py:107
  26.2 1.0 %gather_fusion = f32[512,128]{1,0:T(8,128)S(1)} fusion(f32[1024,128]{1,0:T(8,128)S(1)} %copy-done.1, s32[1024]{0:T(1024)S(1)} %pad_clamp_fusion.1), kind=kCustom, calls=%fused_computation | custom fusion | bytes 526336 | tf_op jit(solution)/shard_map/gather | solution.py:109
  27.3 1.0 %gather_fusion.2 = f32[512,128]{1,0:T(8,128)S(1)} fusion(f32[1024,128]{1,0:T(8,128)S(1)} %copy-done, s32[1024]{0:T(1024)S(1)} %pad_clamp_fusion.1), kind=kCustom, calls=%fused_computation.2 | custom fusion | bytes 526336 | tf_op jit(solution)/shard_map/gather | solution.py:108
  28.3 0.1 multiply_multiply_fusion.1
  28.5 1.1 %fusion = f32[1024,256]{1,0:T(8,128)S(1)} fusion(s32[512]{0:T(512)S(1)} %multiply_add_fusion, f32[512,128]{1,0:T(8,128)S(1)} %get-tuple-element.25, f32[512,128]{1,0:T(8,128)S(1)} %get-tuple-element.24), kind=kOutput, calls=%fused_computation.7 | convolution fusion | flops 1611268096 | bytes 1574912 | tf_op jit(solution)/shard_map/dot_general | solution.py:125
  29.6 0.2 reshape.78
  29.8 0.3 concatenate.43
  30.1 0.8 all_to_all.11
  30.8 31.0 %all_to_all.17 = f32[128,1,2176]{2,1,0:T(1,128)S(1)} all-to-all(f32[128,1,2176]{2,1,0:T(1,128)S(1)} %all_to_all.11), channel_id=1, replica_groups=mesh['row'=4,'col'=32] {'row','col'}, dimensions={0} | all-to-all | bytes 2228224 | tf_op jit(solution)/shard_map/all_to_all | solution.py:134
  61.9 0.1 copy.92
  62.0 0.1 fusion.56
  62.0 0.1 slice.136
  62.1 0.1 eq.110
  62.2 0.2 reshape.80
  62.4 0.1 broadcast_in_dim.56
  62.5 0.0 copy-start.15
  62.5 0.2 fusion.10
  62.7 0.6 fusion.1
  63.4 0.1 fusion.63
  63.5 0.1 fusion.64
  63.6 0.1 fusion.61
  63.6 0.1 fusion.62
  63.7 0.1 fusion.45
  63.8 0.1 fusion.42
  63.9 1.6 %convolution_bitcast_fusion = f32[128,8,256]{2,1,0:T(8,128)} fusion(f32[1024]{0:T(1024)S(1)} %eq.110, f32[16,128]{1,0:T(8,128)S(1)} %fusion.45, f32[16,128]{1,0:T(8,128)S(1)} %fusion.42), kind=kOutput, calls=%fused_computation.12 | convolution fusion | flops 50352128 | bytes 1069056 | tf_op jit(solution)/shard_map/dot_general | solution.py:157
  65.5 4.6 %all-to-all-start.1 = ((f32[128,8,256]{2,1,0:T(8,128)}), f32[128,8,256]{2,1,0:T(8,128)S(1)}, u32[]{:S(2)}, u32[]{:S(2)}) async-start(f32[128,8,256]{2,1,0:T(8,128)} %convolution_bitcast_fusion), calls=%async_computation.1 | async-start | bytes 2097152 | tf_op jit(solution)/shard_map/all_to_all | solution.py:160
  70.2 19.2 %all-to-all-done.1 = f32[128,8,256]{2,1,0:T(8,128)S(1)} async-done(((f32[128,8,256]{2,1,0:T(8,128)}), f32[128,8,256]{2,1,0:T(8,128)S(1)}, u32[]{:S(2)}, u32[]{:S(2)}) %all-to-all-start.1) | async-done | bytes 1048608 | tf_op jit(solution)/shard_map/all_to_all | solution.py:160
  89.4 1.6 %gather_fusion.3 = f32[512,256]{1,0:T(8,128)S(1)} fusion(f32[1024,256]{1,0:T(8,128)S(1)} %bitcast.31, s32[1024]{0:T(1024)S(1)} %pad_clamp_fusion), kind=kCustom, calls=%fused_computation.3 | custom fusion | bytes 1050624 | tf_op jit(solution)/shard_map/gather | solution.py:167
  91.0 0.1 fusion.20
  91.1 0.5 fusion.11
  91.6 0.5 fusion.13
  92.1 0.5 fusion.15
  92.6 0.0 copy-start.6
  92.6 0.5 fusion.17
  93.1 0.5 copy-done.6
  93.6 0.2 copy-done.7
  93.8 1.1 %maximum_add_fusion = (f32[256,512]{1,0:T(8,128)}, f32[256,512]{1,0:T(8,128)}) fusion(f32[256,512]{1,0:T(8,128)S(1)} %copy-done.6, f32[256,128]{1,0:T(8,128)S(1)} %get-tuple-element.33, f32[256,128]{1,0:T(8,128)S(1)} %get-tuple-element.31, f32[256,128]{1,0:T(8,128)S(1)} %get-tuple-element.29, f32[256,128]{1,0:T(8,128)S(1)} %get-tuple-element.27, ...), kind=kLoop, calls=%fused_computation.25 | loop fusion | flops 1048576 | bytes 3145728 | tf_op jit(solution)/shard_map/add | solution.py:185
  (49 shorter events, 0.3 us)
Async XLA Ops:
  0.6 1.3 %copy-start.4 = (f32[256,512]{1,0:T(8,128)S(1)}, f32[256,512]{1,0:T(8,128)}, u32[]{:S(2)}) copy-start(f32[256,512]{1,0:T(8,128)} %depth_ref.1) | copy-start | bytes 1572868
  0.6 1.4 %copy-start.5 = (f32[256,512]{1,0:T(8,128)S(1)}, f32[256,512]{1,0:T(8,128)}, u32[]{:S(2)}) copy-start(f32[256,512]{1,0:T(8,128)} %bed_ref.1) | copy-start | bytes 1572868
  0.7 1.5 %copy-start.3 = (f32[256,512]{1,0:T(8,128)S(1)}, f32[256,512]{1,0:T(8,128)}, u32[]{:S(2)}) copy-start(f32[256,512]{1,0:T(8,128)} %cond_ref.1) | copy-start | bytes 1572868
  0.7 1.6 %copy-start.2 = (f32[256,512]{1,0:T(8,128)S(1)}, f32[256,512]{1,0:T(8,128)}, u32[]{:S(2)}) copy-start(f32[256,512]{1,0:T(8,128)} %mass_ref.1) | copy-start | bytes 1572868
  2.3 13.4 %copy-start.8 = (s32[512]{0:T(512)S(1)}, s32[512]{0:T(512)}, u32[]{:S(2)}) copy-start(s32[512]{0:T(512)} %param.19) | copy-start | bytes 6148
  2.3 13.5 %copy-start.11 = (s32[512,1]{0,1:T(1,128)S(1)}, s32[512,1]{0,1:T(1,128)}, u32[]{:S(2)}) copy-start(s32[512,1]{0,1:T(1,128)} %param.20) | copy-start | bytes 6148
  2.4 15.8 %collective-permute-start.1 = (f32[4,512]{1,0:T(4,128)S(1)}, f32[4,512]{1,0:T(4,128)S(1)}, u32[]{:S(2)}, u32[]{:S(2)}) collective-permute-start(f32[4,512]{1,0:T(4,128)S(1)} %bitcast.44), channel_id=1, source_target_pairs={{32,0},{64,32},{96,64},{33,1},{65,33},{97,65},{34,2},{66,34},{98,6... | collective-permute-start | bytes 24584 | tf_op jit(solution)/shard_map/ppermute | solution.py:13
  3.7 14.5 %collective-permute-start = (f32[4,512]{1,0:T(4,128)S(1)}, f32[4,512]{1,0:T(4,128)S(1)}, u32[]{:S(2)}, u32[]{:S(2)}) collective-permute-start(f32[4,512]{1,0:T(4,128)S(1)} %bitcast.45), channel_id=1, source_target_pairs={{0,32},{32,64},{64,96},{1,33},{33,65},{65,97},{2,34},{34,66},{66,9... | collective-permute-start | bytes 24584 | tf_op jit(solution)/shard_map/ppermute | solution.py:13
  8.9 7.6 %copy-start.16 = (s32[512]{0:T(512)S(1)}, s32[512]{0:T(512)}, u32[]{:S(2)}) copy-start(s32[512]{0:T(512)} %param.21) | copy-start | bytes 6148
  8.9 7.7 %copy-start.12 = (f32[512]{0:T(512)S(1)}, f32[512]{0:T(512)}, u32[]{:S(2)}) copy-start(f32[512]{0:T(512)} %param.22) | copy-start | bytes 6148
  8.9 8.5 %collective-permute-start.3 = (f32[4,256]{1,0:T(4,128)S(1)}, f32[4,256]{1,0:T(4,128)S(1)}, u32[]{:S(2)}, u32[]{:S(2)}) collective-permute-start(f32[4,256]{1,0:T(4,128)S(1)} %get-tuple-element.15), channel_id=1, source_target_pairs={{1,0},{2,1},{3,2},{4,3},{5,4},{6,5},{7,6},{8,7},{9,8},{10,9},{11,1... | collective-permute-start | bytes 12296 | tf_op jit(solution)/shard_map/ppermute | solution.py:13
  12.2 5.2 %collective-permute-start.2 = (f32[4,256]{1,0:T(4,128)S(1)}, f32[4,256]{1,0:T(4,128)S(1)}, u32[]{:S(2)}, u32[]{:S(2)}) collective-permute-start(f32[4,256]{1,0:T(4,128)S(1)} %get-tuple-element.14), channel_id=1, source_target_pairs={{0,1},{1,2},{2,3},{3,4},{4,5},{5,6},{6,7},{7,8},{8,9},{9,10},{10,1... | collective-permute-start | bytes 12296 | tf_op jit(solution)/shard_map/ppermute | solution.py:13
  24.1 2.1 %copy-start.1 = (f32[1024,128]{1,0:T(8,128)S(1)}, f32[1024,128]{1,0:T(8,128)}, u32[]{:S(2)}) copy-start(f32[1024,128]{1,0:T(8,128)} %get-tuple-element.10) | copy-start | bytes 1572868
  26.2 1.1 %copy-start = (f32[1024,128]{1,0:T(8,128)S(1)}, f32[1024,128]{1,0:T(8,128)}, u32[]{:S(2)}) copy-start(f32[1024,128]{1,0:T(8,128)} %get-tuple-element.12) | copy-start | bytes 1572868
  62.5 0.9 copy-start.13
  62.5 0.9 copy-start.14
  62.5 0.9 copy-start.15
  63.8 1.7 %copy-start.9 = (f32[16,128]{1,0:T(8,128)}, f32[16,128]{1,0:T(8,128)S(1)}, u32[]{:S(2)}) copy-start(f32[16,128]{1,0:T(8,128)S(1)} %fusion.45) | copy-start | bytes 24580
  63.9 1.6 %copy-start.10 = (f32[16,128]{1,0:T(8,128)}, f32[16,128]{1,0:T(8,128)S(1)}, u32[]{:S(2)}) copy-start(f32[16,128]{1,0:T(8,128)S(1)} %fusion.42) | copy-start | bytes 24580
  65.5 23.9 %all-to-all-start.1 = ((f32[128,8,256]{2,1,0:T(8,128)}), f32[128,8,256]{2,1,0:T(8,128)S(1)}, u32[]{:S(2)}, u32[]{:S(2)}) async-start(f32[128,8,256]{2,1,0:T(8,128)} %convolution_bitcast_fusion), calls=%async_computation.1 | async-start | bytes 2097152 | tf_op jit(solution)/shard_map/all_to_all | solution.py:160
  92.6 1.0 %copy-start.6 = (f32[256,512]{1,0:T(8,128)S(1)}, f32[256,512]{1,0:T(8,128)}, u32[]{:S(2)}) copy-start(f32[256,512]{1,0:T(8,128)} %get-tuple-element.9) | copy-start | bytes 1572868
  92.6 1.2 %copy-start.7 = (f32[256,512]{1,0:T(8,128)S(1)}, f32[256,512]{1,0:T(8,128)}, u32[]{:S(2)}) copy-start(f32[256,512]{1,0:T(8,128)} %get-tuple-element.13) | copy-start | bytes 1572868

commit v7 on v6

--- a/solution.py
+++ b/solution.py
@@ -14,7 +14,8 @@
 
 
 def stencil_kernel(depth_ref, bed_ref, mass_ref, cond_ref, settle_ref, wet_ref, rows_ref, cols_ref,
-                   depth1_ref, mass1_ref, surf_blocks_ref, mass_blocks_ref, open_blocks_ref):
+                   depth1_ref, mass1_ref, surf_blocks_ref, mass_blocks_ref, open_blocks_ref,
+                   open_surf_ref, open_mass_ref):
     depth = depth_ref[...]
     bed = bed_ref[...]
     mass = mass_ref[...]
@@ -56,9 +57,14 @@
     for j in range(per_row):
         lanes = slice(j * 128, (j + 1) * 128)
         rows_j = pl.ds(j, tile_y, stride=per_row)
-        surf_blocks_ref[rows_j, :] = (depth1 + bed)[:, lanes]
-        mass_blocks_ref[rows_j, :] = mass1[:, lanes]
-        open_blocks_ref[rows_j, :] = opened[:, lanes]
+        surf_j = (depth1 + bed)[:, lanes]
+        mass_j = mass1[:, lanes]
+        open_j = opened[:, lanes]
+        surf_blocks_ref[rows_j, :] = surf_j
+        mass_blocks_ref[rows_j, :] = mass_j
+        open_blocks_ref[rows_j, :] = open_j
+        open_surf_ref[rows_j, :] = open_j * surf_j
+        open_mass_ref[rows_j, :] = open_j * mass_j
 
 
 def smooth_reach(values):
@@ -94,21 +100,15 @@
     vmem = pl.BlockSpec(memory_space=pltpu.VMEM)
     blocks = tile_y * tile_x // 128
     block_rows = jax.ShapeDtypeStruct((blocks, 128), jnp.float32)
-    depth1, mass1, surf_blocks, mass_blocks, open_blocks = pl.pallas_call(
+    depth1, mass1, surf_blocks, mass_blocks, open_blocks, open_surf, open_mass = pl.pallas_call(
         stencil_kernel,
-        out_shape=[tile, tile, block_rows, block_rows, block_rows],
+        out_shape=[tile, tile] + [block_rows] * 5,
         in_specs=[vmem] * 8,
-        out_specs=[vmem] * 5,
+        out_specs=[vmem] * 7,
         cost_estimate=pl.CostEstimate(
-            flops=60 * tile_y * tile_x, transcendentals=tile_y * tile_x, bytes_accessed=44 * tile_y * tile_x
+            flops=60 * tile_y * tile_x, transcendentals=tile_y * tile_x, bytes_accessed=52 * tile_y * tile_x
         ),
     )(depth, bed, mass, conduct, settle, wet, rows, cols)
-
-    surf_rows = surf_blocks[link_block]
-    mass_rows = mass_blocks[link_block]
-    weight = link_coef[:, None] * open_blocks[link_block]
-    ws = weight * surf_rows
-    wm = weight * mass_rows
 
     n_row = lax.axis_size("row")
     n_col = lax.axis_size("col")
@@ -121,10 +121,14 @@
     slot_of = target * slot_cap + ranking
     slot_ids = jnp.arange(devices * slot_cap, dtype=jnp.int32)
     slot_hit = slot_of[None, :] == slot_ids[:, None]
-    hit = slot_hit.astype(jnp.float32)
-    payload = jnp.dot(hit, jnp.concatenate([ws, wm], axis=1), precision=lax.Precision.HIGHEST)
+    slot_block = jnp.max(jnp.where(slot_hit, link_block[None, :], -1), axis=1)
+    block_ids = jnp.arange(blocks, dtype=jnp.int32)
+    slot_hot = (slot_block[:, None] == block_ids[None, :]).astype(jnp.float32)
+    coefs = jnp.maximum(jnp.max(jnp.where(slot_hit, link_coef[None, :], -1.0), axis=1), 0.0)
+    payload = coefs[:, None] * jnp.dot(
+        slot_hot, jnp.concatenate([open_surf, open_mass], axis=1), precision=lax.Precision.HIGHEST
+    )
     tags = jnp.max(jnp.where(slot_hit, link_reach[None, :].astype(jnp.float32), -1.0), axis=1)
-    coefs = jnp.maximum(jnp.max(jnp.where(slot_hit, link_coef[None, :], -1.0), axis=1), 0.0)
     meta = jnp.concatenate(
         [tags.reshape(devices, slot_cap), coefs.reshape(devices, slot_cap),
          jnp.zeros((devices, 128 - 2 * slot_cap), jnp.float32)],
@@ -165,6 +169,9 @@
         tiled=True,
     )
     own_rows = answered.reshape(devices * slot_cap, 256)[slot_of]
+    surf_rows = surf_blocks[link_block]
+    mass_rows = mass_blocks[link_block]
+    weight = link_coef[:, None] * open_blocks[link_block]
     applied = jnp.concatenate(
         [
             0.5 * weight * (own_rows[:, :128] - surf_rows),

time: 95.3 us -> 92.8 us (0.974)
  waiting for transfers between devices: 19.2 us -> 16 us
  matrix products: 5.17 us -> 7.36 us
  local copies, waits for them, and re-layouts: 10.1 us -> 9.02 us
    all_to_all x1, waiting for transfers between devices: 19.2 us -> 16 us  [body(): lax.all_to_all(reply.reshape(devices, slot_cap, 256), ('row', 'col'), spl...]
    dot_general x1, matrix products: 1.1 us -> 3.28 us  [body(): jnp.dot(slot_hot, jnp.concatenate([open_surf, open_mass], axis=1), precis...]
    ppermute x2, starting transfers between devices: 4.64 us -> 3.21 us  [halo_pair(): lax.ppermute(first, axis, backward)]
    gather x1, local copies, waits for them, and re-layouts: 2.13 us -> 1.04 us  [body(): surf_rows = surf_blocks[link_block]]
  transfers between devices with their start and end apart: 5 -> 5, of which waited for: 1 -> 1; matrix products, arithmetic and copies ran while one was open for 3% -> 6% of each run, Pallas kernels for 0% -> 0%
where the time goes in v7:
time: 92.8 us; the launch traced here: 92.4 us
  blocking collectives  30.4 us (33%)
  starting transfers between devices  17 us (18%)
  waiting for transfers between devices  16 us (17%)
  local copies, waits for them, and re-layouts  9.02 us (10%)
  matrix products  7.36 us (8%)
  other arithmetic  5.65 us (6%)
  Pallas kernels  5.65 us (6%)
  between operations  1.23 us (1%)
    all_to_all x1, blocking collectives, body(): lax.all_to_all(outgoing, ('row', 'col'), split_axis=0, concat_axis=0, til...  30.4 us
    all_to_all x1, waiting for transfers between devices, body(): lax.all_to_all(reply.reshape(devices, slot_cap, 256), ('row', 'col'), spl...  16 us
    ppermute x2, starting transfers between devices, halo_pair(): lax.ppermute(last, axis, forward)  9.05 us
    pallas_call x1, Pallas kernels, body(): pl.pallas_call(stencil_kernel, out_shape=[tile, tile] + [block_rows] * 5,...  5.65 us
    all_to_all x1, starting transfers between devices, body(): lax.all_to_all(reply.reshape(devices, slot_cap, 256), ('row', 'col'), spl...  4.75 us
    dot_general x1, matrix products, body(): jnp.dot(slot_hot, jnp.concatenate([open_surf, open_mass], axis=1), precis...  3.28 us
    ppermute x2, starting transfers between devices, halo_pair(): lax.ppermute(first, axis, backward)  3.21 us
  transfers between devices with their start and end apart: 5, of which 1 were waited for; matrix products, arithmetic and copies ran while one was open for 6% of the time, Pallas kernels for 0%

profile of v7, /device:TPU:1, one launch (start us, length us, event | category | flops | bytes accessed | tf_op | source)
XLA Modules:
  0.0 92.4 jit_solution(13186670970034626487)
XLA Ops:
  0.6 0.0 copy-start.6
  0.6 0.0 copy-start.5
  0.7 0.0 copy-start.4
  0.7 0.0 copy-start.3
  0.7 1.2 %convert_bitcast_fusion = f32[1,256,512]{2,1,0:T(8,128)S(1)} fusion(s32[256,512]{1,0:T(8,128)} %wet_ref.1), kind=kLoop, calls=%fused_computation.30 | loop fusion | flops 131072 | bytes 1048576 | tf_op jit(solution)/shard_map/stack | solution.py:94
  1.9 0.1 copy-done.5
  2.0 0.1 add_bitcast_fusion
  2.1 0.1 copy-done.4
  2.2 0.2 copy-done.3
  2.3 0.5 maximum_reduce_fusion
  2.8 0.0 copy-start.12
  2.9 5.1 %collective-permute-start.2 = (f32[4,256]{1,0:T(4,128)S(1)}, f32[4,256]{1,0:T(4,128)S(1)}, u32[]{:S(2)}, u32[]{:S(2)}) collective-permute-start(f32[4,256]{1,0:T(4,128)S(1)} %get-tuple-element.18), channel_id=1, source_target_pairs={{0,1},{1,2},{2,3},{3,4},{4,5},{5,6},{6,7},{7,8},{8,9},{9,10},{10,1... | collective-permute-start | bytes 12296 | tf_op jit(solution)/shard_map/ppermute | solution.py:13
  7.9 1.9 %collective-permute-start.3 = (f32[4,256]{1,0:T(4,128)S(1)}, f32[4,256]{1,0:T(4,128)S(1)}, u32[]{:S(2)}, u32[]{:S(2)}) collective-permute-start(f32[4,256]{1,0:T(4,128)S(1)} %get-tuple-element.19), channel_id=1, source_target_pairs={{1,0},{2,1},{3,2},{4,3},{5,4},{6,5},{7,6},{8,7},{9,8},{10,9},{11,1... | collective-permute-start | bytes 12296 | tf_op jit(solution)/shard_map/ppermute | solution.py:13
  9.9 0.0 copy-start.16
  9.9 1.3 %collective-permute-start.1 = (f32[4,512]{1,0:T(4,128)S(1)}, f32[4,512]{1,0:T(4,128)S(1)}, u32[]{:S(2)}, u32[]{:S(2)}) collective-permute-start(f32[4,512]{1,0:T(4,128)S(1)} %bitcast.44), channel_id=1, source_target_pairs={{32,0},{64,32},{96,64},{33,1},{65,33},{97,65},{34,2},{66,34},{98,6... | collective-permute-start | bytes 24584 | tf_op jit(solution)/shard_map/ppermute | solution.py:13
  11.2 4.0 %collective-permute-start = (f32[4,512]{1,0:T(4,128)S(1)}, f32[4,512]{1,0:T(4,128)S(1)}, u32[]{:S(2)}, u32[]{:S(2)}) collective-permute-start(f32[4,512]{1,0:T(4,128)S(1)} %bitcast.45), channel_id=1, source_target_pairs={{0,32},{32,64},{64,96},{1,33},{33,65},{65,97},{2,34},{34,66},{66,9... | collective-permute-start | bytes 24584 | tf_op jit(solution)/shard_map/ppermute | solution.py:13
  15.2 0.1 copy.72
  15.4 0.2 fusion.23
  15.6 0.1 add_add_fusion
  15.7 0.2 fusion.22
  16.0 0.6 select_reduce_fusion
  16.6 0.4 select_reduce_fusion.1
  17.0 0.1 reshape.83
  17.1 0.1 max.16
  17.2 0.8 copy.71
  18.0 0.6 pad_maximum_fusion.8.rows_ref
  18.6 5.7 %shard_map.156 = (f32[256,512]{1,0:T(8,128)}, f32[256,512]{1,0:T(8,128)}, f32[1024,128]{1,0:T(8,128)}, f32[1024,128]{1,0:T(8,128)}, f32[1024,128]{1,0:T(8,128)},...) custom-call(f32[256,512]{1,0:T(8,128)} %depth_ref.1, f32[256,512]{1,0:T(8,128)} %bed_ref.1, f32[256,512]{1,0:T(8,128)} %mass_ref.1, ...), custom_call_target="tpu_custom_call" | custom-call | flops 7864320 | bytes 6815744 | tf_op jit(solution)/shard_map/pallas_call | solution.py:103
  24.2 3.3 %fusion.6 = f32[1024,256]{1,0:T(8,128)S(1)} fusion(s32[1024]{0:T(1024)S(1)} %select_reduce_fusion.1, f32[1024,128]{1,0:T(8,128)} %get-tuple-element.14, f32[1024,128]{1,0:T(8,128)} %get-tuple-element.13, f32[1024]{0:T(1024)S(1)} %broadcast_maximum_fusion), kind=kOutput, calls=%fused_computation.15 | convolution fusion | flops 3222798336 | bytes 2105344 | tf_op jit(solution)/shard_map/dot_general | solution.py:128
  27.5 0.2 reshape.82
  27.7 0.3 concatenate.43
  28.0 0.8 all_to_all.11
  28.8 30.4 %all_to_all.17 = f32[128,1,2176]{2,1,0:T(1,128)S(1)} all-to-all(f32[128,1,2176]{2,1,0:T(1,128)S(1)} %all_to_all.11), channel_id=1, replica_groups=mesh['row'=4,'col'=32] {'row','col'}, dimensions={0} | all-to-all | bytes 2228224 | tf_op jit(solution)/shard_map/all_to_all | solution.py:138
  59.2 0.1 copy.92
  59.3 0.1 fusion.57
  59.4 0.1 slice.136
  59.5 0.2 reshape.84
  59.7 0.1 broadcast_in_dim.74
  59.8 0.1 eq.126
  59.9 0.0 copy-start.14
  59.9 0.0 copy-start.15
  59.9 0.2 fusion.11
  60.1 0.6 fusion.2
  60.8 0.1 fusion.63
  60.8 0.1 fusion.62
  60.9 0.1 fusion.65
  61.0 0.1 fusion.64
  61.1 0.1 fusion.43
  61.1 0.1 fusion.46
  61.2 1.6 %convolution_bitcast_fusion = f32[128,8,256]{2,1,0:T(8,128)} fusion(f32[1024]{0:T(1024)S(1)} %eq.126, f32[16,128]{1,0:T(8,128)S(1)} %fusion.46, f32[16,128]{1,0:T(8,128)S(1)} %fusion.43), kind=kOutput, calls=%fused_computation.16 | convolution fusion | flops 50352128 | bytes 1069056 | tf_op jit(solution)/shard_map/dot_general | solution.py:161
  62.8 4.8 %all-to-all-start.1 = ((f32[128,8,256]{2,1,0:T(8,128)}), f32[128,8,256]{2,1,0:T(8,128)S(1)}, u32[]{:S(2)}, u32[]{:S(2)}) async-start(f32[128,8,256]{2,1,0:T(8,128)} %convolution_bitcast_fusion), calls=%async_computation.1 | async-start | bytes 2097152 | tf_op jit(solution)/shard_map/all_to_all | solution.py:164
  67.7 1.0 %gather_fusion = f32[512,128]{1,0:T(8,128)S(1)} fusion(f32[1024,128]{1,0:T(8,128)S(1)} %copy-done.2, s32[1024]{0:T(1024)S(1)} %pad_clamp_fusion.1), kind=kCustom, calls=%fused_computation | custom fusion | bytes 526336 | tf_op jit(solution)/shard_map/gather | solution.py:174
  68.8 1.0 %gather_fusion.2 = f32[512,128]{1,0:T(8,128)S(1)} fusion(f32[1024,128]{1,0:T(8,128)S(1)} %copy-done.1, s32[1024]{0:T(1024)S(1)} %pad_clamp_fusion.1), kind=kCustom, calls=%fused_computation.2 | custom fusion | bytes 526336 | tf_op jit(solution)/shard_map/gather | solution.py:172
  69.8 1.0 %gather_fusion.3 = f32[512,128]{1,0:T(8,128)S(1)} fusion(f32[1024,128]{1,0:T(8,128)S(1)} %copy-done, s32[1024]{0:T(1024)S(1)} %pad_clamp_fusion.1), kind=kCustom, calls=%fused_computation.3 | custom fusion | bytes 526336 | tf_op jit(solution)/shard_map/gather | solution.py:173
  70.9 16.0 %all-to-all-done.1 = f32[128,8,256]{2,1,0:T(8,128)S(1)} async-done(((f32[128,8,256]{2,1,0:T(8,128)}), f32[128,8,256]{2,1,0:T(8,128)S(1)}, u32[]{:S(2)}, u32[]{:S(2)}) %all-to-all-start.1) | async-done | bytes 1048608 | tf_op jit(solution)/shard_map/all_to_all | solution.py:164
  86.9 1.6 %gather_fusion.1 = f32[512,256]{1,0:T(8,128)S(1)} fusion(f32[1024,256]{1,0:T(8,128)S(1)} %bitcast.31, s32[1024]{0:T(1024)S(1)} %pad_clamp_fusion), kind=kCustom, calls=%fused_computation.1 | custom fusion | bytes 1050624 | tf_op jit(solution)/shard_map/gather | solution.py:171
  88.5 0.1 fusion.21
  88.6 0.5 fusion.16
  89.1 0.5 fusion.14
  89.6 0.5 fusion.12
  90.1 0.0 copy-start.7
  90.1 0.5 fusion.18
  90.6 0.5 copy-done.7
  91.1 0.2 copy-done.8
  91.3 1.1 %maximum_add_fusion = (f32[256,512]{1,0:T(8,128)}, f32[256,512]{1,0:T(8,128)}) fusion(f32[256,512]{1,0:T(8,128)S(1)} %copy-done.7, f32[256,128]{1,0:T(8,128)S(1)} %get-tuple-element.35, f32[256,128]{1,0:T(8,128)S(1)} %get-tuple-element.33, f32[256,128]{1,0:T(8,128)S(1)} %get-tuple-element.31, f32[256,128]{1,0:T(8,128)S(1)} %get-tuple-element.29, ...), kind=kLoop, calls=%fused_computation.28 | loop fusion | flops 1048576 | bytes 3145728 | tf_op jit(solution)/shard_map/add | solution.py:192
  (51 shorter events, 0.3 us)
Async XLA Ops:
  0.6 1.3 %copy-start.6 = (f32[256,512]{1,0:T(8,128)S(1)}, f32[256,512]{1,0:T(8,128)}, u32[]{:S(2)}) copy-start(f32[256,512]{1,0:T(8,128)} %bed_ref.1) | copy-start | bytes 1572868
  0.6 1.4 %copy-start.5 = (f32[256,512]{1,0:T(8,128)S(1)}, f32[256,512]{1,0:T(8,128)}, u32[]{:S(2)}) copy-start(f32[256,512]{1,0:T(8,128)} %depth_ref.1) | copy-start | bytes 1572868
  0.7 1.5 %copy-start.4 = (f32[256,512]{1,0:T(8,128)S(1)}, f32[256,512]{1,0:T(8,128)}, u32[]{:S(2)}) copy-start(f32[256,512]{1,0:T(8,128)} %cond_ref.1) | copy-start | bytes 1572868
  0.7 1.6 %copy-start.3 = (f32[256,512]{1,0:T(8,128)S(1)}, f32[256,512]{1,0:T(8,128)}, u32[]{:S(2)}) copy-start(f32[256,512]{1,0:T(8,128)} %mass_ref.1) | copy-start | bytes 1572868
  2.8 12.4 %copy-start.17 = (s32[512]{0:T(512)S(1)}, s32[512]{0:T(512)}, u32[]{:S(2)}) copy-start(s32[512]{0:T(512)} %param.21) | copy-start | bytes 6148
  2.8 12.4 %copy-start.12 = (s32[512,1]{0,1:T(1,128)S(1)}, s32[512,1]{0,1:T(1,128)}, u32[]{:S(2)}) copy-start(s32[512,1]{0,1:T(1,128)} %param.20) | copy-start | bytes 6148
  2.9 14.3 %collective-permute-start.2 = (f32[4,256]{1,0:T(4,128)S(1)}, f32[4,256]{1,0:T(4,128)S(1)}, u32[]{:S(2)}, u32[]{:S(2)}) collective-permute-start(f32[4,256]{1,0:T(4,128)S(1)} %get-tuple-element.18), channel_id=1, source_target_pairs={{0,1},{1,2},{2,3},{3,4},{4,5},{5,6},{6,7},{7,8},{8,9},{9,10},{10,1... | collective-permute-start | bytes 12296 | tf_op jit(solution)/shard_map/ppermute | solution.py:13
  7.9 9.3 %collective-permute-start.3 = (f32[4,256]{1,0:T(4,128)S(1)}, f32[4,256]{1,0:T(4,128)S(1)}, u32[]{:S(2)}, u32[]{:S(2)}) collective-permute-start(f32[4,256]{1,0:T(4,128)S(1)} %get-tuple-element.19), channel_id=1, source_target_pairs={{1,0},{2,1},{3,2},{4,3},{5,4},{6,5},{7,6},{8,7},{9,8},{10,9},{11,1... | collective-permute-start | bytes 12296 | tf_op jit(solution)/shard_map/ppermute | solution.py:13
  9.9 6.1 %copy-start.16 = (f32[512]{0:T(512)S(1)}, f32[512]{0:T(512)}, u32[]{:S(2)}) copy-start(f32[512]{0:T(512)} %param.22) | copy-start | bytes 6148
  9.9 6.7 %copy-start.9 = (s32[512]{0:T(512)S(1)}, s32[512]{0:T(512)}, u32[]{:S(2)}) copy-start(s32[512]{0:T(512)} %param.19) | copy-start | bytes 6148
  9.9 8.1 %collective-permute-start.1 = (f32[4,512]{1,0:T(4,128)S(1)}, f32[4,512]{1,0:T(4,128)S(1)}, u32[]{:S(2)}, u32[]{:S(2)}) collective-permute-start(f32[4,512]{1,0:T(4,128)S(1)} %bitcast.44), channel_id=1, source_target_pairs={{32,0},{64,32},{96,64},{33,1},{65,33},{97,65},{34,2},{66,34},{98,6... | collective-permute-start | bytes 24584 | tf_op jit(solution)/shard_map/ppermute | solution.py:13
  11.2 6.8 %collective-permute-start = (f32[4,512]{1,0:T(4,128)S(1)}, f32[4,512]{1,0:T(4,128)S(1)}, u32[]{:S(2)}, u32[]{:S(2)}) collective-permute-start(f32[4,512]{1,0:T(4,128)S(1)} %bitcast.45), channel_id=1, source_target_pairs={{0,32},{32,64},{64,96},{1,33},{33,65},{65,97},{2,34},{34,66},{66,9... | collective-permute-start | bytes 24584 | tf_op jit(solution)/shard_map/ppermute | solution.py:13
  59.8 0.9 copy-start.13
  59.9 0.9 copy-start.14
  59.9 0.9 copy-start.15
  61.1 1.7 %copy-start.10 = (f32[16,128]{1,0:T(8,128)}, f32[16,128]{1,0:T(8,128)S(1)}, u32[]{:S(2)}) copy-start(f32[16,128]{1,0:T(8,128)S(1)} %fusion.43) | copy-start | bytes 24580
  61.2 1.6 %copy-start.11 = (f32[16,128]{1,0:T(8,128)}, f32[16,128]{1,0:T(8,128)S(1)}, u32[]{:S(2)}) copy-start(f32[16,128]{1,0:T(8,128)S(1)} %fusion.46) | copy-start | bytes 24580
  62.8 4.9 %copy-start.2 = (f32[1024,128]{1,0:T(8,128)S(1)}, f32[1024,128]{1,0:T(8,128)}, u32[]{:S(2)}) copy-start(f32[1024,128]{1,0:T(8,128)} %get-tuple-element.12) | copy-start | bytes 1572868
  62.8 24.1 %all-to-all-start.1 = ((f32[128,8,256]{2,1,0:T(8,128)}), f32[128,8,256]{2,1,0:T(8,128)S(1)}, u32[]{:S(2)}, u32[]{:S(2)}) async-start(f32[128,8,256]{2,1,0:T(8,128)} %convolution_bitcast_fusion), calls=%async_computation.1 | async-start | bytes 2097152 | tf_op jit(solution)/shard_map/all_to_all | solution.py:164
  67.7 1.1 %copy-start.1 = (f32[1024,128]{1,0:T(8,128)S(1)}, f32[1024,128]{1,0:T(8,128)}, u32[]{:S(2)}) copy-start(f32[1024,128]{1,0:T(8,128)} %get-tuple-element.15) | copy-start | bytes 1572868
  68.8 1.1 %copy-start = (f32[1024,128]{1,0:T(8,128)S(1)}, f32[1024,128]{1,0:T(8,128)}, u32[]{:S(2)}) copy-start(f32[1024,128]{1,0:T(8,128)} %get-tuple-element.16) | copy-start | bytes 1572868
  90.1 1.0 %copy-start.7 = (f32[256,512]{1,0:T(8,128)S(1)}, f32[256,512]{1,0:T(8,128)}, u32[]{:S(2)}) copy-start(f32[256,512]{1,0:T(8,128)} %get-tuple-element.11) | copy-start | bytes 1572868
  90.1 1.2 %copy-start.8 = (f32[256,512]{1,0:T(8,128)S(1)}, f32[256,512]{1,0:T(8,128)}, u32[]{:S(2)}) copy-start(f32[256,512]{1,0:T(8,128)} %get-tuple-element.17) | copy-start | bytes 1572868

commit v8 on v7

--- a/solution.py
+++ b/solution.py
@@ -67,6 +67,22 @@
         open_mass_ref[rows_j, :] = open_j * mass_j
 
 
+def pick_dot(hot, values):
+    def part(x):
+        return lax.reduce_precision(x, exponent_bits=8, mantissa_bits=7)
+
+    hi = part(values)
+    rest = values - hi
+    mid = part(rest)
+    lo = rest - mid
+    hot = hot.astype(jnp.bfloat16)
+
+    def one(x):
+        return jnp.dot(hot, x.astype(jnp.bfloat16), preferred_element_type=jnp.float32)
+
+    return (one(hi) + one(mid)) + one(lo)
+
+
 def smooth_reach(values):
     left = jnp.concatenate([values[:, :1], values[:, :-1]], axis=1)
     right = jnp.concatenate([values[:, 1:], values[:, -1:]], axis=1)
@@ -125,9 +141,7 @@
     block_ids = jnp.arange(blocks, dtype=jnp.int32)
     slot_hot = (slot_block[:, None] == block_ids[None, :]).astype(jnp.float32)
     coefs = jnp.maximum(jnp.max(jnp.where(slot_hit, link_coef[None, :], -1.0), axis=1), 0.0)
-    payload = coefs[:, None] * jnp.dot(
-        slot_hot, jnp.concatenate([open_surf, open_mass], axis=1), precision=lax.Precision.HIGHEST
-    )
+    payload = coefs[:, None] * pick_dot(slot_hot, jnp.concatenate([open_surf, open_mass], axis=1))
     tags = jnp.max(jnp.where(slot_hit, link_reach[None, :].astype(jnp.float32), -1.0), axis=1)
     meta = jnp.concatenate(
         [tags.reshape(devices, slot_cap), coefs.reshape(devices, slot_cap),
@@ -158,9 +172,7 @@
     conc_new = (chan_area * chan_conc + sediment) / (chan_area + wet_sum)
     phase_out = smooth_reach(phase_new)
     conc_out = smooth_reach(conc_new)
-    reply = jnp.dot(
-        reach_hot.T, jnp.concatenate([phase_out, conc_out], axis=1), precision=lax.Precision.HIGHEST
-    )
+    reply = pick_dot(reach_hot.T, jnp.concatenate([phase_out, conc_out], axis=1))
     answered = lax.all_to_all(
         reply.reshape(devices, slot_cap, 256),
         ("row", "col"),
@@ -182,11 +194,7 @@
     per_row = tile_x // 128
     row_ids = jnp.arange(tile_y, dtype=jnp.int32)[:, None]
     gained = [
-        jnp.dot(
-            (row_ids * per_row + j == link_block[None, :]).astype(jnp.float32),
-            applied,
-            precision=lax.Precision.HIGHEST,
-        )
+        pick_dot((row_ids * per_row + j == link_block[None, :]).astype(jnp.float32), applied)
         for j in range(per_row)
     ]
     depth_out = depth1 + jnp.concatenate([g[:, :128] for g in gained], axis=1)

time: 92.8 us -> 95.3 us (1.027)
  local copies, waits for them, and re-layouts: 9.02 us -> 10.4 us
    unnamed x39 -> x42, local copies, waits for them, and re-layouts: 1.14 us -> 2.52 us
    dot_general x6 -> x18, matrix products: 6.73 us -> 7.55 us  [one(): jnp.dot(hot, x.astype(jnp.bfloat16), preferred_element_type=jnp.float32)]
where the time goes in v8:
time: 95.3 us; the launch traced here: 94.9 us
  blocking collectives  30.4 us (32%)
  starting transfers between devices  17 us (18%)
  waiting for transfers between devices  16 us (17%)
  local copies, waits for them, and re-layouts  10.4 us (11%)
  matrix products  8.18 us (9%)
  other arithmetic  5.79 us (6%)
  Pallas kernels  5.66 us (6%)
  between operations  1.36 us (1%)
    all_to_all x1, blocking collectives, body(): lax.all_to_all(outgoing, ('row', 'col'), split_axis=0, concat_axis=0, til...  30.4 us
    all_to_all x1, waiting for transfers between devices, body(): lax.all_to_all(reply.reshape(devices, slot_cap, 256), ('row', 'col'), spl...  16 us
    ppermute x2, starting transfers between devices, halo_pair(): lax.ppermute(last, axis, forward)  9.05 us
    dot_general x18, matrix products, one(): jnp.dot(hot, x.astype(jnp.bfloat16), preferred_element_type=jnp.float32)  7.55 us
    pallas_call x1, Pallas kernels, body(): pl.pallas_call(stencil_kernel, out_shape=[tile, tile] + [block_rows] * 5,...  5.66 us
    all_to_all x1, starting transfers between devices, body(): lax.all_to_all(reply.reshape(devices, slot_cap, 256), ('row', 'col'), spl...  4.76 us
    ppermute x2, starting transfers between devices, halo_pair(): lax.ppermute(first, axis, backward)  3.21 us
    unnamed x42, local copies, waits for them, and re-layouts  2.52 us
  transfers between devices with their start and end apart: 5, of which 1 were waited for; matrix products, arithmetic and copies ran while one was open for 6% of the time, Pallas kernels for 0%

profile of v8, /device:TPU:1, one launch (start us, length us, event | category | flops | bytes accessed | tf_op | source)
XLA Modules:
  0.0 94.9 jit_solution(17766663893992721479)
XLA Ops:
  0.7 1.2 %convert_bitcast_fusion = f32[1,256,512]{2,1,0:T(8,128)S(1)} fusion(s32[256,512]{1,0:T(8,128)} %wet_ref.1), kind=kLoop, calls=%fused_computation.60 | loop fusion | flops 131072 | bytes 1048576 | tf_op jit(solution)/shard_map/stack | solution.py:110
  1.9 0.1 copy-done.5
  2.0 0.1 add_bitcast_fusion
  2.1 0.1 copy-done.4
  2.2 0.2 copy-done.3
  2.3 0.5 maximum_reduce_fusion
  2.9 5.1 %collective-permute-start.2 = (f32[4,256]{1,0:T(4,128)S(1)}, f32[4,256]{1,0:T(4,128)S(1)}, u32[]{:S(2)}, u32[]{:S(2)}) collective-permute-start(f32[4,256]{1,0:T(4,128)S(1)} %get-tuple-element.18), channel_id=1, source_target_pairs={{0,1},{1,2},{2,3},{3,4},{4,5},{5,6},{6,7},{7,8},{8,9},{9,10},{10,1... | collective-permute-start | bytes 12296 | tf_op jit(solution)/shard_map/ppermute | solution.py:13
  7.9 1.9 %collective-permute-start.3 = (f32[4,256]{1,0:T(4,128)S(1)}, f32[4,256]{1,0:T(4,128)S(1)}, u32[]{:S(2)}, u32[]{:S(2)}) collective-permute-start(f32[4,256]{1,0:T(4,128)S(1)} %get-tuple-element.19), channel_id=1, source_target_pairs={{1,0},{2,1},{3,2},{4,3},{5,4},{6,5},{7,6},{8,7},{9,8},{10,9},{11,1... | collective-permute-start | bytes 12296 | tf_op jit(solution)/shard_map/ppermute | solution.py:13
  9.9 1.3 %collective-permute-start.1 = (f32[4,512]{1,0:T(4,128)S(1)}, f32[4,512]{1,0:T(4,128)S(1)}, u32[]{:S(2)}, u32[]{:S(2)}) collective-permute-start(f32[4,512]{1,0:T(4,128)S(1)} %bitcast.56), channel_id=1, source_target_pairs={{32,0},{64,32},{96,64},{33,1},{65,33},{97,65},{34,2},{66,34},{98,6... | collective-permute-start | bytes 24584 | tf_op jit(solution)/shard_map/ppermute | solution.py:13
  11.2 4.0 %collective-permute-start = (f32[4,512]{1,0:T(4,128)S(1)}, f32[4,512]{1,0:T(4,128)S(1)}, u32[]{:S(2)}, u32[]{:S(2)}) collective-permute-start(f32[4,512]{1,0:T(4,128)S(1)} %bitcast.57), channel_id=1, source_target_pairs={{0,32},{32,64},{64,96},{1,33},{33,65},{65,97},{2,34},{34,66},{66,9... | collective-permute-start | bytes 24584 | tf_op jit(solution)/shard_map/ppermute | solution.py:13
  15.2 0.1 copy.88
  15.4 0.2 fusion.30
  15.7 0.2 fusion.26
  16.0 0.6 select_reduce_fusion
  16.6 0.4 select_reduce_fusion.1
  17.0 0.1 reshape.83
  17.1 0.1 max.16
  17.2 0.8 copy.87
  18.0 0.6 pad_maximum_fusion.4.rows_ref
  18.6 5.7 %shard_map.156 = (f32[256,512]{1,0:T(8,128)}, f32[256,512]{1,0:T(8,128)}, f32[1024,128]{1,0:T(8,128)}, f32[1024,128]{1,0:T(8,128)}, f32[1024,128]{1,0:T(8,128)},...) custom-call(f32[256,512]{1,0:T(8,128)} %depth_ref.1, f32[256,512]{1,0:T(8,128)} %bed_ref.1, f32[256,512]{1,0:T(8,128)} %mass_ref.1, ...), custom_call_target="tpu_custom_call" | custom-call | flops 7864320 | bytes 6815744 | tf_op jit(solution)/shard_map/pallas_call | solution.py:119
  24.3 1.1 %constant_dynamic-update-slice_fusion.1 = f32[1024,256]{1,0:T(8,128)S(1)} fusion(f32[1024,128]{1,0:T(8,128)} %get-tuple-element.13), kind=kLoop, calls=%fused_computation.140 | loop fusion | bytes 1048576
  25.5 0.8 fusion
  26.3 0.7 fusion.1
  27.0 0.8 fusion.13
  27.8 0.2 reshape.82
  28.0 0.3 concatenate.43
  28.3 0.8 all_to_all.11
  29.1 30.4 %all_to_all.17 = f32[128,1,2176]{2,1,0:T(1,128)S(1)} all-to-all(f32[128,1,2176]{2,1,0:T(1,128)S(1)} %all_to_all.11), channel_id=1, replica_groups=mesh['row'=4,'col'=32] {'row','col'}, dimensions={0} | all-to-all | bytes 2228224 | tf_op jit(solution)/shard_map/all_to_all | solution.py:152
  59.6 0.1 fusion.75
  59.7 0.1 slice.136
  59.8 0.2 reshape.84
  59.9 0.1 broadcast_in_dim.74
  60.0 0.1 eq.133
  60.2 0.2 fusion.18
  60.4 0.6 fusion.6
  61.0 0.1 fusion.81
  61.3 0.1 fusion.64
  61.4 0.1 fusion.67
  61.5 0.4 fusion.20
  61.8 0.3 convolution_add_fusion.1
  62.2 1.3 %fusion.12 = f32[128,8,256]{2,1,0:T(8,128)} fusion(f32[1024,256]{1,0:T(8,128)S(1)} %convolution_add_fusion.1, f32[1024]{0:T(1024)S(1)} %eq.133, f32[16,128]{1,0:T(8,128)S(1)} %fusion.67, f32[16,128]{1,0:T(8,128)S(1)} %fusion.64), kind=kOutput, calls=%fused_computation.27 | convolution fusion | flops 8724480 | bytes 2117632 | tf_op jit(solution)/shard_map/dot_general | solution.py:81
  63.6 4.8 %all-to-all-start.1 = ((f32[128,8,256]{2,1,0:T(8,128)}), f32[128,8,256]{2,1,0:T(8,128)S(1)}, u32[]{:S(2)}, u32[]{:S(2)}) async-start(f32[128,8,256]{2,1,0:T(8,128)} %fusion.12), calls=%async_computation.1 | async-start | bytes 2097152 | tf_op jit(solution)/shard_map/all_to_all | solution.py:176
  68.5 1.0 %gather_fusion = f32[512,128]{1,0:T(8,128)S(1)} fusion(f32[1024,128]{1,0:T(8,128)S(1)} %copy-done.2, s32[1024]{0:T(1024)S(1)} %pad_clamp_fusion.1), kind=kCustom, calls=%fused_computation | custom fusion | bytes 526336 | tf_op jit(solution)/shard_map/gather | solution.py:186
  69.5 1.0 %gather_fusion.2 = f32[512,128]{1,0:T(8,128)S(1)} fusion(f32[1024,128]{1,0:T(8,128)S(1)} %copy-done.1, s32[1024]{0:T(1024)S(1)} %pad_clamp_fusion.1), kind=kCustom, calls=%fused_computation.2 | custom fusion | bytes 526336 | tf_op jit(solution)/shard_map/gather | solution.py:184
  70.6 1.0 %gather_fusion.3 = f32[512,128]{1,0:T(8,128)S(1)} fusion(f32[1024,128]{1,0:T(8,128)S(1)} %copy-done, s32[1024]{0:T(1024)S(1)} %pad_clamp_fusion.1), kind=kCustom, calls=%fused_computation.3 | custom fusion | bytes 526336 | tf_op jit(solution)/shard_map/gather | solution.py:185
  71.6 16.0 %all-to-all-done.1 = f32[128,8,256]{2,1,0:T(8,128)S(1)} async-done(((f32[128,8,256]{2,1,0:T(8,128)}), f32[128,8,256]{2,1,0:T(8,128)S(1)}, u32[]{:S(2)}, u32[]{:S(2)}) %all-to-all-start.1) | async-done | bytes 1048608 | tf_op jit(solution)/shard_map/all_to_all | solution.py:176
  87.6 1.6 %gather_fusion.1 = f32[512,256]{1,0:T(8,128)S(1)} fusion(f32[1024,256]{1,0:T(8,128)S(1)} %bitcast.43, s32[1024]{0:T(1024)S(1)} %pad_clamp_fusion), kind=kCustom, calls=%fused_computation.1 | custom fusion | bytes 1050624 | tf_op jit(solution)/shard_map/gather | solution.py:183
  89.2 0.1 fusion.25
  89.3 0.1 fusion.15
  89.5 0.3 fusion.23
  89.8 0.3 convolution_add_fusion.3
  90.0 0.3 convolution_add_fusion.2
  90.3 0.3 fusion.22
  90.6 0.3 convolution_add_fusion.5
  90.9 0.3 convolution_add_fusion.4
  91.2 0.3 fusion.21
  91.5 0.3 fusion.19
  91.7 0.3 convolution_add_fusion.9
  92.0 0.3 convolution_add_fusion.7
  92.3 0.3 convolution_add_fusion.6
  92.6 0.3 convolution_add_fusion.8
  92.9 0.7 copy-done.8
  93.6 0.2 copy-done.9
  93.8 1.1 %maximum_add_fusion = (f32[256,512]{1,0:T(8,128)}, f32[256,512]{1,0:T(8,128)}) fusion(f32[256,512]{1,0:T(8,128)S(1)} %copy-done.8, f32[256,128]{1,0:T(8,128)S(1)} %get-tuple-element.38, f32[256,128]{1,0:T(8,128)S(1)} %get-tuple-element.36, f32[256,128]{1,0:T(8,128)S(1)} %get-tuple-element.34, f32[256,128]{1,0:T(8,128)S(1)} %get-tuple-element.32, ...), kind=kLoop, calls=%fused_computation.52 | loop fusion | flops 1048576 | bytes 3145728 | tf_op jit(solution)/shard_map/add | solution.py:200
  (68 shorter events, 0.8 us)
Async XLA Ops:
  0.6 1.3 %copy-start.6 = (f32[256,512]{1,0:T(8,128)S(1)}, f32[256,512]{1,0:T(8,128)}, u32[]{:S(2)}) copy-start(f32[256,512]{1,0:T(8,128)} %bed_ref.1) | copy-start | bytes 1572868
  0.6 1.4 %copy-start.5 = (f32[256,512]{1,0:T(8,128)S(1)}, f32[256,512]{1,0:T(8,128)}, u32[]{:S(2)}) copy-start(f32[256,512]{1,0:T(8,128)} %depth_ref.1) | copy-start | bytes 1572868
  0.7 1.5 %copy-start.4 = (f32[256,512]{1,0:T(8,128)S(1)}, f32[256,512]{1,0:T(8,128)}, u32[]{:S(2)}) copy-start(f32[256,512]{1,0:T(8,128)} %cond_ref.1) | copy-start | bytes 1572868
  0.7 1.6 %copy-start.3 = (f32[256,512]{1,0:T(8,128)S(1)}, f32[256,512]{1,0:T(8,128)}, u32[]{:S(2)}) copy-start(f32[256,512]{1,0:T(8,128)} %mass_ref.1) | copy-start | bytes 1572868
  2.8 12.4 %copy-start.18 = (s32[512]{0:T(512)S(1)}, s32[512]{0:T(512)}, u32[]{:S(2)}) copy-start(s32[512]{0:T(512)} %param.21) | copy-start | bytes 6148
  2.8 12.4 %copy-start.13 = (s32[512,1]{0,1:T(1,128)S(1)}, s32[512,1]{0,1:T(1,128)}, u32[]{:S(2)}) copy-start(s32[512,1]{0,1:T(1,128)} %param.20) | copy-start | bytes 6148
  2.9 14.3 %collective-permute-start.2 = (f32[4,256]{1,0:T(4,128)S(1)}, f32[4,256]{1,0:T(4,128)S(1)}, u32[]{:S(2)}, u32[]{:S(2)}) collective-permute-start(f32[4,256]{1,0:T(4,128)S(1)} %get-tuple-element.18), channel_id=1, source_target_pairs={{0,1},{1,2},{2,3},{3,4},{4,5},{5,6},{6,7},{7,8},{8,9},{9,10},{10,1... | collective-permute-start | bytes 12296 | tf_op jit(solution)/shard_map/ppermute | solution.py:13
  7.9 9.3 %collective-permute-start.3 = (f32[4,256]{1,0:T(4,128)S(1)}, f32[4,256]{1,0:T(4,128)S(1)}, u32[]{:S(2)}, u32[]{:S(2)}) collective-permute-start(f32[4,256]{1,0:T(4,128)S(1)} %get-tuple-element.19), channel_id=1, source_target_pairs={{1,0},{2,1},{3,2},{4,3},{5,4},{6,5},{7,6},{8,7},{9,8},{10,9},{11,1... | collective-permute-start | bytes 12296 | tf_op jit(solution)/shard_map/ppermute | solution.py:13
  9.9 6.1 %copy-start.17 = (f32[512]{0:T(512)S(1)}, f32[512]{0:T(512)}, u32[]{:S(2)}) copy-start(f32[512]{0:T(512)} %param.22) | copy-start | bytes 6148
  9.9 6.7 %copy-start.10 = (s32[512]{0:T(512)S(1)}, s32[512]{0:T(512)}, u32[]{:S(2)}) copy-start(s32[512]{0:T(512)} %param.19) | copy-start | bytes 6148
  9.9 8.1 %collective-permute-start.1 = (f32[4,512]{1,0:T(4,128)S(1)}, f32[4,512]{1,0:T(4,128)S(1)}, u32[]{:S(2)}, u32[]{:S(2)}) collective-permute-start(f32[4,512]{1,0:T(4,128)S(1)} %bitcast.56), channel_id=1, source_target_pairs={{32,0},{64,32},{96,64},{33,1},{65,33},{97,65},{34,2},{66,34},{98,6... | collective-permute-start | bytes 24584 | tf_op jit(solution)/shard_map/ppermute | solution.py:13
  11.2 6.8 %collective-permute-start = (f32[4,512]{1,0:T(4,128)S(1)}, f32[4,512]{1,0:T(4,128)S(1)}, u32[]{:S(2)}, u32[]{:S(2)}) collective-permute-start(f32[4,512]{1,0:T(4,128)S(1)} %bitcast.57), channel_id=1, source_target_pairs={{0,32},{32,64},{64,96},{1,33},{33,65},{65,97},{2,34},{34,66},{66,9... | collective-permute-start | bytes 24584 | tf_op jit(solution)/shard_map/ppermute | solution.py:13
  24.3 1.2 %copy-start.7 = (f32[1024,128]{1,0:T(8,128)S(1)}, f32[1024,128]{1,0:T(8,128)}, u32[]{:S(2)}) copy-start(f32[1024,128]{1,0:T(8,128)} %get-tuple-element.14) | copy-start | bytes 1572868
  60.1 0.9 copy-start.14
  60.1 0.9 copy-start.15
  60.1 0.9 copy-start.16
  61.4 0.8 copy-start.11
  61.5 0.7 copy-start.12
  63.6 4.9 %copy-start.2 = (f32[1024,128]{1,0:T(8,128)S(1)}, f32[1024,128]{1,0:T(8,128)}, u32[]{:S(2)}) copy-start(f32[1024,128]{1,0:T(8,128)} %get-tuple-element.12) | copy-start | bytes 1572868
  63.6 24.1 %all-to-all-start.1 = ((f32[128,8,256]{2,1,0:T(8,128)}), f32[128,8,256]{2,1,0:T(8,128)S(1)}, u32[]{:S(2)}, u32[]{:S(2)}) async-start(f32[128,8,256]{2,1,0:T(8,128)} %fusion.12), calls=%async_computation.1 | async-start | bytes 2097152 | tf_op jit(solution)/shard_map/all_to_all | solution.py:176
  68.4 1.1 %copy-start.1 = (f32[1024,128]{1,0:T(8,128)S(1)}, f32[1024,128]{1,0:T(8,128)}, u32[]{:S(2)}) copy-start(f32[1024,128]{1,0:T(8,128)} %get-tuple-element.15) | copy-start | bytes 1572868
  69.5 1.1 %copy-start = (f32[1024,128]{1,0:T(8,128)S(1)}, f32[1024,128]{1,0:T(8,128)}, u32[]{:S(2)}) copy-start(f32[1024,128]{1,0:T(8,128)} %get-tuple-element.16) | copy-start | bytes 1572868
  92.6 1.0 %copy-start.8 = (f32[256,512]{1,0:T(8,128)S(1)}, f32[256,512]{1,0:T(8,128)}, u32[]{:S(2)}) copy-start(f32[256,512]{1,0:T(8,128)} %get-tuple-element.11) | copy-start | bytes 1572868
  92.6 1.2 %copy-start.9 = (f32[256,512]{1,0:T(8,128)S(1)}, f32[256,512]{1,0:T(8,128)}, u32[]{:S(2)}) copy-start(f32[256,512]{1,0:T(8,128)} %get-tuple-element.17) | copy-start | bytes 1572868

commit v9 on v7

--- a/solution.py
+++ b/solution.py
@@ -14,8 +14,7 @@
 
 
 def stencil_kernel(depth_ref, bed_ref, mass_ref, cond_ref, settle_ref, wet_ref, rows_ref, cols_ref,
-                   depth1_ref, mass1_ref, surf_blocks_ref, mass_blocks_ref, open_blocks_ref,
-                   open_surf_ref, open_mass_ref):
+                   depth1_ref, mass1_ref, open_surf_ref, open_mass_ref):
     depth = depth_ref[...]
     bed = bed_ref[...]
     mass = mass_ref[...]
@@ -29,42 +28,48 @@
     rows = rows_ref[...]
     cols = cols_ref[...]
 
-    def neighbour(field, step_y, step_x):
+    def coeff(c_i, o_i, c_j, o_j):
+        return 0.5 * (c_i + c_j) * o_i * o_j
+
+    def ahead(field, axis):
         value = own[field]
-        if step_y == 1:
-            edge = rows[4 + field : 5 + field, :]
-            return jnp.where(row_id == tile_y - 1, edge, pltpu.roll(value, tile_y - 1, 0))
-        if step_y == -1:
-            edge = rows[field : field + 1, :]
-            return jnp.where(row_id == 0, edge, pltpu.roll(value, 1, 0))
-        if step_x == 1:
-            edge = cols[:, 4 + field : 5 + field]
-            return jnp.where(col_id == tile_x - 1, edge, pltpu.roll(value, tile_x - 1, 1))
-        edge = cols[:, field : field + 1]
-        return jnp.where(col_id == 0, edge, pltpu.roll(value, 1, 1))
-
-    water_gain = jnp.zeros_like(depth)
-    mass_gain = jnp.zeros_like(depth)
-    for step_y, step_x in ((1, 0), (-1, 0), (0, 1), (0, -1)):
-        coeff = 0.5 * (cond + neighbour(2, step_y, step_x)) * opened * neighbour(3, step_y, step_x)
-        water_gain = water_gain + coeff * (neighbour(0, step_y, step_x) - surface)
-        mass_gain = mass_gain + coeff * (neighbour(1, step_y, step_x) - mass)
-    depth1 = depth + water_gain
-    mass1 = (mass + mass_gain) * jnp.exp(-settle_ref[...])
+        if axis == 0:
+            return jnp.where(row_id == tile_y - 1, rows[4 + field : 5 + field, :], pltpu.roll(value, tile_y - 1, 0))
+        return jnp.where(col_id == tile_x - 1, cols[:, 4 + field : 5 + field], pltpu.roll(value, tile_x - 1, 1))
+
+    flux = []
+    for axis in (0, 1):
+        a = coeff(cond, opened, ahead(2, axis), ahead(3, axis))
+        flux.append((a * (ahead(0, axis) - surface), a * (ahead(1, axis) - mass)))
+
+    top = rows[0:4, :]
+    left = cols[:, 0:4]
+    a_top = coeff(cond[0:1, :], opened[0:1, :], top[2:3, :], top[3:4, :])
+    a_left = coeff(cond[:, 0:1], opened[:, 0:1], left[:, 2:3], left[:, 3:4])
+    edge_y = (a_top * (top[0:1, :] - surface[0:1, :]), a_top * (top[1:2, :] - mass[0:1, :]))
+    edge_x = (a_left * (left[:, 0:1] - surface[:, 0:1]), a_left * (left[:, 1:2] - mass[:, 0:1]))
+
+    def behind(k):
+        from_y = jnp.where(row_id == 0, edge_y[k], -pltpu.roll(flux[0][k], 1, 0))
+        from_x = jnp.where(col_id == 0, edge_x[k], -pltpu.roll(flux[1][k], 1, 1))
+        return from_y, from_x
+
+    gains = []
+    for k in (0, 1):
+        from_y, from_x = behind(k)
+        gains.append(((flux[0][k] + from_y) + flux[1][k]) + from_x)
+    depth1 = depth + gains[0]
+    mass1 = (mass + gains[1]) * jnp.exp(-settle_ref[...])
     depth1_ref[...] = depth1
     mass1_ref[...] = mass1
     per_row = tile_x // 128
+    surface1 = depth1 + bed
     for j in range(per_row):
         lanes = slice(j * 128, (j + 1) * 128)
         rows_j = pl.ds(j, tile_y, stride=per_row)
-        surf_j = (depth1 + bed)[:, lanes]
-        mass_j = mass1[:, lanes]
         open_j = opened[:, lanes]
-        surf_blocks_ref[rows_j, :] = surf_j
-        mass_blocks_ref[rows_j, :] = mass_j
-        open_blocks_ref[rows_j, :] = open_j
-        open_surf_ref[rows_j, :] = open_j * surf_j
-        open_mass_ref[rows_j, :] = open_j * mass_j
+        open_surf_ref[rows_j, :] = open_j * surface1[:, lanes]
+        open_mass_ref[rows_j, :] = open_j * mass1[:, lanes]
 
 
 def smooth_reach(values):
@@ -100,13 +105,13 @@
     vmem = pl.BlockSpec(memory_space=pltpu.VMEM)
     blocks = tile_y * tile_x // 128
     block_rows = jax.ShapeDtypeStruct((blocks, 128), jnp.float32)
-    depth1, mass1, surf_blocks, mass_blocks, open_blocks, open_surf, open_mass = pl.pallas_call(
+    depth1, mass1, open_surf, open_mass = pl.pallas_call(
         stencil_kernel,
-        out_shape=[tile, tile] + [block_rows] * 5,
+        out_shape=[tile, tile] + [block_rows] * 2,
         in_specs=[vmem] * 8,
-        out_specs=[vmem] * 7,
+        out_specs=[vmem] * 4,
         cost_estimate=pl.CostEstimate(
-            flops=60 * tile_y * tile_x, transcendentals=tile_y * tile_x, bytes_accessed=52 * tile_y * tile_x
+            flops=60 * tile_y * tile_x, transcendentals=tile_y * tile_x, bytes_accessed=40 * tile_y * tile_x
         ),
     )(depth, bed, mass, conduct, settle, wet, rows, cols)
 
@@ -169,9 +174,9 @@
         tiled=True,
     )
     own_rows = answered.reshape(devices * slot_cap, 256)[slot_of]
-    surf_rows = surf_blocks[link_block]
-    mass_rows = mass_blocks[link_block]
-    weight = link_coef[:, None] * open_blocks[link_block]
+    surf_rows = (depth1 + bed).reshape(blocks, 128)[link_block]
+    mass_rows = mass1.reshape(blocks, 128)[link_block]
+    weight = link_coef[:, None] * opened.reshape(blocks, 128)[link_block]
     applied = jnp.concatenate(
         [
             0.5 * weight * (own_rows[:, :128] - surf_rows),

time: 92.8 us -> 93.2 us (level)
  blocking collectives: 30.4 us -> 0 us
  waiting for transfers between devices: 16 us -> 35.6 us
  starting transfers between devices: 17 us -> 27.7 us
  local copies, waits for them, and re-layouts: 9.02 us -> 10.4 us
  Pallas kernels: 5.65 us -> 4.67 us
    all_to_all x1 -> x0, blocking collectives: 30.4 us -> none  [body(): lax.all_to_all(outgoing, ('row', 'col'), split_axis=0, concat_axis=0, til...]
    all_to_all x0 -> x1, waiting for transfers between devices: none -> 19.8 us  [body(): lax.all_to_all(outgoing, ('row', 'col'), split_axis=0, concat_axis=0, til...]
    all_to_all x0 -> x1, starting transfers between devices: none -> 10.8 us  [body(): lax.all_to_all(outgoing, ('row', 'col'), split_axis=0, concat_axis=0, til...]
    convert_element_type x0 -> x1, other arithmetic: none -> 1.24 us  [body(): opened = wet.astype(jnp.float32)]
    another operation x2 -> x1, other arithmetic: 1.3 us -> 0.08 us  [body(): stacked = jnp.stack([depth + bed, mass, conduct, opened])]
    all_to_all x1, local copies, waits for them, and re-layouts: 0.77 us -> 1.77 us  [body(): lax.all_to_all(outgoing, ('row', 'col'), split_axis=0, concat_axis=0, til...]
    pallas_call x1, Pallas kernels: 5.65 us -> 4.67 us  [body(): pl.pallas_call(stencil_kernel, out_shape=[tile, tile] + [block_rows] * 2,...]
  transfers between devices with their start and end apart: 5 -> 6, of which waited for: 1 -> 2; matrix products, arithmetic and copies ran while one was open for 6% -> 6% of each run, Pallas kernels for 0% -> 0%
where the time goes in v9:
time: 93.2 us; the launch traced here: 92.7 us
  waiting for transfers between devices  35.6 us (38%)
  starting transfers between devices  27.7 us (30%)
  local copies, waits for them, and re-layouts  10.4 us (11%)
  matrix products  7.37 us (8%)
  other arithmetic  5.76 us (6%)
  Pallas kernels  4.67 us (5%)
  between operations  1.23 us (1%)
    all_to_all x1, waiting for transfers between devices, body(): lax.all_to_all(outgoing, ('row', 'col'), split_axis=0, concat_axis=0, til...  19.8 us
    all_to_all x1, waiting for transfers between devices, body(): lax.all_to_all(reply.reshape(devices, slot_cap, 256), ('row', 'col'), spl...  15.8 us
    all_to_all x1, starting transfers between devices, body(): lax.all_to_all(outgoing, ('row', 'col'), split_axis=0, concat_axis=0, til...  10.8 us
    ppermute x2, starting transfers between devices, halo_pair(): lax.ppermute(last, axis, forward)  9.05 us
    pallas_call x1, Pallas kernels, body(): pl.pallas_call(stencil_kernel, out_shape=[tile, tile] + [block_rows] * 2,...  4.67 us
    all_to_all x1, starting transfers between devices, body(): lax.all_to_all(reply.reshape(devices, slot_cap, 256), ('row', 'col'), spl...  4.62 us
    dot_general x1, matrix products, body(): jnp.dot(slot_hot, jnp.concatenate([open_surf, open_mass], axis=1), precis...  3.28 us
    ppermute x2, starting transfers between devices, halo_pair(): lax.ppermute(first, axis, backward)  3.21 us
  transfers between devices with their start and end apart: 6, of which 2 were waited for; matrix products, arithmetic and copies ran while one was open for 6% of the time, Pallas kernels for 0%

profile of v9, /device:TPU:1, one launch (start us, length us, event | category | flops | bytes accessed | tf_op | source)
XLA Modules:
  0.0 92.7 jit_solution(10666283177830301542)
XLA Ops:
  0.6 0.0 copy-start
  0.6 0.0 copy-start.4
  0.7 1.2 %fusion.58 = (f32[256,512]{1,0:T(8,128)S(1)}, f32[1,256,512]{2,1,0:T(8,128)S(1)}) fusion(s32[256,512]{1,0:T(8,128)} %wet_ref.1), kind=kLoop, calls=%fused_computation.106 | loop fusion | flops 131072 | bytes 1572864 | tf_op jit(solution)/shard_map/convert_element_type | solution.py:97
  1.9 0.1 copy-done.4
  2.0 0.1 add_bitcast_fusion
  2.1 1.0 %copy-done.2 = f32[256,512]{1,0:T(8,128)S(1)} copy-done((f32[256,512]{1,0:T(8,128)S(1)}, f32[256,512]{1,0:T(8,128)}, u32[]{:S(2)}) %copy-start.2) | copy-done | bytes 524312
  3.0 0.2 copy-done.3
  3.2 0.5 maximum_reduce_fusion
  3.7 0.0 copy-start.10
  3.7 5.1 %collective-permute-start.2 = (f32[4,256]{1,0:T(4,128)S(1)}, f32[4,256]{1,0:T(4,128)S(1)}, u32[]{:S(2)}, u32[]{:S(2)}) collective-permute-start(f32[4,256]{1,0:T(4,128)S(1)} %get-tuple-element.12), channel_id=1, source_target_pairs={{0,1},{1,2},{2,3},{3,4},{4,5},{5,6},{6,7},{7,8},{8,9},{9,10},{10,1... | collective-permute-start | bytes 12296 | tf_op jit(solution)/shard_map/ppermute | solution.py:13
  8.8 1.9 %collective-permute-start.3 = (f32[4,256]{1,0:T(4,128)S(1)}, f32[4,256]{1,0:T(4,128)S(1)}, u32[]{:S(2)}, u32[]{:S(2)}) collective-permute-start(f32[4,256]{1,0:T(4,128)S(1)} %get-tuple-element.13), channel_id=1, source_target_pairs={{1,0},{2,1},{3,2},{4,3},{5,4},{6,5},{7,6},{8,7},{9,8},{10,9},{11,1... | collective-permute-start | bytes 12296 | tf_op jit(solution)/shard_map/ppermute | solution.py:13
  10.8 0.0 copy-start.14
  10.8 0.0 copy-start.7
  10.8 1.3 %collective-permute-start.1 = (f32[4,512]{1,0:T(4,128)S(1)}, f32[4,512]{1,0:T(4,128)S(1)}, u32[]{:S(2)}, u32[]{:S(2)}) collective-permute-start(f32[4,512]{1,0:T(4,128)S(1)} %bitcast.44), channel_id=1, source_target_pairs={{32,0},{64,32},{96,64},{33,1},{65,33},{97,65},{34,2},{66,34},{98,6... | collective-permute-start | bytes 24584 | tf_op jit(solution)/shard_map/ppermute | solution.py:13
  12.1 4.0 %collective-permute-start = (f32[4,512]{1,0:T(4,128)S(1)}, f32[4,512]{1,0:T(4,128)S(1)}, u32[]{:S(2)}, u32[]{:S(2)}) collective-permute-start(f32[4,512]{1,0:T(4,128)S(1)} %bitcast.45), channel_id=1, source_target_pairs={{0,32},{32,64},{64,96},{1,33},{33,65},{65,97},{2,34},{34,66},{66,9... | collective-permute-start | bytes 24584 | tf_op jit(solution)/shard_map/ppermute | solution.py:13
  16.1 0.1 copy.72
  16.2 0.2 fusion.23
  16.5 0.1 add_add_fusion
  16.6 0.2 fusion.22
  16.8 0.6 select_reduce_fusion
  17.5 0.4 select_reduce_fusion.1
  17.9 0.1 reshape.93
  18.0 0.1 max.16
  18.1 0.8 copy.71
  18.9 0.6 pad_maximum_fusion.8.rows_ref
  19.5 4.7 %shard_map.156 = (f32[256,512]{1,0:T(8,128)}, f32[256,512]{1,0:T(8,128)}, f32[1024,128]{1,0:T(8,128)}, f32[1024,128]{1,0:T(8,128)}) custom-call(f32[256,512]{1,0:T(8,128)} %depth_ref.1, f32[256,512]{1,0:T(8,128)} %bed_ref.1, f32[256,512]{1,0:T(8,128)} %mass_ref.1, f32[256,512]{1,0:T(8,128)} %cond_ref.1, f32[256,512]{1,0:T(8,128)} %settle_ref.1, ...), custom_call_target="tpu_custom_call" | custom-call | flops 7864320 | bytes 5242880 | tf_op jit(solution)/shard_map/pallas_call | solution.py:108
  24.1 3.3 %fusion.6 = f32[1024,256]{1,0:T(8,128)S(1)} fusion(s32[1024]{0:T(1024)S(1)} %select_reduce_fusion.1, f32[1024,128]{1,0:T(8,128)} %get-tuple-element.10, f32[1024,128]{1,0:T(8,128)} %get-tuple-element.9, f32[1024]{0:T(1024)S(1)} %broadcast_maximum_fusion), kind=kOutput, calls=%fused_computation.15 | convolution fusion | flops 3222798336 | bytes 2105344 | tf_op jit(solution)/shard_map/dot_general | solution.py:133
  27.4 0.2 reshape.92
  27.6 0.3 concatenate.43
  27.9 1.8 %all_to_all.11 = f32[128,1,2176]{2,1,0:T(1,128)} reshape(f32[128,2176]{1,0:T(8,128)S(1)} %concatenate.43) | data formatting | bytes 2228224 | tf_op jit(solution)/shard_map/all_to_all | solution.py:143
  29.7 10.8 %all-to-all-start = ((f32[128,1,2176]{2,1,0:T(1,128)}), f32[128,1,2176]{2,1,0:T(1,128)S(1)}, u32[]{:S(2)}, u32[]{:S(2)}) async-start(f32[128,1,2176]{2,1,0:T(1,128)} %all_to_all.11), calls=%async_computation | async-start | bytes 2228224 | tf_op jit(solution)/shard_map/all_to_all | solution.py:143
  40.5 19.8 %all-to-all-done = f32[128,1,2176]{2,1,0:T(1,128)S(1)} async-done(((f32[128,1,2176]{2,1,0:T(1,128)}), f32[128,1,2176]{2,1,0:T(1,128)S(1)}, u32[]{:S(2)}, u32[]{:S(2)}) %all-to-all-start) | async-done | bytes 1114144 | tf_op jit(solution)/shard_map/all_to_all | solution.py:143
  60.3 0.1 copy.92
  60.4 0.1 fusion.57
  60.5 0.1 slice.136
  60.6 0.2 reshape.94
  60.8 0.1 broadcast_in_dim.74
  60.9 0.1 eq.126
  61.0 0.0 copy-start.13
  61.0 0.2 fusion.11
  61.2 0.6 fusion.2
  61.9 0.1 fusion.64
  61.9 0.1 fusion.63
  62.0 0.1 fusion.66
  62.1 0.1 fusion.65
  62.2 0.1 fusion.43
  62.2 0.1 fusion.46
  62.3 1.6 %convolution_bitcast_fusion = f32[128,8,256]{2,1,0:T(8,128)} fusion(f32[1024]{0:T(1024)S(1)} %eq.126, f32[16,128]{1,0:T(8,128)S(1)} %fusion.46, f32[16,128]{1,0:T(8,128)S(1)} %fusion.43), kind=kOutput, calls=%fused_computation.16 | convolution fusion | flops 50352128 | bytes 1069056 | tf_op jit(solution)/shard_map/dot_general | solution.py:166
  64.0 4.6 %all-to-all-start.1 = ((f32[128,8,256]{2,1,0:T(8,128)}), f32[128,8,256]{2,1,0:T(8,128)S(1)}, u32[]{:S(2)}, u32[]{:S(2)}) async-start(f32[128,8,256]{2,1,0:T(8,128)} %convolution_bitcast_fusion), calls=%async_computation.1 | async-start | bytes 2097152 | tf_op jit(solution)/shard_map/all_to_all | solution.py:169
  68.6 0.0 copy-start.1
  68.6 1.0 %gather_fusion = f32[512,128]{1,0:T(8,128)S(1)} fusion(f32[1024,128]{1,0:T(8,128)S(1)} %reshape.90, s32[1024]{0:T(1024)S(1)} %pad_clamp_fusion.1), kind=kCustom, calls=%fused_computation | custom fusion | bytes 526336 | tf_op jit(solution)/shard_map/gather | solution.py:179
  69.8 0.1 copy-done.5
  69.8 0.1 add.101
  69.9 0.0 copy-start.6
  70.0 1.0 %gather_fusion.2 = f32[512,128]{1,0:T(8,128)S(1)} fusion(f32[1024,128]{1,0:T(8,128)S(1)} %reshape.97, s32[1024]{0:T(1024)S(1)} %pad_clamp_fusion.1), kind=kCustom, calls=%fused_computation.2 | custom fusion | bytes 526336 | tf_op jit(solution)/shard_map/gather | solution.py:177
  71.1 1.0 %gather_fusion.3 = f32[512,128]{1,0:T(8,128)S(1)} fusion(f32[1024,128]{1,0:T(8,128)S(1)} %reshape.98, s32[1024]{0:T(1024)S(1)} %pad_clamp_fusion.1), kind=kCustom, calls=%fused_computation.3 | custom fusion | bytes 526336 | tf_op jit(solution)/shard_map/gather | solution.py:178
  72.1 15.8 %all-to-all-done.1 = f32[128,8,256]{2,1,0:T(8,128)S(1)} async-done(((f32[128,8,256]{2,1,0:T(8,128)}), f32[128,8,256]{2,1,0:T(8,128)S(1)}, u32[]{:S(2)}, u32[]{:S(2)}) %all-to-all-start.1) | async-done | bytes 1048608 | tf_op jit(solution)/shard_map/all_to_all | solution.py:169
  87.9 1.6 %gather_fusion.1 = f32[512,256]{1,0:T(8,128)S(1)} fusion(f32[1024,256]{1,0:T(8,128)S(1)} %bitcast.31, s32[1024]{0:T(1024)S(1)} %pad_clamp_fusion), kind=kCustom, calls=%fused_computation.1 | custom fusion | bytes 1050624 | tf_op jit(solution)/shard_map/gather | solution.py:176
  89.5 0.1 fusion.21
  89.6 0.5 fusion.16
  90.1 0.5 fusion.14
  90.6 0.5 fusion.12
  91.1 0.5 fusion.18
  91.6 1.1 %maximum_add_fusion = (f32[256,512]{1,0:T(8,128)}, f32[256,512]{1,0:T(8,128)}) fusion(f32[256,512]{1,0:T(8,128)S(1)} %copy-done.5, f32[256,128]{1,0:T(8,128)S(1)} %get-tuple-element.31, f32[256,128]{1,0:T(8,128)S(1)} %get-tuple-element.29, f32[256,128]{1,0:T(8,128)S(1)} %get-tuple-element.27, f32[256,128]{1,0:T(8,128)S(1)} %get-tuple-element.25, ...), kind=kLoop, calls=%fused_computation.28 | loop fusion | flops 1048576 | bytes 3145728 | tf_op jit(solution)/shard_map/add | solution.py:197
  (52 shorter events, 0.4 us)
Async XLA Ops:
  0.6 1.3 %copy-start = (f32[256,512]{1,0:T(8,128)S(1)}, f32[256,512]{1,0:T(8,128)}, u32[]{:S(2)}) copy-start(f32[256,512]{1,0:T(8,128)} %bed_ref.1) | copy-start | bytes 1572868
  0.6 1.4 %copy-start.4 = (f32[256,512]{1,0:T(8,128)S(1)}, f32[256,512]{1,0:T(8,128)}, u32[]{:S(2)}) copy-start(f32[256,512]{1,0:T(8,128)} %depth_ref.1) | copy-start | bytes 1572868
  2.0 1.0 %copy-start.2 = (f32[256,512]{1,0:T(8,128)S(1)}, f32[256,512]{1,0:T(8,128)}, u32[]{:S(2)}) copy-start(f32[256,512]{1,0:T(8,128)} %mass_ref.1) | copy-start | bytes 1572868
  2.0 1.2 %copy-start.3 = (f32[256,512]{1,0:T(8,128)S(1)}, f32[256,512]{1,0:T(8,128)}, u32[]{:S(2)}) copy-start(f32[256,512]{1,0:T(8,128)} %cond_ref.1) | copy-start | bytes 1572868
  3.7 12.4 %copy-start.15 = (s32[512]{0:T(512)S(1)}, s32[512]{0:T(512)}, u32[]{:S(2)}) copy-start(s32[512]{0:T(512)} %param.21) | copy-start | bytes 6148
  3.7 12.4 %copy-start.10 = (s32[512,1]{0,1:T(1,128)S(1)}, s32[512,1]{0,1:T(1,128)}, u32[]{:S(2)}) copy-start(s32[512,1]{0,1:T(1,128)} %param.20) | copy-start | bytes 6148
  3.7 14.3 %collective-permute-start.2 = (f32[4,256]{1,0:T(4,128)S(1)}, f32[4,256]{1,0:T(4,128)S(1)}, u32[]{:S(2)}, u32[]{:S(2)}) collective-permute-start(f32[4,256]{1,0:T(4,128)S(1)} %get-tuple-element.12), channel_id=1, source_target_pairs={{0,1},{1,2},{2,3},{3,4},{4,5},{5,6},{6,7},{7,8},{8,9},{9,10},{10,1... | collective-permute-start | bytes 12296 | tf_op jit(solution)/shard_map/ppermute | solution.py:13
  8.8 9.3 %collective-permute-start.3 = (f32[4,256]{1,0:T(4,128)S(1)}, f32[4,256]{1,0:T(4,128)S(1)}, u32[]{:S(2)}, u32[]{:S(2)}) collective-permute-start(f32[4,256]{1,0:T(4,128)S(1)} %get-tuple-element.13), channel_id=1, source_target_pairs={{1,0},{2,1},{3,2},{4,3},{5,4},{6,5},{7,6},{8,7},{9,8},{10,9},{11,1... | collective-permute-start | bytes 12296 | tf_op jit(solution)/shard_map/ppermute | solution.py:13
  10.8 6.1 %copy-start.14 = (f32[512]{0:T(512)S(1)}, f32[512]{0:T(512)}, u32[]{:S(2)}) copy-start(f32[512]{0:T(512)} %param.22) | copy-start | bytes 6148
  10.8 6.7 %copy-start.7 = (s32[512]{0:T(512)S(1)}, s32[512]{0:T(512)}, u32[]{:S(2)}) copy-start(s32[512]{0:T(512)} %param.19) | copy-start | bytes 6148
  10.8 8.1 %collective-permute-start.1 = (f32[4,512]{1,0:T(4,128)S(1)}, f32[4,512]{1,0:T(4,128)S(1)}, u32[]{:S(2)}, u32[]{:S(2)}) collective-permute-start(f32[4,512]{1,0:T(4,128)S(1)} %bitcast.44), channel_id=1, source_target_pairs={{32,0},{64,32},{96,64},{33,1},{65,33},{97,65},{34,2},{66,34},{98,6... | collective-permute-start | bytes 24584 | tf_op jit(solution)/shard_map/ppermute | solution.py:13
  12.1 6.8 %collective-permute-start = (f32[4,512]{1,0:T(4,128)S(1)}, f32[4,512]{1,0:T(4,128)S(1)}, u32[]{:S(2)}, u32[]{:S(2)}) collective-permute-start(f32[4,512]{1,0:T(4,128)S(1)} %bitcast.45), channel_id=1, source_target_pairs={{0,32},{32,64},{64,96},{1,33},{33,65},{65,97},{2,34},{34,66},{66,9... | collective-permute-start | bytes 24584 | tf_op jit(solution)/shard_map/ppermute | solution.py:13
  29.7 30.6 %all-to-all-start = ((f32[128,1,2176]{2,1,0:T(1,128)}), f32[128,1,2176]{2,1,0:T(1,128)S(1)}, u32[]{:S(2)}, u32[]{:S(2)}) async-start(f32[128,1,2176]{2,1,0:T(1,128)} %all_to_all.11), calls=%async_computation | async-start | bytes 2228224 | tf_op jit(solution)/shard_map/all_to_all | solution.py:143
  60.9 0.9 copy-start.11
  61.0 0.9 copy-start.12
  61.0 0.9 copy-start.13
  62.2 1.7 %copy-start.8 = (f32[16,128]{1,0:T(8,128)}, f32[16,128]{1,0:T(8,128)S(1)}, u32[]{:S(2)}) copy-start(f32[16,128]{1,0:T(8,128)S(1)} %fusion.43) | copy-start | bytes 24580
  62.3 1.6 %copy-start.9 = (f32[16,128]{1,0:T(8,128)}, f32[16,128]{1,0:T(8,128)S(1)}, u32[]{:S(2)}) copy-start(f32[16,128]{1,0:T(8,128)S(1)} %fusion.46) | copy-start | bytes 24580
  64.0 23.9 %all-to-all-start.1 = ((f32[128,8,256]{2,1,0:T(8,128)}), f32[128,8,256]{2,1,0:T(8,128)S(1)}, u32[]{:S(2)}, u32[]{:S(2)}) async-start(f32[128,8,256]{2,1,0:T(8,128)} %convolution_bitcast_fusion), calls=%async_computation.1 | async-start | bytes 2097152 | tf_op jit(solution)/shard_map/all_to_all | solution.py:169
  68.6 1.1 %copy-start.1 = (f32[256,512]{1,0:T(8,128)S(1)}, f32[256,512]{1,0:T(8,128)}, u32[]{:S(2)}) copy-start(f32[256,512]{1,0:T(8,128)} %bed_ref.1) | copy-start | bytes 1572868
  68.6 1.2 %copy-start.5 = (f32[256,512]{1,0:T(8,128)S(1)}, f32[256,512]{1,0:T(8,128)}, u32[]{:S(2)}) copy-start(f32[256,512]{1,0:T(8,128)} %get-tuple-element.8) | copy-start | bytes 1572868
  69.9 1.1 %copy-start.6 = (f32[256,512]{1,0:T(8,128)S(1)}, f32[256,512]{1,0:T(8,128)}, u32[]{:S(2)}) copy-start(f32[256,512]{1,0:T(8,128)} %get-tuple-element.11) | copy-start | bytes 1572868

commit v10 on v9

--- a/solution.py
+++ b/solution.py
@@ -13,7 +13,26 @@
     return lax.ppermute(last, axis, forward), lax.ppermute(first, axis, backward)
 
 
-def stencil_kernel(depth_ref, bed_ref, mass_ref, cond_ref, settle_ref, wet_ref, rows_ref, cols_ref,
+def edges_kernel(depth_top, depth_bottom, depth_left, depth_right, bed_top, bed_bottom, bed_left, bed_right,
+                 mass_top, mass_bottom, mass_left, mass_right, cond_top, cond_bottom, cond_left, cond_right,
+                 wet_top, wet_bottom, wet_left, wet_right, last_rows_ref, first_rows_ref, last_cols_ref,
+                 first_cols_ref):
+    def fields(d, b, m, c, w):
+        return [d[...] + b[...], m[...], c[...], w[...].astype(jnp.float32)]
+
+    top = fields(depth_top, bed_top, mass_top, cond_top, wet_top)
+    bottom = fields(depth_bottom, bed_bottom, mass_bottom, cond_bottom, wet_bottom)
+    left = fields(depth_left, bed_left, mass_left, cond_left, wet_left)
+    right = fields(depth_right, bed_right, mass_right, cond_right, wet_right)
+    for f in range(4):
+        first_rows_ref[f : f + 1, :] = top[f][0:1, :]
+        last_rows_ref[f : f + 1, :] = bottom[f][-1:, :]
+        first_cols_ref[f : f + 1, :] = left[f].T[0:1, :]
+        last_cols_ref[f : f + 1, :] = right[f].T[-1:, :]
+
+
+def stencil_kernel(depth_ref, bed_ref, mass_ref, cond_ref, settle_ref, wet_ref, top_ref, bottom_ref, left_ref,
+                   right_ref,
                    depth1_ref, mass1_ref, open_surf_ref, open_mass_ref):
     depth = depth_ref[...]
     bed = bed_ref[...]
@@ -25,8 +44,11 @@
     own = (surface, mass, cond, opened)
     row_id = lax.broadcasted_iota(jnp.int32, (tile_y, tile_x), 0)
     col_id = lax.broadcasted_iota(jnp.int32, (tile_y, tile_x), 1)
-    rows = rows_ref[...]
-    cols = cols_ref[...]
+    rows = jnp.concatenate([top_ref[...], bottom_ref[...]], axis=0)
+    sides = jnp.concatenate(
+        [left_ref[...], right_ref[...], jnp.zeros((120, tile_y), jnp.float32)], axis=0
+    )
+    cols = sides.T
 
     def coeff(c_i, o_i, c_j, o_j):
         return 0.5 * (c_i + c_j) * o_i * o_j
@@ -96,11 +118,32 @@
     tile_y, tile_x = depth.shape
     opened = wet.astype(jnp.float32)
 
-    stacked = jnp.stack([depth + bed, mass, conduct, opened])
-    top, bottom = halo_pair(stacked[:, tile_y - 1, :], stacked[:, 0, :], "row")
-    left, right = halo_pair(stacked[:, :, tile_x - 1], stacked[:, :, 0], "col")
-    rows = jnp.concatenate([top, bottom], axis=0)
-    cols = jnp.concatenate([left, right], axis=0).T
+    line = lambda n: jax.ShapeDtypeStruct((4, n), jnp.float32)
+
+    def edge_specs():
+        last_row = tile_y // 8 - 1
+        last_col = tile_x // 128 - 1
+        return [
+            pl.BlockSpec((8, tile_x), lambda i: (0, 0)),
+            pl.BlockSpec((8, tile_x), lambda i: (last_row, 0)),
+            pl.BlockSpec((tile_y, 128), lambda i: (0, 0)),
+            pl.BlockSpec((tile_y, 128), lambda i: (0, last_col)),
+        ]
+
+    last_rows, first_rows, last_cols, first_cols = pl.pallas_call(
+        edges_kernel,
+        out_shape=[line(tile_x), line(tile_x), line(tile_y), line(tile_y)],
+        grid=(1,),
+        in_specs=edge_specs() * 5,
+        out_specs=[
+            pl.BlockSpec((4, tile_x), lambda i: (0, 0)),
+            pl.BlockSpec((4, tile_x), lambda i: (0, 0)),
+            pl.BlockSpec((4, tile_y), lambda i: (0, 0)),
+            pl.BlockSpec((4, tile_y), lambda i: (0, 0)),
+        ],
+    )(*[a for a in (depth, bed, mass, conduct, wet) for _ in range(4)])
+    top, bottom = halo_pair(last_rows, first_rows, "row")
+    left, right = halo_pair(last_cols, first_cols, "col")
     tile = jax.ShapeDtypeStruct((tile_y, tile_x), jnp.float32)
     vmem = pl.BlockSpec(memory_space=pltpu.VMEM)
     blocks = tile_y * tile_x // 128
@@ -108,12 +151,12 @@
     depth1, mass1, open_surf, open_mass = pl.pallas_call(
         stencil_kernel,
         out_shape=[tile, tile] + [block_rows] * 2,
-        in_specs=[vmem] * 8,
+        in_specs=[vmem] * 10,
         out_specs=[vmem] * 4,
         cost_estimate=pl.CostEstimate(
             flops=60 * tile_y * tile_x, transcendentals=tile_y * tile_x, bytes_accessed=40 * tile_y * tile_x
         ),
-    )(depth, bed, mass, conduct, settle, wet, rows, cols)
+    )(depth, bed, mass, conduct, settle, wet, top, bottom, left, right)
 
     n_row = lax.axis_size("row")
     n_col = lax.axis_size("col")

time: 93.2 us -> 93.5 us (level)
  Pallas kernels: 4.67 us -> 7.13 us
  other arithmetic: 5.76 us -> 3.33 us
  waiting for transfers between devices: 35.6 us -> 36.8 us
    pallas_call x0 -> x1, Pallas kernels: none -> 2.44 us  [body(): pl.pallas_call(edges_kernel, out_shape=[line(tile_x), line(tile_x), line(...]
    ppermute x2, waiting for transfers between devices: 0.01 us -> 1.24 us  [halo_pair(): lax.ppermute(first, axis, backward)]
    convert_element_type x1, other arithmetic: 1.24 us -> 0.04 us  [body(): opened = wet.astype(jnp.float32)]
  transfers between devices with their start and end apart: 6 -> 6, of which waited for: 2 -> 3; matrix products, arithmetic and copies ran while one was open for 6% -> 6% of each run, Pallas kernels for 0% -> 0%
where the time goes in v10:
time: 93.5 us; the launch traced here: 93 us
  waiting for transfers between devices  36.8 us (39%)
  starting transfers between devices  27.6 us (30%)
  local copies, waits for them, and re-layouts  9.62 us (10%)
  matrix products  7.38 us (8%)
  Pallas kernels  7.13 us (8%)
  other arithmetic  3.33 us (4%)
  between operations  1.2 us (1%)
    all_to_all x1, waiting for transfers between devices, body(): lax.all_to_all(outgoing, ('row', 'col'), split_axis=0, concat_axis=0, til...  19.8 us
    all_to_all x1, waiting for transfers between devices, body(): lax.all_to_all(reply.reshape(devices, slot_cap, 256), ('row', 'col'), spl...  15.8 us
    all_to_all x1, starting transfers between devices, body(): lax.all_to_all(outgoing, ('row', 'col'), split_axis=0, concat_axis=0, til...  11.2 us
    ppermute x2, starting transfers between devices, halo_pair(): lax.ppermute(last, axis, forward)  8.55 us
    pallas_call x1, Pallas kernels, body(): pl.pallas_call(stencil_kernel, out_shape=[tile, tile] + [block_rows] * 2,...  4.68 us
    all_to_all x1, starting transfers between devices, body(): lax.all_to_all(reply.reshape(devices, slot_cap, 256), ('row', 'col'), spl...  4.62 us
    dot_general x1, matrix products, body(): jnp.dot(slot_hot, jnp.concatenate([open_surf, open_mass], axis=1), precis...  3.28 us
    ppermute x2, starting transfers between devices, halo_pair(): lax.ppermute(first, axis, backward)  3.21 us
  transfers between devices with their start and end apart: 6, of which 3 were waited for; matrix products, arithmetic and copies ran while one was open for 6% of the time, Pallas kernels for 0%

profile of v10, /device:TPU:1, one launch (start us, length us, event | category | flops | bytes accessed | tf_op | source)
XLA Modules:
  0.0 93.0 jit_solution(9129794033429312983)
XLA Ops:
  0.6 2.4 %shard_map.156 = (f32[4,512]{1,0:T(4,128)}, f32[4,512]{1,0:T(4,128)}, f32[4,256]{1,0:T(4,128)}, f32[4,256]{1,0:T(4,128)}) custom-call(f32[256,512]{1,0:T(8,128)} %depth_ref.1, f32[256,512]{1,0:T(8,128)} %depth_ref.1, f32[256,512]{1,0:T(8,128)} %depth_ref.1, f32[256,512]{1,0:T(8,128)} %depth_ref.1, f32[256,512]{1,0:T(8,128)} %bed_ref.1, f32[256,512]{1,0:T(8,128)} %bed_ref.1, ...), custom_call_target="tpu_custom_call" | custom-call | tf_op jit(solution)/shard_map/pallas_call | solution.py:133
  3.1 0.0 copy-start.13
  3.1 0.0 copy-start.4
  3.1 4.2 %collective-permute-start = (f32[4,512]{1,0:T(4,128)}, f32[4,512]{1,0:T(4,128)S(1)}, u32[]{:S(2)}, u32[]{:S(2)}) collective-permute-start(f32[4,512]{1,0:T(4,128)} %get-tuple-element.12), channel_id=1, source_target_pairs={{0,32},{32,64},{64,96},{1,33},{33,65},{65,97},{2,34},{34,66},{66,9... | collective-permute-start | bytes 24584 | tf_op jit(solution)/shard_map/ppermute | solution.py:13
  7.3 1.3 %collective-permute-start.1 = (f32[4,512]{1,0:T(4,128)}, f32[4,512]{1,0:T(4,128)S(1)}, u32[]{:S(2)}, u32[]{:S(2)}) collective-permute-start(f32[4,512]{1,0:T(4,128)} %get-tuple-element.13), channel_id=1, source_target_pairs={{32,0},{64,32},{96,64},{33,1},{65,33},{97,65},{34,2},{66,34},{98,6... | collective-permute-start | bytes 24584 | tf_op jit(solution)/shard_map/ppermute | solution.py:13
  8.6 4.4 %collective-permute-start.2 = (f32[4,256]{1,0:T(4,128)}, f32[4,256]{1,0:T(4,128)S(1)}, u32[]{:S(2)}, u32[]{:S(2)}) collective-permute-start(f32[4,256]{1,0:T(4,128)} %get-tuple-element.14), channel_id=1, source_target_pairs={{0,1},{1,2},{2,3},{3,4},{4,5},{5,6},{6,7},{7,8},{8,9},{9,10},{10,1... | collective-permute-start | bytes 12296 | tf_op jit(solution)/shard_map/ppermute | solution.py:13
  13.0 1.9 %collective-permute-start.3 = (f32[4,256]{1,0:T(4,128)}, f32[4,256]{1,0:T(4,128)S(1)}, u32[]{:S(2)}, u32[]{:S(2)}) collective-permute-start(f32[4,256]{1,0:T(4,128)} %get-tuple-element.15), channel_id=1, source_target_pairs={{1,0},{2,1},{3,2},{4,3},{5,4},{6,5},{7,6},{8,7},{9,8},{10,9},{11,1... | collective-permute-start | bytes 12296 | tf_op jit(solution)/shard_map/ppermute | solution.py:13
  14.9 0.1 copy.46
  15.0 0.2 fusion.22
  15.3 0.1 add_add_fusion
  15.4 0.2 fusion.21
  15.7 0.6 select_reduce_fusion
  16.3 0.4 select_reduce_fusion.1
  16.7 0.1 reshape.93
  16.8 0.1 max.16
  16.9 0.0 collective-permute-done.2.left_ref
  16.9 1.2 %collective-permute-done.3.right_ref = f32[4,256]{1,0:T(4,128)S(1)} collective-permute-done((f32[4,256]{1,0:T(4,128)}, f32[4,256]{1,0:T(4,128)S(1)}, u32[]{:S(2)}, u32[]{:S(2)}) %collective-permute-start.3) | collective-permute-done | bytes 4128 | tf_op jit(solution)/shard_map/ppermute | solution.py:13
  18.1 0.0 collective-permute-done.top_ref
  18.1 0.6 copy-done.15
  18.7 0.0 copy-done.8
  18.7 0.6 copy-done.9
  19.3 4.7 %shard_map.157 = (f32[256,512]{1,0:T(8,128)}, f32[256,512]{1,0:T(8,128)}, f32[1024,128]{1,0:T(8,128)}, f32[1024,128]{1,0:T(8,128)}) custom-call(f32[256,512]{1,0:T(8,128)} %depth_ref.1, f32[256,512]{1,0:T(8,128)} %bed_ref.1, f32[256,512]{1,0:T(8,128)} %mass_ref.1, f32[256,512]{1,0:T(8,128)} %cond_ref.1, f32[256,512]{1,0:T(8,128)} %settle_ref.1, ...), custom_call_target="tpu_custom_call" | custom-call | flops 7864320 | bytes 5242880 | tf_op jit(solution)/shard_map/pallas_call | solution.py:151
  24.0 3.3 %fusion.6 = f32[1024,256]{1,0:T(8,128)S(1)} fusion(s32[1024]{0:T(1024)S(1)} %select_reduce_fusion.1, f32[1024,128]{1,0:T(8,128)} %get-tuple-element.18, f32[1024,128]{1,0:T(8,128)} %get-tuple-element.17, f32[1024]{0:T(1024)S(1)} %broadcast_maximum_fusion), kind=kOutput, calls=%fused_computation.15 | convolution fusion | flops 3222798336 | bytes 2105344 | tf_op jit(solution)/shard_map/dot_general | solution.py:176
  27.3 0.2 reshape.92
  27.5 0.3 concatenate.35
  27.8 1.8 %all_to_all.11 = f32[128,1,2176]{2,1,0:T(1,128)} reshape(f32[128,2176]{1,0:T(8,128)S(1)} %concatenate.35) | data formatting | bytes 2228224 | tf_op jit(solution)/shard_map/all_to_all | solution.py:186
  29.6 11.2 %all-to-all-start = ((f32[128,1,2176]{2,1,0:T(1,128)}), f32[128,1,2176]{2,1,0:T(1,128)S(1)}, u32[]{:S(2)}, u32[]{:S(2)}) async-start(f32[128,1,2176]{2,1,0:T(1,128)} %all_to_all.11), calls=%async_computation | async-start | bytes 2228224 | tf_op jit(solution)/shard_map/all_to_all | solution.py:186
  40.9 19.8 %all-to-all-done = f32[128,1,2176]{2,1,0:T(1,128)S(1)} async-done(((f32[128,1,2176]{2,1,0:T(1,128)}), f32[128,1,2176]{2,1,0:T(1,128)S(1)}, u32[]{:S(2)}, u32[]{:S(2)}) %all-to-all-start) | async-done | bytes 1114144 | tf_op jit(solution)/shard_map/all_to_all | solution.py:186
  60.6 0.1 copy.62
  60.7 0.1 fusion.56
  60.8 0.1 slice.120
  60.9 0.1 eq.126
  61.0 0.2 reshape.94
  61.2 0.1 broadcast_in_dim.74
  61.3 0.0 copy-start.10
  61.3 0.0 copy-start.11
  61.3 0.0 copy-start.12
  61.3 0.2 fusion.10
  61.5 0.6 fusion.2
  62.1 0.0 copy-done.10
  62.2 0.1 fusion.63
  62.3 0.1 fusion.64
  62.3 0.1 fusion.61
  62.4 0.1 fusion.62
  62.5 0.1 fusion.45
  62.6 0.1 fusion.42
  62.6 1.6 %convolution_bitcast_fusion = f32[128,8,256]{2,1,0:T(8,128)} fusion(f32[1024]{0:T(1024)S(1)} %eq.126, f32[16,128]{1,0:T(8,128)S(1)} %fusion.45, f32[16,128]{1,0:T(8,128)S(1)} %fusion.42), kind=kOutput, calls=%fused_computation.16 | convolution fusion | flops 50352128 | bytes 1069056 | tf_op jit(solution)/shard_map/dot_general | solution.py:209
  64.3 4.6 %all-to-all-start.1 = ((f32[128,8,256]{2,1,0:T(8,128)}), f32[128,8,256]{2,1,0:T(8,128)S(1)}, u32[]{:S(2)}, u32[]{:S(2)}) async-start(f32[128,8,256]{2,1,0:T(8,128)} %convolution_bitcast_fusion), calls=%async_computation.1 | async-start | bytes 2097152 | tf_op jit(solution)/shard_map/all_to_all | solution.py:212
  68.9 0.0 copy-start
  69.0 0.0 copy-start.2
  69.0 1.0 %gather_fusion = f32[512,128]{1,0:T(8,128)S(1)} fusion(f32[1024,128]{1,0:T(8,128)S(1)} %reshape.90, s32[1024]{0:T(1024)S(1)} %pad_clamp_fusion.1), kind=kCustom, calls=%fused_computation | custom fusion | bytes 526336 | tf_op jit(solution)/shard_map/gather | solution.py:222
  70.1 0.1 copy-done.2
  70.2 0.1 add.97
  70.3 0.0 copy-start.3
  70.3 1.0 %gather_fusion.2 = f32[512,128]{1,0:T(8,128)S(1)} fusion(f32[1024,128]{1,0:T(8,128)S(1)} %reshape.97, s32[1024]{0:T(1024)S(1)} %pad_clamp_fusion.1), kind=kCustom, calls=%fused_computation.2 | custom fusion | bytes 526336 | tf_op jit(solution)/shard_map/gather | solution.py:220
  71.4 1.0 %gather_fusion.3 = f32[512,128]{1,0:T(8,128)S(1)} fusion(f32[1024,128]{1,0:T(8,128)S(1)} %reshape.98, s32[1024]{0:T(1024)S(1)} %pad_clamp_fusion.1), kind=kCustom, calls=%fused_computation.3 | custom fusion | bytes 526336 | tf_op jit(solution)/shard_map/gather | solution.py:221
  72.4 15.8 %all-to-all-done.1 = f32[128,8,256]{2,1,0:T(8,128)S(1)} async-done(((f32[128,8,256]{2,1,0:T(8,128)}), f32[128,8,256]{2,1,0:T(8,128)S(1)}, u32[]{:S(2)}, u32[]{:S(2)}) %all-to-all-start.1) | async-done | bytes 1048608 | tf_op jit(solution)/shard_map/all_to_all | solution.py:212
  88.2 1.6 %gather_fusion.1 = f32[512,256]{1,0:T(8,128)S(1)} fusion(f32[1024,256]{1,0:T(8,128)S(1)} %bitcast.18, s32[1024]{0:T(1024)S(1)} %pad_clamp_fusion), kind=kCustom, calls=%fused_computation.1 | custom fusion | bytes 1050624 | tf_op jit(solution)/shard_map/gather | solution.py:219
  89.8 0.1 fusion.20
  89.9 0.5 fusion.11
  90.4 0.5 fusion.13
  90.9 0.5 fusion.15
  91.4 0.5 fusion.17
  91.9 1.1 %maximum_add_fusion = (f32[256,512]{1,0:T(8,128)}, f32[256,512]{1,0:T(8,128)}) fusion(f32[256,512]{1,0:T(8,128)S(1)} %copy-done.2, f32[256,128]{1,0:T(8,128)S(1)} %get-tuple-element.33, f32[256,128]{1,0:T(8,128)S(1)} %get-tuple-element.31, f32[256,128]{1,0:T(8,128)S(1)} %get-tuple-element.29, f32[256,128]{1,0:T(8,128)S(1)} %get-tuple-element.27, ...), kind=kLoop, calls=%fused_computation.23 | loop fusion | flops 1048576 | bytes 3145728 | tf_op jit(solution)/shard_map/add | solution.py:240
  (47 shorter events, 0.4 us)
Async XLA Ops:
  0.6 14.3 %copy-start.7 = (s32[512,1]{0,1:T(1,128)S(1)}, s32[512,1]{0,1:T(1,128)}, u32[]{:S(2)}) copy-start(s32[512,1]{0,1:T(1,128)} %param.20) | copy-start | bytes 6148
  3.1 12.5 %copy-start.16 = (s32[512]{0:T(512)S(1)}, s32[512]{0:T(512)}, u32[]{:S(2)}) copy-start(s32[512]{0:T(512)} %param.21) | copy-start | bytes 6148
  3.1 12.6 %copy-start.13 = (f32[512]{0:T(512)S(1)}, f32[512]{0:T(512)}, u32[]{:S(2)}) copy-start(f32[512]{0:T(512)} %param.22) | copy-start | bytes 6148
  3.1 13.2 %copy-start.4 = (s32[512]{0:T(512)S(1)}, s32[512]{0:T(512)}, u32[]{:S(2)}) copy-start(s32[512]{0:T(512)} %param.19) | copy-start | bytes 6148
  3.1 15.0 %collective-permute-start = (f32[4,512]{1,0:T(4,128)}, f32[4,512]{1,0:T(4,128)S(1)}, u32[]{:S(2)}, u32[]{:S(2)}) collective-permute-start(f32[4,512]{1,0:T(4,128)} %get-tuple-element.12), channel_id=1, source_target_pairs={{0,32},{32,64},{64,96},{1,33},{33,65},{65,97},{2,34},{34,66},{66,9... | collective-permute-start | bytes 24584 | tf_op jit(solution)/shard_map/ppermute | solution.py:13
  7.3 10.8 %collective-permute-start.1 = (f32[4,512]{1,0:T(4,128)}, f32[4,512]{1,0:T(4,128)S(1)}, u32[]{:S(2)}, u32[]{:S(2)}) collective-permute-start(f32[4,512]{1,0:T(4,128)} %get-tuple-element.13), channel_id=1, source_target_pairs={{32,0},{64,32},{96,64},{33,1},{65,33},{97,65},{34,2},{66,34},{98,6... | collective-permute-start | bytes 24584 | tf_op jit(solution)/shard_map/ppermute | solution.py:13
  8.6 8.3 %collective-permute-start.2 = (f32[4,256]{1,0:T(4,128)}, f32[4,256]{1,0:T(4,128)S(1)}, u32[]{:S(2)}, u32[]{:S(2)}) collective-permute-start(f32[4,256]{1,0:T(4,128)} %get-tuple-element.14), channel_id=1, source_target_pairs={{0,1},{1,2},{2,3},{3,4},{4,5},{5,6},{6,7},{7,8},{8,9},{9,10},{10,1... | collective-permute-start | bytes 12296 | tf_op jit(solution)/shard_map/ppermute | solution.py:13
  13.0 5.1 %collective-permute-start.3 = (f32[4,256]{1,0:T(4,128)}, f32[4,256]{1,0:T(4,128)S(1)}, u32[]{:S(2)}, u32[]{:S(2)}) collective-permute-start(f32[4,256]{1,0:T(4,128)} %get-tuple-element.15), channel_id=1, source_target_pairs={{1,0},{2,1},{3,2},{4,3},{5,4},{6,5},{7,6},{8,7},{9,8},{10,9},{11,1... | collective-permute-start | bytes 12296 | tf_op jit(solution)/shard_map/ppermute | solution.py:13
  16.9 1.3 %copy-start.14 = (f32[4,256]{1,0:T(4,128)}, f32[4,256]{1,0:T(4,128)S(1)}, u32[]{:S(2)}) copy-start(f32[4,256]{1,0:T(4,128)S(1)} %collective-permute-done.2.left_ref) | copy-start | bytes 12292
  18.1 0.6 copy-start.15
  18.1 0.6 copy-start.8
  18.7 0.6 copy-start.9
  29.6 11.2 %copy-start.1 = (s32[256,512]{1,0:T(8,128)S(1)}, s32[256,512]{1,0:T(8,128)}, u32[]{:S(2)}) copy-start(s32[256,512]{1,0:T(8,128)} %wet_ref.1) | copy-start | bytes 1572868
  29.6 31.1 %all-to-all-start = ((f32[128,1,2176]{2,1,0:T(1,128)}), f32[128,1,2176]{2,1,0:T(1,128)S(1)}, u32[]{:S(2)}, u32[]{:S(2)}) async-start(f32[128,1,2176]{2,1,0:T(1,128)} %all_to_all.11), calls=%async_computation | async-start | bytes 2228224 | tf_op jit(solution)/shard_map/all_to_all | solution.py:186
  61.3 0.9 copy-start.10
  61.3 0.9 copy-start.11
  61.3 0.9 copy-start.12
  62.6 1.7 %copy-start.5 = (f32[16,128]{1,0:T(8,128)}, f32[16,128]{1,0:T(8,128)S(1)}, u32[]{:S(2)}) copy-start(f32[16,128]{1,0:T(8,128)S(1)} %fusion.45) | copy-start | bytes 24580
  62.6 1.6 %copy-start.6 = (f32[16,128]{1,0:T(8,128)}, f32[16,128]{1,0:T(8,128)S(1)}, u32[]{:S(2)}) copy-start(f32[16,128]{1,0:T(8,128)S(1)} %fusion.42) | copy-start | bytes 24580
  64.3 23.9 %all-to-all-start.1 = ((f32[128,8,256]{2,1,0:T(8,128)}), f32[128,8,256]{2,1,0:T(8,128)S(1)}, u32[]{:S(2)}, u32[]{:S(2)}) async-start(f32[128,8,256]{2,1,0:T(8,128)} %convolution_bitcast_fusion), calls=%async_computation.1 | async-start | bytes 2097152 | tf_op jit(solution)/shard_map/all_to_all | solution.py:212
  68.9 1.1 %copy-start = (f32[256,512]{1,0:T(8,128)S(1)}, f32[256,512]{1,0:T(8,128)}, u32[]{:S(2)}) copy-start(f32[256,512]{1,0:T(8,128)} %bed_ref.1) | copy-start | bytes 1572868
  69.0 1.2 %copy-start.2 = (f32[256,512]{1,0:T(8,128)S(1)}, f32[256,512]{1,0:T(8,128)}, u32[]{:S(2)}) copy-start(f32[256,512]{1,0:T(8,128)} %get-tuple-element.16) | copy-start | bytes 1572868
  70.3 1.1 %copy-start.3 = (f32[256,512]{1,0:T(8,128)S(1)}, f32[256,512]{1,0:T(8,128)}, u32[]{:S(2)}) copy-start(f32[256,512]{1,0:T(8,128)} %get-tuple-element.19) | copy-start | bytes 1572868

commit v11 on v9

--- a/solution.py
+++ b/solution.py
@@ -139,8 +139,10 @@
          jnp.zeros((devices, 128 - 2 * slot_cap), jnp.float32)],
         axis=1,
     )
-    outgoing = jnp.concatenate([payload.reshape(devices, 2 * slot_cap * 128), meta], axis=1)
-    arrived = lax.all_to_all(outgoing, ("row", "col"), split_axis=0, concat_axis=0, tiled=True)
+    outgoing = jnp.concatenate(
+        [payload.reshape(devices, 1, 2 * slot_cap * 128), meta.reshape(devices, 1, 128)], axis=2
+    )
+    arrived = lax.all_to_all(outgoing, ("row", "col"), split_axis=0, concat_axis=0, tiled=True)[:, 0, :]
     got = arrived[:, : 2 * slot_cap * 128].reshape(devices * slot_cap, 256)
     arrived_tags = arrived[:, 2 * slot_cap * 128 : 2 * slot_cap * 128 + slot_cap].reshape(devices * slot_cap)
     arrived_coef = arrived[:, 2 * slot_cap * 128 + slot_cap : 2 * slot_cap * 128 + 2 * slot_cap].reshape(

time: 93.2 us -> 94.1 us (level)
  other arithmetic: 5.76 us -> 7.81 us
  local copies, waits for them, and re-layouts: 10.4 us -> 9.3 us
    concatenate x0 -> x2, other arithmetic: none -> 2.06 us  [the longest x1 1.97 us: body(): jnp.concatenate([payload.reshape(devices, 1, 2 * slot_cap * 128), meta.re...]
    all_to_all x1 -> x0, local copies, waits for them, and re-layouts: 1.77 us -> none  [body(): lax.all_to_all(outgoing, ('row', 'col'), split_axis=0, concat_axis=0, til...]
  transfers between devices with their start and end apart: 6 -> 6, of which waited for: 2 -> 2; matrix products, arithmetic and copies ran while one was open for 6% -> 7% of each run, Pallas kernels for 0% -> 0%
where the time goes in v11:
time: 94.1 us; the launch traced here: 93.6 us
  waiting for transfers between devices  35.6 us (38%)
  starting transfers between devices  27.7 us (29%)
  local copies, waits for them, and re-layouts  9.3 us (10%)
  other arithmetic  7.81 us (8%)
  matrix products  7.36 us (8%)
  Pallas kernels  4.67 us (5%)
  between operations  1.23 us (1%)
    all_to_all x1, waiting for transfers between devices, body(): lax.all_to_all(outgoing, ('row', 'col'), split_axis=0, concat_axis=0, til...  19.8 us
    all_to_all x1, waiting for transfers between devices, body(): lax.all_to_all(reply.reshape(devices, slot_cap, 256), ('row', 'col'), spl...  15.8 us
    all_to_all x1, starting transfers between devices, body(): lax.all_to_all(outgoing, ('row', 'col'), split_axis=0, concat_axis=0, til...  10.8 us
    ppermute x2, starting transfers between devices, halo_pair(): lax.ppermute(last, axis, forward)  9.05 us
    pallas_call x1, Pallas kernels, body(): pl.pallas_call(stencil_kernel, out_shape=[tile, tile] + [block_rows] * 2,...  4.67 us
    all_to_all x1, starting transfers between devices, body(): lax.all_to_all(reply.reshape(devices, slot_cap, 256), ('row', 'col'), spl...  4.62 us
    dot_general x1, matrix products, body(): jnp.dot(slot_hot, jnp.concatenate([open_surf, open_mass], axis=1), precis...  3.28 us
    ppermute x2, starting transfers between devices, halo_pair(): lax.ppermute(first, axis, backward)  3.21 us
  transfers between devices with their start and end apart: 6, of which 2 were waited for; matrix products, arithmetic and copies ran while one was open for 7% of the time, Pallas kernels for 0%

profile of v11, /device:TPU:1, one launch (start us, length us, event | category | flops | bytes accessed | tf_op | source)
XLA Modules:
  0.0 93.6 jit_solution(9589629421381086631)
XLA Ops:
  0.6 0.0 copy-start
  0.6 0.0 copy-start.4
  0.7 1.2 %fusion.58 = (f32[256,512]{1,0:T(8,128)S(1)}, f32[1,256,512]{2,1,0:T(8,128)S(1)}) fusion(s32[256,512]{1,0:T(8,128)} %wet_ref.1), kind=kLoop, calls=%fused_computation.108 | loop fusion | flops 131072 | bytes 1572864 | tf_op jit(solution)/shard_map/convert_element_type | solution.py:97
  1.9 0.1 copy-done.4
  2.0 0.1 add_bitcast_fusion
  2.1 1.0 %copy-done.2 = f32[256,512]{1,0:T(8,128)S(1)} copy-done((f32[256,512]{1,0:T(8,128)S(1)}, f32[256,512]{1,0:T(8,128)}, u32[]{:S(2)}) %copy-start.2) | copy-done | bytes 524312
  3.0 0.2 copy-done.3
  3.2 0.5 maximum_reduce_fusion
  3.7 0.0 copy-start.10
  3.7 5.1 %collective-permute-start.2 = (f32[4,256]{1,0:T(4,128)S(1)}, f32[4,256]{1,0:T(4,128)S(1)}, u32[]{:S(2)}, u32[]{:S(2)}) collective-permute-start(f32[4,256]{1,0:T(4,128)S(1)} %get-tuple-element.12), channel_id=1, source_target_pairs={{0,1},{1,2},{2,3},{3,4},{4,5},{5,6},{6,7},{7,8},{8,9},{9,10},{10,1... | collective-permute-start | bytes 12296 | tf_op jit(solution)/shard_map/ppermute | solution.py:13
  8.8 1.9 %collective-permute-start.3 = (f32[4,256]{1,0:T(4,128)S(1)}, f32[4,256]{1,0:T(4,128)S(1)}, u32[]{:S(2)}, u32[]{:S(2)}) collective-permute-start(f32[4,256]{1,0:T(4,128)S(1)} %get-tuple-element.13), channel_id=1, source_target_pairs={{1,0},{2,1},{3,2},{4,3},{5,4},{6,5},{7,6},{8,7},{9,8},{10,9},{11,1... | collective-permute-start | bytes 12296 | tf_op jit(solution)/shard_map/ppermute | solution.py:13
  10.8 0.0 copy-start.14
  10.8 1.3 %collective-permute-start.1 = (f32[4,512]{1,0:T(4,128)S(1)}, f32[4,512]{1,0:T(4,128)S(1)}, u32[]{:S(2)}, u32[]{:S(2)}) collective-permute-start(f32[4,512]{1,0:T(4,128)S(1)} %bitcast.46), channel_id=1, source_target_pairs={{32,0},{64,32},{96,64},{33,1},{65,33},{97,65},{34,2},{66,34},{98,6... | collective-permute-start | bytes 24584 | tf_op jit(solution)/shard_map/ppermute | solution.py:13
  12.1 4.0 %collective-permute-start = (f32[4,512]{1,0:T(4,128)S(1)}, f32[4,512]{1,0:T(4,128)S(1)}, u32[]{:S(2)}, u32[]{:S(2)}) collective-permute-start(f32[4,512]{1,0:T(4,128)S(1)} %bitcast.47), channel_id=1, source_target_pairs={{0,32},{32,64},{64,96},{1,33},{33,65},{65,97},{2,34},{34,66},{66,9... | collective-permute-start | bytes 24584 | tf_op jit(solution)/shard_map/ppermute | solution.py:13
  16.1 0.1 copy.74
  16.2 0.2 fusion.23
  16.5 0.1 add_add_fusion
  16.6 0.2 fusion.22
  16.8 0.6 select_reduce_fusion
  17.5 0.1 reshape.94
  17.6 0.1 max.16
  17.7 0.1 pad.26.clone
  17.8 0.1 maximum_maximum_fusion
  17.9 0.4 select_reduce_fusion.1
  18.3 0.8 copy.73
  19.0 0.6 pad_maximum_fusion.9.rows_ref
  19.7 4.7 %shard_map.156 = (f32[256,512]{1,0:T(8,128)}, f32[256,512]{1,0:T(8,128)}, f32[1024,128]{1,0:T(8,128)}, f32[1024,128]{1,0:T(8,128)}) custom-call(f32[256,512]{1,0:T(8,128)} %depth_ref.1, f32[256,512]{1,0:T(8,128)} %bed_ref.1, f32[256,512]{1,0:T(8,128)} %mass_ref.1, f32[256,512]{1,0:T(8,128)} %cond_ref.1, f32[256,512]{1,0:T(8,128)} %settle_ref.1, ...), custom_call_target="tpu_custom_call" | custom-call | flops 7864320 | bytes 5242880 | tf_op jit(solution)/shard_map/pallas_call | solution.py:108
  24.3 3.3 %fusion.6 = f32[1024,256]{1,0:T(8,128)S(1)} fusion(s32[1024]{0:T(1024)S(1)} %select_reduce_fusion.1, f32[1024,128]{1,0:T(8,128)} %get-tuple-element.10, f32[1024,128]{1,0:T(8,128)} %get-tuple-element.9, f32[1024]{0:T(1024)S(1)} %broadcast_maximum_fusion), kind=kOutput, calls=%fused_computation.15 | convolution fusion | flops 3222798336 | bytes 2105344 | tf_op jit(solution)/shard_map/dot_general | solution.py:133
  27.6 1.1 %reshape.136 = f32[128,1,2048]{2,1,0:T(1,128)S(1)} reshape(f32[1024,256]{1,0:T(8,128)S(1)} %fusion.6) | data formatting | bytes 2097152 | tf_op jit(solution)/shard_map/reshape | solution.py:143
  28.7 2.0 %pad_maximum_fusion = f32[128,1,2176]{2,1,0:T(1,128)} fusion(f32[128,1,128]{2,1,0:T(1,128)S(1)} %bitcast.40, f32[128,1,2048]{2,1,0:T(1,128)S(1)} %reshape.136), kind=kLoop, calls=%fused_computation.17 | loop fusion | flops 278528 | bytes 2228224 | tf_op jit(solution)/shard_map/concatenate | solution.py:142
  30.6 10.8 %all-to-all-start = ((f32[128,1,2176]{2,1,0:T(1,128)}), f32[128,1,2176]{2,1,0:T(1,128)S(1)}, u32[]{:S(2)}, u32[]{:S(2)}) async-start(f32[128,1,2176]{2,1,0:T(1,128)} %pad_maximum_fusion), calls=%async_computation | async-start | bytes 2228224 | tf_op jit(solution)/shard_map/all_to_all | solution.py:145
  41.5 19.8 %all-to-all-done = f32[128,1,2176]{2,1,0:T(1,128)S(1)} async-done(((f32[128,1,2176]{2,1,0:T(1,128)}), f32[128,1,2176]{2,1,0:T(1,128)S(1)}, u32[]{:S(2)}, u32[]{:S(2)}) %all-to-all-start) | async-done | bytes 1114144 | tf_op jit(solution)/shard_map/all_to_all | solution.py:145
  61.3 0.1 copy.95
  61.4 0.1 fusion.57
  61.4 0.1 slice.136
  61.5 0.2 reshape.96
  61.7 0.1 broadcast_in_dim.74
  61.8 0.1 eq.126
  61.9 0.0 copy-start.11
  61.9 0.0 copy-start.12
  61.9 0.2 fusion.11
  62.1 0.6 fusion.2
  62.8 0.1 fusion.64
  62.9 0.1 fusion.63
  63.0 0.1 fusion.66
  63.0 0.1 fusion.65
  63.1 0.1 fusion.43
  63.2 0.1 fusion.46
  63.3 1.6 %convolution_bitcast_fusion = f32[128,8,256]{2,1,0:T(8,128)} fusion(f32[1024]{0:T(1024)S(1)} %eq.126, f32[16,128]{1,0:T(8,128)S(1)} %fusion.46, f32[16,128]{1,0:T(8,128)S(1)} %fusion.43), kind=kOutput, calls=%fused_computation.16 | convolution fusion | flops 50352128 | bytes 1069056 | tf_op jit(solution)/shard_map/dot_general | solution.py:168
  64.9 4.6 %all-to-all-start.1 = ((f32[128,8,256]{2,1,0:T(8,128)}), f32[128,8,256]{2,1,0:T(8,128)S(1)}, u32[]{:S(2)}, u32[]{:S(2)}) async-start(f32[128,8,256]{2,1,0:T(8,128)} %convolution_bitcast_fusion), calls=%async_computation.1 | async-start | bytes 2097152 | tf_op jit(solution)/shard_map/all_to_all | solution.py:171
  69.6 0.0 copy-start.1
  69.6 1.0 %gather_fusion = f32[512,128]{1,0:T(8,128)S(1)} fusion(f32[1024,128]{1,0:T(8,128)S(1)} %reshape.91, s32[1024]{0:T(1024)S(1)} %pad_clamp_fusion.1), kind=kCustom, calls=%fused_computation | custom fusion | bytes 526336 | tf_op jit(solution)/shard_map/gather | solution.py:181
  70.7 0.1 copy-done.5
  70.8 0.1 add.101
  70.9 1.0 %gather_fusion.2 = f32[512,128]{1,0:T(8,128)S(1)} fusion(f32[1024,128]{1,0:T(8,128)S(1)} %reshape.99, s32[1024]{0:T(1024)S(1)} %pad_clamp_fusion.1), kind=kCustom, calls=%fused_computation.2 | custom fusion | bytes 526336 | tf_op jit(solution)/shard_map/gather | solution.py:179
  72.0 1.0 %gather_fusion.3 = f32[512,128]{1,0:T(8,128)S(1)} fusion(f32[1024,128]{1,0:T(8,128)S(1)} %reshape.100, s32[1024]{0:T(1024)S(1)} %pad_clamp_fusion.1), kind=kCustom, calls=%fused_computation.3 | custom fusion | bytes 526336 | tf_op jit(solution)/shard_map/gather | solution.py:180
  73.0 15.8 %all-to-all-done.1 = f32[128,8,256]{2,1,0:T(8,128)S(1)} async-done(((f32[128,8,256]{2,1,0:T(8,128)}), f32[128,8,256]{2,1,0:T(8,128)S(1)}, u32[]{:S(2)}, u32[]{:S(2)}) %all-to-all-start.1) | async-done | bytes 1048608 | tf_op jit(solution)/shard_map/all_to_all | solution.py:171
  88.8 1.6 %gather_fusion.1 = f32[512,256]{1,0:T(8,128)S(1)} fusion(f32[1024,256]{1,0:T(8,128)S(1)} %bitcast.32, s32[1024]{0:T(1024)S(1)} %pad_clamp_fusion), kind=kCustom, calls=%fused_computation.1 | custom fusion | bytes 1050624 | tf_op jit(solution)/shard_map/gather | solution.py:178
  90.4 0.1 fusion.21
  90.6 0.5 fusion.16
  91.0 0.5 fusion.14
  91.5 0.5 fusion.12
  92.0 0.5 fusion.18
  92.5 1.1 %maximum_add_fusion = (f32[256,512]{1,0:T(8,128)}, f32[256,512]{1,0:T(8,128)}) fusion(f32[256,512]{1,0:T(8,128)S(1)} %copy-done.5, f32[256,128]{1,0:T(8,128)S(1)} %get-tuple-element.31, f32[256,128]{1,0:T(8,128)S(1)} %get-tuple-element.29, f32[256,128]{1,0:T(8,128)S(1)} %get-tuple-element.27, f32[256,128]{1,0:T(8,128)S(1)} %get-tuple-element.25, ...), kind=kLoop, calls=%fused_computation.29 | loop fusion | flops 1048576 | bytes 3145728 | tf_op jit(solution)/shard_map/add | solution.py:199
  (53 shorter events, 0.4 us)
Async XLA Ops:
  0.6 1.3 %copy-start = (f32[256,512]{1,0:T(8,128)S(1)}, f32[256,512]{1,0:T(8,128)}, u32[]{:S(2)}) copy-start(f32[256,512]{1,0:T(8,128)} %bed_ref.1) | copy-start | bytes 1572868
  0.6 1.4 %copy-start.4 = (f32[256,512]{1,0:T(8,128)S(1)}, f32[256,512]{1,0:T(8,128)}, u32[]{:S(2)}) copy-start(f32[256,512]{1,0:T(8,128)} %depth_ref.1) | copy-start | bytes 1572868
  2.0 1.0 %copy-start.2 = (f32[256,512]{1,0:T(8,128)S(1)}, f32[256,512]{1,0:T(8,128)}, u32[]{:S(2)}) copy-start(f32[256,512]{1,0:T(8,128)} %mass_ref.1) | copy-start | bytes 1572868
  2.0 1.2 %copy-start.3 = (f32[256,512]{1,0:T(8,128)S(1)}, f32[256,512]{1,0:T(8,128)}, u32[]{:S(2)}) copy-start(f32[256,512]{1,0:T(8,128)} %cond_ref.1) | copy-start | bytes 1572868
  3.7 12.4 %copy-start.15 = (s32[512]{0:T(512)S(1)}, s32[512]{0:T(512)}, u32[]{:S(2)}) copy-start(s32[512]{0:T(512)} %param.21) | copy-start | bytes 6148
  3.7 12.4 %copy-start.10 = (s32[512,1]{0,1:T(1,128)S(1)}, s32[512,1]{0,1:T(1,128)}, u32[]{:S(2)}) copy-start(s32[512,1]{0,1:T(1,128)} %param.20) | copy-start | bytes 6148
  3.7 14.5 %collective-permute-start.2 = (f32[4,256]{1,0:T(4,128)S(1)}, f32[4,256]{1,0:T(4,128)S(1)}, u32[]{:S(2)}, u32[]{:S(2)}) collective-permute-start(f32[4,256]{1,0:T(4,128)S(1)} %get-tuple-element.12), channel_id=1, source_target_pairs={{0,1},{1,2},{2,3},{3,4},{4,5},{5,6},{6,7},{7,8},{8,9},{9,10},{10,1... | collective-permute-start | bytes 12296 | tf_op jit(solution)/shard_map/ppermute | solution.py:13
  8.8 9.4 %collective-permute-start.3 = (f32[4,256]{1,0:T(4,128)S(1)}, f32[4,256]{1,0:T(4,128)S(1)}, u32[]{:S(2)}, u32[]{:S(2)}) collective-permute-start(f32[4,256]{1,0:T(4,128)S(1)} %get-tuple-element.13), channel_id=1, source_target_pairs={{1,0},{2,1},{3,2},{4,3},{5,4},{6,5},{7,6},{8,7},{9,8},{10,9},{11,1... | collective-permute-start | bytes 12296 | tf_op jit(solution)/shard_map/ppermute | solution.py:13
  10.8 6.1 %copy-start.14 = (f32[512]{0:T(512)S(1)}, f32[512]{0:T(512)}, u32[]{:S(2)}) copy-start(f32[512]{0:T(512)} %param.22) | copy-start | bytes 6148
  10.8 7.1 %copy-start.7 = (s32[512]{0:T(512)S(1)}, s32[512]{0:T(512)}, u32[]{:S(2)}) copy-start(s32[512]{0:T(512)} %param.19) | copy-start | bytes 6148
  10.8 8.3 %collective-permute-start.1 = (f32[4,512]{1,0:T(4,128)S(1)}, f32[4,512]{1,0:T(4,128)S(1)}, u32[]{:S(2)}, u32[]{:S(2)}) collective-permute-start(f32[4,512]{1,0:T(4,128)S(1)} %bitcast.46), channel_id=1, source_target_pairs={{32,0},{64,32},{96,64},{33,1},{65,33},{97,65},{34,2},{66,34},{98,6... | collective-permute-start | bytes 24584 | tf_op jit(solution)/shard_map/ppermute | solution.py:13
  12.1 6.9 %collective-permute-start = (f32[4,512]{1,0:T(4,128)S(1)}, f32[4,512]{1,0:T(4,128)S(1)}, u32[]{:S(2)}, u32[]{:S(2)}) collective-permute-start(f32[4,512]{1,0:T(4,128)S(1)} %bitcast.47), channel_id=1, source_target_pairs={{0,32},{32,64},{64,96},{1,33},{33,65},{65,97},{2,34},{34,66},{66,9... | collective-permute-start | bytes 24584 | tf_op jit(solution)/shard_map/ppermute | solution.py:13
  30.6 30.6 %all-to-all-start = ((f32[128,1,2176]{2,1,0:T(1,128)}), f32[128,1,2176]{2,1,0:T(1,128)S(1)}, u32[]{:S(2)}, u32[]{:S(2)}) async-start(f32[128,1,2176]{2,1,0:T(1,128)} %pad_maximum_fusion), calls=%async_computation | async-start | bytes 2228224 | tf_op jit(solution)/shard_map/all_to_all | solution.py:145
  61.9 0.9 copy-start.11
  61.9 0.9 copy-start.12
  61.9 0.9 copy-start.13
  63.2 1.7 %copy-start.8 = (f32[16,128]{1,0:T(8,128)}, f32[16,128]{1,0:T(8,128)S(1)}, u32[]{:S(2)}) copy-start(f32[16,128]{1,0:T(8,128)S(1)} %fusion.43) | copy-start | bytes 24580
  63.3 1.6 %copy-start.9 = (f32[16,128]{1,0:T(8,128)}, f32[16,128]{1,0:T(8,128)S(1)}, u32[]{:S(2)}) copy-start(f32[16,128]{1,0:T(8,128)S(1)} %fusion.46) | copy-start | bytes 24580
  64.9 23.9 %all-to-all-start.1 = ((f32[128,8,256]{2,1,0:T(8,128)}), f32[128,8,256]{2,1,0:T(8,128)S(1)}, u32[]{:S(2)}, u32[]{:S(2)}) async-start(f32[128,8,256]{2,1,0:T(8,128)} %convolution_bitcast_fusion), calls=%async_computation.1 | async-start | bytes 2097152 | tf_op jit(solution)/shard_map/all_to_all | solution.py:171
  69.6 1.1 %copy-start.1 = (f32[256,512]{1,0:T(8,128)S(1)}, f32[256,512]{1,0:T(8,128)}, u32[]{:S(2)}) copy-start(f32[256,512]{1,0:T(8,128)} %bed_ref.1) | copy-start | bytes 1572868
  69.6 1.2 %copy-start.5 = (f32[256,512]{1,0:T(8,128)S(1)}, f32[256,512]{1,0:T(8,128)}, u32[]{:S(2)}) copy-start(f32[256,512]{1,0:T(8,128)} %get-tuple-element.8) | copy-start | bytes 1572868
  70.9 1.1 %copy-start.6 = (f32[256,512]{1,0:T(8,128)S(1)}, f32[256,512]{1,0:T(8,128)}, u32[]{:S(2)}) copy-start(f32[256,512]{1,0:T(8,128)} %get-tuple-element.11) | copy-start | bytes 1572868

commit v12 on v9

--- a/solution.py
+++ b/solution.py
@@ -186,16 +186,11 @@
     )
     per_row = tile_x // 128
     row_ids = jnp.arange(tile_y, dtype=jnp.int32)[:, None]
-    gained = [
-        jnp.dot(
-            (row_ids * per_row + j == link_block[None, :]).astype(jnp.float32),
-            applied,
-            precision=lax.Precision.HIGHEST,
-        )
-        for j in range(per_row)
-    ]
-    depth_out = depth1 + jnp.concatenate([g[:, :128] for g in gained], axis=1)
-    mass_out = mass1 + jnp.concatenate([g[:, 128:] for g in gained], axis=1)
+    column_ids = jnp.arange(per_row, dtype=jnp.int32)[:, None, None]
+    block_hot = (row_ids[None] * per_row + column_ids == link_block[None, None, :]).astype(jnp.float32)
+    gained = jnp.einsum("jyl,lc->jyc", block_hot, applied, precision=lax.Precision.HIGHEST)
+    depth_out = depth1 + jnp.concatenate([gained[j, :, :128] for j in range(per_row)], axis=1)
+    mass_out = mass1 + jnp.concatenate([gained[j, :, 128:] for j in range(per_row)], axis=1)
     return (depth_out, mass_out, phase_out, conc_out)
 
 

time: 93.2 us -> 92.3 us (level)
  blocking collectives: 0 us -> 30.9 us
  waiting for transfers between devices: 35.6 us -> 15.4 us
  starting transfers between devices: 27.7 us -> 17.4 us
    all_to_all x0 -> x1, blocking collectives: none -> 30.9 us  [body(): lax.all_to_all(outgoing, ('row', 'col'), split_axis=0, concat_axis=0, til...]
    all_to_all x1 -> x0, waiting for transfers between devices: 19.8 us -> none  [body(): lax.all_to_all(outgoing, ('row', 'col'), split_axis=0, concat_axis=0, til...]
    all_to_all x1 -> x0, starting transfers between devices: 10.8 us -> none  [body(): lax.all_to_all(outgoing, ('row', 'col'), split_axis=0, concat_axis=0, til...]
    ppermute x2, starting transfers between devices: 3.21 us -> 4.64 us  [halo_pair(): lax.ppermute(first, axis, backward)]
    all_to_all x1, local copies, waits for them, and re-layouts: 1.77 us -> 0.77 us  [body(): lax.all_to_all(outgoing, ('row', 'col'), split_axis=0, concat_axis=0, til...]
  transfers between devices with their start and end apart: 6 -> 5, of which waited for: 2 -> 1; matrix products, arithmetic and copies ran while one was open for 6% -> 7% of each run, Pallas kernels for 0% -> 0%
where the time goes in v12:
time: 92.3 us; the launch traced here: 91.9 us
  blocking collectives  30.9 us (33%)
  starting transfers between devices  17.4 us (19%)
  waiting for transfers between devices  15.4 us (17%)
  local copies, waits for them, and re-layouts  10 us (11%)
  matrix products  6.6 us (7%)
  other arithmetic  5.75 us (6%)
  Pallas kernels  4.65 us (5%)
  between operations  1.23 us (1%)
    all_to_all x1, blocking collectives, body(): lax.all_to_all(outgoing, ('row', 'col'), split_axis=0, concat_axis=0, til...  30.9 us
    all_to_all x1, waiting for transfers between devices, body(): lax.all_to_all(reply.reshape(devices, slot_cap, 256), ('row', 'col'), spl...  15.4 us
    ppermute x2, starting transfers between devices, halo_pair(): lax.ppermute(last, axis, forward)  8.18 us
    pallas_call x1, Pallas kernels, body(): pl.pallas_call(stencil_kernel, out_shape=[tile, tile] + [block_rows] * 2,...  4.65 us
    ppermute x2, starting transfers between devices, halo_pair(): lax.ppermute(first, axis, backward)  4.64 us
    all_to_all x1, starting transfers between devices, body(): lax.all_to_all(reply.reshape(devices, slot_cap, 256), ('row', 'col'), spl...  4.62 us
    dot_general x1, matrix products, body(): jnp.dot(slot_hot, jnp.concatenate([open_surf, open_mass], axis=1), precis...  3.28 us
  transfers between devices with their start and end apart: 5, of which 1 were waited for; matrix products, arithmetic and copies ran while one was open for 7% of the time, Pallas kernels for 0%

profile of v12, /device:TPU:1, one launch (start us, length us, event | category | flops | bytes accessed | tf_op | source)
XLA Modules:
  0.0 91.9 jit_solution(14583268652523521769)
XLA Ops:
  0.6 0.0 copy-start.4
  0.6 0.0 copy-start
  0.7 1.2 %fusion.41 = (f32[256,512]{1,0:T(8,128)S(1)}, f32[1,256,512]{2,1,0:T(8,128)S(1)}) fusion(s32[256,512]{1,0:T(8,128)} %wet_ref.1), kind=kLoop, calls=%fused_computation.98 | loop fusion | flops 131072 | bytes 1572864 | tf_op jit(solution)/shard_map/convert_element_type | solution.py:97
  1.9 0.1 copy-done
  2.0 0.1 add_bitcast_fusion
  2.1 1.0 %copy-done.2 = f32[256,512]{1,0:T(8,128)S(1)} copy-done((f32[256,512]{1,0:T(8,128)S(1)}, f32[256,512]{1,0:T(8,128)}, u32[]{:S(2)}) %copy-start.2) | copy-done | bytes 524312
  3.0 0.2 copy-done.3
  3.2 0.0 copy-start.9
  3.2 1.3 %collective-permute-start.1 = (f32[4,512]{1,0:T(4,128)S(1)}, f32[4,512]{1,0:T(4,128)S(1)}, u32[]{:S(2)}, u32[]{:S(2)}) collective-permute-start(f32[4,512]{1,0:T(4,128)S(1)} %bitcast.63), channel_id=1, source_target_pairs={{32,0},{64,32},{96,64},{33,1},{65,33},{97,65},{34,2},{66,34},{98,6... | collective-permute-start | bytes 24584 | tf_op jit(solution)/shard_map/ppermute | solution.py:13
  4.5 4.7 %collective-permute-start = (f32[4,512]{1,0:T(4,128)S(1)}, f32[4,512]{1,0:T(4,128)S(1)}, u32[]{:S(2)}, u32[]{:S(2)}) collective-permute-start(f32[4,512]{1,0:T(4,128)S(1)} %bitcast.64), channel_id=1, source_target_pairs={{0,32},{32,64},{64,96},{1,33},{33,65},{65,97},{2,34},{34,66},{66,9... | collective-permute-start | bytes 24584 | tf_op jit(solution)/shard_map/ppermute | solution.py:13
  9.2 0.5 maximum_reduce_fusion
  9.7 0.0 copy-start.14
  9.8 0.0 copy-start.10
  9.8 3.3 %collective-permute-start.3 = (f32[4,256]{1,0:T(4,128)S(1)}, f32[4,256]{1,0:T(4,128)S(1)}, u32[]{:S(2)}, u32[]{:S(2)}) collective-permute-start(f32[4,256]{1,0:T(4,128)S(1)} %get-tuple-element.13), channel_id=1, source_target_pairs={{1,0},{2,1},{3,2},{4,3},{5,4},{6,5},{7,6},{8,7},{9,8},{10,9},{11,1... | collective-permute-start | bytes 12296 | tf_op jit(solution)/shard_map/ppermute | solution.py:13
  13.1 3.5 %collective-permute-start.2 = (f32[4,256]{1,0:T(4,128)S(1)}, f32[4,256]{1,0:T(4,128)S(1)}, u32[]{:S(2)}, u32[]{:S(2)}) collective-permute-start(f32[4,256]{1,0:T(4,128)S(1)} %get-tuple-element.12), channel_id=1, source_target_pairs={{0,1},{1,2},{2,3},{3,4},{4,5},{5,6},{6,7},{7,8},{8,9},{9,10},{10,1... | collective-permute-start | bytes 12296 | tf_op jit(solution)/shard_map/ppermute | solution.py:13
  16.7 0.1 copy.93
  16.8 0.2 fusion.19
  17.0 0.1 add_add_fusion
  17.1 0.2 fusion.18
  17.4 0.6 select_reduce_fusion
  18.1 0.4 select_reduce_fusion.1
  18.4 0.1 reshape.108
  18.5 0.1 max.16
  18.6 0.8 copy.91
  19.4 0.6 pad_maximum_fusion.3.rows_ref
  20.0 4.7 %shard_map.156 = (f32[256,512]{1,0:T(8,128)}, f32[256,512]{1,0:T(8,128)}, f32[1024,128]{1,0:T(8,128)}, f32[1024,128]{1,0:T(8,128)}) custom-call(f32[256,512]{1,0:T(8,128)} %depth_ref.1, f32[256,512]{1,0:T(8,128)} %bed_ref.1, f32[256,512]{1,0:T(8,128)} %mass_ref.1, f32[256,512]{1,0:T(8,128)} %cond_ref.1, f32[256,512]{1,0:T(8,128)} %settle_ref.1, ...), custom_call_target="tpu_custom_call" | custom-call | flops 7864320 | bytes 5242880 | tf_op jit(solution)/shard_map/pallas_call | solution.py:108
  24.7 3.3 %fusion.8 = f32[1024,256]{1,0:T(8,128)S(1)} fusion(s32[1024]{0:T(1024)S(1)} %select_reduce_fusion.1, f32[1024,128]{1,0:T(8,128)} %get-tuple-element.10, f32[1024,128]{1,0:T(8,128)} %get-tuple-element.9, f32[1024]{0:T(1024)S(1)} %broadcast_maximum_fusion), kind=kOutput, calls=%fused_computation.17 | convolution fusion | flops 3222798336 | bytes 2105344 | tf_op jit(solution)/shard_map/dot_general | solution.py:133
  28.0 0.2 reshape.107
  28.2 0.3 concatenate.43
  28.5 0.8 all_to_all.11
  29.2 30.9 %all_to_all.17 = f32[128,1,2176]{2,1,0:T(1,128)S(1)} all-to-all(f32[128,1,2176]{2,1,0:T(1,128)S(1)} %all_to_all.11), channel_id=1, replica_groups=mesh['row'=4,'col'=32] {'row','col'}, dimensions={0} | all-to-all | bytes 2228224 | tf_op jit(solution)/shard_map/all_to_all | solution.py:143
  60.1 0.1 copy.116
  60.2 0.1 fusion.39
  60.3 0.1 slice.136
  60.4 0.1 eq.93
  60.5 0.2 reshape.109
  60.6 0.1 broadcast_in_dim.71
  60.7 0.0 copy-start.12
  60.7 0.0 copy-start.13
  60.7 0.2 fusion.17
  61.0 0.6 fusion.4
  61.6 0.1 fusion.44
  61.7 0.1 fusion.45
  61.8 0.1 fusion.42
  61.8 0.1 fusion.43
  61.9 0.1 fusion.34
  62.0 0.1 fusion.31
  62.1 1.6 %convolution_bitcast_fusion = f32[128,8,256]{2,1,0:T(8,128)} fusion(f32[1024]{0:T(1024)S(1)} %eq.93, f32[16,128]{1,0:T(8,128)S(1)} %fusion.34, f32[16,128]{1,0:T(8,128)S(1)} %fusion.31), kind=kOutput, calls=%fused_computation.18 | convolution fusion | flops 50352128 | bytes 1069056 | tf_op jit(solution)/shard_map/dot_general | solution.py:166
  63.7 4.6 %all-to-all-start.1 = ((f32[128,8,256]{2,1,0:T(8,128)}), f32[128,8,256]{2,1,0:T(8,128)S(1)}, u32[]{:S(2)}, u32[]{:S(2)}) async-start(f32[128,8,256]{2,1,0:T(8,128)} %convolution_bitcast_fusion), calls=%async_computation.1 | async-start | bytes 2097152 | tf_op jit(solution)/shard_map/all_to_all | solution.py:169
  68.4 1.0 %gather_fusion = f32[512,128]{1,0:T(8,128)S(1)} fusion(f32[1024,128]{1,0:T(8,128)S(1)} %reshape.105, s32[1024]{0:T(1024)S(1)} %pad_clamp_fusion.1), kind=kCustom, calls=%fused_computation | custom fusion | bytes 526336 | tf_op jit(solution)/shard_map/gather | solution.py:179
  69.5 0.1 copy.92
  69.7 0.1 add.89
  69.8 1.0 %gather_fusion.2 = f32[512,128]{1,0:T(8,128)S(1)} fusion(f32[1024,128]{1,0:T(8,128)S(1)} %reshape.112, s32[1024]{0:T(1024)S(1)} %pad_clamp_fusion.1), kind=kCustom, calls=%fused_computation.2 | custom fusion | bytes 526336 | tf_op jit(solution)/shard_map/gather | solution.py:177
  70.9 0.1 copy.96
  71.1 1.0 %gather_fusion.3 = f32[512,128]{1,0:T(8,128)S(1)} fusion(f32[1024,128]{1,0:T(8,128)S(1)} %reshape.113, s32[1024]{0:T(1024)S(1)} %pad_clamp_fusion.1), kind=kCustom, calls=%fused_computation.3 | custom fusion | bytes 526336 | tf_op jit(solution)/shard_map/gather | solution.py:178
  72.1 0.1 copy.98
  72.2 15.4 %all-to-all-done.1 = f32[128,8,256]{2,1,0:T(8,128)S(1)} async-done(((f32[128,8,256]{2,1,0:T(8,128)}), f32[128,8,256]{2,1,0:T(8,128)S(1)}, u32[]{:S(2)}, u32[]{:S(2)}) %all-to-all-start.1) | async-done | bytes 1048608 | tf_op jit(solution)/shard_map/all_to_all | solution.py:169
  87.6 1.6 %gather_fusion.1 = f32[512,256]{1,0:T(8,128)S(1)} fusion(f32[1024,256]{1,0:T(8,128)S(1)} %bitcast.50, s32[1024]{0:T(1024)S(1)} %pad_clamp_fusion), kind=kCustom, calls=%fused_computation.1 | custom fusion | bytes 1050624 | tf_op jit(solution)/shard_map/gather | solution.py:176
  89.2 0.1 copy.111
  89.4 0.1 copy.112
  89.5 0.1 subtract_multiply_fusion.1
  89.7 1.1 %fusion.2 = f32[4,256,256]{2,1,0:T(8,128)S(1)} fusion(s32[512]{0:T(512)S(1)} %copy-done.10, s32[4,256]{1,0:T(4,128)S(1)} %iota_add_fusion, f32[512,128]{0,1:T(8,128)S(1)} %get-tuple-element.33, f32[512,128]{0,1:T(8,128)S(1)} %get-tuple-element.32), kind=kOutput, calls=%fused_computation.11 | convolution fusion | flops 1611268096 | bytes 1579008 | tf_op jit(solution)/shard_map/jyl,lc->jyc/dot_general | solution.py:191
  90.8 0.1 slice_bitcast_fusion.3
  90.8 1.1 %maximum_add_fusion = (f32[256,512]{1,0:T(8,128)}, f32[256,512]{1,0:T(8,128)}) fusion(f32[256,512]{1,0:T(8,128)S(1)} %copy-done.5, f32[256,128]{1,0:T(8,128)S(1)} %get-tuple-element.23, f32[256,128]{1,0:T(8,128)S(1)} %get-tuple-element.24, f32[256,128]{1,0:T(8,128)S(1)} %get-tuple-element.25, f32[256,128]{1,0:T(8,128)S(1)} %get-tuple-element.26, ...), kind=kLoop, calls=%fused_computation.34 | loop fusion | flops 1048576 | bytes 3145728 | tf_op jit(solution)/shard_map/add | solution.py:192
  (49 shorter events, 0.4 us)
Async XLA Ops:
  0.6 1.3 %copy-start.4 = (f32[256,512]{1,0:T(8,128)S(1)}, f32[256,512]{1,0:T(8,128)}, u32[]{:S(2)}) copy-start(f32[256,512]{1,0:T(8,128)} %depth_ref.1) | copy-start | bytes 1572868
  0.6 1.4 %copy-start = (f32[256,512]{1,0:T(8,128)S(1)}, f32[256,512]{1,0:T(8,128)}, u32[]{:S(2)}) copy-start(f32[256,512]{1,0:T(8,128)} %bed_ref.1) | copy-start | bytes 1572868
  2.0 1.0 %copy-start.2 = (f32[256,512]{1,0:T(8,128)S(1)}, f32[256,512]{1,0:T(8,128)}, u32[]{:S(2)}) copy-start(f32[256,512]{1,0:T(8,128)} %mass_ref.1) | copy-start | bytes 1572868
  2.0 1.2 %copy-start.3 = (f32[256,512]{1,0:T(8,128)S(1)}, f32[256,512]{1,0:T(8,128)}, u32[]{:S(2)}) copy-start(f32[256,512]{1,0:T(8,128)} %cond_ref.1) | copy-start | bytes 1572868
  3.2 13.4 %copy-start.9 = (s32[512,1]{0,1:T(1,128)S(1)}, s32[512,1]{0,1:T(1,128)}, u32[]{:S(2)}) copy-start(s32[512,1]{0,1:T(1,128)} %param.20) | copy-start | bytes 6148
  3.2 16.2 %collective-permute-start.1 = (f32[4,512]{1,0:T(4,128)S(1)}, f32[4,512]{1,0:T(4,128)S(1)}, u32[]{:S(2)}, u32[]{:S(2)}) collective-permute-start(f32[4,512]{1,0:T(4,128)S(1)} %bitcast.63), channel_id=1, source_target_pairs={{32,0},{64,32},{96,64},{33,1},{65,33},{97,65},{34,2},{66,34},{98,6... | collective-permute-start | bytes 24584 | tf_op jit(solution)/shard_map/ppermute | solution.py:13
  4.5 14.9 %collective-permute-start = (f32[4,512]{1,0:T(4,128)S(1)}, f32[4,512]{1,0:T(4,128)S(1)}, u32[]{:S(2)}, u32[]{:S(2)}) collective-permute-start(f32[4,512]{1,0:T(4,128)S(1)} %bitcast.64), channel_id=1, source_target_pairs={{0,32},{32,64},{64,96},{1,33},{33,65},{65,97},{2,34},{34,66},{66,9... | collective-permute-start | bytes 24584 | tf_op jit(solution)/shard_map/ppermute | solution.py:13
  9.7 7.6 %copy-start.15 = (s32[512]{0:T(512)S(1)}, s32[512]{0:T(512)}, u32[]{:S(2)}) copy-start(s32[512]{0:T(512)} %param.21) | copy-start | bytes 6148
  9.7 7.7 %copy-start.14 = (f32[512]{0:T(512)S(1)}, f32[512]{0:T(512)}, u32[]{:S(2)}) copy-start(f32[512]{0:T(512)} %param.22) | copy-start | bytes 6148
  9.8 8.3 %copy-start.10 = (s32[512]{0:T(512)S(1)}, s32[512]{0:T(512)}, u32[]{:S(2)}) copy-start(s32[512]{0:T(512)} %param.19) | copy-start | bytes 6148
  9.8 8.8 %collective-permute-start.3 = (f32[4,256]{1,0:T(4,128)S(1)}, f32[4,256]{1,0:T(4,128)S(1)}, u32[]{:S(2)}, u32[]{:S(2)}) collective-permute-start(f32[4,256]{1,0:T(4,128)S(1)} %get-tuple-element.13), channel_id=1, source_target_pairs={{1,0},{2,1},{3,2},{4,3},{5,4},{6,5},{7,6},{8,7},{9,8},{10,9},{11,1... | collective-permute-start | bytes 12296 | tf_op jit(solution)/shard_map/ppermute | solution.py:13
  13.1 5.5 %collective-permute-start.2 = (f32[4,256]{1,0:T(4,128)S(1)}, f32[4,256]{1,0:T(4,128)S(1)}, u32[]{:S(2)}, u32[]{:S(2)}) collective-permute-start(f32[4,256]{1,0:T(4,128)S(1)} %get-tuple-element.12), channel_id=1, source_target_pairs={{0,1},{1,2},{2,3},{3,4},{4,5},{5,6},{6,7},{7,8},{8,9},{9,10},{10,1... | collective-permute-start | bytes 12296 | tf_op jit(solution)/shard_map/ppermute | solution.py:13
  60.7 0.9 copy-start.11
  60.7 0.9 copy-start.12
  60.7 0.9 copy-start.13
  62.0 1.7 %copy-start.7 = (f32[16,128]{1,0:T(8,128)}, f32[16,128]{1,0:T(8,128)S(1)}, u32[]{:S(2)}) copy-start(f32[16,128]{1,0:T(8,128)S(1)} %fusion.34) | copy-start | bytes 24580
  62.1 1.6 %copy-start.8 = (f32[16,128]{1,0:T(8,128)}, f32[16,128]{1,0:T(8,128)S(1)}, u32[]{:S(2)}) copy-start(f32[16,128]{1,0:T(8,128)S(1)} %fusion.31) | copy-start | bytes 24580
  63.7 23.9 %all-to-all-start.1 = ((f32[128,8,256]{2,1,0:T(8,128)}), f32[128,8,256]{2,1,0:T(8,128)S(1)}, u32[]{:S(2)}, u32[]{:S(2)}) async-start(f32[128,8,256]{2,1,0:T(8,128)} %convolution_bitcast_fusion), calls=%async_computation.1 | async-start | bytes 2097152 | tf_op jit(solution)/shard_map/all_to_all | solution.py:169
  68.4 1.3 %copy-start.1 = (f32[256,512]{1,0:T(8,128)S(1)}, f32[256,512]{1,0:T(8,128)}, u32[]{:S(2)}) copy-start(f32[256,512]{1,0:T(8,128)} %bed_ref.1) | copy-start | bytes 1572868
  68.4 1.3 %copy-start.5 = (f32[256,512]{1,0:T(8,128)S(1)}, f32[256,512]{1,0:T(8,128)}, u32[]{:S(2)}) copy-start(f32[256,512]{1,0:T(8,128)} %get-tuple-element.8) | copy-start | bytes 1572868
  69.8 1.2 %copy-start.6 = (f32[256,512]{1,0:T(8,128)S(1)}, f32[256,512]{1,0:T(8,128)}, u32[]{:S(2)}) copy-start(f32[256,512]{1,0:T(8,128)} %get-tuple-element.11) | copy-start | bytes 1572868

commit v13 on v12

--- a/solution.py
+++ b/solution.py
@@ -70,6 +70,31 @@
         open_j = opened[:, lanes]
         open_surf_ref[rows_j, :] = open_j * surface1[:, lanes]
         open_mass_ref[rows_j, :] = open_j * mass1[:, lanes]
+
+
+def owner_kernel(ws_ref, wm_ref, w_ref, hot_ref, hot_t_ref, phase_ref, conc_ref, area_ref,
+                 phase_out_ref, conc_out_ref, reply_ref):
+    gathered = jnp.concatenate([ws_ref[...], wm_ref[...], w_ref[...]], axis=1)
+    totals = jnp.dot(hot_ref[...], gathered, precision=lax.Precision.HIGHEST,
+                     preferred_element_type=jnp.float32)
+    sections = phase_ref.shape[1]
+    inflow = totals[:, :sections]
+    sediment = totals[:, sections : 2 * sections]
+    wet_sum = totals[:, 2 * sections :]
+    area = area_ref[...]
+    lane = lax.broadcasted_iota(jnp.int32, area.shape, 1)
+
+    def smooth(values):
+        left = jnp.where(lane == 0, values, pltpu.roll(values, 1, 1))
+        right = jnp.where(lane == sections - 1, values, pltpu.roll(values, sections - 1, 1))
+        return values + 0.25 * (left - 2.0 * values + right)
+
+    phase_out = smooth((area * phase_ref[...] + inflow) / (area + wet_sum))
+    conc_out = smooth((area * conc_ref[...] + sediment) / (area + wet_sum))
+    phase_out_ref[...] = phase_out
+    conc_out_ref[...] = conc_out
+    reply_ref[...] = jnp.dot(hot_t_ref[...], jnp.concatenate([phase_out, conc_out], axis=1),
+                             precision=lax.Precision.HIGHEST, preferred_element_type=jnp.float32)
 
 
 def smooth_reach(values):
@@ -150,22 +175,16 @@
     got_wm = got[:, 128:]
     got_w = jnp.where(got_wm > 0.0, arrived_coef[:, None], 0.0)
     reach_dev = chan_phase.shape[0]
-    reach_hot = (arrived_tags[None, :] == jnp.arange(reach_dev, dtype=jnp.float32)[:, None]).astype(
-        jnp.float32
-    )
-    totals = jnp.dot(
-        reach_hot, jnp.concatenate([got_ws, got_wm, got_w], axis=1), precision=lax.Precision.HIGHEST
-    )
-    inflow = totals[:, :128]
-    sediment = totals[:, 128:256]
-    wet_sum = totals[:, 256:]
-    phase_new = (chan_area * chan_phase + inflow) / (chan_area + wet_sum)
-    conc_new = (chan_area * chan_conc + sediment) / (chan_area + wet_sum)
-    phase_out = smooth_reach(phase_new)
-    conc_out = smooth_reach(conc_new)
-    reply = jnp.dot(
-        reach_hot.T, jnp.concatenate([phase_out, conc_out], axis=1), precision=lax.Precision.HIGHEST
-    )
+    reach_ids = jnp.arange(reach_dev, dtype=jnp.float32)
+    reach_hot = (arrived_tags[None, :] == reach_ids[:, None]).astype(jnp.float32)
+    reach_hot_t = (arrived_tags[:, None] == reach_ids[None, :]).astype(jnp.float32)
+    reach_rows = jax.ShapeDtypeStruct(chan_phase.shape, jnp.float32)
+    phase_out, conc_out, reply = pl.pallas_call(
+        owner_kernel,
+        out_shape=[reach_rows, reach_rows, jax.ShapeDtypeStruct((devices * slot_cap, 256), jnp.float32)],
+        in_specs=[vmem] * 8,
+        out_specs=[vmem] * 3,
+    )(got_ws, got_wm, got_w, reach_hot, reach_hot_t, chan_phase, chan_conc, chan_area)
     answered = lax.all_to_all(
         reply.reshape(devices, slot_cap, 256),
         ("row", "col"),

time: 92.3 us -> 96.1 us (1.041)
  Pallas kernels: 4.65 us -> 9.42 us
  other arithmetic: 5.75 us -> 8.38 us
  matrix products: 6.6 us -> 4.36 us
    pallas_call x0 -> x1, Pallas kernels: none -> 4.73 us  [body(): pl.pallas_call(owner_kernel, out_shape=[reach_rows, reach_rows, jax.Shape...]
    dot_general x2 -> x0, matrix products: 2.24 us -> none  [the longest x1 1.61 us: body(): jnp.dot(reach_hot.T, jnp.concatenate([phase_out, conc_out], axis=1), prec...]
    convert_element_type x0 -> x2, other arithmetic: none -> 1.63 us  [the longest x1 1 us: body(): (arrived_tags[:, None] == reach_ids[None, :]).astype(jnp.float32)]
    ppermute x2, starting transfers between devices: 4.64 us -> 3.21 us  [halo_pair(): lax.ppermute(first, axis, backward)]
    select_n x1, other arithmetic: 0.2 us -> 1.35 us  [body(): got_w = jnp.where(got_wm > 0.0, arrived_coef[:, None], 0.0)]
where the time goes in v13:
time: 96.1 us; the launch traced here: 95.7 us
  blocking collectives  30.4 us (32%)
  starting transfers between devices  16.9 us (18%)
  waiting for transfers between devices  15.4 us (16%)
  local copies, waits for them, and re-layouts  9.67 us (10%)
  Pallas kernels  9.42 us (10%)
  other arithmetic  8.38 us (9%)
  matrix products  4.36 us (5%)
  between operations  1.16 us (1%)
    all_to_all x1, blocking collectives, body(): lax.all_to_all(outgoing, ('row', 'col'), split_axis=0, concat_axis=0, til...  30.4 us
    all_to_all x1, waiting for transfers between devices, body(): lax.all_to_all(reply.reshape(devices, slot_cap, 256), ('row', 'col'), spl...  15.4 us
    ppermute x2, starting transfers between devices, halo_pair(): lax.ppermute(last, axis, forward)  9.05 us
    pallas_call x1, Pallas kernels, body(): pl.pallas_call(owner_kernel, out_shape=[reach_rows, reach_rows, jax.Shape...  4.73 us
    pallas_call x1, Pallas kernels, body(): pl.pallas_call(stencil_kernel, out_shape=[tile, tile] + [block_rows] * 2,...  4.69 us
    all_to_all x1, starting transfers between devices, body(): lax.all_to_all(reply.reshape(devices, slot_cap, 256), ('row', 'col'), spl...  4.63 us
    dot_general x1, matrix products, body(): jnp.dot(slot_hot, jnp.concatenate([open_surf, open_mass], axis=1), precis...  3.28 us
    ppermute x2, starting transfers between devices, halo_pair(): lax.ppermute(first, axis, backward)  3.21 us
  transfers between devices with their start and end apart: 5, of which 1 were waited for; matrix products, arithmetic and copies ran while one was open for 7% of the time, Pallas kernels for 0%

profile of v13, /device:TPU:1, one launch (start us, length us, event | category | flops | bytes accessed | tf_op | source)
XLA Modules:
  0.0 95.7 jit_solution(250279496678343215)
XLA Ops:
  0.6 0.0 copy-start
  0.6 0.0 copy-start.4
  0.7 1.3 %fusion.23 = (f32[256,512]{1,0:T(8,128)S(1)}, f32[1,256,512]{2,1,0:T(8,128)S(1)}) fusion(s32[256,512]{1,0:T(8,128)} %wet_ref.1), kind=kLoop, calls=%fused_computation.75 | loop fusion | flops 131072 | bytes 1572864 | tf_op jit(solution)/shard_map/convert_element_type | solution.py:122
  1.9 0.1 copy-done.4
  2.0 0.1 add_bitcast_fusion
  2.1 1.0 copy-done.2
  3.0 0.2 copy-done.3
  3.2 0.5 maximum_reduce_fusion
  3.7 0.0 copy-start.7
  3.7 5.1 %collective-permute-start.2 = (f32[4,256]{1,0:T(4,128)S(1)}, f32[4,256]{1,0:T(4,128)S(1)}, u32[]{:S(2)}, u32[]{:S(2)}) collective-permute-start(f32[4,256]{1,0:T(4,128)S(1)} %get-tuple-element.18), channel_id=1, source_target_pairs={{0,1},{1,2},{2,3},{3,4},{4,5},{5,6},{6,7},{7,8},{8,9},{9,10},{10,1... | collective-permute-start | bytes 12296 | tf_op jit(solution)/shard_map/ppermute | solution.py:13
  8.8 1.9 %collective-permute-start.3 = (f32[4,256]{1,0:T(4,128)S(1)}, f32[4,256]{1,0:T(4,128)S(1)}, u32[]{:S(2)}, u32[]{:S(2)}) collective-permute-start(f32[4,256]{1,0:T(4,128)S(1)} %get-tuple-element.19), channel_id=1, source_target_pairs={{1,0},{2,1},{3,2},{4,3},{5,4},{6,5},{7,6},{8,7},{9,8},{10,9},{11,1... | collective-permute-start | bytes 12296 | tf_op jit(solution)/shard_map/ppermute | solution.py:13
  10.8 0.0 copy-start.9
  10.8 0.0 copy-start.8
  10.8 1.3 %collective-permute-start.1 = (f32[4,512]{1,0:T(4,128)S(1)}, f32[4,512]{1,0:T(4,128)S(1)}, u32[]{:S(2)}, u32[]{:S(2)}) collective-permute-start(f32[4,512]{1,0:T(4,128)S(1)} %bitcast.63), channel_id=1, source_target_pairs={{32,0},{64,32},{96,64},{33,1},{65,33},{97,65},{34,2},{66,34},{98,6... | collective-permute-start | bytes 24584 | tf_op jit(solution)/shard_map/ppermute | solution.py:13
  12.1 4.0 %collective-permute-start = (f32[4,512]{1,0:T(4,128)S(1)}, f32[4,512]{1,0:T(4,128)S(1)}, u32[]{:S(2)}, u32[]{:S(2)}) collective-permute-start(f32[4,512]{1,0:T(4,128)S(1)} %bitcast.64), channel_id=1, source_target_pairs={{0,32},{32,64},{64,96},{1,33},{33,65},{65,97},{2,34},{34,66},{66,9... | collective-permute-start | bytes 24584 | tf_op jit(solution)/shard_map/ppermute | solution.py:13
  16.1 0.1 copy.93
  16.2 0.2 fusion.15
  16.5 0.1 add_add_fusion
  16.6 0.2 fusion.14
  16.8 0.6 select_reduce_fusion
  17.5 0.4 select_reduce_fusion.1
  17.9 0.1 reshape.109
  18.0 0.1 max.16
  18.0 0.0 collective-permute-done.2
  18.1 0.0 collective-permute-done.3
  18.1 0.8 copy.91
  18.9 0.0 collective-permute-done.1
  18.9 0.0 collective-permute-done
  18.9 0.6 pad_maximum_fusion.3.rows_ref
  19.5 4.7 %shard_map.156 = (f32[256,512]{1,0:T(8,128)}, f32[256,512]{1,0:T(8,128)}, f32[1024,128]{1,0:T(8,128)}, f32[1024,128]{1,0:T(8,128)}) custom-call(f32[256,512]{1,0:T(8,128)} %depth_ref.1, f32[256,512]{1,0:T(8,128)} %bed_ref.1, f32[256,512]{1,0:T(8,128)} %mass_ref.1, f32[256,512]{1,0:T(8,128)} %cond_ref.1, f32[256,512]{1,0:T(8,128)} %settle_ref.1, ...), custom_call_target="tpu_custom_call" | custom-call | flops 7864320 | bytes 5242880 | tf_op jit(solution)/shard_map/pallas_call | solution.py:133
  24.2 3.3 %fusion.4 = f32[1024,256]{1,0:T(8,128)S(1)} fusion(s32[1024]{0:T(1024)S(1)} %select_reduce_fusion.1, f32[1024,128]{1,0:T(8,128)} %get-tuple-element.13, f32[1024,128]{1,0:T(8,128)} %get-tuple-element.12, f32[1024]{0:T(1024)S(1)} %broadcast_maximum_fusion), kind=kOutput, calls=%fused_computation.13 | convolution fusion | flops 3222798336 | bytes 2105344 | tf_op jit(solution)/shard_map/dot_general | solution.py:158
  27.5 0.2 reshape.108
  27.6 0.3 concatenate.24
  27.9 0.8 all_to_all.11
  28.7 30.4 %all_to_all.17 = f32[128,1,2176]{2,1,0:T(1,128)S(1)} all-to-all(f32[128,1,2176]{2,1,0:T(1,128)S(1)} %all_to_all.11), channel_id=1, replica_groups=mesh['row'=4,'col'=32] {'row','col'}, dimensions={0} | all-to-all | bytes 2228224 | tf_op jit(solution)/shard_map/all_to_all | solution.py:168
  59.2 0.1 copy.116
  59.2 0.1 fusion.21
  59.3 0.1 slice.93
  59.4 0.1 eq.106
  59.5 0.6 fusion.18.hot_ref
  60.1 1.0 %fusion.13.hot_t_ref = f32[1024,16]{1,0:T(8,128)} fusion(f32[1024]{0:T(1024)S(1)} %eq.106), kind=kLoop, calls=%fused_computation.32 | loop fusion | flops 32768 | bytes 69632 | tf_op jit(solution)/shard_map/convert_element_type | solution.py:180
  61.1 0.2 reshape.110
  61.3 0.1 broadcast_in_dim.72
  61.4 1.4 %compare_select_fusion = (f32[1024,128]{1,0:T(8,128)}, f32[1024,128]{1,0:T(8,128)}, f32[1024,128]{1,0:T(8,128)}) fusion(f32[1024]{0:T(1024)S(1)} %broadcast_in_dim.72, f32[1024,256]{1,0:T(8,128)S(1)} %reshape.110), kind=kLoop, calls=%fused_computation.33 | loop fusion | flops 262144 | bytes 2625536 | tf_op jit(solution)/shard_map/jit(_where)/select_n | solution.py:176
  62.8 4.7 %shard_map.157 = (f32[16,128]{1,0:T(8,128)}, f32[16,128]{1,0:T(8,128)}, f32[1024,256]{1,0:T(8,128)}) custom-call(f32[1024,128]{1,0:T(8,128)} %get-tuple-element.36.ws_ref, f32[1024,128]{1,0:T(8,128)} %get-tuple-element.35.wm_ref, f32[1024,128]{1,0:T(8,128)} %get-tuple-element.34.w_ref, f32[16,1024]{1,0:T(8,128)} %fusion.18.hot_ref, ...), custom_call_target="tpu_custom_call" | custom-call | tf_op jit(solution)/shard_map/pallas_call | solution.py:182
  67.5 4.6 %all-to-all-start.1 = ((f32[128,8,256]{2,1,0:T(8,128)}), f32[128,8,256]{2,1,0:T(8,128)S(1)}, u32[]{:S(2)}, u32[]{:S(2)}) async-start(f32[128,8,256]{2,1,0:T(8,128)} %bitcast.56), calls=%async_computation.1 | async-start | bytes 2097152 | tf_op jit(solution)/shard_map/all_to_all | solution.py:188
  72.2 0.0 copy-start.1
  72.2 0.0 copy-start.5
  72.2 1.0 %gather_fusion = f32[512,128]{1,0:T(8,128)S(1)} fusion(f32[1024,128]{1,0:T(8,128)S(1)} %reshape.106, s32[1024]{0:T(1024)S(1)} %pad_clamp_fusion.1), kind=kCustom, calls=%fused_computation | custom fusion | bytes 526336 | tf_op jit(solution)/shard_map/gather | solution.py:198
  73.3 0.1 copy.92
  73.5 0.1 add.60
  73.6 0.0 copy-start.6
  73.6 1.0 %gather_fusion.2 = f32[512,128]{1,0:T(8,128)S(1)} fusion(f32[1024,128]{1,0:T(8,128)S(1)} %reshape.113, s32[1024]{0:T(1024)S(1)} %pad_clamp_fusion.1), kind=kCustom, calls=%fused_computation.2 | custom fusion | bytes 526336 | tf_op jit(solution)/shard_map/gather | solution.py:196
  74.7 0.1 copy.96
  74.8 1.0 %gather_fusion.3 = f32[512,128]{1,0:T(8,128)S(1)} fusion(f32[1024,128]{1,0:T(8,128)S(1)} %reshape.114, s32[1024]{0:T(1024)S(1)} %pad_clamp_fusion.1), kind=kCustom, calls=%fused_computation.3 | custom fusion | bytes 526336 | tf_op jit(solution)/shard_map/gather | solution.py:197
  75.9 0.1 copy.98
  76.0 15.4 %all-to-all-done.1 = f32[128,8,256]{2,1,0:T(8,128)S(1)} async-done(((f32[128,8,256]{2,1,0:T(8,128)}), f32[128,8,256]{2,1,0:T(8,128)S(1)}, u32[]{:S(2)}, u32[]{:S(2)}) %all-to-all-start.1) | async-done | bytes 1048608 | tf_op jit(solution)/shard_map/all_to_all | solution.py:188
  91.4 1.6 %gather_fusion.1 = f32[512,256]{1,0:T(8,128)S(1)} fusion(f32[1024,256]{1,0:T(8,128)S(1)} %bitcast.49, s32[1024]{0:T(1024)S(1)} %pad_clamp_fusion), kind=kCustom, calls=%fused_computation.1 | custom fusion | bytes 1050624 | tf_op jit(solution)/shard_map/gather | solution.py:195
  93.0 0.1 copy.111
  93.2 0.1 copy.112
  93.3 0.1 subtract_multiply_fusion.1
  93.4 1.1 %fusion.2 = f32[4,256,256]{2,1,0:T(8,128)S(1)} fusion(s32[512]{0:T(512)S(1)} %copy-done.8, s32[4,256]{1,0:T(4,128)S(1)} %iota_add_fusion, f32[512,128]{0,1:T(8,128)S(1)} %get-tuple-element.42, f32[512,128]{0,1:T(8,128)S(1)} %get-tuple-element.41), kind=kOutput, calls=%fused_computation.11 | convolution fusion | flops 1611268096 | bytes 1579008 | tf_op jit(solution)/shard_map/jyl,lc->jyc/dot_general | solution.py:210
  94.5 0.1 slice_bitcast_fusion.3
  94.6 1.1 %maximum_add_fusion = (f32[256,512]{1,0:T(8,128)}, f32[256,512]{1,0:T(8,128)}) fusion(f32[256,512]{1,0:T(8,128)S(1)} %copy-done.5, f32[256,128]{1,0:T(8,128)S(1)} %get-tuple-element.29, f32[256,128]{1,0:T(8,128)S(1)} %get-tuple-element.30, f32[256,128]{1,0:T(8,128)S(1)} %get-tuple-element.31, f32[256,128]{1,0:T(8,128)S(1)} %get-tuple-element.32, ...), kind=kLoop, calls=%fused_computation.28 | loop fusion | flops 1048576 | bytes 3145728 | tf_op jit(solution)/shard_map/add | solution.py:211
  (33 shorter events, 0.3 us)
Async XLA Ops:
  0.6 1.3 %copy-start = (f32[256,512]{1,0:T(8,128)S(1)}, f32[256,512]{1,0:T(8,128)}, u32[]{:S(2)}) copy-start(f32[256,512]{1,0:T(8,128)} %bed_ref.1) | copy-start | bytes 1572868
  0.6 1.4 %copy-start.4 = (f32[256,512]{1,0:T(8,128)S(1)}, f32[256,512]{1,0:T(8,128)}, u32[]{:S(2)}) copy-start(f32[256,512]{1,0:T(8,128)} %depth_ref.1) | copy-start | bytes 1572868
  2.0 1.0 %copy-start.2 = (f32[256,512]{1,0:T(8,128)S(1)}, f32[256,512]{1,0:T(8,128)}, u32[]{:S(2)}) copy-start(f32[256,512]{1,0:T(8,128)} %mass_ref.1) | copy-start | bytes 1572868
  2.0 1.2 %copy-start.3 = (f32[256,512]{1,0:T(8,128)S(1)}, f32[256,512]{1,0:T(8,128)}, u32[]{:S(2)}) copy-start(f32[256,512]{1,0:T(8,128)} %cond_ref.1) | copy-start | bytes 1572868
  3.7 12.4 %copy-start.10 = (s32[512]{0:T(512)S(1)}, s32[512]{0:T(512)}, u32[]{:S(2)}) copy-start(s32[512]{0:T(512)} %param.21) | copy-start | bytes 6148
  3.7 12.4 %copy-start.7 = (s32[512,1]{0,1:T(1,128)S(1)}, s32[512,1]{0,1:T(1,128)}, u32[]{:S(2)}) copy-start(s32[512,1]{0,1:T(1,128)} %param.20) | copy-start | bytes 6148
  3.7 14.3 %collective-permute-start.2 = (f32[4,256]{1,0:T(4,128)S(1)}, f32[4,256]{1,0:T(4,128)S(1)}, u32[]{:S(2)}, u32[]{:S(2)}) collective-permute-start(f32[4,256]{1,0:T(4,128)S(1)} %get-tuple-element.18), channel_id=1, source_target_pairs={{0,1},{1,2},{2,3},{3,4},{4,5},{5,6},{6,7},{7,8},{8,9},{9,10},{10,1... | collective-permute-start | bytes 12296 | tf_op jit(solution)/shard_map/ppermute | solution.py:13
  8.8 9.3 %collective-permute-start.3 = (f32[4,256]{1,0:T(4,128)S(1)}, f32[4,256]{1,0:T(4,128)S(1)}, u32[]{:S(2)}, u32[]{:S(2)}) collective-permute-start(f32[4,256]{1,0:T(4,128)S(1)} %get-tuple-element.19), channel_id=1, source_target_pairs={{1,0},{2,1},{3,2},{4,3},{5,4},{6,5},{7,6},{8,7},{9,8},{10,9},{11,1... | collective-permute-start | bytes 12296 | tf_op jit(solution)/shard_map/ppermute | solution.py:13
  10.8 6.1 %copy-start.9 = (f32[512]{0:T(512)S(1)}, f32[512]{0:T(512)}, u32[]{:S(2)}) copy-start(f32[512]{0:T(512)} %param.22) | copy-start | bytes 6148
  10.8 6.7 %copy-start.8 = (s32[512]{0:T(512)S(1)}, s32[512]{0:T(512)}, u32[]{:S(2)}) copy-start(s32[512]{0:T(512)} %param.19) | copy-start | bytes 6148
  10.8 8.1 %collective-permute-start.1 = (f32[4,512]{1,0:T(4,128)S(1)}, f32[4,512]{1,0:T(4,128)S(1)}, u32[]{:S(2)}, u32[]{:S(2)}) collective-permute-start(f32[4,512]{1,0:T(4,128)S(1)} %bitcast.63), channel_id=1, source_target_pairs={{32,0},{64,32},{96,64},{33,1},{65,33},{97,65},{34,2},{66,34},{98,6... | collective-permute-start | bytes 24584 | tf_op jit(solution)/shard_map/ppermute | solution.py:13
  12.1 6.8 %collective-permute-start = (f32[4,512]{1,0:T(4,128)S(1)}, f32[4,512]{1,0:T(4,128)S(1)}, u32[]{:S(2)}, u32[]{:S(2)}) collective-permute-start(f32[4,512]{1,0:T(4,128)S(1)} %bitcast.64), channel_id=1, source_target_pairs={{0,32},{32,64},{64,96},{1,33},{33,65},{65,97},{2,34},{34,66},{66,9... | collective-permute-start | bytes 24584 | tf_op jit(solution)/shard_map/ppermute | solution.py:13
  67.5 23.9 %all-to-all-start.1 = ((f32[128,8,256]{2,1,0:T(8,128)}), f32[128,8,256]{2,1,0:T(8,128)S(1)}, u32[]{:S(2)}, u32[]{:S(2)}) async-start(f32[128,8,256]{2,1,0:T(8,128)} %bitcast.56), calls=%async_computation.1 | async-start | bytes 2097152 | tf_op jit(solution)/shard_map/all_to_all | solution.py:188
  72.2 1.3 %copy-start.1 = (f32[256,512]{1,0:T(8,128)S(1)}, f32[256,512]{1,0:T(8,128)}, u32[]{:S(2)}) copy-start(f32[256,512]{1,0:T(8,128)} %bed_ref.1) | copy-start | bytes 1572868
  72.2 1.3 %copy-start.5 = (f32[256,512]{1,0:T(8,128)S(1)}, f32[256,512]{1,0:T(8,128)}, u32[]{:S(2)}) copy-start(f32[256,512]{1,0:T(8,128)} %get-tuple-element.11) | copy-start | bytes 1572868
  73.6 1.2 %copy-start.6 = (f32[256,512]{1,0:T(8,128)S(1)}, f32[256,512]{1,0:T(8,128)}, u32[]{:S(2)}) copy-start(f32[256,512]{1,0:T(8,128)} %get-tuple-element.15) | copy-start | bytes 1572868

commit v14 on v12

--- a/solution.py
+++ b/solution.py
@@ -131,7 +131,7 @@
     slot_hot = (slot_block[:, None] == block_ids[None, :]).astype(jnp.float32)
     coefs = jnp.maximum(jnp.max(jnp.where(slot_hit, link_coef[None, :], -1.0), axis=1), 0.0)
     payload = coefs[:, None] * jnp.dot(
-        slot_hot, jnp.concatenate([open_surf, open_mass], axis=1), precision=lax.Precision.HIGHEST
+        slot_hot, jnp.concatenate([open_surf, open_mass], axis=1), precision=lax.Precision.HIGH
     )
     tags = jnp.max(jnp.where(slot_hit, link_reach[None, :].astype(jnp.float32), -1.0), axis=1)
     meta = jnp.concatenate(
@@ -164,7 +164,7 @@
     phase_out = smooth_reach(phase_new)
     conc_out = smooth_reach(conc_new)
     reply = jnp.dot(
-        reach_hot.T, jnp.concatenate([phase_out, conc_out], axis=1), precision=lax.Precision.HIGHEST
+        reach_hot.T, jnp.concatenate([phase_out, conc_out], axis=1), precision=lax.Precision.HIGH
     )
     answered = lax.all_to_all(
         reply.reshape(devices, slot_cap, 256),
@@ -188,7 +188,7 @@
     row_ids = jnp.arange(tile_y, dtype=jnp.int32)[:, None]
     column_ids = jnp.arange(per_row, dtype=jnp.int32)[:, None, None]
     block_hot = (row_ids[None] * per_row + column_ids == link_block[None, None, :]).astype(jnp.float32)
-    gained = jnp.einsum("jyl,lc->jyc", block_hot, applied, precision=lax.Precision.HIGHEST)
+    gained = jnp.einsum("jyl,lc->jyc", block_hot, applied, precision=lax.Precision.HIGH)
     depth_out = depth1 + jnp.concatenate([gained[j, :, :128] for j in range(per_row)], axis=1)
     mass_out = mass1 + jnp.concatenate([gained[j, :, 128:] for j in range(per_row)], axis=1)
     return (depth_out, mass_out, phase_out, conc_out)

time: 92.3 us -> 91.1 us (0.987)
  matrix products: 6.6 us -> 5.35 us
  transfers between devices with their start and end apart: 5 -> 5, of which waited for: 1 -> 1; matrix products, arithmetic and copies ran while one was open for 7% -> 8% of each run, Pallas kernels for 0% -> 0%
where the time goes in v14:
time: 91.1 us; the launch traced here: 90.7 us
  blocking collectives  30.9 us (34%)
  starting transfers between devices  17.4 us (19%)
  waiting for transfers between devices  15.4 us (17%)
  local copies, waits for them, and re-layouts  10 us (11%)
  other arithmetic  5.75 us (6%)
  matrix products  5.35 us (6%)
  Pallas kernels  4.65 us (5%)
  between operations  1.23 us (1%)
    all_to_all x1, blocking collectives, body(): lax.all_to_all(outgoing, ('row', 'col'), split_axis=0, concat_axis=0, til...  30.9 us
    all_to_all x1, waiting for transfers between devices, body(): lax.all_to_all(reply.reshape(devices, slot_cap, 256), ('row', 'col'), spl...  15.4 us
    ppermute x2, starting transfers between devices, halo_pair(): lax.ppermute(last, axis, forward)  8.18 us
    pallas_call x1, Pallas kernels, body(): pl.pallas_call(stencil_kernel, out_shape=[tile, tile] + [block_rows] * 2,...  4.65 us
    ppermute x2, starting transfers between devices, halo_pair(): lax.ppermute(first, axis, backward)  4.64 us
    all_to_all x1, starting transfers between devices, body(): lax.all_to_all(reply.reshape(devices, slot_cap, 256), ('row', 'col'), spl...  4.62 us
    dot_general x1, matrix products, body(): jnp.dot(slot_hot, jnp.concatenate([open_surf, open_mass], axis=1), precis...  2.5 us
  transfers between devices with their start and end apart: 5, of which 1 were waited for; matrix products, arithmetic and copies ran while one was open for 8% of the time, Pallas kernels for 0%

profile of v14, /device:TPU:1, one launch (start us, length us, event | category | flops | bytes accessed | tf_op | source)
XLA Modules:
  0.0 90.7 jit_solution(13749945261236640179)
XLA Ops:
  0.6 0.0 copy-start.4
  0.6 0.0 copy-start
  0.7 1.2 %fusion.41 = (f32[256,512]{1,0:T(8,128)S(1)}, f32[1,256,512]{2,1,0:T(8,128)S(1)}) fusion(s32[256,512]{1,0:T(8,128)} %wet_ref.1), kind=kLoop, calls=%fused_computation.98 | loop fusion | flops 131072 | bytes 1572864 | tf_op jit(solution)/shard_map/convert_element_type | solution.py:97
  1.9 0.1 copy-done
  2.0 0.1 add_bitcast_fusion
  2.1 1.0 %copy-done.2 = f32[256,512]{1,0:T(8,128)S(1)} copy-done((f32[256,512]{1,0:T(8,128)S(1)}, f32[256,512]{1,0:T(8,128)}, u32[]{:S(2)}) %copy-start.2) | copy-done | bytes 524312
  3.0 0.2 copy-done.3
  3.2 1.3 %collective-permute-start.1 = (f32[4,512]{1,0:T(4,128)S(1)}, f32[4,512]{1,0:T(4,128)S(1)}, u32[]{:S(2)}, u32[]{:S(2)}) collective-permute-start(f32[4,512]{1,0:T(4,128)S(1)} %bitcast.63), channel_id=1, source_target_pairs={{32,0},{64,32},{96,64},{33,1},{65,33},{97,65},{34,2},{66,34},{98,6... | collective-permute-start | bytes 24584 | tf_op jit(solution)/shard_map/ppermute | solution.py:13
  4.5 4.7 %collective-permute-start = (f32[4,512]{1,0:T(4,128)S(1)}, f32[4,512]{1,0:T(4,128)S(1)}, u32[]{:S(2)}, u32[]{:S(2)}) collective-permute-start(f32[4,512]{1,0:T(4,128)S(1)} %bitcast.64), channel_id=1, source_target_pairs={{0,32},{32,64},{64,96},{1,33},{33,65},{65,97},{2,34},{34,66},{66,9... | collective-permute-start | bytes 24584 | tf_op jit(solution)/shard_map/ppermute | solution.py:13
  9.2 0.5 maximum_reduce_fusion
  9.7 0.0 copy-start.14
  9.8 3.3 %collective-permute-start.3 = (f32[4,256]{1,0:T(4,128)S(1)}, f32[4,256]{1,0:T(4,128)S(1)}, u32[]{:S(2)}, u32[]{:S(2)}) collective-permute-start(f32[4,256]{1,0:T(4,128)S(1)} %get-tuple-element.13), channel_id=1, source_target_pairs={{1,0},{2,1},{3,2},{4,3},{5,4},{6,5},{7,6},{8,7},{9,8},{10,9},{11,1... | collective-permute-start | bytes 12296 | tf_op jit(solution)/shard_map/ppermute | solution.py:13
  13.1 3.5 %collective-permute-start.2 = (f32[4,256]{1,0:T(4,128)S(1)}, f32[4,256]{1,0:T(4,128)S(1)}, u32[]{:S(2)}, u32[]{:S(2)}) collective-permute-start(f32[4,256]{1,0:T(4,128)S(1)} %get-tuple-element.12), channel_id=1, source_target_pairs={{0,1},{1,2},{2,3},{3,4},{4,5},{5,6},{6,7},{7,8},{8,9},{9,10},{10,1... | collective-permute-start | bytes 12296 | tf_op jit(solution)/shard_map/ppermute | solution.py:13
  16.7 0.1 copy.93
  16.8 0.2 fusion.19
  17.0 0.1 add_add_fusion
  17.1 0.2 fusion.18
  17.4 0.6 select_reduce_fusion
  18.1 0.4 select_reduce_fusion.1
  18.4 0.1 reshape.108
  18.5 0.1 max.16
  18.6 0.8 copy.91
  19.4 0.6 pad_maximum_fusion.3.rows_ref
  20.0 4.7 %shard_map.156 = (f32[256,512]{1,0:T(8,128)}, f32[256,512]{1,0:T(8,128)}, f32[1024,128]{1,0:T(8,128)}, f32[1024,128]{1,0:T(8,128)}) custom-call(f32[256,512]{1,0:T(8,128)} %depth_ref.1, f32[256,512]{1,0:T(8,128)} %bed_ref.1, f32[256,512]{1,0:T(8,128)} %mass_ref.1, f32[256,512]{1,0:T(8,128)} %cond_ref.1, f32[256,512]{1,0:T(8,128)} %settle_ref.1, ...), custom_call_target="tpu_custom_call" | custom-call | flops 7864320 | bytes 5242880 | tf_op jit(solution)/shard_map/pallas_call | solution.py:108
  24.7 2.5 %fusion.8 = f32[1024,256]{1,0:T(8,128)S(1)} fusion(s32[1024]{0:T(1024)S(1)} %select_reduce_fusion.1, f32[1024,128]{1,0:T(8,128)} %get-tuple-element.10, f32[1024,128]{1,0:T(8,128)} %get-tuple-element.9, f32[1024]{0:T(1024)S(1)} %broadcast_maximum_fusion), kind=kOutput, calls=%fused_computation.17 | convolution fusion | flops 1612185600 | bytes 2105344 | tf_op jit(solution)/shard_map/dot_general | solution.py:133
  27.2 0.2 reshape.107
  27.4 0.3 concatenate.43
  27.7 0.8 all_to_all.11
  28.4 30.9 %all_to_all.17 = f32[128,1,2176]{2,1,0:T(1,128)S(1)} all-to-all(f32[128,1,2176]{2,1,0:T(1,128)S(1)} %all_to_all.11), channel_id=1, replica_groups=mesh['row'=4,'col'=32] {'row','col'}, dimensions={0} | all-to-all | bytes 2228224 | tf_op jit(solution)/shard_map/all_to_all | solution.py:143
  59.3 0.1 copy.116
  59.4 0.1 fusion.39
  59.5 0.1 slice.136
  59.6 0.1 eq.93
  59.7 0.2 reshape.109
  59.8 0.1 broadcast_in_dim.71
  59.9 0.0 copy-start.13
  60.0 0.2 fusion.17
  60.2 0.6 fusion.4
  60.8 0.1 fusion.44
  60.9 0.1 fusion.45
  61.0 0.1 fusion.42
  61.1 0.1 fusion.43
  61.1 0.1 fusion.34
  61.2 0.1 fusion.31
  61.3 1.5 %convolution_bitcast_fusion = f32[128,8,256]{2,1,0:T(8,128)} fusion(f32[1024]{0:T(1024)S(1)} %eq.93, f32[16,128]{1,0:T(8,128)S(1)} %fusion.34, f32[16,128]{1,0:T(8,128)S(1)} %fusion.31), kind=kOutput, calls=%fused_computation.18 | convolution fusion | flops 25186304 | bytes 1069056 | tf_op jit(solution)/shard_map/dot_general | solution.py:166
  62.8 4.6 %all-to-all-start.1 = ((f32[128,8,256]{2,1,0:T(8,128)}), f32[128,8,256]{2,1,0:T(8,128)S(1)}, u32[]{:S(2)}, u32[]{:S(2)}) async-start(f32[128,8,256]{2,1,0:T(8,128)} %convolution_bitcast_fusion), calls=%async_computation.1 | async-start | bytes 2097152 | tf_op jit(solution)/shard_map/all_to_all | solution.py:169
  67.5 0.0 copy-start.1
  67.5 0.0 copy-start.5
  67.5 1.0 %gather_fusion = f32[512,128]{1,0:T(8,128)S(1)} fusion(f32[1024,128]{1,0:T(8,128)S(1)} %reshape.105, s32[1024]{0:T(1024)S(1)} %pad_clamp_fusion.1), kind=kCustom, calls=%fused_computation | custom fusion | bytes 526336 | tf_op jit(solution)/shard_map/gather | solution.py:179
  68.5 0.1 copy.92
  68.8 0.1 add.89
  68.9 0.0 copy-start.6
  68.9 1.0 %gather_fusion.2 = f32[512,128]{1,0:T(8,128)S(1)} fusion(f32[1024,128]{1,0:T(8,128)S(1)} %reshape.112, s32[1024]{0:T(1024)S(1)} %pad_clamp_fusion.1), kind=kCustom, calls=%fused_computation.2 | custom fusion | bytes 526336 | tf_op jit(solution)/shard_map/gather | solution.py:177
  69.9 0.1 copy.96
  70.1 1.0 %gather_fusion.3 = f32[512,128]{1,0:T(8,128)S(1)} fusion(f32[1024,128]{1,0:T(8,128)S(1)} %reshape.113, s32[1024]{0:T(1024)S(1)} %pad_clamp_fusion.1), kind=kCustom, calls=%fused_computation.3 | custom fusion | bytes 526336 | tf_op jit(solution)/shard_map/gather | solution.py:178
  71.2 0.1 copy.98
  71.3 15.4 %all-to-all-done.1 = f32[128,8,256]{2,1,0:T(8,128)S(1)} async-done(((f32[128,8,256]{2,1,0:T(8,128)}), f32[128,8,256]{2,1,0:T(8,128)S(1)}, u32[]{:S(2)}, u32[]{:S(2)}) %all-to-all-start.1) | async-done | bytes 1048608 | tf_op jit(solution)/shard_map/all_to_all | solution.py:169
  86.7 1.6 %gather_fusion.1 = f32[512,256]{1,0:T(8,128)S(1)} fusion(f32[1024,256]{1,0:T(8,128)S(1)} %bitcast.50, s32[1024]{0:T(1024)S(1)} %pad_clamp_fusion), kind=kCustom, calls=%fused_computation.1 | custom fusion | bytes 1050624 | tf_op jit(solution)/shard_map/gather | solution.py:176
  88.3 0.1 copy.111
  88.5 0.1 copy.112
  88.6 0.1 subtract_multiply_fusion.1
  88.7 0.8 fusion.2
  89.5 0.1 slice_bitcast_fusion.3
  89.6 1.1 %maximum_add_fusion = (f32[256,512]{1,0:T(8,128)}, f32[256,512]{1,0:T(8,128)}) fusion(f32[256,512]{1,0:T(8,128)S(1)} %copy-done.5, f32[256,128]{1,0:T(8,128)S(1)} %get-tuple-element.23, f32[256,128]{1,0:T(8,128)S(1)} %get-tuple-element.24, f32[256,128]{1,0:T(8,128)S(1)} %get-tuple-element.25, f32[256,128]{1,0:T(8,128)S(1)} %get-tuple-element.26, ...), kind=kLoop, calls=%fused_computation.34 | loop fusion | flops 1048576 | bytes 3145728 | tf_op jit(solution)/shard_map/add | solution.py:192
  (49 shorter events, 0.4 us)
Async XLA Ops:
  0.6 1.3 %copy-start.4 = (f32[256,512]{1,0:T(8,128)S(1)}, f32[256,512]{1,0:T(8,128)}, u32[]{:S(2)}) copy-start(f32[256,512]{1,0:T(8,128)} %depth_ref.1) | copy-start | bytes 1572868
  0.6 1.4 %copy-start = (f32[256,512]{1,0:T(8,128)S(1)}, f32[256,512]{1,0:T(8,128)}, u32[]{:S(2)}) copy-start(f32[256,512]{1,0:T(8,128)} %bed_ref.1) | copy-start | bytes 1572868
  2.0 1.0 %copy-start.2 = (f32[256,512]{1,0:T(8,128)S(1)}, f32[256,512]{1,0:T(8,128)}, u32[]{:S(2)}) copy-start(f32[256,512]{1,0:T(8,128)} %mass_ref.1) | copy-start | bytes 1572868
  2.0 1.2 %copy-start.3 = (f32[256,512]{1,0:T(8,128)S(1)}, f32[256,512]{1,0:T(8,128)}, u32[]{:S(2)}) copy-start(f32[256,512]{1,0:T(8,128)} %cond_ref.1) | copy-start | bytes 1572868
  3.2 13.4 %copy-start.9 = (s32[512,1]{0,1:T(1,128)S(1)}, s32[512,1]{0,1:T(1,128)}, u32[]{:S(2)}) copy-start(s32[512,1]{0,1:T(1,128)} %param.20) | copy-start | bytes 6148
  3.2 16.2 %collective-permute-start.1 = (f32[4,512]{1,0:T(4,128)S(1)}, f32[4,512]{1,0:T(4,128)S(1)}, u32[]{:S(2)}, u32[]{:S(2)}) collective-permute-start(f32[4,512]{1,0:T(4,128)S(1)} %bitcast.63), channel_id=1, source_target_pairs={{32,0},{64,32},{96,64},{33,1},{65,33},{97,65},{34,2},{66,34},{98,6... | collective-permute-start | bytes 24584 | tf_op jit(solution)/shard_map/ppermute | solution.py:13
  4.5 14.9 %collective-permute-start = (f32[4,512]{1,0:T(4,128)S(1)}, f32[4,512]{1,0:T(4,128)S(1)}, u32[]{:S(2)}, u32[]{:S(2)}) collective-permute-start(f32[4,512]{1,0:T(4,128)S(1)} %bitcast.64), channel_id=1, source_target_pairs={{0,32},{32,64},{64,96},{1,33},{33,65},{65,97},{2,34},{34,66},{66,9... | collective-permute-start | bytes 24584 | tf_op jit(solution)/shard_map/ppermute | solution.py:13
  9.7 7.6 %copy-start.15 = (s32[512]{0:T(512)S(1)}, s32[512]{0:T(512)}, u32[]{:S(2)}) copy-start(s32[512]{0:T(512)} %param.21) | copy-start | bytes 6148
  9.7 7.7 %copy-start.14 = (f32[512]{0:T(512)S(1)}, f32[512]{0:T(512)}, u32[]{:S(2)}) copy-start(f32[512]{0:T(512)} %param.22) | copy-start | bytes 6148
  9.8 8.3 %copy-start.10 = (s32[512]{0:T(512)S(1)}, s32[512]{0:T(512)}, u32[]{:S(2)}) copy-start(s32[512]{0:T(512)} %param.19) | copy-start | bytes 6148
  9.8 8.8 %collective-permute-start.3 = (f32[4,256]{1,0:T(4,128)S(1)}, f32[4,256]{1,0:T(4,128)S(1)}, u32[]{:S(2)}, u32[]{:S(2)}) collective-permute-start(f32[4,256]{1,0:T(4,128)S(1)} %get-tuple-element.13), channel_id=1, source_target_pairs={{1,0},{2,1},{3,2},{4,3},{5,4},{6,5},{7,6},{8,7},{9,8},{10,9},{11,1... | collective-permute-start | bytes 12296 | tf_op jit(solution)/shard_map/ppermute | solution.py:13
  13.1 5.5 %collective-permute-start.2 = (f32[4,256]{1,0:T(4,128)S(1)}, f32[4,256]{1,0:T(4,128)S(1)}, u32[]{:S(2)}, u32[]{:S(2)}) collective-permute-start(f32[4,256]{1,0:T(4,128)S(1)} %get-tuple-element.12), channel_id=1, source_target_pairs={{0,1},{1,2},{2,3},{3,4},{4,5},{5,6},{6,7},{7,8},{8,9},{9,10},{10,1... | collective-permute-start | bytes 12296 | tf_op jit(solution)/shard_map/ppermute | solution.py:13
  59.9 0.9 copy-start.11
  59.9 0.9 copy-start.12
  59.9 0.9 copy-start.13
  61.2 1.6 %copy-start.7 = (f32[16,128]{1,0:T(8,128)}, f32[16,128]{1,0:T(8,128)S(1)}, u32[]{:S(2)}) copy-start(f32[16,128]{1,0:T(8,128)S(1)} %fusion.34) | copy-start | bytes 24580
  61.3 1.5 %copy-start.8 = (f32[16,128]{1,0:T(8,128)}, f32[16,128]{1,0:T(8,128)S(1)}, u32[]{:S(2)}) copy-start(f32[16,128]{1,0:T(8,128)S(1)} %fusion.31) | copy-start | bytes 24580
  62.8 23.9 %all-to-all-start.1 = ((f32[128,8,256]{2,1,0:T(8,128)}), f32[128,8,256]{2,1,0:T(8,128)S(1)}, u32[]{:S(2)}, u32[]{:S(2)}) async-start(f32[128,8,256]{2,1,0:T(8,128)} %convolution_bitcast_fusion), calls=%async_computation.1 | async-start | bytes 2097152 | tf_op jit(solution)/shard_map/all_to_all | solution.py:169
  67.5 1.3 %copy-start.1 = (f32[256,512]{1,0:T(8,128)S(1)}, f32[256,512]{1,0:T(8,128)}, u32[]{:S(2)}) copy-start(f32[256,512]{1,0:T(8,128)} %bed_ref.1) | copy-start | bytes 1572868
  67.5 1.3 %copy-start.5 = (f32[256,512]{1,0:T(8,128)S(1)}, f32[256,512]{1,0:T(8,128)}, u32[]{:S(2)}) copy-start(f32[256,512]{1,0:T(8,128)} %get-tuple-element.8) | copy-start | bytes 1572868
  68.9 1.2 %copy-start.6 = (f32[256,512]{1,0:T(8,128)S(1)}, f32[256,512]{1,0:T(8,128)}, u32[]{:S(2)}) copy-start(f32[256,512]{1,0:T(8,128)} %get-tuple-element.11) | copy-start | bytes 1572868

commit v15 on v14

--- a/solution.py
+++ b/solution.py
@@ -173,10 +173,11 @@
         concat_axis=0,
         tiled=True,
     )
-    own_rows = answered.reshape(devices * slot_cap, 256)[slot_of]
-    surf_rows = (depth1 + bed).reshape(blocks, 128)[link_block]
-    mass_rows = mass1.reshape(blocks, 128)[link_block]
-    weight = link_coef[:, None] * opened.reshape(blocks, 128)[link_block]
+    own_rows = answered.reshape(devices * slot_cap, 256)
+    slot_read = jnp.maximum(slot_block, 0)
+    surf_rows = (depth1 + bed).reshape(blocks, 128)[slot_read]
+    mass_rows = mass1.reshape(blocks, 128)[slot_read]
+    weight = coefs[:, None] * opened.reshape(blocks, 128)[slot_read]
     applied = jnp.concatenate(
         [
             0.5 * weight * (own_rows[:, :128] - surf_rows),
@@ -187,7 +188,7 @@
     per_row = tile_x // 128
     row_ids = jnp.arange(tile_y, dtype=jnp.int32)[:, None]
     column_ids = jnp.arange(per_row, dtype=jnp.int32)[:, None, None]
-    block_hot = (row_ids[None] * per_row + column_ids == link_block[None, None, :]).astype(jnp.float32)
+    block_hot = (row_ids[None] * per_row + column_ids == slot_block[None, None, :]).astype(jnp.float32)
     gained = jnp.einsum("jyl,lc->jyc", block_hot, applied, precision=lax.Precision.HIGH)
     depth_out = depth1 + jnp.concatenate([gained[j, :, :128] for j in range(per_row)], axis=1)
     mass_out = mass1 + jnp.concatenate([gained[j, :, 128:] for j in range(per_row)], axis=1)

time: 91.1 us -> 95.5 us (1.048)
  local copies, waits for them, and re-layouts: 10 us -> 22.9 us
  waiting for transfers between devices: 15.4 us -> 5.11 us
  other arithmetic: 5.75 us -> 6.87 us
    all_to_all x1, waiting for transfers between devices: 15.4 us -> 5.1 us  [body(): lax.all_to_all(reply.reshape(devices, slot_cap, 256), ('row', 'col'), spl...]
    gather x7 -> x6, local copies, waits for them, and re-layouts: 5.06 us -> 12.9 us  [the longest x2 6.09 us: body(): mass_rows = mass1.reshape(blocks, 128)[slot_read]]
    unnamed x37 -> x41, local copies, waits for them, and re-layouts: 1.61 us -> 5.67 us
    mul x1, other arithmetic: 0.13 us -> 1.28 us  [body(): 0.5 * weight * (own_rows[:, :128] - surf_rows)]
    slice x1, local copies, waits for them, and re-layouts: 0.04 us -> 1.03 us  [body(): own_rows[:, :128] - surf_rows]
  transfers between devices with their start and end apart: 5 -> 5, of which waited for: 1 -> 1; matrix products, arithmetic and copies ran while one was open for 8% -> 17% of each run, Pallas kernels for 0% -> 0%
where the time goes in v15:
time: 95.5 us; the launch traced here: 94.9 us
  blocking collectives  30.9 us (32%)
  local copies, waits for them, and re-layouts  22.9 us (24%)
  starting transfers between devices  17.4 us (18%)
  other arithmetic  6.87 us (7%)
  matrix products  5.9 us (6%)
  waiting for transfers between devices  5.11 us (5%)
  Pallas kernels  4.66 us (5%)
  between operations  1.13 us (1%)
    all_to_all x1, blocking collectives, body(): lax.all_to_all(outgoing, ('row', 'col'), split_axis=0, concat_axis=0, til...  30.9 us
    ppermute x2, starting transfers between devices, halo_pair(): lax.ppermute(last, axis, forward)  8.18 us
    gather x2, local copies, waits for them, and re-layouts, body(): mass_rows = mass1.reshape(blocks, 128)[slot_read]  6.09 us
    unnamed x41, local copies, waits for them, and re-layouts  5.67 us
    all_to_all x1, waiting for transfers between devices, body(): lax.all_to_all(reply.reshape(devices, slot_cap, 256), ('row', 'col'), spl...  5.1 us
    pallas_call x1, Pallas kernels, body(): pl.pallas_call(stencil_kernel, out_shape=[tile, tile] + [block_rows] * 2,...  4.66 us
    ppermute x2, starting transfers between devices, halo_pair(): lax.ppermute(first, axis, backward)  4.64 us
    all_to_all x1, starting transfers between devices, body(): lax.all_to_all(reply.reshape(devices, slot_cap, 256), ('row', 'col'), spl...  4.62 us
  transfers between devices with their start and end apart: 5, of which 1 were waited for; matrix products, arithmetic and copies ran while one was open for 17% of the time, Pallas kernels for 0%

profile of v15, /device:TPU:1, one launch (start us, length us, event | category | flops | bytes accessed | tf_op | source)
XLA Modules:
  0.0 94.9 jit_solution(9923962507622060413)
XLA Ops:
  0.7 1.2 %fusion.41 = (f32[256,512]{1,0:T(8,128)S(1)}, f32[1,256,512]{2,1,0:T(8,128)S(1)}) fusion(s32[256,512]{1,0:T(8,128)} %wet_ref.1), kind=kLoop, calls=%fused_computation.94 | loop fusion | flops 131072 | bytes 1572864 | tf_op jit(solution)/shard_map/convert_element_type | solution.py:97
  1.9 0.1 copy-done
  2.0 0.1 add_bitcast_fusion
  2.1 1.0 %copy-done.2 = f32[256,512]{1,0:T(8,128)S(1)} copy-done((f32[256,512]{1,0:T(8,128)S(1)}, f32[256,512]{1,0:T(8,128)}, u32[]{:S(2)}) %copy-start.2) | copy-done | bytes 524312
  3.0 0.2 copy-done.3
  3.2 0.0 copy-start.11
  3.2 1.3 %collective-permute-start.1 = (f32[4,512]{1,0:T(4,128)S(1)}, f32[4,512]{1,0:T(4,128)S(1)}, u32[]{:S(2)}, u32[]{:S(2)}) collective-permute-start(f32[4,512]{1,0:T(4,128)S(1)} %bitcast.59), channel_id=1, source_target_pairs={{32,0},{64,32},{96,64},{33,1},{65,33},{97,65},{34,2},{66,34},{98,6... | collective-permute-start | bytes 24584 | tf_op jit(solution)/shard_map/ppermute | solution.py:13
  4.5 4.7 %collective-permute-start = (f32[4,512]{1,0:T(4,128)S(1)}, f32[4,512]{1,0:T(4,128)S(1)}, u32[]{:S(2)}, u32[]{:S(2)}) collective-permute-start(f32[4,512]{1,0:T(4,128)S(1)} %bitcast.60), channel_id=1, source_target_pairs={{0,32},{32,64},{64,96},{1,33},{33,65},{65,97},{2,34},{34,66},{66,9... | collective-permute-start | bytes 24584 | tf_op jit(solution)/shard_map/ppermute | solution.py:13
  9.2 0.5 maximum_reduce_fusion
  9.8 0.0 copy-start.17
  9.8 3.3 %collective-permute-start.3 = (f32[4,256]{1,0:T(4,128)S(1)}, f32[4,256]{1,0:T(4,128)S(1)}, u32[]{:S(2)}, u32[]{:S(2)}) collective-permute-start(f32[4,256]{1,0:T(4,128)S(1)} %get-tuple-element.13), channel_id=1, source_target_pairs={{1,0},{2,1},{3,2},{4,3},{5,4},{6,5},{7,6},{8,7},{9,8},{10,9},{11,1... | collective-permute-start | bytes 12296 | tf_op jit(solution)/shard_map/ppermute | solution.py:13
  13.1 3.5 %collective-permute-start.2 = (f32[4,256]{1,0:T(4,128)S(1)}, f32[4,256]{1,0:T(4,128)S(1)}, u32[]{:S(2)}, u32[]{:S(2)}) collective-permute-start(f32[4,256]{1,0:T(4,128)S(1)} %get-tuple-element.12), channel_id=1, source_target_pairs={{0,1},{1,2},{2,3},{3,4},{4,5},{5,6},{6,7},{7,8},{8,9},{9,10},{10,1... | collective-permute-start | bytes 12296 | tf_op jit(solution)/shard_map/ppermute | solution.py:13
  16.7 0.1 copy.91
  16.8 0.2 fusion.19
  17.0 0.1 add_add_fusion
  17.1 0.2 fusion.18
  17.4 0.6 select_reduce_fusion
  18.1 0.4 select_reduce_fusion.2
  18.4 0.1 reshape.115
  18.5 0.1 max.31
  18.6 0.8 copy.90
  19.4 0.6 pad_maximum_fusion.3.rows_ref
  20.0 4.7 %shard_map.156 = (f32[256,512]{1,0:T(8,128)}, f32[256,512]{1,0:T(8,128)}, f32[1024,128]{1,0:T(8,128)}, f32[1024,128]{1,0:T(8,128)}) custom-call(f32[256,512]{1,0:T(8,128)} %depth_ref.1, f32[256,512]{1,0:T(8,128)} %bed_ref.1, f32[256,512]{1,0:T(8,128)} %mass_ref.1, f32[256,512]{1,0:T(8,128)} %cond_ref.1, f32[256,512]{1,0:T(8,128)} %settle_ref.1, ...), custom_call_target="tpu_custom_call" | custom-call | flops 7864320 | bytes 5242880 | tf_op jit(solution)/shard_map/pallas_call | solution.py:108
  24.7 2.5 %fusion.10 = f32[1024,256]{1,0:T(8,128)S(1)} fusion(s32[1024]{0:T(1024)S(1)} %select_reduce_fusion.2, f32[1024,128]{1,0:T(8,128)} %get-tuple-element.10, f32[1024,128]{1,0:T(8,128)} %get-tuple-element.9, f32[1024]{0:T(1024)S(1)} %broadcast_maximum_fusion), kind=kOutput, calls=%fused_computation.18 | convolution fusion | flops 1612185600 | bytes 2105344 | tf_op jit(solution)/shard_map/dot_general | solution.py:133
  27.2 0.2 reshape.114
  27.4 0.3 concatenate.43
  27.7 0.8 all_to_all.11
  28.5 30.9 %all_to_all.17 = f32[128,1,2176]{2,1,0:T(1,128)S(1)} all-to-all(f32[128,1,2176]{2,1,0:T(1,128)S(1)} %all_to_all.11), channel_id=1, replica_groups=mesh['row'=4,'col'=32] {'row','col'}, dimensions={0} | all-to-all | bytes 2228224 | tf_op jit(solution)/shard_map/all_to_all | solution.py:143
  59.3 0.1 copy.115
  59.4 0.1 fusion.39
  59.5 0.1 slice.134
  59.6 0.1 eq.93
  59.7 0.2 reshape.116
  59.8 0.1 broadcast_in_dim.67
  60.0 0.0 copy-start.14
  60.0 0.2 fusion.17
  60.2 0.6 fusion.6
  60.8 0.1 fusion.44
  60.9 0.1 fusion.45
  61.0 0.1 fusion.42
  61.1 0.1 fusion.43
  61.1 0.1 fusion.34
  61.2 0.1 fusion.31
  61.3 1.5 %convolution_bitcast_fusion = f32[128,8,256]{2,1,0:T(8,128)} fusion(f32[1024]{0:T(1024)S(1)} %eq.93, f32[16,128]{1,0:T(8,128)S(1)} %fusion.34, f32[16,128]{1,0:T(8,128)S(1)} %fusion.31), kind=kOutput, calls=%fused_computation.19 | convolution fusion | flops 25186304 | bytes 1069056 | tf_op jit(solution)/shard_map/dot_general | solution.py:166
  62.8 4.6 %all-to-all-start.1 = ((f32[128,8,256]{2,1,0:T(8,128)}), f32[128,8,256]{2,1,0:T(8,128)S(1)}, u32[]{:S(2)}, u32[]{:S(2)}) async-start(f32[128,8,256]{2,1,0:T(8,128)} %convolution_bitcast_fusion), calls=%async_computation.1 | async-start | bytes 2097152 | tf_op jit(solution)/shard_map/all_to_all | solution.py:169
  67.5 2.8 %gather_fusion = f32[1024,128]{1,0:T(8,128)S(1)} fusion(f32[1024,128]{1,0:T(8,128)S(1)} %reshape.113, s32[1024]{0:T(1024)S(1)} %maximum_clamp_fusion), kind=kCustom, calls=%fused_computation | custom fusion | bytes 1052672 | tf_op jit(solution)/shard_map/gather | solution.py:180
  70.3 0.0 copy-start.1
  70.3 0.0 copy-start.5
  70.3 0.2 copy.93
  70.6 0.8 copy-done.1
  71.3 0.2 copy-done.5
  71.5 0.1 add.77
  71.6 2.8 %gather_fusion.1 = f32[1024,128]{1,0:T(8,128)S(1)} fusion(f32[1024,128]{1,0:T(8,128)S(1)} %reshape.119, s32[1024]{0:T(1024)S(1)} %maximum_clamp_fusion), kind=kCustom, calls=%fused_computation.1 | custom fusion | bytes 1052672 | tf_op jit(solution)/shard_map/gather | solution.py:178
  74.5 1.0 %copy.95 = f32[1024,128]{0,1:T(8,128)} copy(f32[1024,128]{1,0:T(8,128)S(1)} %gather_fusion.1) | data formatting | bytes 1048576 | tf_op jit(solution)/shard_map/gather | solution.py:178
  75.5 4.0 %gather_fusion.2 = f32[1024,128]{1,0:T(8,128)} fusion(f32[1024,128]{1,0:T(8,128)S(1)} %reshape.120, s32[1024]{0:T(1024)S(1)} %maximum_clamp_fusion), kind=kCustom, calls=%fused_computation.2 | custom fusion | bytes 1052672 | tf_op jit(solution)/shard_map/gather | solution.py:179
  79.6 2.1 %copy.97 = f32[1024,128]{0,1:T(8,128)} copy(f32[1024,128]{1,0:T(8,128)} %gather_fusion.2) | data formatting | bytes 1048576 | tf_op jit(solution)/shard_map/gather | solution.py:179
  81.6 5.1 %all-to-all-done.1 = f32[128,8,256]{2,1,0:T(8,128)S(1)} async-done(((f32[128,8,256]{2,1,0:T(8,128)}), f32[128,8,256]{2,1,0:T(8,128)S(1)}, u32[]{:S(2)}, u32[]{:S(2)}) %all-to-all-start.1) | async-done | bytes 1048608 | tf_op jit(solution)/shard_map/all_to_all | solution.py:169
  86.7 1.0 %fusion.40 = (f32[1024,128]{1,0:T(8,128)}, f32[1024,128]{1,0:T(8,128)}) fusion(f32[1024,256]{1,0:T(8,128)S(1)} %bitcast.54), kind=kLoop, calls=%fused_computation.93 | loop fusion | bytes 2097152 | tf_op jit(solution)/shard_map/slice | solution.py:183
  87.8 1.3 %copy.110 = f32[1024,128]{0,1:T(8,128)S(1)} copy(f32[1024,128]{1,0:T(8,128)} %get-tuple-element.28) | data formatting | bytes 1048576
  89.1 2.0 %copy.111 = f32[1024,128]{0,1:T(8,128)} copy(f32[1024,128]{1,0:T(8,128)} %get-tuple-element.29) | data formatting | bytes 1048576
  91.1 1.3 %subtract_multiply_fusion.1 = (f32[1024,128]{0,1:T(8,128)S(1)}, f32[1024,128]{0,1:T(8,128)S(1)}) fusion(f32[1024,128]{0,1:T(8,128)S(1)} %copy.110, f32[1024,128]{0,1:T(8,128)S(1)} %copy-done.7, f32[1024,128]{0,1:T(8,128)S(1)} %copy.93, f32[1024]{0:T(1024)S(1)} %broadcast_maximum_fusion, f32[1024,128]{0,1:T(8,128)} %copy.111, f32[1024,128]{0,1:T(8,128)S(1)} %copy-done.8), kind=kLoop, calls=%fused_computation.36 | loop fusion | flops 786432 | bytes 3674112 | tf_op jit(solution)/shard_map/mul | solution.py:183
  92.4 1.3 %fusion.1 = f32[4,256,256]{2,1,0:T(8,128)S(1)} fusion(s32[1024]{0:T(1024)S(1)} %select_reduce_fusion.2, s32[4,256]{1,0:T(4,128)S(1)} %iota_add_fusion, f32[1024,128]{0,1:T(8,128)S(1)} %get-tuple-element.31, f32[1024,128]{0,1:T(8,128)S(1)} %get-tuple-element.30), kind=kOutput, calls=%fused_computation.5 | convolution fusion | flops 1611923456 | bytes 2105344 | tf_op jit(solution)/shard_map/jyl,lc->jyc/dot_general | solution.py:192
  93.7 0.1 slice_bitcast_fusion.3
  93.8 1.1 %maximum_add_fusion = (f32[256,512]{1,0:T(8,128)}, f32[256,512]{1,0:T(8,128)}) fusion(f32[256,512]{1,0:T(8,128)S(1)} %copy-done.5, f32[256,128]{1,0:T(8,128)S(1)} %get-tuple-element.23, f32[256,128]{1,0:T(8,128)S(1)} %get-tuple-element.24, f32[256,128]{1,0:T(8,128)S(1)} %get-tuple-element.25, f32[256,128]{1,0:T(8,128)S(1)} %get-tuple-element.26, ...), kind=kLoop, calls=%fused_computation.33 | loop fusion | flops 1048576 | bytes 3145728 | tf_op jit(solution)/shard_map/add | solution.py:193
  (49 shorter events, 0.3 us)
Async XLA Ops:
  0.6 1.3 %copy-start.4 = (f32[256,512]{1,0:T(8,128)S(1)}, f32[256,512]{1,0:T(8,128)}, u32[]{:S(2)}) copy-start(f32[256,512]{1,0:T(8,128)} %depth_ref.1) | copy-start | bytes 1572868
  0.6 1.4 %copy-start = (f32[256,512]{1,0:T(8,128)S(1)}, f32[256,512]{1,0:T(8,128)}, u32[]{:S(2)}) copy-start(f32[256,512]{1,0:T(8,128)} %bed_ref.1) | copy-start | bytes 1572868
  2.0 1.0 %copy-start.2 = (f32[256,512]{1,0:T(8,128)S(1)}, f32[256,512]{1,0:T(8,128)}, u32[]{:S(2)}) copy-start(f32[256,512]{1,0:T(8,128)} %mass_ref.1) | copy-start | bytes 1572868
  2.0 1.2 %copy-start.3 = (f32[256,512]{1,0:T(8,128)S(1)}, f32[256,512]{1,0:T(8,128)}, u32[]{:S(2)}) copy-start(f32[256,512]{1,0:T(8,128)} %cond_ref.1) | copy-start | bytes 1572868
  3.2 13.4 %copy-start.11 = (s32[512,1]{0,1:T(1,128)S(1)}, s32[512,1]{0,1:T(1,128)}, u32[]{:S(2)}) copy-start(s32[512,1]{0,1:T(1,128)} %param.20) | copy-start | bytes 6148
  3.2 16.2 %collective-permute-start.1 = (f32[4,512]{1,0:T(4,128)S(1)}, f32[4,512]{1,0:T(4,128)S(1)}, u32[]{:S(2)}, u32[]{:S(2)}) collective-permute-start(f32[4,512]{1,0:T(4,128)S(1)} %bitcast.59), channel_id=1, source_target_pairs={{32,0},{64,32},{96,64},{33,1},{65,33},{97,65},{34,2},{66,34},{98,6... | collective-permute-start | bytes 24584 | tf_op jit(solution)/shard_map/ppermute | solution.py:13
  4.5 14.9 %collective-permute-start = (f32[4,512]{1,0:T(4,128)S(1)}, f32[4,512]{1,0:T(4,128)S(1)}, u32[]{:S(2)}, u32[]{:S(2)}) collective-permute-start(f32[4,512]{1,0:T(4,128)S(1)} %bitcast.60), channel_id=1, source_target_pairs={{0,32},{32,64},{64,96},{1,33},{33,65},{65,97},{2,34},{34,66},{66,9... | collective-permute-start | bytes 24584 | tf_op jit(solution)/shard_map/ppermute | solution.py:13
  9.7 7.6 %copy-start.16 = (s32[512]{0:T(512)S(1)}, s32[512]{0:T(512)}, u32[]{:S(2)}) copy-start(s32[512]{0:T(512)} %param.21) | copy-start | bytes 6148
  9.7 7.7 %copy-start.15 = (f32[512]{0:T(512)S(1)}, f32[512]{0:T(512)}, u32[]{:S(2)}) copy-start(f32[512]{0:T(512)} %param.22) | copy-start | bytes 6148
  9.8 8.3 %copy-start.17 = (s32[512]{0:T(512)S(1)}, s32[512]{0:T(512)}, u32[]{:S(2)}) copy-start(s32[512]{0:T(512)} %param.19) | copy-start | bytes 6148
  9.8 8.8 %collective-permute-start.3 = (f32[4,256]{1,0:T(4,128)S(1)}, f32[4,256]{1,0:T(4,128)S(1)}, u32[]{:S(2)}, u32[]{:S(2)}) collective-permute-start(f32[4,256]{1,0:T(4,128)S(1)} %get-tuple-element.13), channel_id=1, source_target_pairs={{1,0},{2,1},{3,2},{4,3},{5,4},{6,5},{7,6},{8,7},{9,8},{10,9},{11,1... | collective-permute-start | bytes 12296 | tf_op jit(solution)/shard_map/ppermute | solution.py:13
  13.1 5.5 %collective-permute-start.2 = (f32[4,256]{1,0:T(4,128)S(1)}, f32[4,256]{1,0:T(4,128)S(1)}, u32[]{:S(2)}, u32[]{:S(2)}) collective-permute-start(f32[4,256]{1,0:T(4,128)S(1)} %get-tuple-element.12), channel_id=1, source_target_pairs={{0,1},{1,2},{2,3},{3,4},{4,5},{5,6},{6,7},{7,8},{8,9},{9,10},{10,1... | collective-permute-start | bytes 12296 | tf_op jit(solution)/shard_map/ppermute | solution.py:13
  59.9 0.9 copy-start.12
  59.9 0.9 copy-start.13
  60.0 0.9 copy-start.14
  61.2 1.6 %copy-start.9 = (f32[16,128]{1,0:T(8,128)}, f32[16,128]{1,0:T(8,128)S(1)}, u32[]{:S(2)}) copy-start(f32[16,128]{1,0:T(8,128)S(1)} %fusion.34) | copy-start | bytes 24580
  61.3 1.5 %copy-start.10 = (f32[16,128]{1,0:T(8,128)}, f32[16,128]{1,0:T(8,128)S(1)}, u32[]{:S(2)}) copy-start(f32[16,128]{1,0:T(8,128)S(1)} %fusion.31) | copy-start | bytes 24580
  62.8 23.9 %all-to-all-start.1 = ((f32[128,8,256]{2,1,0:T(8,128)}), f32[128,8,256]{2,1,0:T(8,128)S(1)}, u32[]{:S(2)}, u32[]{:S(2)}) async-start(f32[128,8,256]{2,1,0:T(8,128)} %convolution_bitcast_fusion), calls=%async_computation.1 | async-start | bytes 2097152 | tf_op jit(solution)/shard_map/all_to_all | solution.py:169
  70.3 1.0 %copy-start.1 = (f32[256,512]{1,0:T(8,128)S(1)}, f32[256,512]{1,0:T(8,128)}, u32[]{:S(2)}) copy-start(f32[256,512]{1,0:T(8,128)} %bed_ref.1) | copy-start | bytes 1572868
  70.3 1.2 %copy-start.5 = (f32[256,512]{1,0:T(8,128)S(1)}, f32[256,512]{1,0:T(8,128)}, u32[]{:S(2)}) copy-start(f32[256,512]{1,0:T(8,128)} %get-tuple-element.8) | copy-start | bytes 1572868
  74.4 1.0 %copy-start.6 = (f32[256,512]{1,0:T(8,128)S(1)}, f32[256,512]{1,0:T(8,128)}, u32[]{:S(2)}) copy-start(f32[256,512]{1,0:T(8,128)} %get-tuple-element.11) | copy-start | bytes 1572868
  87.8 3.4 %copy-start.7 = (f32[1024,128]{0,1:T(8,128)S(1)}, f32[1024,128]{0,1:T(8,128)}, u32[]{:S(2)}) copy-start(f32[1024,128]{0,1:T(8,128)} %copy.95) | copy-start | bytes 1572868
  87.8 3.4 %copy-start.8 = (f32[1024,128]{0,1:T(8,128)S(1)}, f32[1024,128]{0,1:T(8,128)}, u32[]{:S(2)}) copy-start(f32[1024,128]{0,1:T(8,128)} %copy.97) | copy-start | bytes 1572868

commit v16 on v14

--- a/solution.py
+++ b/solution.py
@@ -154,7 +154,7 @@
         jnp.float32
     )
     totals = jnp.dot(
-        reach_hot, jnp.concatenate([got_ws, got_wm, got_w], axis=1), precision=lax.Precision.HIGHEST
+        reach_hot, jnp.concatenate([got_ws, got_wm, got_w], axis=1), precision=lax.Precision.HIGH
     )
     inflow = totals[:, :128]
     sediment = totals[:, 128:256]
@@ -173,7 +173,9 @@
         concat_axis=0,
         tiled=True,
     )
-    own_rows = answered.reshape(devices * slot_cap, 256)[slot_of]
+    own_rows = jnp.dot(
+        slot_hit.T.astype(jnp.float32), answered.reshape(devices * slot_cap, 256), precision=lax.Precision.HIGH
+    )
     surf_rows = (depth1 + bed).reshape(blocks, 128)[link_block]
     mass_rows = mass1.reshape(blocks, 128)[link_block]
     weight = link_coef[:, None] * opened.reshape(blocks, 128)[link_block]

time: 91.1 us -> 90.9 us (level)
  matrix products: 5.35 us -> 7.21 us
  local copies, waits for them, and re-layouts: 10 us -> 8.26 us
    dot_general x0 -> x1, matrix products: none -> 2.07 us  [body(): jnp.dot(slot_hit.T.astype(jnp.float32), answered.reshape(devices * slot_c...]
    gather x1 -> x0, local copies, waits for them, and re-layouts: 1.56 us -> none  [body(): own_rows = answered.reshape(devices * slot_cap, 256)[slot_of]]
    ppermute x2, starting transfers between devices: 4.64 us -> 3.21 us  [halo_pair(): lax.ppermute(first, axis, backward)]
    all_to_all x1, starting transfers between devices: 4.62 us -> 5.68 us  [body(): lax.all_to_all(reply.reshape(devices, slot_cap, 256), ('row', 'col'), spl...]
  transfers between devices with their start and end apart: 5 -> 5, of which waited for: 1 -> 1; matrix products, arithmetic and copies ran while one was open for 8% -> 7% of each run, Pallas kernels for 0% -> 0%
where the time goes in v16:
time: 90.9 us; the launch traced here: 90.5 us
  blocking collectives  30.4 us (33%)
  starting transfers between devices  17.9 us (20%)
  waiting for transfers between devices  15.1 us (17%)
  local copies, waits for them, and re-layouts  8.26 us (9%)
  matrix products  7.21 us (8%)
  other arithmetic  5.72 us (6%)
  Pallas kernels  4.66 us (5%)
  between operations  1.16 us (1%)
    all_to_all x1, blocking collectives, body(): lax.all_to_all(outgoing, ('row', 'col'), split_axis=0, concat_axis=0, til...  30.4 us
    all_to_all x1, waiting for transfers between devices, body(): lax.all_to_all(reply.reshape(devices, slot_cap, 256), ('row', 'col'), spl...  15.1 us
    ppermute x2, starting transfers between devices, halo_pair(): lax.ppermute(last, axis, forward)  9.05 us
    all_to_all x1, starting transfers between devices, body(): lax.all_to_all(reply.reshape(devices, slot_cap, 256), ('row', 'col'), spl...  5.68 us
    pallas_call x1, Pallas kernels, body(): pl.pallas_call(stencil_kernel, out_shape=[tile, tile] + [block_rows] * 2,...  4.66 us
    ppermute x2, starting transfers between devices, halo_pair(): lax.ppermute(first, axis, backward)  3.21 us
    dot_general x1, matrix products, body(): jnp.dot(slot_hot, jnp.concatenate([open_surf, open_mass], axis=1), precis...  2.49 us
    dot_general x1, matrix products, body(): jnp.dot(slot_hit.T.astype(jnp.float32), answered.reshape(devices * slot_c...  2.07 us
  transfers between devices with their start and end apart: 5, of which 1 were waited for; matrix products, arithmetic and copies ran while one was open for 7% of the time, Pallas kernels for 0%

profile of v16, /device:TPU:1, one launch (start us, length us, event | category | flops | bytes accessed | tf_op | source)
XLA Modules:
  0.0 90.5 jit_solution(16791413630022505050)
XLA Ops:
  0.6 0.0 copy-start
  0.7 1.2 %fusion.45 = (f32[256,512]{1,0:T(8,128)S(1)}, f32[1,256,512]{2,1,0:T(8,128)S(1)}) fusion(s32[256,512]{1,0:T(8,128)} %wet_ref.1), kind=kLoop, calls=%fused_computation.99 | loop fusion | flops 131072 | bytes 1572864 | tf_op jit(solution)/shard_map/convert_element_type | solution.py:97
  1.9 0.1 copy-done.4
  2.0 0.1 add_bitcast_fusion
  2.1 1.0 %copy-done.2 = f32[256,512]{1,0:T(8,128)S(1)} copy-done((f32[256,512]{1,0:T(8,128)S(1)}, f32[256,512]{1,0:T(8,128)}, u32[]{:S(2)}) %copy-start.2) | copy-done | bytes 524312
  3.0 0.2 copy-done.3
  3.2 0.5 maximum_reduce_fusion
  3.7 5.1 %collective-permute-start.2 = (f32[4,256]{1,0:T(4,128)S(1)}, f32[4,256]{1,0:T(4,128)S(1)}, u32[]{:S(2)}, u32[]{:S(2)}) collective-permute-start(f32[4,256]{1,0:T(4,128)S(1)} %get-tuple-element.12), channel_id=1, source_target_pairs={{0,1},{1,2},{2,3},{3,4},{4,5},{5,6},{6,7},{7,8},{8,9},{9,10},{10,1... | collective-permute-start | bytes 12296 | tf_op jit(solution)/shard_map/ppermute | solution.py:13
  8.8 1.9 %collective-permute-start.3 = (f32[4,256]{1,0:T(4,128)S(1)}, f32[4,256]{1,0:T(4,128)S(1)}, u32[]{:S(2)}, u32[]{:S(2)}) collective-permute-start(f32[4,256]{1,0:T(4,128)S(1)} %get-tuple-element.13), channel_id=1, source_target_pairs={{1,0},{2,1},{3,2},{4,3},{5,4},{6,5},{7,6},{8,7},{9,8},{10,9},{11,1... | collective-permute-start | bytes 12296 | tf_op jit(solution)/shard_map/ppermute | solution.py:13
  10.8 1.3 %collective-permute-start.1 = (f32[4,512]{1,0:T(4,128)S(1)}, f32[4,512]{1,0:T(4,128)S(1)}, u32[]{:S(2)}, u32[]{:S(2)}) collective-permute-start(f32[4,512]{1,0:T(4,128)S(1)} %bitcast.60), channel_id=1, source_target_pairs={{32,0},{64,32},{96,64},{33,1},{65,33},{97,65},{34,2},{66,34},{98,6... | collective-permute-start | bytes 24584 | tf_op jit(solution)/shard_map/ppermute | solution.py:13
  12.1 4.0 %collective-permute-start = (f32[4,512]{1,0:T(4,128)S(1)}, f32[4,512]{1,0:T(4,128)S(1)}, u32[]{:S(2)}, u32[]{:S(2)}) collective-permute-start(f32[4,512]{1,0:T(4,128)S(1)} %bitcast.61), channel_id=1, source_target_pairs={{0,32},{32,64},{64,96},{1,33},{33,65},{65,97},{2,34},{34,66},{66,9... | collective-permute-start | bytes 24584 | tf_op jit(solution)/shard_map/ppermute | solution.py:13
  16.1 0.1 copy.85
  16.2 0.2 fusion.24
  16.5 0.1 add_add_fusion
  16.6 0.2 fusion.23
  16.8 0.6 select_reduce_fusion
  17.5 0.4 select_reduce_fusion.1
  17.9 0.1 reshape.107
  18.0 0.1 max.16
  18.1 0.8 copy.83
  18.9 0.6 pad_maximum_fusion.3.rows_ref
  19.5 4.7 %shard_map.156 = (f32[256,512]{1,0:T(8,128)}, f32[256,512]{1,0:T(8,128)}, f32[1024,128]{1,0:T(8,128)}, f32[1024,128]{1,0:T(8,128)}) custom-call(f32[256,512]{1,0:T(8,128)} %depth_ref.1, f32[256,512]{1,0:T(8,128)} %bed_ref.1, f32[256,512]{1,0:T(8,128)} %mass_ref.1, f32[256,512]{1,0:T(8,128)} %cond_ref.1, f32[256,512]{1,0:T(8,128)} %settle_ref.1, ...), custom_call_target="tpu_custom_call" | custom-call | flops 7864320 | bytes 5242880 | tf_op jit(solution)/shard_map/pallas_call | solution.py:108
  24.1 2.5 %fusion.9 = f32[1024,256]{1,0:T(8,128)S(1)} fusion(s32[1024]{0:T(1024)S(1)} %select_reduce_fusion.1, f32[1024,128]{1,0:T(8,128)} %get-tuple-element.10, f32[1024,128]{1,0:T(8,128)} %get-tuple-element.9, f32[1024]{0:T(1024)S(1)} %broadcast_maximum_fusion), kind=kOutput, calls=%fused_computation.17 | convolution fusion | flops 1612185600 | bytes 2105344 | tf_op jit(solution)/shard_map/dot_general | solution.py:133
  26.6 0.2 reshape.106
  26.8 0.3 concatenate.43
  27.1 0.8 all_to_all.11
  27.9 30.4 %all_to_all.17 = f32[128,1,2176]{2,1,0:T(1,128)S(1)} all-to-all(f32[128,1,2176]{2,1,0:T(1,128)S(1)} %all_to_all.11), channel_id=1, replica_groups=mesh['row'=4,'col'=32] {'row','col'}, dimensions={0} | all-to-all | bytes 2228224 | tf_op jit(solution)/shard_map/all_to_all | solution.py:143
  58.3 0.1 copy.104
  58.4 0.1 fusion.44
  58.5 0.1 slice.134
  58.6 0.2 reshape.108
  58.8 0.1 broadcast_in_dim.70
  58.9 0.1 eq.93
  58.9 0.0 copy-start.11
  59.0 0.0 copy-start.12
  59.0 0.2 fusion.20
  59.2 0.4 fusion.5
  59.6 0.1 copy-done.11
  59.6 0.0 copy-done.12
  59.7 0.0 copy-done.13
  59.7 0.1 fusion.47
  59.8 0.1 fusion.46
  59.8 0.1 fusion.49
  59.9 0.1 fusion.48
  60.0 0.1 fusion.36
  60.1 0.1 fusion.39
  60.1 1.5 %convolution_bitcast_fusion = f32[128,8,256]{2,1,0:T(8,128)} fusion(f32[1024]{0:T(1024)S(1)} %eq.93, f32[16,128]{1,0:T(8,128)S(1)} %fusion.39, f32[16,128]{1,0:T(8,128)S(1)} %fusion.36), kind=kOutput, calls=%fused_computation.18 | convolution fusion | flops 25186304 | bytes 1069056 | tf_op jit(solution)/shard_map/dot_general | solution.py:166
  61.7 5.7 %all-to-all-start.1 = ((f32[128,8,256]{2,1,0:T(8,128)}), f32[128,8,256]{2,1,0:T(8,128)}, u32[]{:S(2)}, u32[]{:S(2)}) async-start(f32[128,8,256]{2,1,0:T(8,128)} %convolution_bitcast_fusion), calls=%async_computation.1 | async-start | bytes 2097152 | tf_op jit(solution)/shard_map/all_to_all | solution.py:169
  67.4 0.0 copy-start.1
  67.4 0.0 copy-start.5
  67.4 1.0 %gather_fusion = f32[512,128]{1,0:T(8,128)S(1)} fusion(f32[1024,128]{1,0:T(8,128)S(1)} %reshape.104, s32[1024]{0:T(1024)S(1)} %pad_clamp_fusion), kind=kCustom, calls=%fused_computation | custom fusion | bytes 526336 | tf_op jit(solution)/shard_map/gather | solution.py:181
  68.5 0.1 copy.84
  68.7 0.1 add.80
  68.8 0.0 copy-start.6
  68.8 1.0 %gather_fusion.1 = f32[512,128]{1,0:T(8,128)S(1)} fusion(f32[1024,128]{1,0:T(8,128)S(1)} %reshape.111, s32[1024]{0:T(1024)S(1)} %pad_clamp_fusion), kind=kCustom, calls=%fused_computation.1 | custom fusion | bytes 526336 | tf_op jit(solution)/shard_map/gather | solution.py:179
  69.9 0.1 copy.87
  70.0 1.0 %gather_fusion.2 = f32[512,128]{1,0:T(8,128)S(1)} fusion(f32[1024,128]{1,0:T(8,128)S(1)} %reshape.112, s32[1024]{0:T(1024)S(1)} %pad_clamp_fusion), kind=kCustom, calls=%fused_computation.2 | custom fusion | bytes 526336 | tf_op jit(solution)/shard_map/gather | solution.py:180
  71.1 0.1 copy.88
  71.2 15.1 %all-to-all-done.1 = f32[128,8,256]{2,1,0:T(8,128)} async-done(((f32[128,8,256]{2,1,0:T(8,128)}), f32[128,8,256]{2,1,0:T(8,128)}, u32[]{:S(2)}, u32[]{:S(2)}) %all-to-all-start.1) | async-done | bytes 1048608 | tf_op jit(solution)/shard_map/all_to_all | solution.py:169
  86.3 2.1 %fusion.2 = f32[512,256]{0,1:T(8,128)S(1)} fusion(f32[128,8,256]{2,1,0:T(8,128)} %all-to-all-done.1, s32[512]{0:T(512)S(1)} %multiply_add_fusion), kind=kOutput, calls=%fused_computation.10 | convolution fusion | flops 805830656 | bytes 1574912 | tf_op jit(solution)/shard_map/dot_general | solution.py:176
  88.4 0.1 fusion.22
  88.5 0.8 fusion.3
  89.3 0.1 slice_bitcast_fusion.3
  89.4 1.1 %maximum_add_fusion = (f32[256,512]{1,0:T(8,128)}, f32[256,512]{1,0:T(8,128)}) fusion(f32[256,512]{1,0:T(8,128)S(1)} %copy-done.5, f32[256,128]{1,0:T(8,128)S(1)} %get-tuple-element.23, f32[256,128]{1,0:T(8,128)S(1)} %get-tuple-element.24, f32[256,128]{1,0:T(8,128)S(1)} %get-tuple-element.25, f32[256,128]{1,0:T(8,128)S(1)} %get-tuple-element.26, ...), kind=kLoop, calls=%fused_computation.36 | loop fusion | flops 1048576 | bytes 3145728 | tf_op jit(solution)/shard_map/add | solution.py:194
  (44 shorter events, 0.3 us)
Async XLA Ops:
  0.6 1.3 %copy-start = (f32[256,512]{1,0:T(8,128)S(1)}, f32[256,512]{1,0:T(8,128)}, u32[]{:S(2)}) copy-start(f32[256,512]{1,0:T(8,128)} %bed_ref.1) | copy-start | bytes 1572868
  0.6 1.4 %copy-start.4 = (f32[256,512]{1,0:T(8,128)S(1)}, f32[256,512]{1,0:T(8,128)}, u32[]{:S(2)}) copy-start(f32[256,512]{1,0:T(8,128)} %depth_ref.1) | copy-start | bytes 1572868
  2.0 1.0 %copy-start.2 = (f32[256,512]{1,0:T(8,128)S(1)}, f32[256,512]{1,0:T(8,128)}, u32[]{:S(2)}) copy-start(f32[256,512]{1,0:T(8,128)} %mass_ref.1) | copy-start | bytes 1572868
  2.0 1.2 %copy-start.3 = (f32[256,512]{1,0:T(8,128)S(1)}, f32[256,512]{1,0:T(8,128)}, u32[]{:S(2)}) copy-start(f32[256,512]{1,0:T(8,128)} %cond_ref.1) | copy-start | bytes 1572868
  3.7 12.4 %copy-start.15 = (s32[512]{0:T(512)S(1)}, s32[512]{0:T(512)}, u32[]{:S(2)}) copy-start(s32[512]{0:T(512)} %param.21) | copy-start | bytes 6148
  3.7 12.4 %copy-start.9 = (s32[512,1]{0,1:T(1,128)S(1)}, s32[512,1]{0,1:T(1,128)}, u32[]{:S(2)}) copy-start(s32[512,1]{0,1:T(1,128)} %param.20) | copy-start | bytes 6148
  3.7 14.3 %collective-permute-start.2 = (f32[4,256]{1,0:T(4,128)S(1)}, f32[4,256]{1,0:T(4,128)S(1)}, u32[]{:S(2)}, u32[]{:S(2)}) collective-permute-start(f32[4,256]{1,0:T(4,128)S(1)} %get-tuple-element.12), channel_id=1, source_target_pairs={{0,1},{1,2},{2,3},{3,4},{4,5},{5,6},{6,7},{7,8},{8,9},{9,10},{10,1... | collective-permute-start | bytes 12296 | tf_op jit(solution)/shard_map/ppermute | solution.py:13
  8.8 9.3 %collective-permute-start.3 = (f32[4,256]{1,0:T(4,128)S(1)}, f32[4,256]{1,0:T(4,128)S(1)}, u32[]{:S(2)}, u32[]{:S(2)}) collective-permute-start(f32[4,256]{1,0:T(4,128)S(1)} %get-tuple-element.13), channel_id=1, source_target_pairs={{1,0},{2,1},{3,2},{4,3},{5,4},{6,5},{7,6},{8,7},{9,8},{10,9},{11,1... | collective-permute-start | bytes 12296 | tf_op jit(solution)/shard_map/ppermute | solution.py:13
  10.8 6.1 %copy-start.14 = (f32[512]{0:T(512)S(1)}, f32[512]{0:T(512)}, u32[]{:S(2)}) copy-start(f32[512]{0:T(512)} %param.22) | copy-start | bytes 6148
  10.8 6.7 %copy-start.10 = (s32[512]{0:T(512)S(1)}, s32[512]{0:T(512)}, u32[]{:S(2)}) copy-start(s32[512]{0:T(512)} %param.19) | copy-start | bytes 6148
  10.8 8.1 %collective-permute-start.1 = (f32[4,512]{1,0:T(4,128)S(1)}, f32[4,512]{1,0:T(4,128)S(1)}, u32[]{:S(2)}, u32[]{:S(2)}) collective-permute-start(f32[4,512]{1,0:T(4,128)S(1)} %bitcast.60), channel_id=1, source_target_pairs={{32,0},{64,32},{96,64},{33,1},{65,33},{97,65},{34,2},{66,34},{98,6... | collective-permute-start | bytes 24584 | tf_op jit(solution)/shard_map/ppermute | solution.py:13
  12.1 6.8 %collective-permute-start = (f32[4,512]{1,0:T(4,128)S(1)}, f32[4,512]{1,0:T(4,128)S(1)}, u32[]{:S(2)}, u32[]{:S(2)}) collective-permute-start(f32[4,512]{1,0:T(4,128)S(1)} %bitcast.61), channel_id=1, source_target_pairs={{0,32},{32,64},{64,96},{1,33},{33,65},{65,97},{2,34},{34,66},{66,9... | collective-permute-start | bytes 24584 | tf_op jit(solution)/shard_map/ppermute | solution.py:13
  58.9 0.7 copy-start.11
  59.0 0.7 copy-start.12
  59.0 0.7 copy-start.13
  60.1 1.6 %copy-start.7 = (f32[16,128]{1,0:T(8,128)}, f32[16,128]{1,0:T(8,128)S(1)}, u32[]{:S(2)}) copy-start(f32[16,128]{1,0:T(8,128)S(1)} %fusion.36) | copy-start | bytes 24580
  60.1 1.5 %copy-start.8 = (f32[16,128]{1,0:T(8,128)}, f32[16,128]{1,0:T(8,128)S(1)}, u32[]{:S(2)}) copy-start(f32[16,128]{1,0:T(8,128)S(1)} %fusion.39) | copy-start | bytes 24580
  61.7 24.6 %all-to-all-start.1 = ((f32[128,8,256]{2,1,0:T(8,128)}), f32[128,8,256]{2,1,0:T(8,128)}, u32[]{:S(2)}, u32[]{:S(2)}) async-start(f32[128,8,256]{2,1,0:T(8,128)} %convolution_bitcast_fusion), calls=%async_computation.1 | async-start | bytes 2097152 | tf_op jit(solution)/shard_map/all_to_all | solution.py:169
  67.4 1.2 %copy-start.1 = (f32[256,512]{1,0:T(8,128)S(1)}, f32[256,512]{1,0:T(8,128)}, u32[]{:S(2)}) copy-start(f32[256,512]{1,0:T(8,128)} %bed_ref.1) | copy-start | bytes 1572868
  67.4 1.2 %copy-start.5 = (f32[256,512]{1,0:T(8,128)S(1)}, f32[256,512]{1,0:T(8,128)}, u32[]{:S(2)}) copy-start(f32[256,512]{1,0:T(8,128)} %get-tuple-element.8) | copy-start | bytes 1572868
  68.8 1.2 %copy-start.6 = (f32[256,512]{1,0:T(8,128)S(1)}, f32[256,512]{1,0:T(8,128)}, u32[]{:S(2)}) copy-start(f32[256,512]{1,0:T(8,128)} %get-tuple-element.11) | copy-start | bytes 1572868

commit v17 on v14

--- a/solution.py
+++ b/solution.py
@@ -154,7 +154,7 @@
         jnp.float32
     )
     totals = jnp.dot(
-        reach_hot, jnp.concatenate([got_ws, got_wm, got_w], axis=1), precision=lax.Precision.HIGHEST
+        reach_hot, jnp.concatenate([got_ws, got_wm, got_w], axis=1), precision=lax.Precision.HIGH
     )
     inflow = totals[:, :128]
     sediment = totals[:, 128:256]

time: 91.1 us -> 90.9 us (level)
  no operation moved by 1% of the time
where the time goes in v17:
time: 90.9 us; the launch traced here: 90.5 us
  blocking collectives  30.9 us (34%)
  starting transfers between devices  17.5 us (19%)
  waiting for transfers between devices  15.4 us (17%)
  local copies, waits for them, and re-layouts  10.1 us (11%)
  other arithmetic  5.75 us (6%)
  matrix products  5.11 us (6%)
  Pallas kernels  4.65 us (5%)
  between operations  1.2 us (1%)
    all_to_all x1, blocking collectives, body(): lax.all_to_all(outgoing, ('row', 'col'), split_axis=0, concat_axis=0, til...  30.9 us
    all_to_all x1, waiting for transfers between devices, body(): lax.all_to_all(reply.reshape(devices, slot_cap, 256), ('row', 'col'), spl...  15.4 us
    ppermute x2, starting transfers between devices, halo_pair(): lax.ppermute(last, axis, forward)  8.18 us
    pallas_call x1, Pallas kernels, body(): pl.pallas_call(stencil_kernel, out_shape=[tile, tile] + [block_rows] * 2,...  4.65 us
    ppermute x2, starting transfers between devices, halo_pair(): lax.ppermute(first, axis, backward)  4.64 us
    all_to_all x1, starting transfers between devices, body(): lax.all_to_all(reply.reshape(devices, slot_cap, 256), ('row', 'col'), spl...  4.62 us
    dot_general x1, matrix products, body(): jnp.dot(slot_hot, jnp.concatenate([open_surf, open_mass], axis=1), precis...  2.5 us
  transfers between devices with their start and end apart: 5, of which 1 were waited for; matrix products, arithmetic and copies ran while one was open for 8% of the time, Pallas kernels for 0%

profile of v17, /device:TPU:1, one launch (start us, length us, event | category | flops | bytes accessed | tf_op | source)
XLA Modules:
  0.0 90.5 jit_solution(10360219728747029015)
XLA Ops:
  0.6 0.0 copy-start
  0.7 1.2 %fusion.41 = (f32[256,512]{1,0:T(8,128)S(1)}, f32[1,256,512]{2,1,0:T(8,128)S(1)}) fusion(s32[256,512]{1,0:T(8,128)} %wet_ref.1), kind=kLoop, calls=%fused_computation.98 | loop fusion | flops 131072 | bytes 1572864 | tf_op jit(solution)/shard_map/convert_element_type | solution.py:97
  1.9 0.1 copy-done
  2.0 0.1 add_bitcast_fusion
  2.1 1.0 %copy-done.2 = f32[256,512]{1,0:T(8,128)S(1)} copy-done((f32[256,512]{1,0:T(8,128)S(1)}, f32[256,512]{1,0:T(8,128)}, u32[]{:S(2)}) %copy-start.2) | copy-done | bytes 524312
  3.0 0.2 copy-done.3
  3.2 0.0 copy-start.9
  3.2 1.3 %collective-permute-start.1 = (f32[4,512]{1,0:T(4,128)S(1)}, f32[4,512]{1,0:T(4,128)S(1)}, u32[]{:S(2)}, u32[]{:S(2)}) collective-permute-start(f32[4,512]{1,0:T(4,128)S(1)} %bitcast.63), channel_id=1, source_target_pairs={{32,0},{64,32},{96,64},{33,1},{65,33},{97,65},{34,2},{66,34},{98,6... | collective-permute-start | bytes 24584 | tf_op jit(solution)/shard_map/ppermute | solution.py:13
  4.5 4.7 %collective-permute-start = (f32[4,512]{1,0:T(4,128)S(1)}, f32[4,512]{1,0:T(4,128)S(1)}, u32[]{:S(2)}, u32[]{:S(2)}) collective-permute-start(f32[4,512]{1,0:T(4,128)S(1)} %bitcast.64), channel_id=1, source_target_pairs={{0,32},{32,64},{64,96},{1,33},{33,65},{65,97},{2,34},{34,66},{66,9... | collective-permute-start | bytes 24584 | tf_op jit(solution)/shard_map/ppermute | solution.py:13
  9.2 0.5 maximum_reduce_fusion
  9.8 0.0 copy-start.10
  9.8 3.3 %collective-permute-start.3 = (f32[4,256]{1,0:T(4,128)S(1)}, f32[4,256]{1,0:T(4,128)S(1)}, u32[]{:S(2)}, u32[]{:S(2)}) collective-permute-start(f32[4,256]{1,0:T(4,128)S(1)} %get-tuple-element.13), channel_id=1, source_target_pairs={{1,0},{2,1},{3,2},{4,3},{5,4},{6,5},{7,6},{8,7},{9,8},{10,9},{11,1... | collective-permute-start | bytes 12296 | tf_op jit(solution)/shard_map/ppermute | solution.py:13
  13.1 3.5 %collective-permute-start.2 = (f32[4,256]{1,0:T(4,128)S(1)}, f32[4,256]{1,0:T(4,128)S(1)}, u32[]{:S(2)}, u32[]{:S(2)}) collective-permute-start(f32[4,256]{1,0:T(4,128)S(1)} %get-tuple-element.12), channel_id=1, source_target_pairs={{0,1},{1,2},{2,3},{3,4},{4,5},{5,6},{6,7},{7,8},{8,9},{9,10},{10,1... | collective-permute-start | bytes 12296 | tf_op jit(solution)/shard_map/ppermute | solution.py:13
  16.7 0.1 copy.93
  16.8 0.2 fusion.19
  17.0 0.1 add_add_fusion
  17.1 0.2 fusion.18
  17.4 0.6 select_reduce_fusion
  18.1 0.4 select_reduce_fusion.1
  18.4 0.1 reshape.108
  18.5 0.1 max.16
  18.6 0.8 copy.91
  19.4 0.6 pad_maximum_fusion.3.rows_ref
  20.0 4.7 %shard_map.156 = (f32[256,512]{1,0:T(8,128)}, f32[256,512]{1,0:T(8,128)}, f32[1024,128]{1,0:T(8,128)}, f32[1024,128]{1,0:T(8,128)}) custom-call(f32[256,512]{1,0:T(8,128)} %depth_ref.1, f32[256,512]{1,0:T(8,128)} %bed_ref.1, f32[256,512]{1,0:T(8,128)} %mass_ref.1, f32[256,512]{1,0:T(8,128)} %cond_ref.1, f32[256,512]{1,0:T(8,128)} %settle_ref.1, ...), custom_call_target="tpu_custom_call" | custom-call | flops 7864320 | bytes 5242880 | tf_op jit(solution)/shard_map/pallas_call | solution.py:108
  24.7 2.5 %fusion.8 = f32[1024,256]{1,0:T(8,128)S(1)} fusion(s32[1024]{0:T(1024)S(1)} %select_reduce_fusion.1, f32[1024,128]{1,0:T(8,128)} %get-tuple-element.10, f32[1024,128]{1,0:T(8,128)} %get-tuple-element.9, f32[1024]{0:T(1024)S(1)} %broadcast_maximum_fusion), kind=kOutput, calls=%fused_computation.17 | convolution fusion | flops 1612185600 | bytes 2105344 | tf_op jit(solution)/shard_map/dot_general | solution.py:133
  27.2 0.2 reshape.107
  27.4 0.3 concatenate.43
  27.7 0.8 all_to_all.11
  28.4 30.9 %all_to_all.17 = f32[128,1,2176]{2,1,0:T(1,128)S(1)} all-to-all(f32[128,1,2176]{2,1,0:T(1,128)S(1)} %all_to_all.11), channel_id=1, replica_groups=mesh['row'=4,'col'=32] {'row','col'}, dimensions={0} | all-to-all | bytes 2228224 | tf_op jit(solution)/shard_map/all_to_all | solution.py:143
  59.3 0.1 copy.116
  59.4 0.1 fusion.39
  59.5 0.1 slice.136
  59.6 0.1 eq.93
  59.7 0.2 reshape.109
  59.8 0.1 broadcast_in_dim.71
  59.9 0.0 copy-start.11
  60.0 0.2 fusion.17
  60.2 0.4 fusion.4
  60.5 0.1 copy-done.11
  60.6 0.0 copy-done.12
  60.6 0.0 copy-done.13
  60.7 0.1 fusion.44
  60.7 0.1 fusion.45
  60.8 0.1 fusion.42
  60.9 0.1 fusion.43
  61.0 0.1 fusion.34
  61.0 0.1 fusion.31
  61.1 1.5 %convolution_bitcast_fusion = f32[128,8,256]{2,1,0:T(8,128)} fusion(f32[1024]{0:T(1024)S(1)} %eq.93, f32[16,128]{1,0:T(8,128)S(1)} %fusion.34, f32[16,128]{1,0:T(8,128)S(1)} %fusion.31), kind=kOutput, calls=%fused_computation.18 | convolution fusion | flops 25186304 | bytes 1069056 | tf_op jit(solution)/shard_map/dot_general | solution.py:166
  62.6 4.6 %all-to-all-start.1 = ((f32[128,8,256]{2,1,0:T(8,128)}), f32[128,8,256]{2,1,0:T(8,128)S(1)}, u32[]{:S(2)}, u32[]{:S(2)}) async-start(f32[128,8,256]{2,1,0:T(8,128)} %convolution_bitcast_fusion), calls=%async_computation.1 | async-start | bytes 2097152 | tf_op jit(solution)/shard_map/all_to_all | solution.py:169
  67.3 1.0 %gather_fusion = f32[512,128]{1,0:T(8,128)S(1)} fusion(f32[1024,128]{1,0:T(8,128)S(1)} %reshape.105, s32[1024]{0:T(1024)S(1)} %pad_clamp_fusion.1), kind=kCustom, calls=%fused_computation | custom fusion | bytes 526336 | tf_op jit(solution)/shard_map/gather | solution.py:179
  68.4 0.1 copy.92
  68.6 0.1 add.89
  68.7 1.0 %gather_fusion.2 = f32[512,128]{1,0:T(8,128)S(1)} fusion(f32[1024,128]{1,0:T(8,128)S(1)} %reshape.112, s32[1024]{0:T(1024)S(1)} %pad_clamp_fusion.1), kind=kCustom, calls=%fused_computation.2 | custom fusion | bytes 526336 | tf_op jit(solution)/shard_map/gather | solution.py:177
  69.8 0.1 copy.96
  70.0 1.0 %gather_fusion.3 = f32[512,128]{1,0:T(8,128)S(1)} fusion(f32[1024,128]{1,0:T(8,128)S(1)} %reshape.113, s32[1024]{0:T(1024)S(1)} %pad_clamp_fusion.1), kind=kCustom, calls=%fused_computation.3 | custom fusion | bytes 526336 | tf_op jit(solution)/shard_map/gather | solution.py:178
  71.0 0.1 copy.98
  71.1 15.4 %all-to-all-done.1 = f32[128,8,256]{2,1,0:T(8,128)S(1)} async-done(((f32[128,8,256]{2,1,0:T(8,128)}), f32[128,8,256]{2,1,0:T(8,128)S(1)}, u32[]{:S(2)}, u32[]{:S(2)}) %all-to-all-start.1) | async-done | bytes 1048608 | tf_op jit(solution)/shard_map/all_to_all | solution.py:169
  86.5 1.6 %gather_fusion.1 = f32[512,256]{1,0:T(8,128)S(1)} fusion(f32[1024,256]{1,0:T(8,128)S(1)} %bitcast.50, s32[1024]{0:T(1024)S(1)} %pad_clamp_fusion), kind=kCustom, calls=%fused_computation.1 | custom fusion | bytes 1050624 | tf_op jit(solution)/shard_map/gather | solution.py:176
  88.2 0.1 copy.111
  88.3 0.1 copy.112
  88.4 0.1 subtract_multiply_fusion.1
  88.6 0.8 fusion.2
  89.3 0.1 slice_bitcast_fusion.3
  89.4 1.1 %maximum_add_fusion = (f32[256,512]{1,0:T(8,128)}, f32[256,512]{1,0:T(8,128)}) fusion(f32[256,512]{1,0:T(8,128)S(1)} %copy-done.5, f32[256,128]{1,0:T(8,128)S(1)} %get-tuple-element.23, f32[256,128]{1,0:T(8,128)S(1)} %get-tuple-element.24, f32[256,128]{1,0:T(8,128)S(1)} %get-tuple-element.25, f32[256,128]{1,0:T(8,128)S(1)} %get-tuple-element.26, ...), kind=kLoop, calls=%fused_computation.34 | loop fusion | flops 1048576 | bytes 3145728 | tf_op jit(solution)/shard_map/add | solution.py:192
  (49 shorter events, 0.4 us)
Async XLA Ops:
  0.6 1.3 %copy-start.4 = (f32[256,512]{1,0:T(8,128)S(1)}, f32[256,512]{1,0:T(8,128)}, u32[]{:S(2)}) copy-start(f32[256,512]{1,0:T(8,128)} %depth_ref.1) | copy-start | bytes 1572868
  0.6 1.4 %copy-start = (f32[256,512]{1,0:T(8,128)S(1)}, f32[256,512]{1,0:T(8,128)}, u32[]{:S(2)}) copy-start(f32[256,512]{1,0:T(8,128)} %bed_ref.1) | copy-start | bytes 1572868
  2.0 1.0 %copy-start.2 = (f32[256,512]{1,0:T(8,128)S(1)}, f32[256,512]{1,0:T(8,128)}, u32[]{:S(2)}) copy-start(f32[256,512]{1,0:T(8,128)} %mass_ref.1) | copy-start | bytes 1572868
  2.0 1.2 %copy-start.3 = (f32[256,512]{1,0:T(8,128)S(1)}, f32[256,512]{1,0:T(8,128)}, u32[]{:S(2)}) copy-start(f32[256,512]{1,0:T(8,128)} %cond_ref.1) | copy-start | bytes 1572868
  3.2 13.4 %copy-start.9 = (s32[512,1]{0,1:T(1,128)S(1)}, s32[512,1]{0,1:T(1,128)}, u32[]{:S(2)}) copy-start(s32[512,1]{0,1:T(1,128)} %param.20) | copy-start | bytes 6148
  3.2 16.2 %collective-permute-start.1 = (f32[4,512]{1,0:T(4,128)S(1)}, f32[4,512]{1,0:T(4,128)S(1)}, u32[]{:S(2)}, u32[]{:S(2)}) collective-permute-start(f32[4,512]{1,0:T(4,128)S(1)} %bitcast.63), channel_id=1, source_target_pairs={{32,0},{64,32},{96,64},{33,1},{65,33},{97,65},{34,2},{66,34},{98,6... | collective-permute-start | bytes 24584 | tf_op jit(solution)/shard_map/ppermute | solution.py:13
  4.5 14.9 %collective-permute-start = (f32[4,512]{1,0:T(4,128)S(1)}, f32[4,512]{1,0:T(4,128)S(1)}, u32[]{:S(2)}, u32[]{:S(2)}) collective-permute-start(f32[4,512]{1,0:T(4,128)S(1)} %bitcast.64), channel_id=1, source_target_pairs={{0,32},{32,64},{64,96},{1,33},{33,65},{65,97},{2,34},{34,66},{66,9... | collective-permute-start | bytes 24584 | tf_op jit(solution)/shard_map/ppermute | solution.py:13
  9.7 7.6 %copy-start.15 = (s32[512]{0:T(512)S(1)}, s32[512]{0:T(512)}, u32[]{:S(2)}) copy-start(s32[512]{0:T(512)} %param.21) | copy-start | bytes 6148
  9.7 7.7 %copy-start.14 = (f32[512]{0:T(512)S(1)}, f32[512]{0:T(512)}, u32[]{:S(2)}) copy-start(f32[512]{0:T(512)} %param.22) | copy-start | bytes 6148
  9.8 8.3 %copy-start.10 = (s32[512]{0:T(512)S(1)}, s32[512]{0:T(512)}, u32[]{:S(2)}) copy-start(s32[512]{0:T(512)} %param.19) | copy-start | bytes 6148
  9.8 8.8 %collective-permute-start.3 = (f32[4,256]{1,0:T(4,128)S(1)}, f32[4,256]{1,0:T(4,128)S(1)}, u32[]{:S(2)}, u32[]{:S(2)}) collective-permute-start(f32[4,256]{1,0:T(4,128)S(1)} %get-tuple-element.13), channel_id=1, source_target_pairs={{1,0},{2,1},{3,2},{4,3},{5,4},{6,5},{7,6},{8,7},{9,8},{10,9},{11,1... | collective-permute-start | bytes 12296 | tf_op jit(solution)/shard_map/ppermute | solution.py:13
  13.1 5.5 %collective-permute-start.2 = (f32[4,256]{1,0:T(4,128)S(1)}, f32[4,256]{1,0:T(4,128)S(1)}, u32[]{:S(2)}, u32[]{:S(2)}) collective-permute-start(f32[4,256]{1,0:T(4,128)S(1)} %get-tuple-element.12), channel_id=1, source_target_pairs={{0,1},{1,2},{2,3},{3,4},{4,5},{5,6},{6,7},{7,8},{8,9},{9,10},{10,1... | collective-permute-start | bytes 12296 | tf_op jit(solution)/shard_map/ppermute | solution.py:13
  59.9 0.7 copy-start.11
  59.9 0.7 copy-start.12
  59.9 0.7 copy-start.13
  61.0 1.6 %copy-start.7 = (f32[16,128]{1,0:T(8,128)}, f32[16,128]{1,0:T(8,128)S(1)}, u32[]{:S(2)}) copy-start(f32[16,128]{1,0:T(8,128)S(1)} %fusion.34) | copy-start | bytes 24580
  61.1 1.5 %copy-start.8 = (f32[16,128]{1,0:T(8,128)}, f32[16,128]{1,0:T(8,128)S(1)}, u32[]{:S(2)}) copy-start(f32[16,128]{1,0:T(8,128)S(1)} %fusion.31) | copy-start | bytes 24580
  62.6 23.9 %all-to-all-start.1 = ((f32[128,8,256]{2,1,0:T(8,128)}), f32[128,8,256]{2,1,0:T(8,128)S(1)}, u32[]{:S(2)}, u32[]{:S(2)}) async-start(f32[128,8,256]{2,1,0:T(8,128)} %convolution_bitcast_fusion), calls=%async_computation.1 | async-start | bytes 2097152 | tf_op jit(solution)/shard_map/all_to_all | solution.py:169
  67.3 1.3 %copy-start.1 = (f32[256,512]{1,0:T(8,128)S(1)}, f32[256,512]{1,0:T(8,128)}, u32[]{:S(2)}) copy-start(f32[256,512]{1,0:T(8,128)} %bed_ref.1) | copy-start | bytes 1572868
  67.3 1.3 %copy-start.5 = (f32[256,512]{1,0:T(8,128)S(1)}, f32[256,512]{1,0:T(8,128)}, u32[]{:S(2)}) copy-start(f32[256,512]{1,0:T(8,128)} %get-tuple-element.8) | copy-start | bytes 1572868
  68.7 1.2 %copy-start.6 = (f32[256,512]{1,0:T(8,128)S(1)}, f32[256,512]{1,0:T(8,128)}, u32[]{:S(2)}) copy-start(f32[256,512]{1,0:T(8,128)} %get-tuple-element.11) | copy-start | bytes 1572868
